TPU v7x, 32 devices: a whole 2x2x4 slice. The times are simulated.
32 devices in a mesh: section: 2 (over y), dp: 2 (over x), expert: 8 (over z, core).
Axes of the slice: x: 2, y: 2, z: 4, core: 2. Of those that a mesh axis runs over, the one named last changes fastest.
Arguments:
- activations: bfloat16 [2, 2048, 4096], P('section', ('dp', 'expert')), may hold values from -6 to 6
- norm_gain: float32 [2, 4096], P('section'), may hold values from 0.25 to 1.75
- route_ids: int32 [2, 2048, 2], P('section', ('dp', 'expert')), may hold values from 0 to 3, all different within a row; in each aligned block of 128 rows (0 to 127, 128 to 255, ..., all dimensions but the last counted through in order) at most 72 rows name the same one
- route_gates: float32 [2, 2048, 2], P('section', ('dp', 'expert')), may hold values from 0.2 to 1
- gate_weight: bfloat16 [2, 4096, 3072], P('section', None, 'expert'), may hold values from -0.09375 to 0.09375
- up_weight: bfloat16 [2, 4096, 3072], P('section', None, 'expert'), may hold values from -0.09375 to 0.09375
- leak_rates: float32 [2, 3072], P('section', 'expert'), may hold values from 0.2 to 0.9
- down_weight: bfloat16 [2, 3072, 4096], P('section', 'expert', 'dp'), may hold values from -0.21875 to 0.21875
- cotangent: bfloat16 [2, 2048, 4096], P('section', ('dp', 'expert')), may hold values from -6 to 6
Outputs:
- passed_on: bfloat16 [2, 2048, 4096], P('section', ('dp', 'expert'))
- passed_back: bfloat16 [2, 2048, 4096], P('section', ('dp', 'expert'))
- up_grad: bfloat16 [2, 4096, 3072], P('section', 'dp', 'expert')
Inputs may be any that keep to these rules, and one draw needn't show every extreme that they name: `route_ids`: within one section, the 128 tokens of one device name each expert at most 72 times, and some device reaches 72 for some expert; the two experts of a token differ.
All inputs are finite; a program needn't handle non-finite values.
Results may differ from a plain program's by a relative error of at most 0.015.
Values may be sent and summed in bfloat16 or wider, within the bound.
No kernel may reach another device: no remote copies, remote signals or barrier semaphores. Data moves between devices by JAX's collectives and lax.ppermute only.
A program may use at most 192 MiB of HBM per device.

v0:
```python
import jax
import jax.numpy as jnp
from jax import lax
from jax.sharding import PartitionSpec as P

TSTEPS = 4


EPS = 1e-06
THETA = 0.5
SHARP = 4.0


def passed_along(value, axis, steps):
    count = lax.axis_size(axis)
    leading, last = (max(0, -steps), min(count, count - steps))
    return lax.ppermute(value, axis, [(source, source + steps) for source in range(leading, last)])


def lif_rate(gate_act, up_act, leak_rate):
    drive = jax.nn.silu(gate_act) * up_act
    volts = jnp.zeros_like(drive)
    spike_sum = jnp.zeros_like(drive)
    for timestep in range(TSTEPS):
        volts = leak_rate * volts + drive
        spikes = jax.nn.sigmoid(SHARP * (volts - THETA)) - jax.nn.sigmoid(SHARP * (-volts - THETA))
        volts = volts - THETA * spikes
        spike_sum = spike_sum + spikes
    return spike_sum / TSTEPS


def to_experts(slot_rows):
    model_width = slot_rows.shape[2]
    doubled = jnp.repeat(slot_rows, 2, axis=0)
    gathered = lax.all_to_all(doubled, "expert", split_axis=0, concat_axis=0, tiled=True)
    return gathered.reshape(-1, model_width)


def from_experts(partials, experts, capacity):
    model_width = partials.shape[2]
    returned = lax.all_to_all(
        partials.astype(jnp.bfloat16), "expert", split_axis=0, concat_axis=0, tiled=True
    ).astype(partials.dtype)
    paired = returned.reshape(experts, 2, capacity, model_width)
    summed = jnp.sum(paired, axis=1).astype(jnp.bfloat16)
    return summed.reshape(experts * capacity, model_width).astype(jnp.float32)


def per_device(
    activations,
    norm_gain,
    route_ids,
    route_gates,
    gate_weight,
    up_weight,
    leak_rates,
    down_weight,
    cotangent,
):
    tok_count = activations.shape[1]
    model_width = activations.shape[2]
    experts = lax.axis_size("expert") // 2
    capacity = min(tok_count, 2 * (9 * tok_count // (8 * experts)))
    tokens = activations[0].astype(jnp.float32)
    gain_row = norm_gain[0]
    inv_rms = lax.rsqrt(jnp.mean(tokens * tokens, axis=-1, keepdims=True) + EPS)
    normed = (tokens * inv_rms * gain_row).astype(jnp.bfloat16)
    flat_ids = route_ids[0].reshape(-1)
    onehot = (flat_ids[:, None] == jnp.arange(experts, dtype=jnp.int32)[None, :]).astype(jnp.int32)
    slot_index = jnp.sum(onehot * (jnp.cumsum(onehot, axis=0) - 1), axis=1)
    places = (flat_ids * capacity + slot_index).reshape(tok_count, 2)
    positions = jnp.arange(experts * capacity, dtype=jnp.int32)[:, None]
    pick_first = positions == places[None, :, 0]
    pick_second = positions == places[None, :, 1]
    pick_both = jnp.logical_or(pick_first, pick_second)
    slot_rows = jnp.dot(
        pick_both.astype(jnp.bfloat16), normed, preferred_element_type=jnp.float32
    ).astype(jnp.bfloat16)
    arrived = to_experts(slot_rows.reshape(experts, capacity, model_width))
    gate_local = gate_weight[0]
    up_local = up_weight[0]
    leak_local = leak_rates[0]
    down_full = lax.all_gather(down_weight[0], "dp", axis=1, tiled=True)
    gate_act = jnp.dot(arrived, gate_local, preferred_element_type=jnp.float32)
    up_act = jnp.dot(arrived, up_local, preferred_element_type=jnp.float32)
    spike_rate = lif_rate(gate_act, up_act, leak_local).astype(jnp.bfloat16)
    out_part = jnp.dot(spike_rate, down_full, preferred_element_type=jnp.float32)
    expert_out = from_experts(out_part.reshape(-1, capacity, model_width), experts, capacity)
    weights = route_gates[0]
    mixing = jnp.where(pick_first.T, weights[:, 0:1], 0.0) + jnp.where(
        pick_second.T, weights[:, 1:2], 0.0
    )
    moe_sum = jnp.dot(
        mixing, expert_out, precision=lax.Precision.HIGHEST, preferred_element_type=jnp.float32
    )
    section_out = (tokens + moe_sum).astype(jnp.bfloat16)
    passed_on = passed_along(section_out[None], "section", 1)
    upstream = cotangent[0].astype(jnp.float32)
    grad_first = (weights[:, 0:1] * upstream).astype(jnp.bfloat16)
    grad_second = (weights[:, 1:2] * upstream).astype(jnp.bfloat16)
    grad_slots = jnp.dot(
        pick_first.astype(jnp.bfloat16), grad_first, preferred_element_type=jnp.float32
    )
    grad_slots = grad_slots + jnp.dot(
        pick_second.astype(jnp.bfloat16), grad_second, preferred_element_type=jnp.float32
    )
    grad_rows = to_experts(grad_slots.astype(jnp.bfloat16).reshape(experts, capacity, model_width))
    rate_grad = lax.dot_general(
        grad_rows, down_full, (((1,), (1,)), ((), ())), preferred_element_type=jnp.float32
    )
    unused_rate, pullback = jax.vjp(
        lambda gate_in, up_in: lif_rate(gate_in, up_in, leak_local), gate_act, up_act
    )
    gate_grad, up_act_grad = pullback(rate_grad)
    gate_grad = gate_grad.astype(jnp.bfloat16)
    up_act_grad = up_act_grad.astype(jnp.bfloat16)
    back_part = lax.dot_general(
        gate_grad, gate_local, (((1,), (1,)), ((), ())), preferred_element_type=jnp.float32
    )
    back_part = back_part + lax.dot_general(
        up_act_grad, up_local, (((1,), (1,)), ((), ())), preferred_element_type=jnp.float32
    )
    route_back = from_experts(back_part.reshape(-1, capacity, model_width), experts, capacity)
    norm_grad = (
        jnp.dot(
            pick_both.T.astype(jnp.float32),
            route_back,
            precision=lax.Precision.HIGHEST,
            preferred_element_type=jnp.float32,
        )
        * gain_row
    )
    section_back = (
        upstream
        + inv_rms * norm_grad
        - tokens
        * (inv_rms * inv_rms * inv_rms)
        * jnp.mean(tokens * norm_grad, axis=-1, keepdims=True)
    )
    passed_back = passed_along(section_back.astype(jnp.bfloat16)[None], "section", -1)
    up_term = lax.dot_general(
        arrived, up_act_grad, (((0,), (0,)), ((), ())), preferred_element_type=jnp.float32
    )
    up_term = up_term.astype(jnp.bfloat16).astype(jnp.float32)
    up_grad = lax.psum_scatter(up_term.astype(jnp.bfloat16), "dp", scatter_dimension=0, tiled=True)[
        None
    ]
    return (passed_on, passed_back, up_grad)


def solution(mesh):
    return jax.shard_map(
        per_device,
        mesh=mesh,
        in_specs=(
            P("section", ("dp", "expert"), None),
            P("section", None),
            P("section", ("dp", "expert"), None),
            P("section", ("dp", "expert"), None),
            P("section", None, "expert"),
            P("section", None, "expert"),
            P("section", "expert"),
            P("section", "expert", "dp"),
            P("section", ("dp", "expert"), None),
        ),
        out_specs=(
            P("section", ("dp", "expert"), None),
            P("section", ("dp", "expert"), None),
            P("section", "dp", "expert"),
        ),
        check_vma=False,
    )
```

profile of v0, /device:TPU:0, one launch (start us, length us, event | category | flops | bytes accessed | tf_op | source)
XLA Modules:
  0.0 506.5 jit_solution(14458750092874741639)
XLA Ops:
  7.2 0.0 copy-start
  7.2 0.9 copy.19
  8.1 0.1 eq.74
  8.3 0.1 eq.70
  8.4 1.5 fusion.17
  9.9 1.2 reduce-window.6
  11.2 0.1 slice.26
  11.2 0.1 copy.22
  11.4 0.1 copy.23
  11.5 0.1 add_bitcast_fusion
  11.6 0.1 reduce_sum.48
  11.7 0.2 slice_reduce_fusion.1
  11.9 2.1 convolution_convert_fusion.2
  14.0 2.7 broadcast_in_dim.46
  16.8 6.5 %all-to-all-start = ((bf16[8,72,4096]{2,1,0:T(8,128)(2,1)}), bf16[8,72,4096]{2,1,0:T(8,128)(2,1)}, u32[]{:S(2)}, u32[]{:S(2)}) async-start(bf16[8,72,4096]{2,1,0:T(8,128)(2,1)} %bitcast.94), calls=%async_computation | async-start | bytes 9437184 | tf_op jit(solution)/shard_map/all_to_all | solution.py:35
  23.3 2.2 fusion.28
  25.5 2.3 fusion
  27.7 100.8 %all-to-all-done = bf16[8,72,4096]{2,1,0:T(8,128)(2,1)} async-done(((bf16[8,72,4096]{2,1,0:T(8,128)(2,1)}), bf16[8,72,4096]{2,1,0:T(8,128)(2,1)}, u32[]{:S(2)}, u32[]{:S(2)}) %all-to-all-start) | async-done | bytes 4718624 | tf_op jit(solution)/shard_map/all_to_all | solution.py:35
  128.6 4.4 broadcast_in_dim.48
  133.0 4.7 all-to-all-start.2
  137.7 0.0 all-gather.3.cloned.1.call-start
  137.8 0.7 all-gather.3.cloned.1.call-update
  138.5 6.8 %fusion.7 = f32[576,384]{1,0:T(8,128)} fusion(bf16[576,4096]{1,0:T(8,128)(2,1)} %bitcast.11, bf16[1,4096,384]{2,1,0:T(8,128)(2,1)} %param.14), kind=kOutput, calls=%fused_computation.23 | convolution fusion | flops 1811939328 | bytes 8749056 | tf_op jit(solution)/shard_map/dot_general | solution.py:85
  145.3 6.0 %fusion.11 = f32[576,384]{1,0:T(8,128)} fusion(bf16[576,4096]{1,0:T(8,128)(2,1)} %bitcast.11, bf16[1,4096,384]{2,1,0:T(8,128)(2,1)S(1)} %copy-done), kind=kOutput, calls=%fused_computation.27 | convolution fusion | flops 1811939328 | bytes 8749056 | tf_op jit(solution)/shard_map/dot_general | solution.py:84
  151.3 35.0 %all-gather.3.cloned.1.call-done = bf16[1,384,4096]{2,1,0:T(8,128)(2,1)} async-done(((bf16[1,384,2048]{2,1,0:T(8,128)(2,1)}), bf16[1,384,4096]{2,1,0:T(8,128)(2,1)}) %all-gather.3.cloned.1.call-update) | async-done | bytes 3145744 | tf_op jit(solution)/shard_map/all_gather | solution.py:83
  186.4 9.5 %convolution_convert_fusion = bf16[576,4096]{1,0:T(8,128)(2,1)} fusion(bf16[1,384,4096]{2,1,0:T(8,128)(2,1)} %all-gather.3.cloned.1.call-done, f32[384]{0:T(512)S(1)} %reduce.4, f32[384]{0:T(512)S(1)} %broadcast_multiply_fusion, f32[576,384]{1,0:T(8,128)} %fusion.7, f32[576,384]{1,0:T(8,128)} %fusion.11), kind=kOutput, calls=%fused_computation.1 | convolution fusion | flops 1830002688 | bytes 9636864 | tf_op jit(solution)/shard_map/dot_general | solution.py:87
  195.8 47.1 %all-to-all-done.2 = bf16[8,72,4096]{2,1,0:T(8,128)(2,1)} async-done(((bf16[8,72,4096]{2,1,0:T(8,128)(2,1)}), bf16[8,72,4096]{2,1,0:T(8,128)(2,1)}, u32[]{:S(2)}, u32[]{:S(2)}) %all-to-all-start.2) | async-done | bytes 4718624 | tf_op jit(solution)/shard_map/all_to_all | solution.py:35
  242.9 4.8 all-to-all-start.1
  247.7 10.1 %multiply_convert_fusion = (bf16[576,384]{1,0:T(8,128)(2,1)S(1)}, f32[576,384]{1,0:T(8,128)S(1)}) fusion(f32[576,384]{1,0:T(8,128)} %fusion.11, f32[576,384]{1,0:T(8,128)} %fusion.7, f32[384]{0:T(512)S(1)} %broadcast_multiply_fusion, f32[384]{0:T(512)S(1)} %reduce.4, bf16[576,4096]{1,0:T(8,128)(2,1)} %bitcast.23, ...), kind=kOutput, calls=%fused_computation.87 | convolution fusion | flops 1840693248 | bytes 10963968 | tf_op jit(solution)/shard_map/dot_general | solution.py:108
  257.9 2.7 fusion.9
  260.7 4.4 add_convert_fusion
  265.1 87.9 %all-to-all-done.1 = bf16[8,72,4096]{2,1,0:T(8,128)(2,1)} async-done(((bf16[8,72,4096]{2,1,0:T(8,128)(2,1)}), bf16[8,72,4096]{2,1,0:T(8,128)(2,1)}, u32[]{:S(2)}, u32[]{:S(2)}) %all-to-all-start.1) | async-done | bytes 4718624 | tf_op jit(solution)/shard_map/all_to_all | solution.py:41
  352.9 4.6 all-to-all-start.3
  357.5 0.3 reduce-scatter.2.cloned.1.call-start
  357.8 7.3 %convolution_convert_fusion.1 = bf16[4096,384]{1,0:T(8,128)(2,1)} fusion(bf16[576,4096]{1,0:T(8,128)(2,1)} %bitcast.11, bf16[576,384]{1,0:T(8,128)(2,1)} %copy-done.8), kind=kOutput, calls=%fused_computation.2 | convolution fusion | flops 1813512192 | bytes 8306688 | tf_op jit(solution)/shard_map/dot_general | solution.py:141
  365.2 0.0 reduce-scatter.2.cloned.1.call-update
  365.2 3.7 bitcast_reduce_fusion.1
  368.9 2.9 fusion.2
  371.8 4.5 collective-permute-start
  376.3 86.5 %all-to-all-done.3 = bf16[8,72,4096]{2,1,0:T(8,128)(2,1)} async-done(((bf16[8,72,4096]{2,1,0:T(8,128)(2,1)}), bf16[8,72,4096]{2,1,0:T(8,128)(2,1)}, u32[]{:S(2)}, u32[]{:S(2)}) %all-to-all-start.3) | async-done | bytes 4718624 | tf_op jit(solution)/shard_map/all_to_all | solution.py:41
  462.8 3.7 bitcast_reduce_fusion
  466.5 0.9 fusion.21
  467.3 0.3 copy-done.4
  467.7 0.8 fusion.26
  468.5 1.3 collective-permute-start.1
  469.8 25.3 %collective-permute-done.1 = bf16[1,128,4096]{2,1,0:T(8,128)(2,1)} collective-permute-done((bf16[1,128,4096]{2,1,0:T(8,128)(2,1)S(1)}, bf16[1,128,4096]{2,1,0:T(8,128)(2,1)}, u32[]{:S(2)}, u32[]{:S(2)}) %collective-permute-start.1) | collective-permute-done | bytes 1048608 | tf_op jit(solution)/shard_map/ppermute | solution.py:17
  495.1 2.3 copy.28
  497.4 2.3 copy.29
  (34 shorter events, 0.2 us)
Async XLA Ops:
  7.2 138.2 %copy-start = (bf16[1,4096,384]{2,1,0:T(8,128)(2,1)S(1)}, bf16[1,4096,384]{2,1,0:T(8,128)(2,1)}, u32[]{:S(2)}) copy-start(bf16[1,4096,384]{2,1,0:T(8,128)(2,1)} %param.13) | copy-start | bytes 9437188
  16.8 6.5 %copy-start.11 = (f32[1,128,2]{1,2,0:T(2,128)S(1)}, f32[1,128,2]{1,2,0:T(2,128)}, u32[]{:S(2)}) copy-start(f32[1,128,2]{1,2,0:T(2,128)} %param.12) | copy-start | bytes 3076
  16.8 111.8 %all-to-all-start = ((bf16[8,72,4096]{2,1,0:T(8,128)(2,1)}), bf16[8,72,4096]{2,1,0:T(8,128)(2,1)}, u32[]{:S(2)}, u32[]{:S(2)}) async-start(bf16[8,72,4096]{2,1,0:T(8,128)(2,1)} %bitcast.94), calls=%async_computation | async-start | bytes 9437184 | tf_op jit(solution)/shard_map/all_to_all | solution.py:35
  23.3 2.2 copy-start.3
  133.0 5.5 %copy-start.10 = (f32[1,384]{1,0:T(1,128)S(1)}, f32[1,384]{1,0:T(1,128)}, u32[]{:S(2)}) copy-start(f32[1,384]{1,0:T(1,128)} %param.15) | copy-start | bytes 4612
  133.0 109.9 %all-to-all-start.2 = ((bf16[8,72,4096]{2,1,0:T(8,128)(2,1)}), bf16[8,72,4096]{2,1,0:T(8,128)(2,1)}, u32[]{:S(2)}, u32[]{:S(2)}) async-start(bf16[8,72,4096]{2,1,0:T(8,128)(2,1)} %bitcast.93), calls=%async_computation.2 | async-start | bytes 9437184 | tf_op jit(solution)/shard_map/all_to_all | solution.py:35
  137.7 48.6 %all-gather.3.cloned.1.call-start = ((), (), s32[]{:S(2)}) async-start(), calls=%async_computation.6 | async-start | bytes 4718592 | tf_op jit(solution)/shard_map/all_gather | solution.py:83
  242.9 110.0 %all-to-all-start.1 = ((bf16[8,72,4096]{2,1,0:T(8,128)(2,1)}), bf16[8,72,4096]{2,1,0:T(8,128)(2,1)}, u32[]{:S(2)}, u32[]{:S(2)}) async-start(bf16[8,72,4096]{2,1,0:T(8,128)(2,1)} %bitcast.99), calls=%async_computation.1 | async-start | bytes 9437184 | tf_op jit(solution)/shard_map/all_to_all | solution.py:41
  247.7 10.2 %copy-start.6 = (f32[576,384]{1,0:T(8,128)S(1)}, f32[576,384]{1,0:T(8,128)}, u32[]{:S(2)}) copy-start(f32[576,384]{1,0:T(8,128)} %fusion.7) | copy-start | bytes 2654212
  247.7 10.2 %copy-start.7 = (f32[576,384]{1,0:T(8,128)S(1)}, f32[576,384]{1,0:T(8,128)}, u32[]{:S(2)}) copy-start(f32[576,384]{1,0:T(8,128)} %fusion.11) | copy-start | bytes 2654212
  257.9 2.8 copy-start.8
  257.9 2.7 copy-start.5
  352.9 109.8 %all-to-all-start.3 = ((bf16[8,72,4096]{2,1,0:T(8,128)(2,1)}), bf16[8,72,4096]{2,1,0:T(8,128)(2,1)}, u32[]{:S(2)}, u32[]{:S(2)}) async-start(bf16[8,72,4096]{2,1,0:T(8,128)(2,1)} %bitcast.92), calls=%async_computation.3 | async-start | bytes 9437184 | tf_op jit(solution)/shard_map/all_to_all | solution.py:41
  357.5 137.6 %reduce-scatter.2.cloned.1.call-start = ((), (), s32[]{:S(2)}) async-start(), calls=%async_computation.5 | async-start | bytes 4718592 | tf_op jit(solution)/shard_map/reduce_scatter | solution.py:145
  365.2 3.7 copy-start.1
  371.8 94.7 %copy-start.9 = (f32[1,4096]{1,0:T(1,128)S(1)}, f32[1,4096]{1,0:T(1,128)}, u32[]{:S(2)}) copy-start(f32[1,4096]{1,0:T(1,128)} %param.10) | copy-start | bytes 49156
  371.8 98.0 %collective-permute-start = (bf16[1,128,4096]{2,1,0:T(8,128)(2,1)}, bf16[1,128,4096]{2,1,0:T(8,128)(2,1)}, u32[]{:S(2)}, u32[]{:S(2)}) collective-permute-start(bf16[1,128,4096]{2,1,0:T(8,128)(2,1)} %fusion.2), channel_id=1, source_target_pairs={{0,16},{1,17},{2,18},{3,19},{4,20},{5,21},{6,22},{7,23},{8,24},{9,... | collective-permute-start | bytes 3145736 | tf_op jit(solution)/shard_map/ppermute | solution.py:17
  462.8 3.7 copy-start.2
  466.5 1.2 copy-start.4
  468.5 26.6 %collective-permute-start.1 = (bf16[1,128,4096]{2,1,0:T(8,128)(2,1)S(1)}, bf16[1,128,4096]{2,1,0:T(8,128)(2,1)}, u32[]{:S(2)}, u32[]{:S(2)}) collective-permute-start(bf16[1,128,4096]{2,1,0:T(8,128)(2,1)S(1)} %fusion.26), channel_id=1, source_target_pairs={{16,0},{17,1},{18,2},{19,3},{20,4},{21,5},{22,6},{23,7},{24,8},{25... | collective-permute-start | bytes 3145736 | tf_op jit(solution)/shard_map/ppermute | solution.py:17
Sparse Core Ops, SparseCore 0:
  140.1 46.2 all-gather.2
  365.3 44.5 reduce-scatter.1
where the time goes:
time: 507 us
  waiting for transfers between devices  383 us (76%)
  matrix products  57.2 us (11%)
  starting transfers between devices  26.7 us (5%)
  between operations  14.3 us (3%)
  local copies, waits for them, and re-layouts  13.9 us (3%)
  other arithmetic  11.1 us (2%)
    all_to_all x2, waiting for transfers between devices, from_experts(): lax.all_to_all(partials.astype(jnp.bfloat16), 'expert', split_axis=0, con...  174 us
    all_to_all x2, waiting for transfers between devices, to_experts(): lax.all_to_all(doubled, 'expert', split_axis=0, concat_axis=0, tiled=True)  148 us
    all_gather x1, waiting for transfers between devices, per_device(): down_full = lax.all_gather(down_weight[0], 'dp', axis=1, tiled=True)  35 us
    ppermute x2, waiting for transfers between devices, passed_along(): lax.ppermute(value, axis, [(source, source + steps) for source in range(l...  25.3 us
    all_to_all x2, starting transfers between devices, to_experts(): lax.all_to_all(doubled, 'expert', split_axis=0, concat_axis=0, tiled=True)  11.2 us
  transfers between devices with their start and end apart: 8, of which 6 were waited for; matrix products, arithmetic and copies ran while one was open for 12% of the time, Pallas kernels for 0%

commit v1 on v0

--- a/solution.py
+++ b/solution.py
@@ -1,7 +1,7 @@
 import jax
 import jax.numpy as jnp
 from jax import lax
-from jax.sharding import PartitionSpec as P
+from jax.sharding import Mesh, PartitionSpec as P
 
 TSTEPS = 4
 
@@ -29,21 +29,24 @@
     return spike_sum / TSTEPS
 
 
+def swap_cores(value):
+    return lax.ppermute(value, "core", [(0, 1), (1, 0)])
+
+
 def to_experts(slot_rows):
     model_width = slot_rows.shape[2]
-    doubled = jnp.repeat(slot_rows, 2, axis=0)
-    gathered = lax.all_to_all(doubled, "expert", split_axis=0, concat_axis=0, tiled=True)
-    return gathered.reshape(-1, model_width)
+    mine = lax.all_to_all(slot_rows, "chip", split_axis=0, concat_axis=0, tiled=True)
+    both = jnp.concatenate([mine, swap_cores(mine)], axis=0)
+    return both.reshape(-1, model_width)
 
 
 def from_experts(partials, experts, capacity):
-    model_width = partials.shape[2]
-    returned = lax.all_to_all(
-        partials.astype(jnp.bfloat16), "expert", split_axis=0, concat_axis=0, tiled=True
-    ).astype(partials.dtype)
-    paired = returned.reshape(experts, 2, capacity, model_width)
-    summed = jnp.sum(paired, axis=1).astype(jnp.bfloat16)
-    return summed.reshape(experts * capacity, model_width).astype(jnp.float32)
+    model_width = partials.shape[1]
+    paired = partials.reshape(2, experts, capacity, model_width)
+    other = swap_cores(paired[1].astype(jnp.bfloat16))
+    summed = (paired[0] + other.astype(jnp.float32)).astype(jnp.bfloat16)
+    returned = lax.all_to_all(summed, "chip", split_axis=0, concat_axis=0, tiled=True)
+    return returned.reshape(experts * capacity, model_width).astype(jnp.float32)
 
 
 def per_device(
@@ -59,7 +62,7 @@
 ):
     tok_count = activations.shape[1]
     model_width = activations.shape[2]
-    experts = lax.axis_size("expert") // 2
+    experts = lax.axis_size("chip")
     capacity = min(tok_count, 2 * (9 * tok_count // (8 * experts)))
     tokens = activations[0].astype(jnp.float32)
     gain_row = norm_gain[0]
@@ -85,7 +88,7 @@
     up_act = jnp.dot(arrived, up_local, preferred_element_type=jnp.float32)
     spike_rate = lif_rate(gate_act, up_act, leak_local).astype(jnp.bfloat16)
     out_part = jnp.dot(spike_rate, down_full, preferred_element_type=jnp.float32)
-    expert_out = from_experts(out_part.reshape(-1, capacity, model_width), experts, capacity)
+    expert_out = from_experts(out_part, experts, capacity)
     weights = route_gates[0]
     mixing = jnp.where(pick_first.T, weights[:, 0:1], 0.0) + jnp.where(
         pick_second.T, weights[:, 1:2], 0.0
@@ -120,7 +123,7 @@
     back_part = back_part + lax.dot_general(
         up_act_grad, up_local, (((1,), (1,)), ((), ())), preferred_element_type=jnp.float32
     )
-    route_back = from_experts(back_part.reshape(-1, capacity, model_width), experts, capacity)
+    route_back = from_experts(back_part, experts, capacity)
     norm_grad = (
         jnp.dot(
             pick_both.T.astype(jnp.float32),
@@ -148,25 +151,27 @@
     return (passed_on, passed_back, up_grad)
 
 
+def chip_mesh(mesh):
+    sections, replicas, width = mesh.devices.shape
+    return Mesh(mesh.devices.reshape(sections, replicas, width // 2, 2), ("section", "dp", "chip", "core"))
+
+
 def solution(mesh):
+    tokens = P("section", ("dp", "chip", "core"), None)
     return jax.shard_map(
         per_device,
-        mesh=mesh,
+        mesh=chip_mesh(mesh),
         in_specs=(
-            P("section", ("dp", "expert"), None),
+            tokens,
             P("section", None),
-            P("section", ("dp", "expert"), None),
-            P("section", ("dp", "expert"), None),
-            P("section", None, "expert"),
-            P("section", None, "expert"),
-            P("section", "expert"),
-            P("section", "expert", "dp"),
-            P("section", ("dp", "expert"), None),
+            tokens,
+            tokens,
+            P("section", None, ("chip", "core")),
+            P("section", None, ("chip", "core")),
+            P("section", ("chip", "core")),
+            P("section", ("chip", "core"), "dp"),
+            tokens,
         ),
-        out_specs=(
-            P("section", ("dp", "expert"), None),
-            P("section", ("dp", "expert"), None),
-            P("section", "dp", "expert"),
-        ),
+        out_specs=(tokens, tokens, P("section", "dp", ("chip", "core"))),
         check_vma=False,
     )

time: 507 us -> 333 us (0.66)
  waiting for transfers between devices: 383 us -> 203 us
  other arithmetic: 11.1 us -> 17.1 us
    all_to_all x4, waiting for transfers between devices: 322 us -> 177 us  [the longest x2 102 us: to_experts(): lax.all_to_all(slot_rows, 'chip', split_axis=0, concat_axis=0, tiled=True)]
    all_gather x1, waiting for transfers between devices: 35 us -> 0.01 us  [per_device(): down_full = lax.all_gather(down_weight[0], 'dp', axis=1, tiled=True)]
    convert_element_type x0 -> x2, other arithmetic: none -> 7.45 us  [from_experts(): summed = (paired[0] + other.astype(jnp.float32)).astype(jnp.bfloat16)]
    reduce_sum x2 -> x0, other arithmetic: 7.38 us -> none  [from_experts(): summed = jnp.sum(paired, axis=1).astype(jnp.bfloat16)]
    broadcast_in_dim x2 -> x0, local copies, waits for them, and re-layouts: 7.15 us -> none  [to_experts(): doubled = jnp.repeat(slot_rows, 2, axis=0)]
    concatenate x0 -> x2, other arithmetic: none -> 5.87 us  [to_experts(): both = jnp.concatenate([mine, swap_cores(mine)], axis=0)]
    unnamed x27 -> x35, local copies, waits for them, and re-layouts: 5.91 us -> 11.3 us
  transfers between devices with their start and end apart: 8 -> 12, of which waited for: 6 -> 5; matrix products, arithmetic and copies ran while one was open for 12% -> 20% of each run, Pallas kernels for 0% -> 0%
where the time goes in v1:
time: 333 us; the launch traced here: 332 us
  waiting for transfers between devices  203 us (61%)
  matrix products  54.6 us (16%)
  starting transfers between devices  26.2 us (8%)
  local copies, waits for them, and re-layouts  17.2 us (5%)
  other arithmetic  17.1 us (5%)
  between operations  14.3 us (4%)
    all_to_all x2, waiting for transfers between devices, to_experts(): lax.all_to_all(slot_rows, 'chip', split_axis=0, concat_axis=0, tiled=True)  102 us
    all_to_all x2, waiting for transfers between devices, from_experts(): lax.all_to_all(summed, 'chip', split_axis=0, concat_axis=0, tiled=True)  75.3 us
    ppermute x2, waiting for transfers between devices, passed_along(): lax.ppermute(value, axis, [(source, source + steps) for source in range(l...  24.9 us
    unnamed x35, local copies, waits for them, and re-layouts  11.3 us
    all_to_all x2, starting transfers between devices, to_experts(): lax.all_to_all(slot_rows, 'chip', split_axis=0, concat_axis=0, tiled=True)  11.2 us
    all_to_all x2, starting transfers between devices, from_experts(): lax.all_to_all(summed, 'chip', split_axis=0, concat_axis=0, tiled=True)  9 us
    convert_element_type x2, other arithmetic, from_experts(): summed = (paired[0] + other.astype(jnp.float32)).astype(jnp.bfloat16)  7.45 us
    dot_general x1, matrix products, per_device(): lax.dot_general(up_act_grad, up_local, (((1,), (1,)), ((), ())), preferre...  7.41 us
  transfers between devices with their start and end apart: 12, of which 5 were waited for; matrix products, arithmetic and copies ran while one was open for 20% of the time, Pallas kernels for 0%

profile of v1, /device:TPU:0, one launch (start us, length us, event | category | flops | bytes accessed | tf_op | source)
XLA Modules:
  0.0 332.1 jit_solution(669864996145932222)
XLA Ops:
  7.2 0.9 copy.19
  8.1 0.1 eq.74
  8.3 0.1 eq.70
  8.4 1.5 fusion.18
  9.9 1.2 reduce-window.6
  11.6 0.1 reduce_sum.30
  11.7 0.2 slice_reduce_fusion.1
  11.9 3.5 %convolution_convert_fusion.1 = bf16[288,4096]{1,0:T(8,128)(2,1)} fusion(bf16[1,128,4096]{2,1,0:T(8,128)(2,1)} %param.9, f32[4096]{0:T(1024)} %bitcast.99, f32[128]{0:T(128)S(1)} %get-tuple-element.8, s32[128]{0:T(128)S(1)} %get-tuple-element.4, s32[128]{0:T(128)S(1)} %get-tuple-element.3), kind=kOutput, calls=%fused_computation.4 | convolution fusion | flops 305377280 | bytes 3425792 | tf_op jit(solution)/shard_map/dot_general | solution.py:79
  15.4 6.5 %all-to-all-start = ((bf16[4,72,4096]{2,1,0:T(8,128)(2,1)}), bf16[4,72,4096]{2,1,0:T(8,128)(2,1)}, u32[]{:S(2)}, u32[]{:S(2)}) async-start(bf16[4,72,4096]{2,1,0:T(8,128)(2,1)} %bitcast.90), calls=%async_computation | async-start | bytes 4718592 | tf_op jit(solution)/shard_map/all_to_all | solution.py:38
  21.9 2.2 fusion.29
  24.1 2.3 fusion
  26.4 49.4 %all-to-all-done = bf16[4,72,4096]{2,1,0:T(8,128)(2,1)} async-done(((bf16[4,72,4096]{2,1,0:T(8,128)(2,1)}), bf16[4,72,4096]{2,1,0:T(8,128)(2,1)}, u32[]{:S(2)}, u32[]{:S(2)}) %all-to-all-start) | async-done | bytes 2359328 | tf_op jit(solution)/shard_map/all_to_all | solution.py:38
  75.8 4.7 %all-to-all-start.2 = ((bf16[4,72,4096]{2,1,0:T(8,128)(2,1)}), bf16[4,72,4096]{2,1,0:T(8,128)(2,1)}, u32[]{:S(2)}, u32[]{:S(2)}) async-start(bf16[4,72,4096]{2,1,0:T(8,128)(2,1)} %bitcast.91), calls=%async_computation.2 | async-start | bytes 4718592 | tf_op jit(solution)/shard_map/all_to_all | solution.py:38
  80.5 0.2 all-gather.3.cloned.1.call-start
  80.8 0.4 all-gather.3.cloned.1.call-update
  81.3 52.7 %all-to-all-done.2 = bf16[4,72,4096]{2,1,0:T(8,128)(2,1)} async-done(((bf16[4,72,4096]{2,1,0:T(8,128)(2,1)}), bf16[4,72,4096]{2,1,0:T(8,128)(2,1)}, u32[]{:S(2)}, u32[]{:S(2)}) %all-to-all-start.2) | async-done | bytes 2359328 | tf_op jit(solution)/shard_map/all_to_all | solution.py:38
  134.0 2.9 pad_maximum_fusion
  136.9 0.4 copy-done.6
  137.3 3.5 %fusion.8 = f32[576,384]{1,0:T(8,128)} fusion(bf16[576,4096]{1,0:T(8,128)(2,1)S(1)} %bitcast.92, bf16[1,4096,384]{2,1,0:T(8,128)(2,1)S(1)} %copy-done.6), kind=kOutput, calls=%fused_computation.27 | convolution fusion | flops 1811939328 | bytes 8749056 | tf_op jit(solution)/shard_map/dot_general | solution.py:88
  140.8 3.5 %fusion.12 = f32[576,384]{1,0:T(8,128)} fusion(bf16[576,4096]{1,0:T(8,128)(2,1)S(1)} %bitcast.93, bf16[1,4096,384]{2,1,0:T(8,128)(2,1)S(1)} %copy-done), kind=kOutput, calls=%fused_computation.31 | convolution fusion | flops 1811939328 | bytes 8749056 | tf_op jit(solution)/shard_map/dot_general | solution.py:87
  144.3 7.3 %fusion.5 = f32[576,4096]{1,0:T(8,128)S(1)} fusion(bf16[1,384,4096]{2,1,0:T(8,128)(2,1)} %all-gather.3.cloned.1.call-done, f32[384]{0:T(512)S(1)} %reduce.2, f32[384]{0:T(512)S(1)} %broadcast_multiply_fusion, f32[576,384]{1,0:T(8,128)} %fusion.8, f32[576,384]{1,0:T(8,128)} %fusion.12), kind=kOutput, calls=%fused_computation.24 | convolution fusion | flops 1827643392 | bytes 14355456 | tf_op jit(solution)/shard_map/dot_general | solution.py:90
  151.6 0.3 slice.62
  152.0 3.3 copy-done.2
  155.3 2.9 pad_maximum_fusion.1
  158.3 0.9 copy-done.13
  159.1 7.3 %multiply_convert_fusion = (bf16[576,384]{1,0:T(8,128)(2,1)}, f32[576,384]{1,0:T(8,128)S(1)}) fusion(f32[576,384]{1,0:T(8,128)S(1)} %copy-done.8, f32[576,384]{1,0:T(8,128)S(1)} %copy-done.7, f32[384]{0:T(512)S(1)} %broadcast_multiply_fusion, f32[384]{0:T(512)S(1)} %reduce.2, bf16[576,4096]{1,0:T(8,128)(2,1)S(1)} %bitcast.97, ...), kind=kOutput, calls=%fused_computation.91 | convolution fusion | flops 1840693248 | bytes 10963968 | tf_op jit(solution)/shard_map/dot_general | solution.py:111
  166.4 5.2 %fusion.10 = f32[576,4096]{1,0:T(8,128)} fusion(bf16[1,4096,384]{2,1,0:T(8,128)(2,1)S(1)} %copy-done, f32[576,384]{1,0:T(8,128)S(1)} %copy-done.8, f32[576,384]{1,0:T(8,128)S(1)} %get-tuple-element.10, f32[576,384]{1,0:T(8,128)S(1)} %copy-done.7), kind=kOutput, calls=%fused_computation.29 | convolution fusion | flops 1814372352 | bytes 15237120 | tf_op jit(solution)/shard_map/dot_general | solution.py:120
  171.6 2.2 add_convert_fusion.1
  173.9 4.5 %all-to-all-start.1 = ((bf16[4,72,4096]{2,1,0:T(8,128)(2,1)}), bf16[4,72,4096]{2,1,0:T(8,128)(2,1)}, u32[]{:S(2)}, u32[]{:S(2)}) async-start(bf16[4,72,4096]{2,1,0:T(8,128)(2,1)} %add_convert_fusion.1), calls=%async_computation.1 | async-start | bytes 4718592 | tf_op jit(solution)/shard_map/all_to_all | solution.py:48
  178.4 7.4 %convolution_add_fusion = f32[576,4096]{1,0:T(8,128)S(1)} fusion(f32[576,4096]{1,0:T(8,128)} %fusion.10, bf16[576,384]{1,0:T(8,128)(2,1)} %get-tuple-element.9, bf16[1,4096,384]{2,1,0:T(8,128)(2,1)} %param.14), kind=kOutput, calls=%fused_computation | convolution fusion | flops 1814298624 | bytes 22462464 | tf_op jit(solution)/shard_map/dot_general | solution.py:123
  185.8 1.8 slice.61
  187.7 2.9 slice.53
  190.6 1.0 slice-done.1
  191.5 0.1 slice-done.2
  191.6 0.1 copy-done.9
  191.8 4.6 %convolution_convert_fusion = bf16[4096,384]{1,0:T(8,128)(2,1)} fusion(bf16[576,4096]{1,0:T(8,128)(2,1)S(1)} %bitcast.96, bf16[576,384]{1,0:T(8,128)(2,1)S(1)} %copy-done.9), kind=kOutput, calls=%fused_computation.1 | convolution fusion | flops 1813512192 | bytes 8306688 | tf_op jit(solution)/shard_map/dot_general | solution.py:144
  196.4 5.2 %add_convert_fusion = bf16[4,72,4096]{2,1,0:T(8,128)(2,1)} fusion(f32[4,72,4096]{2,1,0:T(8,128)} %bitcast.89, bf16[4,72,4096]{2,1,0:T(8,128)(2,1)} %collective-permute-done.4), kind=kLoop, calls=%fused_computation.12 | loop fusion | flops 3538944 | bytes 9437184 | tf_op jit(solution)/shard_map/convert_element_type | solution.py:47
  201.7 31.0 %all-to-all-done.1 = bf16[4,72,4096]{2,1,0:T(8,128)(2,1)} async-done(((bf16[4,72,4096]{2,1,0:T(8,128)(2,1)}), bf16[4,72,4096]{2,1,0:T(8,128)(2,1)}, u32[]{:S(2)}, u32[]{:S(2)}) %all-to-all-start.1) | async-done | bytes 2359328 | tf_op jit(solution)/shard_map/all_to_all | solution.py:48
  232.7 4.5 %all-to-all-start.3 = ((bf16[4,72,4096]{2,1,0:T(8,128)(2,1)}), bf16[4,72,4096]{2,1,0:T(8,128)(2,1)}, u32[]{:S(2)}, u32[]{:S(2)}) async-start(bf16[4,72,4096]{2,1,0:T(8,128)(2,1)} %add_convert_fusion), calls=%async_computation.3 | async-start | bytes 4718592 | tf_op jit(solution)/shard_map/all_to_all | solution.py:48
  237.2 4.8 %fusion.2 = bf16[1,128,4096]{2,1,0:T(8,128)(2,1)} fusion(bf16[288,4096]{1,0:T(8,128)(2,1)} %bitcast.16, bf16[1,128,4096]{2,1,0:T(8,128)(2,1)} %param.9, f32[128]{0:T(128)S(1)} %get-tuple-element.6, s32[128]{0:T(128)S(1)} %get-tuple-element.4, f32[128]{0:T(128)S(1)} %get-tuple-element.5, s32[128]{0:T(128)S(1)} %get-tuple-element.3), kind=kOutput, calls=%fused_computation.14 | convolution fusion | flops 1813696512 | bytes 4458496 | tf_op jit(solution)/shard_map/dot_general | solution.py:96
  242.0 4.4 %collective-permute-start.2 = (bf16[1,128,4096]{2,1,0:T(8,128)(2,1)}, bf16[1,128,4096]{2,1,0:T(8,128)(2,1)}, u32[]{:S(2)}, u32[]{:S(2)}) collective-permute-start(bf16[1,128,4096]{2,1,0:T(8,128)(2,1)} %fusion.2), channel_id=1, source_target_pairs={{0,16},{1,17},{2,18},{3,19},{4,20},{5,21},{6,22},{7,23},{8,24},{9,... | collective-permute-start | bytes 3145736 | tf_op jit(solution)/shard_map/ppermute | solution.py:17
  246.4 44.3 %all-to-all-done.3 = bf16[4,72,4096]{2,1,0:T(8,128)(2,1)} async-done(((bf16[4,72,4096]{2,1,0:T(8,128)(2,1)}), bf16[4,72,4096]{2,1,0:T(8,128)(2,1)}, u32[]{:S(2)}, u32[]{:S(2)}) %all-to-all-start.3) | async-done | bytes 2359328 | tf_op jit(solution)/shard_map/all_to_all | solution.py:48
  290.7 2.9 fusion.22
  293.7 0.8 fusion.27
  294.5 1.3 collective-permute-start.5
  295.8 24.9 %collective-permute-done.5 = bf16[1,128,4096]{2,1,0:T(8,128)(2,1)} collective-permute-done((bf16[1,128,4096]{2,1,0:T(8,128)(2,1)S(1)}, bf16[1,128,4096]{2,1,0:T(8,128)(2,1)}, u32[]{:S(2)}, u32[]{:S(2)}) %collective-permute-start.5) | collective-permute-done | bytes 1048608 | tf_op jit(solution)/shard_map/ppermute | solution.py:17
  320.7 2.3 copy.28
  323.0 2.3 copy.29
  (56 shorter events, 0.7 us)
Async XLA Ops:
  7.2 133.6 %copy-start = (bf16[1,4096,384]{2,1,0:T(8,128)(2,1)S(1)}, bf16[1,4096,384]{2,1,0:T(8,128)(2,1)}, u32[]{:S(2)}) copy-start(bf16[1,4096,384]{2,1,0:T(8,128)(2,1)} %param.13) | copy-start | bytes 9437188
  15.4 6.5 %copy-start.12 = (f32[1,128,2]{1,2,0:T(2,128)S(1)}, f32[1,128,2]{1,2,0:T(2,128)}, u32[]{:S(2)}) copy-start(f32[1,128,2]{1,2,0:T(2,128)} %param.12) | copy-start | bytes 3076
  15.4 60.4 %all-to-all-start = ((bf16[4,72,4096]{2,1,0:T(8,128)(2,1)}), bf16[4,72,4096]{2,1,0:T(8,128)(2,1)}, u32[]{:S(2)}, u32[]{:S(2)}) async-start(bf16[4,72,4096]{2,1,0:T(8,128)(2,1)} %bitcast.90), calls=%async_computation | async-start | bytes 4718592 | tf_op jit(solution)/shard_map/all_to_all | solution.py:38
  21.9 2.2 copy-start.3
  75.8 5.4 %copy-start.11 = (f32[1,384]{1,0:T(1,128)S(1)}, f32[1,384]{1,0:T(1,128)}, u32[]{:S(2)}) copy-start(f32[1,384]{1,0:T(1,128)} %param.15) | copy-start | bytes 4612
  75.8 58.1 %all-to-all-start.2 = ((bf16[4,72,4096]{2,1,0:T(8,128)(2,1)}), bf16[4,72,4096]{2,1,0:T(8,128)(2,1)}, u32[]{:S(2)}, u32[]{:S(2)}) async-start(bf16[4,72,4096]{2,1,0:T(8,128)(2,1)} %bitcast.91), calls=%async_computation.2 | async-start | bytes 4718592 | tf_op jit(solution)/shard_map/all_to_all | solution.py:38
  80.5 63.8 %all-gather.3.cloned.1.call-start = ((), (), s32[]{:S(2)}) async-start(), calls=%async_computation.6 | async-start | bytes 4718592 | tf_op jit(solution)/shard_map/all_gather | solution.py:86
  80.8 53.2 %collective-permute-start = (bf16[4,72,4096]{2,1,0:T(8,128)(2,1)}, bf16[4,72,4096]{2,1,0:T(8,128)(2,1)}, u32[]{:S(2)}, u32[]{:S(2)}) collective-permute-start(bf16[4,72,4096]{2,1,0:T(8,128)(2,1)} %all-to-all-done), channel_id=1, source_target_pairs={{0,1},{1,0},{2,3},{3,2},{4,5},{5,4},{6,7},{7,6},{8,9},{9,8},{10,11... | collective-permute-start | bytes 7077896 | tf_op jit(solution)/shard_map/ppermute | solution.py:33
  134.0 3.3 copy-start.6
  134.0 21.3 %collective-permute-start.3 = (bf16[4,72,4096]{2,1,0:T(8,128)(2,1)}, bf16[4,72,4096]{2,1,0:T(8,128)(2,1)}, u32[]{:S(2)}, u32[]{:S(2)}) collective-permute-start(bf16[4,72,4096]{2,1,0:T(8,128)(2,1)} %all-to-all-done.2), channel_id=1, source_target_pairs={{0,1},{1,0},{2,3},{3,2},{4,5},{5,4},{6,7},{7,6},{8,9},{9,8},{10,11... | collective-permute-start | bytes 7077896 | tf_op jit(solution)/shard_map/ppermute | solution.py:33
  136.9 3.9 %copy-start.5 = (bf16[8,72,4096]{2,1,0:T(8,128)(2,1)}, bf16[8,72,4096]{2,1,0:T(8,128)(2,1)S(1)}, u32[]{:S(2)}) copy-start(bf16[8,72,4096]{2,1,0:T(8,128)(2,1)S(1)} %pad_maximum_fusion) | copy-start | bytes 14155780
  151.6 3.7 %copy-start.2 = (f32[576,4096]{1,0:T(8,128)}, f32[576,4096]{1,0:T(8,128)S(1)}, u32[]{:S(2)}) copy-start(f32[576,4096]{1,0:T(8,128)S(1)} %fusion.5) | copy-start | bytes 28311556
  155.3 3.0 copy-start.7
  155.3 3.0 copy-start.8
  155.3 3.8 %copy-start.13 = (bf16[1,384,4096]{2,1,0:T(8,128)(2,1)S(1)}, bf16[1,384,4096]{2,1,0:T(8,128)(2,1)}, u32[]{:S(2)}) copy-start(bf16[1,384,4096]{2,1,0:T(8,128)(2,1)} %all-gather.3.cloned.1.call-done) | copy-start | bytes 9437188
  155.3 16.4 %collective-permute-start.1 = (bf16[4,72,4096]{2,1,0:T(8,128)(2,1)S(1)}, bf16[4,72,4096]{2,1,0:T(8,128)(2,1)S(1)}, u32[]{:S(2)}, u32[]{:S(2)}) collective-permute-start(bf16[4,72,4096]{2,1,0:T(8,128)(2,1)S(1)} %bitcast.98), channel_id=1, source_target_pairs={{0,1},{1,0},{2,3},{3,2},{4,5},{5,4},{6,7},{7,6},{8,9},{9,8},{10,11... | collective-permute-start | bytes 7077896 | tf_op jit(solution)/shard_map/ppermute | solution.py:33
  166.4 5.2 %slice-start = ((f32[576,4096]{1,0:T(8,128)}), f32[288,4096]{1,0:T(8,128)S(1)}, s32[]{:S(2)}) async-start(f32[576,4096]{1,0:T(8,128)} %copy-done.2), calls=%async_computation.7 | async-start | bytes 9437184 | tf_op jit(solution)/shard_map/slice | solution.py:47
  173.9 58.8 %all-to-all-start.1 = ((bf16[4,72,4096]{2,1,0:T(8,128)(2,1)}), bf16[4,72,4096]{2,1,0:T(8,128)(2,1)}, u32[]{:S(2)}, u32[]{:S(2)}) async-start(bf16[4,72,4096]{2,1,0:T(8,128)(2,1)} %add_convert_fusion.1), calls=%async_computation.1 | async-start | bytes 4718592 | tf_op jit(solution)/shard_map/all_to_all | solution.py:48
  178.4 142.3 %reduce-scatter.2.cloned.1.call-start = ((), (), s32[]{:S(2)}) async-start(), calls=%async_computation.5 | async-start | bytes 4718592 | tf_op jit(solution)/shard_map/reduce_scatter | solution.py:148
  187.6 3.9 %slice-start.1 = ((s8[4718592]{0:T(1024)(128)(4,1)}), s8[4194304]{0:T(1024)(128)(4,1)S(1)}, s32[]{:S(2)}) async-start(s8[4718592]{0:T(1024)(128)(4,1)} %bitcast.94), calls=%async_computation.8 | async-start | bytes 8388608
  187.6 4.0 %slice-start.2 = ((s8[4718592]{0:T(1024)(128)(4,1)}), s8[524288]{0:T(1024)(128)(4,1)S(1)}, s32[]{:S(2)}) async-start(s8[4718592]{0:T(1024)(128)(4,1)} %bitcast.94), calls=%async_computation.9 | async-start | bytes 1048576
  187.6 4.1 %copy-start.9 = (bf16[576,384]{1,0:T(8,128)(2,1)S(1)}, bf16[576,384]{1,0:T(8,128)(2,1)}, u32[]{:S(2)}) copy-start(bf16[576,384]{1,0:T(8,128)(2,1)} %get-tuple-element.9) | copy-start | bytes 1327108
  187.6 8.8 %collective-permute-start.4 = (bf16[4,72,4096]{2,1,0:T(8,128)(2,1)}, bf16[4,72,4096]{2,1,0:T(8,128)(2,1)}, u32[]{:S(2)}, u32[]{:S(2)}) collective-permute-start(bf16[4,72,4096]{2,1,0:T(8,128)(2,1)} %bitcast.23), channel_id=1, source_target_pairs={{0,1},{1,0},{2,3},{3,2},{4,5},{5,4},{6,7},{7,6},{8,9},{9,8},{10,11... | collective-permute-start | bytes 7077896 | tf_op jit(solution)/shard_map/ppermute | solution.py:33
  232.7 58.0 %all-to-all-start.3 = ((bf16[4,72,4096]{2,1,0:T(8,128)(2,1)}), bf16[4,72,4096]{2,1,0:T(8,128)(2,1)}, u32[]{:S(2)}, u32[]{:S(2)}) async-start(bf16[4,72,4096]{2,1,0:T(8,128)(2,1)} %add_convert_fusion), calls=%async_computation.3 | async-start | bytes 4718592 | tf_op jit(solution)/shard_map/all_to_all | solution.py:48
  237.2 53.5 %copy-start.10 = (f32[1,4096]{1,0:T(1,128)S(1)}, f32[1,4096]{1,0:T(1,128)}, u32[]{:S(2)}) copy-start(f32[1,4096]{1,0:T(1,128)} %param.10) | copy-start | bytes 49156
  242.0 53.8 %collective-permute-start.2 = (bf16[1,128,4096]{2,1,0:T(8,128)(2,1)}, bf16[1,128,4096]{2,1,0:T(8,128)(2,1)}, u32[]{:S(2)}, u32[]{:S(2)}) collective-permute-start(bf16[1,128,4096]{2,1,0:T(8,128)(2,1)} %fusion.2), channel_id=1, source_target_pairs={{0,16},{1,17},{2,18},{3,19},{4,20},{5,21},{6,22},{7,23},{8,24},{9,... | collective-permute-start | bytes 3145736 | tf_op jit(solution)/shard_map/ppermute | solution.py:17
  290.7 3.0 copy-start.1
  290.7 3.0 copy-start.4
  294.5 26.2 %collective-permute-start.5 = (bf16[1,128,4096]{2,1,0:T(8,128)(2,1)S(1)}, bf16[1,128,4096]{2,1,0:T(8,128)(2,1)}, u32[]{:S(2)}, u32[]{:S(2)}) collective-permute-start(bf16[1,128,4096]{2,1,0:T(8,128)(2,1)S(1)} %fusion.27), channel_id=1, source_target_pairs={{16,0},{17,1},{18,2},{19,3},{20,4},{21,5},{22,6},{23,7},{24,8},{25... | collective-permute-start | bytes 3145736 | tf_op jit(solution)/shard_map/ppermute | solution.py:17
Sparse Core Ops, SparseCore 0:
  82.9 46.2 all-gather.2
  196.5 44.7 reduce-scatter.1

commit v2 on v1

--- a/solution.py
+++ b/solution.py
@@ -33,9 +33,14 @@
     return lax.ppermute(value, "core", [(0, 1), (1, 0)])
 
 
-def to_experts(slot_rows):
-    model_width = slot_rows.shape[2]
-    mine = lax.all_to_all(slot_rows, "chip", split_axis=0, concat_axis=0, tiled=True)
+def shifted(value, steps):
+    count = lax.axis_size("chip")
+    return lax.ppermute(value, "chip", [(source, (source + steps) % count) for source in range(count)])
+
+
+def to_experts(blocks):
+    model_width = blocks.shape[2]
+    mine = jnp.stack([blocks[0]] + [shifted(blocks[k], k) for k in range(1, blocks.shape[0])])
     both = jnp.concatenate([mine, swap_cores(mine)], axis=0)
     return both.reshape(-1, model_width)
 
@@ -45,7 +50,7 @@
     paired = partials.reshape(2, experts, capacity, model_width)
     other = swap_cores(paired[1].astype(jnp.bfloat16))
     summed = (paired[0] + other.astype(jnp.float32)).astype(jnp.bfloat16)
-    returned = lax.all_to_all(summed, "chip", split_axis=0, concat_axis=0, tiled=True)
+    returned = jnp.stack([summed[0]] + [shifted(summed[k], -k) for k in range(1, experts)])
     return returned.reshape(experts * capacity, model_width).astype(jnp.float32)
 
 
@@ -68,7 +73,7 @@
     gain_row = norm_gain[0]
     inv_rms = lax.rsqrt(jnp.mean(tokens * tokens, axis=-1, keepdims=True) + EPS)
     normed = (tokens * inv_rms * gain_row).astype(jnp.bfloat16)
-    flat_ids = route_ids[0].reshape(-1)
+    flat_ids = (route_ids[0].reshape(-1) - lax.axis_index("chip")) % experts
     onehot = (flat_ids[:, None] == jnp.arange(experts, dtype=jnp.int32)[None, :]).astype(jnp.int32)
     slot_index = jnp.sum(onehot * (jnp.cumsum(onehot, axis=0) - 1), axis=1)
     places = (flat_ids * capacity + slot_index).reshape(tok_count, 2)
@@ -107,7 +112,8 @@
     grad_slots = grad_slots + jnp.dot(
         pick_second.astype(jnp.bfloat16), grad_second, preferred_element_type=jnp.float32
     )
-    grad_rows = to_experts(grad_slots.astype(jnp.bfloat16).reshape(experts, capacity, model_width))
+    grad_slots, unused_arrived = lax.optimization_barrier((grad_slots.astype(jnp.bfloat16), arrived))
+    grad_rows = to_experts(grad_slots.reshape(experts, capacity, model_width))
     rate_grad = lax.dot_general(
         grad_rows, down_full, (((1,), (1,)), ((), ())), preferred_element_type=jnp.float32
     )

time: 333 us -> 315 us (0.946)
  the two profiles are of different devices: /device:TPU:0 before, /device:TPU:8 now
where the time goes in v2:
time: 315 us
  waiting for transfers between devices  184 us (58%)
  matrix products  40.8 us (13%)
  starting transfers between devices  29.5 us (9%)
  local copies, waits for them, and re-layouts  28.7 us (9%)
  other arithmetic  17.2 us (5%)
  between operations  14.5 us (5%)
    ppermute x12, waiting for transfers between devices, shifted(): lax.ppermute(value, 'chip', [(source, (source + steps) % count) for sourc...  156 us
    ppermute x2, waiting for transfers between devices, passed_along(): lax.ppermute(value, axis, [(source, source + steps) for source in range(l...  25.4 us
    ppermute x12, starting transfers between devices, shifted(): lax.ppermute(value, 'chip', [(source, (source + steps) % count) for sourc...  23 us
    unnamed x53, local copies, waits for them, and re-layouts  15.8 us
    convert_element_type x2, other arithmetic, from_experts(): summed = (paired[0] + other.astype(jnp.float32)).astype(jnp.bfloat16)  9.35 us
    dot_general x1, matrix products, per_device(): jnp.dot(spike_rate, down_full, preferred_element_type=jnp.float32)  7.3 us
    dot_general x1, matrix products, per_device(): lax.dot_general(grad_rows, down_full, (((1,), (1,)), ((), ())), preferred...  6.51 us
  transfers between devices with their start and end apart: 20, of which 13 were waited for; matrix products, arithmetic and copies ran while one was open for 25% of the time, Pallas kernels for 0%

profile of v2, /device:TPU:8, one launch (start us, length us, event | category | flops | bytes accessed | tf_op | source)
XLA Modules:
  0.0 314.5 jit_solution(9686479693350115958)
XLA Ops:
  9.2 1.5 fusion.18
  10.8 1.2 reduce-window.6
  12.8 2.1 convolution_convert_fusion.1
  14.9 1.4 slice_bitcast_fusion.6
  16.4 3.0 collective-permute-start.1
  19.4 2.5 collective-permute-start
  22.8 2.2 fusion.29
  26.0 32.2 %collective-permute-done.2 = bf16[72,4096]{1,0:T(8,128)(2,1)} collective-permute-done((bf16[72,4096]{1,0:T(8,128)(2,1)}, bf16[72,4096]{1,0:T(8,128)(2,1)}, u32[]{:S(2)}, u32[]{:S(2)}) %collective-permute-start.2) | collective-permute-done | bytes 589856 | tf_op jit(solution)/shard_map/ppermute | solution.py:38
  58.2 11.8 %collective-permute-done = bf16[72,4096]{1,0:T(8,128)(2,1)} collective-permute-done((bf16[72,4096]{1,0:T(8,128)(2,1)}, bf16[72,4096]{1,0:T(8,128)(2,1)}, u32[]{:S(2)}, u32[]{:S(2)}) %collective-permute-start) | collective-permute-done | bytes 589856 | tf_op jit(solution)/shard_map/ppermute | solution.py:38
  70.0 1.7 pad_maximum_fusion
  75.1 1.2 collective-permute-done.3
  76.6 1.4 slice_bitcast_fusion.7
  78.0 1.1 collective-permute-start.11
  79.1 2.8 collective-permute-start.10
  81.9 3.5 %fusion.8 = f32[576,384]{1,0:T(8,128)} fusion(bf16[576,4096]{1,0:T(8,128)(2,1)S(1)} %bitcast.141, bf16[1,4096,384]{2,1,0:T(8,128)(2,1)S(1)} %copy-done.5), kind=kOutput, calls=%fused_computation.25 | convolution fusion | flops 1811939328 | bytes 8749056 | tf_op jit(solution)/shard_map/dot_general | solution.py:93
  85.5 3.5 %fusion.12 = f32[576,384]{1,0:T(8,128)} fusion(bf16[576,4096]{1,0:T(8,128)(2,1)S(1)} %bitcast.142, bf16[1,4096,384]{2,1,0:T(8,128)(2,1)S(1)} %copy-done), kind=kOutput, calls=%fused_computation.29 | convolution fusion | flops 1811939328 | bytes 8749056 | tf_op jit(solution)/shard_map/dot_general | solution.py:92
  89.8 7.3 %fusion.5 = f32[576,4096]{1,0:T(8,128)S(1)} fusion(bf16[1,384,4096]{2,1,0:T(8,128)(2,1)} %all-gather.3.cloned.1.call-done, f32[384]{0:T(512)S(1)} %reduce.2, f32[384]{0:T(512)S(1)} %broadcast_multiply_fusion, f32[576,384]{1,0:T(8,128)} %fusion.8, f32[576,384]{1,0:T(8,128)} %fusion.12), kind=kOutput, calls=%fused_computation.22 | convolution fusion | flops 1827643392 | bytes 14355456 | tf_op jit(solution)/shard_map/dot_general | solution.py:95
  97.1 1.8 slice.164
  99.5 18.0 %collective-permute-done.10 = bf16[72,4096]{1,0:T(8,128)(2,1)} collective-permute-done((bf16[72,4096]{1,0:T(8,128)(2,1)}, bf16[72,4096]{1,0:T(8,128)(2,1)}, u32[]{:S(2)}, u32[]{:S(2)}) %collective-permute-start.10) | collective-permute-done | bytes 589856 | tf_op jit(solution)/shard_map/ppermute | solution.py:38
  117.5 12.5 %collective-permute-done.9 = bf16[72,4096]{1,0:T(8,128)(2,1)} collective-permute-done((bf16[72,4096]{1,0:T(8,128)(2,1)}, bf16[72,4096]{1,0:T(8,128)(2,1)}, u32[]{:S(2)}, u32[]{:S(2)}) %collective-permute-start.9) | collective-permute-done | bytes 589856 | tf_op jit(solution)/shard_map/ppermute | solution.py:38
  130.0 1.7 pad_maximum_fusion.2
  134.0 1.3 constant_dynamic-update-slice_fusion.6
  136.9 6.5 %multiply_convert_fusion = (bf16[576,384]{1,0:T(8,128)(2,1)S(1)}, f32[576,384]{1,0:T(8,128)S(1)}) fusion(f32[576,384]{1,0:T(8,128)S(1)} %copy-done.9, f32[576,384]{1,0:T(8,128)S(1)} %copy-done.8, f32[384]{0:T(512)S(1)} %broadcast_multiply_fusion, f32[384]{0:T(512)S(1)} %reduce.2, bf16[576,4096]{1,0:T(8,128)(2,1)S(1)} %bitcast.138, ...), kind=kOutput, calls=%fused_computation.93 | convolution fusion | flops 1840693248 | bytes 10963968 | tf_op jit(solution)/shard_map/dot_general | solution.py:117
  143.5 2.7 fusion.10
  146.2 4.5 %convolution_add_fusion = f32[576,4096]{1,0:T(8,128)S(1)} fusion(f32[576,4096]{1,0:T(8,128)S(1)} %fusion.10, bf16[576,384]{1,0:T(8,128)(2,1)S(1)} %get-tuple-element.27, bf16[1,4096,384]{2,1,0:T(8,128)(2,1)} %param.14), kind=kOutput, calls=%fused_computation | convolution fusion | flops 1814298624 | bytes 22462464 | tf_op jit(solution)/shard_map/dot_general | solution.py:129
  150.7 1.8 slice.163
  153.0 6.9 %add_convert_fusion.1 = bf16[4,72,4096]{2,1,0:T(8,128)(2,1)} fusion(f32[4,72,4096]{2,1,0:T(8,128)S(1)} %bitcast.127, bf16[4,72,4096]{2,1,0:T(8,128)(2,1)} %collective-permute-done.4), kind=kLoop, calls=%fused_computation.11 | loop fusion | flops 3538944 | bytes 9437184 | tf_op jit(solution)/shard_map/convert_element_type | solution.py:52
  159.9 4.7 %convolution_convert_fusion = bf16[4096,384]{1,0:T(8,128)(2,1)} fusion(bf16[576,4096]{1,0:T(8,128)(2,1)S(1)} %bitcast.145, bf16[576,384]{1,0:T(8,128)(2,1)S(1)} %get-tuple-element.27), kind=kOutput, calls=%fused_computation.1 | convolution fusion | flops 1813512192 | bytes 8306688 | tf_op jit(solution)/shard_map/dot_general | solution.py:150
  164.7 1.8 fusion.111
  166.4 2.5 collective-permute-start.7
  169.0 3.7 %collective-permute-start.6 = (bf16[72,4096]{1,0:T(8,128)(2,1)S(1)}, bf16[72,4096]{1,0:T(8,128)(2,1)S(1)}, u32[]{:S(2)}, u32[]{:S(2)}) collective-permute-start(bf16[72,4096]{1,0:T(8,128)(2,1)S(1)} %get-tuple-element.17), channel_id=1, source_target_pairs={{0,4},{2,6},{4,0},{6,2},{1,5},{3,7},{5,1},{7,3},{8,12},{10,14},{12... | collective-permute-start | bytes 1769480 | tf_op jit(solution)/shard_map/ppermute | solution.py:38
  172.6 2.9 slice-done
  175.5 2.4 add_convert_fusion
  178.1 1.8 collective-permute-start.16
  179.9 1.5 collective-permute-start.15
  181.5 3.0 collective-permute-done.7
  184.4 4.0 %collective-permute-start.14 = (bf16[72,4096]{1,0:T(8,128)(2,1)S(1)}, bf16[72,4096]{1,0:T(8,128)(2,1)S(1)}, u32[]{:S(2)}, u32[]{:S(2)}) collective-permute-start(bf16[72,4096]{1,0:T(8,128)(2,1)S(1)} %get-tuple-element.10), channel_id=1, source_target_pairs={{0,6},{2,0},{4,2},{6,4},{1,7},{3,1},{5,3},{7,5},{8,14},{10,8},{12,... | collective-permute-start | bytes 1769480 | tf_op jit(solution)/shard_map/ppermute | solution.py:38
  188.4 32.2 %collective-permute-done.6 = bf16[72,4096]{1,0:T(8,128)(2,1)S(1)} collective-permute-done((bf16[72,4096]{1,0:T(8,128)(2,1)S(1)}, bf16[72,4096]{1,0:T(8,128)(2,1)S(1)}, u32[]{:S(2)}, u32[]{:S(2)}) %collective-permute-start.6) | collective-permute-done | bytes 589856 | tf_op jit(solution)/shard_map/ppermute | solution.py:38
  220.6 28.7 %collective-permute-done.5 = bf16[72,4096]{1,0:T(8,128)(2,1)S(1)} collective-permute-done((bf16[72,4096]{1,0:T(8,128)(2,1)S(1)}, bf16[72,4096]{1,0:T(8,128)(2,1)S(1)}, u32[]{:S(2)}, u32[]{:S(2)}) %collective-permute-start.5) | collective-permute-done | bytes 589856 | tf_op jit(solution)/shard_map/ppermute | solution.py:38
  250.5 1.9 fusion.2
  252.4 4.4 %collective-permute-start.8 = (bf16[1,128,4096]{2,1,0:T(8,128)(2,1)S(1)}, bf16[1,128,4096]{2,1,0:T(8,128)(2,1)}, u32[]{:S(2)}, u32[]{:S(2)}) collective-permute-start(bf16[1,128,4096]{2,1,0:T(8,128)(2,1)S(1)} %fusion.2), channel_id=1, source_target_pairs={{0,16},{1,17},{2,18},{3,19},{4,20},{5,21},{6,22},{7,23},{8,24},{9,... | collective-permute-start | bytes 3145736 | tf_op jit(solution)/shard_map/ppermute | solution.py:17
  256.8 1.7 collective-permute-done.16
  258.5 12.2 %collective-permute-done.15 = bf16[72,4096]{1,0:T(8,128)(2,1)S(1)} collective-permute-done((bf16[72,4096]{1,0:T(8,128)(2,1)S(1)}, bf16[72,4096]{1,0:T(8,128)(2,1)S(1)}, u32[]{:S(2)}, u32[]{:S(2)}) %collective-permute-start.15) | collective-permute-done | bytes 589856 | tf_op jit(solution)/shard_map/ppermute | solution.py:38
  270.7 3.4 %collective-permute-done.14 = bf16[72,4096]{1,0:T(8,128)(2,1)S(1)} collective-permute-done((bf16[72,4096]{1,0:T(8,128)(2,1)S(1)}, bf16[72,4096]{1,0:T(8,128)(2,1)S(1)}, u32[]{:S(2)}, u32[]{:S(2)}) %collective-permute-start.14) | collective-permute-done | bytes 589856 | tf_op jit(solution)/shard_map/ppermute | solution.py:38
  276.4 1.3 collective-permute-start.17
  277.7 25.4 %collective-permute-done.17 = bf16[1,128,4096]{2,1,0:T(8,128)(2,1)} collective-permute-done((bf16[1,128,4096]{2,1,0:T(8,128)(2,1)S(1)}, bf16[1,128,4096]{2,1,0:T(8,128)(2,1)}, u32[]{:S(2)}, u32[]{:S(2)}) %collective-permute-start.17) | collective-permute-done | bytes 1048608 | tf_op jit(solution)/shard_map/ppermute | solution.py:17
  303.1 2.3 copy.32
  305.4 2.3 copy.33
  (103 shorter events, 17.8 us)
Async XLA Ops:
  7.2 78.3 %copy-start = (bf16[1,4096,384]{2,1,0:T(8,128)(2,1)S(1)}, bf16[1,4096,384]{2,1,0:T(8,128)(2,1)}, u32[]{:S(2)}) copy-start(bf16[1,4096,384]{2,1,0:T(8,128)(2,1)} %param.13) | copy-start | bytes 9437188
  7.2 5.6 %copy-start.11 = (f32[1,4096]{1,0:T(1,128)S(1)}, f32[1,4096]{1,0:T(1,128)}, u32[]{:S(2)}) copy-start(f32[1,4096]{1,0:T(1,128)} %param.10) | copy-start | bytes 49156
  7.2 82.6 %all-gather.3.cloned.1.call-start = ((), (), s32[]{:S(2)}) async-start(), calls=%async_computation.2 | async-start | bytes 4718592 | tf_op jit(solution)/shard_map/all_gather | solution.py:91
  7.9 295.2 %reduce-scatter.2.cloned.1.call-start = ((), (), s32[]{:S(2)}) async-start(), calls=%async_computation.1 | async-start | bytes 4718592 | tf_op jit(solution)/shard_map/reduce_scatter | solution.py:154
  14.9 7.8 %copy-start.13 = (f32[1,128,2]{1,2,0:T(2,128)S(1)}, f32[1,128,2]{1,2,0:T(2,128)}, u32[]{:S(2)}) copy-start(f32[1,128,2]{1,2,0:T(2,128)} %param.12) | copy-start | bytes 3076
  14.9 7.8 %copy-start.12 = (f32[1,384]{1,0:T(1,128)S(1)}, f32[1,384]{1,0:T(1,128)}, u32[]{:S(2)}) copy-start(f32[1,384]{1,0:T(1,128)} %param.15) | copy-start | bytes 4612
  16.4 41.8 %collective-permute-start.2 = (bf16[72,4096]{1,0:T(8,128)(2,1)}, bf16[72,4096]{1,0:T(8,128)(2,1)}, u32[]{:S(2)}, u32[]{:S(2)}) collective-permute-start(bf16[72,4096]{1,0:T(8,128)(2,1)} %get-tuple-element.20), channel_id=1, source_target_pairs={{0,6},{2,0},{4,2},{6,4},{1,7},{3,1},{5,3},{7,5},{8,14},{10,8},{12,... | collective-permute-start | bytes 1769480 | tf_op jit(solution)/shard_map/ppermute | solution.py:38
  16.4 41.8 %collective-permute-start.1 = (bf16[72,4096]{1,0:T(8,128)(2,1)}, bf16[72,4096]{1,0:T(8,128)(2,1)}, u32[]{:S(2)}, u32[]{:S(2)}) collective-permute-start(bf16[72,4096]{1,0:T(8,128)(2,1)} %get-tuple-element.21), channel_id=1, source_target_pairs={{0,4},{2,6},{4,0},{6,2},{1,5},{3,7},{5,1},{7,3},{8,12},{10,14},{12... | collective-permute-start | bytes 1769480 | tf_op jit(solution)/shard_map/ppermute | solution.py:38
  19.4 50.6 %collective-permute-start = (bf16[72,4096]{1,0:T(8,128)(2,1)}, bf16[72,4096]{1,0:T(8,128)(2,1)}, u32[]{:S(2)}, u32[]{:S(2)}) collective-permute-start(bf16[72,4096]{1,0:T(8,128)(2,1)} %get-tuple-element.22), channel_id=1, source_target_pairs={{0,2},{2,4},{4,6},{6,0},{1,3},{3,5},{5,7},{7,1},{8,10},{10,12},{12... | collective-permute-start | bytes 1769480 | tf_op jit(solution)/shard_map/ppermute | solution.py:38
  22.8 2.3 copy-start.3
  22.8 49.0 %slice-start.3 = ((s8[4718592]{0:T(1024)(128)(4,1)}), s8[4194304]{0:T(1024)(128)(4,1)S(1)}, s32[]{:S(2)}) async-start(s8[4718592]{0:T(1024)(128)(4,1)} %bitcast.139), calls=%async_computation.6 | async-start | bytes 8388608
  25.0 45.0 %copy-start.7 = (bf16[1,72,4096]{2,1,0:T(8,128)(2,1)S(1)}, bf16[1,72,4096]{2,1,0:T(8,128)(2,1)}, u32[]{:S(2)}) copy-start(bf16[1,72,4096]{2,1,0:T(8,128)(2,1)} %get-tuple-element.19) | copy-start | bytes 1769476
  25.0 46.7 %slice-start.4 = ((s8[4718592]{0:T(1024)(128)(4,1)}), s8[524288]{0:T(1024)(128)(4,1)S(1)}, s32[]{:S(2)}) async-start(s8[4718592]{0:T(1024)(128)(4,1)} %bitcast.139), calls=%async_computation.7 | async-start | bytes 1048576
  71.7 4.6 %collective-permute-start.3 = (bf16[4,72,4096]{2,1,0:T(8,128)(2,1)S(1)}, bf16[4,72,4096]{2,1,0:T(8,128)(2,1)S(1)}, u32[]{:S(2)}, u32[]{:S(2)}) collective-permute-start(bf16[4,72,4096]{2,1,0:T(8,128)(2,1)S(1)} %pad_maximum_fusion), channel_id=1, source_target_pairs={{0,1},{1,0},{2,3},{3,2},{4,5},{5,4},{6,7},{7,6},{8,9},{9,8},{10,11... | collective-permute-start | bytes 7077896 | tf_op jit(solution)/shard_map/ppermute | solution.py:33
  76.6 8.9 %copy-start.10 = (bf16[8,72,4096]{2,1,0:T(8,128)(2,1)}, bf16[8,72,4096]{2,1,0:T(8,128)(2,1)S(1)}, u32[]{:S(2)}) copy-start(bf16[8,72,4096]{2,1,0:T(8,128)(2,1)S(1)} %constant_dynamic-update-slice_fusion) | copy-start | bytes 14155780
  76.6 5.4 %copy-start.5 = (bf16[1,4096,384]{2,1,0:T(8,128)(2,1)S(1)}, bf16[1,4096,384]{2,1,0:T(8,128)(2,1)}, u32[]{:S(2)}) copy-start(bf16[1,4096,384]{2,1,0:T(8,128)(2,1)} %param.14) | copy-start | bytes 9437188
  78.0 21.5 %collective-permute-start.11 = (bf16[72,4096]{1,0:T(8,128)(2,1)}, bf16[72,4096]{1,0:T(8,128)(2,1)}, u32[]{:S(2)}, u32[]{:S(2)}) collective-permute-start(bf16[72,4096]{1,0:T(8,128)(2,1)} %get-tuple-element.12), channel_id=1, source_target_pairs={{0,6},{2,0},{4,2},{6,4},{1,7},{3,1},{5,3},{7,5},{8,14},{10,8},{12,... | collective-permute-start | bytes 1769480 | tf_op jit(solution)/shard_map/ppermute | solution.py:38
  79.1 38.3 %collective-permute-start.10 = (bf16[72,4096]{1,0:T(8,128)(2,1)}, bf16[72,4096]{1,0:T(8,128)(2,1)}, u32[]{:S(2)}, u32[]{:S(2)}) collective-permute-start(bf16[72,4096]{1,0:T(8,128)(2,1)} %get-tuple-element.13), channel_id=1, source_target_pairs={{0,4},{2,6},{4,0},{6,2},{1,5},{3,7},{5,1},{7,3},{8,12},{10,14},{12... | collective-permute-start | bytes 1769480 | tf_op jit(solution)/shard_map/ppermute | solution.py:38
  81.9 48.1 %collective-permute-start.9 = (bf16[72,4096]{1,0:T(8,128)(2,1)}, bf16[72,4096]{1,0:T(8,128)(2,1)}, u32[]{:S(2)}, u32[]{:S(2)}) collective-permute-start(bf16[72,4096]{1,0:T(8,128)(2,1)} %get-tuple-element.14), channel_id=1, source_target_pairs={{0,2},{2,4},{4,6},{6,0},{1,3},{3,5},{5,7},{7,1},{8,10},{10,12},{12... | collective-permute-start | bytes 1769480 | tf_op jit(solution)/shard_map/ppermute | solution.py:38
  97.1 34.7 %slice-start.1 = ((s8[4718592]{0:T(1024)(128)(4,1)}), s8[4194304]{0:T(1024)(128)(4,1)S(1)}, s32[]{:S(2)}) async-start(s8[4718592]{0:T(1024)(128)(4,1)} %bitcast.136), calls=%async_computation.4 | async-start | bytes 8388608
  98.9 31.1 %copy-start.6 = (bf16[1,72,4096]{2,1,0:T(8,128)(2,1)S(1)}, bf16[1,72,4096]{2,1,0:T(8,128)(2,1)}, u32[]{:S(2)}) copy-start(bf16[1,72,4096]{2,1,0:T(8,128)(2,1)} %get-tuple-element.11) | copy-start | bytes 1769476
  98.9 32.9 %slice-start.2 = ((s8[4718592]{0:T(1024)(128)(4,1)}), s8[524288]{0:T(1024)(128)(4,1)S(1)}, s32[]{:S(2)}) async-start(s8[4718592]{0:T(1024)(128)(4,1)} %bitcast.136), calls=%async_computation.5 | async-start | bytes 1048576
  99.4 53.6 %collective-permute-start.4 = (bf16[4,72,4096]{2,1,0:T(8,128)(2,1)}, bf16[4,72,4096]{2,1,0:T(8,128)(2,1)}, u32[]{:S(2)}, u32[]{:S(2)}) collective-permute-start(bf16[4,72,4096]{2,1,0:T(8,128)(2,1)} %bitcast.18), channel_id=1, source_target_pairs={{0,1},{1,0},{2,3},{3,2},{4,5},{5,4},{6,7},{7,6},{8,9},{9,8},{10,11... | collective-permute-start | bytes 7077896 | tf_op jit(solution)/shard_map/ppermute | solution.py:33
  131.7 4.6 %collective-permute-start.12 = (bf16[4,72,4096]{2,1,0:T(8,128)(2,1)S(1)}, bf16[4,72,4096]{2,1,0:T(8,128)(2,1)S(1)}, u32[]{:S(2)}, u32[]{:S(2)}) collective-permute-start(bf16[4,72,4096]{2,1,0:T(8,128)(2,1)S(1)} %pad_maximum_fusion.2), channel_id=1, source_target_pairs={{0,1},{1,0},{2,3},{3,2},{4,5},{5,4},{6,7},{7,6},{8,9},{9,8},{10,11... | collective-permute-start | bytes 7077896 | tf_op jit(solution)/shard_map/ppermute | solution.py:33
  134.0 2.4 copy-start.14
  135.3 1.4 copy-start.8
  135.3 1.6 copy-start.9
  150.7 9.2 %copy-start.1 = (f32[576,4096]{1,0:T(8,128)}, f32[576,4096]{1,0:T(8,128)S(1)}, u32[]{:S(2)}) copy-start(f32[576,4096]{1,0:T(8,128)S(1)} %convolution_add_fusion) | copy-start | bytes 28311556
  150.7 9.2 %slice-start.5 = ((s8[4718592]{0:T(1024)(128)(4,1)}), s8[4194304]{0:T(1024)(128)(4,1)S(1)}, s32[]{:S(2)}) async-start(s8[4718592]{0:T(1024)(128)(4,1)} %bitcast.143), calls=%async_computation.8 | async-start | bytes 8388608
  152.5 20.1 %collective-permute-start.13 = (bf16[4,72,4096]{2,1,0:T(8,128)(2,1)}, bf16[4,72,4096]{2,1,0:T(8,128)(2,1)}, u32[]{:S(2)}, u32[]{:S(2)}) collective-permute-start(bf16[4,72,4096]{2,1,0:T(8,128)(2,1)} %bitcast.35), channel_id=1, source_target_pairs={{0,1},{1,0},{2,3},{3,2},{4,5},{5,4},{6,7},{7,6},{8,9},{9,8},{10,11... | collective-permute-start | bytes 7077896 | tf_op jit(solution)/shard_map/ppermute | solution.py:33
  153.0 6.9 %slice-start.6 = ((s8[4718592]{0:T(1024)(128)(4,1)}), s8[524288]{0:T(1024)(128)(4,1)S(1)}, s32[]{:S(2)}) async-start(s8[4718592]{0:T(1024)(128)(4,1)} %bitcast.143), calls=%async_computation.9 | async-start | bytes 1048576
  166.4 18.0 %collective-permute-start.7 = (bf16[72,4096]{1,0:T(8,128)(2,1)S(1)}, bf16[72,4096]{1,0:T(8,128)(2,1)S(1)}, u32[]{:S(2)}, u32[]{:S(2)}) collective-permute-start(bf16[72,4096]{1,0:T(8,128)(2,1)S(1)} %get-tuple-element.16), channel_id=1, source_target_pairs={{0,2},{2,4},{4,6},{6,0},{1,3},{3,5},{5,7},{7,1},{8,10},{10,12},{12... | collective-permute-start | bytes 1769480 | tf_op jit(solution)/shard_map/ppermute | solution.py:38
  169.0 51.6 %collective-permute-start.6 = (bf16[72,4096]{1,0:T(8,128)(2,1)S(1)}, bf16[72,4096]{1,0:T(8,128)(2,1)S(1)}, u32[]{:S(2)}, u32[]{:S(2)}) collective-permute-start(bf16[72,4096]{1,0:T(8,128)(2,1)S(1)} %get-tuple-element.17), channel_id=1, source_target_pairs={{0,4},{2,6},{4,0},{6,2},{1,5},{3,7},{5,1},{7,3},{8,12},{10,14},{12... | collective-permute-start | bytes 1769480 | tf_op jit(solution)/shard_map/ppermute | solution.py:38
  172.6 76.6 %collective-permute-start.5 = (bf16[72,4096]{1,0:T(8,128)(2,1)S(1)}, bf16[72,4096]{1,0:T(8,128)(2,1)S(1)}, u32[]{:S(2)}, u32[]{:S(2)}) collective-permute-start(bf16[72,4096]{1,0:T(8,128)(2,1)S(1)} %get-tuple-element.18), channel_id=1, source_target_pairs={{0,6},{2,0},{4,2},{6,4},{1,7},{3,1},{5,3},{7,5},{8,14},{10,8},{12,... | collective-permute-start | bytes 1769480 | tf_op jit(solution)/shard_map/ppermute | solution.py:38
  172.6 2.9 slice-start
  178.1 80.4 %collective-permute-start.16 = (bf16[72,4096]{1,0:T(8,128)(2,1)S(1)}, bf16[72,4096]{1,0:T(8,128)(2,1)S(1)}, u32[]{:S(2)}, u32[]{:S(2)}) collective-permute-start(bf16[72,4096]{1,0:T(8,128)(2,1)S(1)} %get-tuple-element.8), channel_id=1, source_target_pairs={{0,2},{2,4},{4,6},{6,0},{1,3},{3,5},{5,7},{7,1},{8,10},{10,12},{12... | collective-permute-start | bytes 1769480 | tf_op jit(solution)/shard_map/ppermute | solution.py:38
  179.9 90.8 %collective-permute-start.15 = (bf16[72,4096]{1,0:T(8,128)(2,1)S(1)}, bf16[72,4096]{1,0:T(8,128)(2,1)S(1)}, u32[]{:S(2)}, u32[]{:S(2)}) collective-permute-start(bf16[72,4096]{1,0:T(8,128)(2,1)S(1)} %get-tuple-element.9), channel_id=1, source_target_pairs={{0,4},{2,6},{4,0},{6,2},{1,5},{3,7},{5,1},{7,3},{8,12},{10,14},{12... | collective-permute-start | bytes 1769480 | tf_op jit(solution)/shard_map/ppermute | solution.py:38
  184.4 89.6 %collective-permute-start.14 = (bf16[72,4096]{1,0:T(8,128)(2,1)S(1)}, bf16[72,4096]{1,0:T(8,128)(2,1)S(1)}, u32[]{:S(2)}, u32[]{:S(2)}) collective-permute-start(bf16[72,4096]{1,0:T(8,128)(2,1)S(1)} %get-tuple-element.10), channel_id=1, source_target_pairs={{0,6},{2,0},{4,2},{6,4},{1,7},{3,1},{5,3},{7,5},{8,14},{10,8},{12,... | collective-permute-start | bytes 1769480 | tf_op jit(solution)/shard_map/ppermute | solution.py:38
  249.3 1.2 copy-start.2
  252.4 25.3 %collective-permute-start.8 = (bf16[1,128,4096]{2,1,0:T(8,128)(2,1)S(1)}, bf16[1,128,4096]{2,1,0:T(8,128)(2,1)}, u32[]{:S(2)}, u32[]{:S(2)}) collective-permute-start(bf16[1,128,4096]{2,1,0:T(8,128)(2,1)S(1)} %fusion.2), channel_id=1, source_target_pairs={{0,16},{1,17},{2,18},{3,19},{4,20},{5,21},{6,22},{7,23},{8,24},{9,... | collective-permute-start | bytes 3145736 | tf_op jit(solution)/shard_map/ppermute | solution.py:17
  274.4 1.2 copy-start.4
  276.4 26.7 %collective-permute-start.17 = (bf16[1,128,4096]{2,1,0:T(8,128)(2,1)S(1)}, bf16[1,128,4096]{2,1,0:T(8,128)(2,1)}, u32[]{:S(2)}, u32[]{:S(2)}) collective-permute-start(bf16[1,128,4096]{2,1,0:T(8,128)(2,1)S(1)} %fusion.27), channel_id=1, source_target_pairs={{16,0},{17,1},{18,2},{19,3},{20,4},{21,5},{22,6},{23,7},{24,8},{25... | collective-permute-start | bytes 3145736 | tf_op jit(solution)/shard_map/ppermute | solution.py:17
Sparse Core Ops, SparseCore 0:
  9.5 46.0 all-gather.2
  164.8 44.9 reduce-scatter.1

commit v3 on v2

--- a/solution.py
+++ b/solution.py
@@ -45,11 +45,15 @@
     return both.reshape(-1, model_width)
 
 
-def from_experts(partials, experts, capacity):
+def combine_cores(partials, experts, capacity):
     model_width = partials.shape[1]
     paired = partials.reshape(2, experts, capacity, model_width)
     other = swap_cores(paired[1].astype(jnp.bfloat16))
-    summed = (paired[0] + other.astype(jnp.float32)).astype(jnp.bfloat16)
+    return (paired[0] + other.astype(jnp.float32)).astype(jnp.bfloat16)
+
+
+def from_experts(summed):
+    experts, capacity, model_width = summed.shape
     returned = jnp.stack([summed[0]] + [shifted(summed[k], -k) for k in range(1, experts)])
     return returned.reshape(experts * capacity, model_width).astype(jnp.float32)
 
@@ -93,16 +97,8 @@
     up_act = jnp.dot(arrived, up_local, preferred_element_type=jnp.float32)
     spike_rate = lif_rate(gate_act, up_act, leak_local).astype(jnp.bfloat16)
     out_part = jnp.dot(spike_rate, down_full, preferred_element_type=jnp.float32)
-    expert_out = from_experts(out_part, experts, capacity)
+    out_summed = combine_cores(out_part, experts, capacity)
     weights = route_gates[0]
-    mixing = jnp.where(pick_first.T, weights[:, 0:1], 0.0) + jnp.where(
-        pick_second.T, weights[:, 1:2], 0.0
-    )
-    moe_sum = jnp.dot(
-        mixing, expert_out, precision=lax.Precision.HIGHEST, preferred_element_type=jnp.float32
-    )
-    section_out = (tokens + moe_sum).astype(jnp.bfloat16)
-    passed_on = passed_along(section_out[None], "section", 1)
     upstream = cotangent[0].astype(jnp.float32)
     grad_first = (weights[:, 0:1] * upstream).astype(jnp.bfloat16)
     grad_second = (weights[:, 1:2] * upstream).astype(jnp.bfloat16)
@@ -114,6 +110,16 @@
     )
     grad_slots, unused_arrived = lax.optimization_barrier((grad_slots.astype(jnp.bfloat16), arrived))
     grad_rows = to_experts(grad_slots.reshape(experts, capacity, model_width))
+    grad_rows, out_summed = lax.optimization_barrier((grad_rows, out_summed))
+    expert_out = from_experts(out_summed)
+    mixing = jnp.where(pick_first.T, weights[:, 0:1], 0.0) + jnp.where(
+        pick_second.T, weights[:, 1:2], 0.0
+    )
+    moe_sum = jnp.dot(
+        mixing, expert_out, precision=lax.Precision.HIGHEST, preferred_element_type=jnp.float32
+    )
+    section_out = (tokens + moe_sum).astype(jnp.bfloat16)
+    passed_on = passed_along(section_out[None], "section", 1)
     rate_grad = lax.dot_general(
         grad_rows, down_full, (((1,), (1,)), ((), ())), preferred_element_type=jnp.float32
     )
@@ -129,7 +135,7 @@
     back_part = back_part + lax.dot_general(
         up_act_grad, up_local, (((1,), (1,)), ((), ())), preferred_element_type=jnp.float32
     )
-    route_back = from_experts(back_part, experts, capacity)
+    route_back = from_experts(combine_cores(back_part, experts, capacity))
     norm_grad = (
         jnp.dot(
             pick_both.T.astype(jnp.float32),

time: 315 us -> 315 us (level)
  the two profiles are of different devices: /device:TPU:8 before, /device:TPU:0 now
where the time goes in v3:
time: 315 us; the launch traced here: 314 us
  waiting for transfers between devices  140 us (44%)
  starting transfers between devices  74.8 us (24%)
  matrix products  41.3 us (13%)
  local copies, waits for them, and re-layouts  31.1 us (10%)
  between operations  14.5 us (5%)
  other arithmetic  12.9 us (4%)
    ppermute x12, waiting for transfers between devices, shifted(): lax.ppermute(value, 'chip', [(source, (source + steps) % count) for sourc...  114 us
    ppermute x12, starting transfers between devices, shifted(): lax.ppermute(value, 'chip', [(source, (source + steps) % count) for sourc...  68.3 us
    ppermute x2, waiting for transfers between devices, passed_along(): lax.ppermute(value, axis, [(source, source + steps) for source in range(l...  24.9 us
    unnamed x53, local copies, waits for them, and re-layouts  22.3 us
    dot_general x1, matrix products, per_device(): jnp.dot(spike_rate, down_full, preferred_element_type=jnp.float32)  7.3 us
    dot_general x1, matrix products, per_device(): lax.dot_general(arrived, up_act_grad, (((0,), (0,)), ((), ())), preferred...  7.18 us
    dot_general x1, matrix products, per_device(): lax.dot_general(grad_rows, down_full, (((1,), (1,)), ((), ())), preferred...  6.52 us
  transfers between devices with their start and end apart: 20, of which 8 were waited for; matrix products, arithmetic and copies ran while one was open for 16% of the time, Pallas kernels for 0%

profile of v3, /device:TPU:0, one launch (start us, length us, event | category | flops | bytes accessed | tf_op | source)
XLA Modules:
  0.0 314.4 jit_solution(13996394498284377739)
XLA Ops:
  8.5 1.2 reduce-window.6
  10.5 1.5 fusion.18
  12.0 2.1 convolution_convert_fusion.1
  14.1 1.5 slice_bitcast_fusion.3
  16.4 3.1 collective-permute-start
  19.4 2.6 collective-permute-start.1
  22.0 1.3 collective-permute-start.2
  23.4 1.9 constant_dynamic-update-slice_fusion.4
  25.4 2.2 fusion.29
  28.6 7.5 %collective-permute-done = bf16[72,4096]{1,0:T(8,128)(2,1)} collective-permute-done((bf16[72,4096]{1,0:T(8,128)(2,1)}, bf16[72,4096]{1,0:T(8,128)(2,1)}, u32[]{:S(2)}, u32[]{:S(2)}) %collective-permute-start) | collective-permute-done | bytes 589856 | tf_op jit(solution)/shard_map/ppermute | solution.py:38
  36.1 24.4 %collective-permute-done.1 = bf16[72,4096]{1,0:T(8,128)(2,1)} collective-permute-done((bf16[72,4096]{1,0:T(8,128)(2,1)}, bf16[72,4096]{1,0:T(8,128)(2,1)}, u32[]{:S(2)}, u32[]{:S(2)}) %collective-permute-start.1) | collective-permute-done | bytes 589856 | tf_op jit(solution)/shard_map/ppermute | solution.py:38
  60.5 1.7 pad_maximum_fusion
  62.3 1.1 constant_dynamic-update-slice_fusion.3
  63.4 1.1 constant_dynamic-update-slice_fusion.2
  64.6 1.1 constant_dynamic-update-slice_fusion.1
  65.7 1.2 collective-permute-done.3
  67.1 1.5 slice_bitcast_fusion.7
  68.6 13.1 %collective-permute-start.4 = (bf16[72,4096]{1,0:T(8,128)(2,1)}, bf16[72,4096]{1,0:T(8,128)(2,1)}, u32[]{:S(2)}, u32[]{:S(2)}) collective-permute-start(bf16[72,4096]{1,0:T(8,128)(2,1)} %get-tuple-element.22), channel_id=1, source_target_pairs={{0,2},{2,4},{4,6},{6,0},{1,3},{3,5},{5,7},{7,1},{8,10},{10,12},{12... | collective-permute-start | bytes 1769480 | tf_op jit(solution)/shard_map/ppermute | solution.py:38
  81.7 1.6 collective-permute-start.5
  84.1 3.5 %fusion.12 = f32[576,384]{1,0:T(8,128)} fusion(bf16[576,4096]{1,0:T(8,128)(2,1)S(1)} %bitcast.142, bf16[1,4096,384]{2,1,0:T(8,128)(2,1)S(1)} %copy-done), kind=kOutput, calls=%fused_computation.26 | convolution fusion | flops 1811939328 | bytes 8749056 | tf_op jit(solution)/shard_map/dot_general | solution.py:96
  87.6 3.5 %fusion.8 = f32[576,384]{1,0:T(8,128)} fusion(bf16[576,4096]{1,0:T(8,128)(2,1)S(1)} %bitcast.143, bf16[1,4096,384]{2,1,0:T(8,128)(2,1)S(1)} %copy-done.6), kind=kOutput, calls=%fused_computation.22 | convolution fusion | flops 1811939328 | bytes 8749056 | tf_op jit(solution)/shard_map/dot_general | solution.py:97
  92.0 7.3 %fusion.5 = f32[576,4096]{1,0:T(8,128)S(1)} fusion(bf16[1,384,4096]{2,1,0:T(8,128)(2,1)} %all-gather.3.cloned.1.call-done, f32[384]{0:T(512)S(1)} %reduce.2, f32[384]{0:T(512)S(1)} %broadcast_multiply_fusion, f32[576,384]{1,0:T(8,128)} %fusion.8, f32[576,384]{1,0:T(8,128)} %fusion.12), kind=kOutput, calls=%fused_computation.19 | convolution fusion | flops 1827643392 | bytes 14355456 | tf_op jit(solution)/shard_map/dot_general | solution.py:99
  100.2 21.8 %collective-permute-done.5 = bf16[72,4096]{1,0:T(8,128)(2,1)} collective-permute-done((bf16[72,4096]{1,0:T(8,128)(2,1)}, bf16[72,4096]{1,0:T(8,128)(2,1)}, u32[]{:S(2)}, u32[]{:S(2)}) %collective-permute-start.5) | collective-permute-done | bytes 589856 | tf_op jit(solution)/shard_map/ppermute | solution.py:38
  122.1 1.7 pad_maximum_fusion.1
  123.9 1.1 constant_dynamic-update-slice_fusion.8
  125.0 1.1 constant_dynamic-update-slice_fusion.7
  126.1 1.1 constant_dynamic-update-slice_fusion.6
  127.3 2.1 add_convert_fusion.1
  130.9 6.5 %multiply_convert_fusion = (bf16[576,384]{1,0:T(8,128)(2,1)S(1)}, f32[576,384]{1,0:T(8,128)S(1)}) fusion(f32[576,384]{1,0:T(8,128)S(1)} %copy-done.10, f32[576,384]{1,0:T(8,128)S(1)} %copy-done.11, f32[384]{0:T(512)S(1)} %broadcast_multiply_fusion, f32[384]{0:T(512)S(1)} %reduce.2, bf16[576,4096]{1,0:T(8,128)(2,1)S(1)} %bitcast.139, ...), kind=kOutput, calls=%fused_computation.93 | convolution fusion | flops 1840693248 | bytes 10963968 | tf_op jit(solution)/shard_map/dot_general | solution.py:123
  137.4 2.7 fusion.10
  140.2 2.6 convolution_add_fusion
  142.8 3.6 %copy-done.1 = f32[576,4096]{1,0:T(8,128)} copy-done((f32[576,4096]{1,0:T(8,128)}, f32[576,4096]{1,0:T(8,128)S(1)}, u32[]{:S(2)}) %copy-start.1) | copy-done | bytes 9437208
  146.5 1.7 slice.159
  148.6 7.2 %convolution_convert_fusion = bf16[4096,384]{1,0:T(8,128)(2,1)} fusion(bf16[576,4096]{1,0:T(8,128)(2,1)} %bitcast.144, bf16[576,384]{1,0:T(8,128)(2,1)S(1)} %get-tuple-element.31), kind=kOutput, calls=%fused_computation.1 | convolution fusion | flops 1813512192 | bytes 8306688 | tf_op jit(solution)/shard_map/dot_general | solution.py:156
  155.8 1.8 fusion.111
  157.6 13.9 %collective-permute-start.9 = (bf16[72,4096]{1,0:T(8,128)(2,1)S(1)}, bf16[72,4096]{1,0:T(8,128)(2,1)S(1)}, u32[]{:S(2)}, u32[]{:S(2)}) collective-permute-start(bf16[72,4096]{1,0:T(8,128)(2,1)S(1)} %get-tuple-element.18), channel_id=1, source_target_pairs={{0,6},{2,0},{4,2},{6,4},{1,7},{3,1},{5,3},{7,5},{8,14},{10,8},{12,... | collective-permute-start | bytes 1769480 | tf_op jit(solution)/shard_map/ppermute | solution.py:38
  172.3 3.0 add_convert_fusion
  175.4 4.0 %collective-permute-start.14 = (bf16[72,4096]{1,0:T(8,128)(2,1)S(1)}, bf16[72,4096]{1,0:T(8,128)(2,1)S(1)}, u32[]{:S(2)}, u32[]{:S(2)}) collective-permute-start(bf16[72,4096]{1,0:T(8,128)(2,1)S(1)} %get-tuple-element.14), channel_id=1, source_target_pairs={{0,6},{2,0},{4,2},{6,4},{1,7},{3,1},{5,3},{7,5},{8,14},{10,8},{12,... | collective-permute-start | bytes 1769480 | tf_op jit(solution)/shard_map/ppermute | solution.py:38
  179.7 5.7 %collective-permute-done.9 = bf16[72,4096]{1,0:T(8,128)(2,1)S(1)} collective-permute-done((bf16[72,4096]{1,0:T(8,128)(2,1)S(1)}, bf16[72,4096]{1,0:T(8,128)(2,1)S(1)}, u32[]{:S(2)}, u32[]{:S(2)}) %collective-permute-start.9) | collective-permute-done | bytes 589856 | tf_op jit(solution)/shard_map/ppermute | solution.py:38
  185.3 26.9 %collective-permute-start.16 = (bf16[72,4096]{1,0:T(8,128)(2,1)S(1)}, bf16[72,4096]{1,0:T(8,128)(2,1)S(1)}, u32[]{:S(2)}, u32[]{:S(2)}) collective-permute-start(bf16[72,4096]{1,0:T(8,128)(2,1)S(1)} %get-tuple-element.12), channel_id=1, source_target_pairs={{0,2},{2,4},{4,6},{6,0},{1,3},{3,5},{5,7},{7,1},{8,10},{10,12},{12... | collective-permute-start | bytes 1769480 | tf_op jit(solution)/shard_map/ppermute | solution.py:38
  212.3 37.4 %collective-permute-done.10 = bf16[72,4096]{1,0:T(8,128)(2,1)S(1)} collective-permute-done((bf16[72,4096]{1,0:T(8,128)(2,1)S(1)}, bf16[72,4096]{1,0:T(8,128)(2,1)S(1)}, u32[]{:S(2)}, u32[]{:S(2)}) %collective-permute-start.10) | collective-permute-done | bytes 589856 | tf_op jit(solution)/shard_map/ppermute | solution.py:38
  250.8 1.9 fusion.2
  252.7 4.4 %collective-permute-start.12 = (bf16[1,128,4096]{2,1,0:T(8,128)(2,1)S(1)}, bf16[1,128,4096]{2,1,0:T(8,128)(2,1)}, u32[]{:S(2)}, u32[]{:S(2)}) collective-permute-start(bf16[1,128,4096]{2,1,0:T(8,128)(2,1)S(1)} %fusion.2), channel_id=1, source_target_pairs={{0,16},{1,17},{2,18},{3,19},{4,20},{5,21},{6,22},{7,23},{8,24},{9,... | collective-permute-start | bytes 3145736 | tf_op jit(solution)/shard_map/ppermute | solution.py:17
  257.2 16.8 %collective-permute-done.15 = bf16[72,4096]{1,0:T(8,128)(2,1)S(1)} collective-permute-done((bf16[72,4096]{1,0:T(8,128)(2,1)S(1)}, bf16[72,4096]{1,0:T(8,128)(2,1)S(1)}, u32[]{:S(2)}, u32[]{:S(2)}) %collective-permute-start.15) | collective-permute-done | bytes 589856 | tf_op jit(solution)/shard_map/ppermute | solution.py:38
  276.8 1.3 collective-permute-start.17
  278.1 24.9 %collective-permute-done.17 = bf16[1,128,4096]{2,1,0:T(8,128)(2,1)} collective-permute-done((bf16[1,128,4096]{2,1,0:T(8,128)(2,1)S(1)}, bf16[1,128,4096]{2,1,0:T(8,128)(2,1)}, u32[]{:S(2)}, u32[]{:S(2)}) %collective-permute-start.17) | collective-permute-done | bytes 1048608 | tf_op jit(solution)/shard_map/ppermute | solution.py:17
  303.0 2.3 copy.32
  305.3 2.3 copy.33
  (102 shorter events, 13.9 us)
Async XLA Ops:
  7.2 76.9 %copy-start = (bf16[1,4096,384]{2,1,0:T(8,128)(2,1)S(1)}, bf16[1,4096,384]{2,1,0:T(8,128)(2,1)}, u32[]{:S(2)}) copy-start(bf16[1,4096,384]{2,1,0:T(8,128)(2,1)} %param.13) | copy-start | bytes 9437188
  7.2 84.8 %all-gather.3.cloned.1.call-start = ((), (), s32[]{:S(2)}) async-start(), calls=%async_computation.2 | async-start | bytes 4718592 | tf_op jit(solution)/shard_map/all_gather | solution.py:95
  14.1 2.2 copy-start.3
  16.4 9.0 %copy-start.15 = (f32[1,128,2]{1,2,0:T(2,128)S(1)}, f32[1,128,2]{1,2,0:T(2,128)}, u32[]{:S(2)}) copy-start(f32[1,128,2]{1,2,0:T(2,128)} %param.12) | copy-start | bytes 3076
  16.4 9.0 %copy-start.14 = (f32[1,384]{1,0:T(1,128)S(1)}, f32[1,384]{1,0:T(1,128)}, u32[]{:S(2)}) copy-start(f32[1,384]{1,0:T(1,128)} %param.15) | copy-start | bytes 4612
  16.4 19.7 %collective-permute-start = (bf16[72,4096]{1,0:T(8,128)(2,1)}, bf16[72,4096]{1,0:T(8,128)(2,1)}, u32[]{:S(2)}, u32[]{:S(2)}) collective-permute-start(bf16[72,4096]{1,0:T(8,128)(2,1)} %get-tuple-element.26), channel_id=1, source_target_pairs={{0,2},{2,4},{4,6},{6,0},{1,3},{3,5},{5,7},{7,1},{8,10},{10,12},{12... | collective-permute-start | bytes 1769480 | tf_op jit(solution)/shard_map/ppermute | solution.py:38
  19.4 41.1 %collective-permute-start.1 = (bf16[72,4096]{1,0:T(8,128)(2,1)}, bf16[72,4096]{1,0:T(8,128)(2,1)}, u32[]{:S(2)}, u32[]{:S(2)}) collective-permute-start(bf16[72,4096]{1,0:T(8,128)(2,1)} %get-tuple-element.25), channel_id=1, source_target_pairs={{0,4},{2,6},{4,0},{6,2},{1,5},{3,7},{5,1},{7,3},{8,12},{10,14},{12... | collective-permute-start | bytes 1769480 | tf_op jit(solution)/shard_map/ppermute | solution.py:38
  22.0 38.5 %collective-permute-start.2 = (bf16[72,4096]{1,0:T(8,128)(2,1)}, bf16[72,4096]{1,0:T(8,128)(2,1)}, u32[]{:S(2)}, u32[]{:S(2)}) collective-permute-start(bf16[72,4096]{1,0:T(8,128)(2,1)} %get-tuple-element.24), channel_id=1, source_target_pairs={{0,6},{2,0},{4,2},{6,4},{1,7},{3,1},{5,3},{7,5},{8,14},{10,8},{12,... | collective-permute-start | bytes 1769480 | tf_op jit(solution)/shard_map/ppermute | solution.py:38
  23.4 279.6 %reduce-scatter.2.cloned.1.call-start = ((), (), s32[]{:S(2)}) async-start(), calls=%async_computation.1 | async-start | bytes 4718592 | tf_op jit(solution)/shard_map/reduce_scatter | solution.py:160
  25.4 2.3 copy-start.4
  25.4 36.9 %slice-start.3 = ((s8[4718592]{0:T(1024)(128)(4,1)}), s8[4194304]{0:T(1024)(128)(4,1)S(1)}, s32[]{:S(2)}) async-start(s8[4718592]{0:T(1024)(128)(4,1)} %bitcast.140), calls=%async_computation.6 | async-start | bytes 8388608
  27.7 32.9 %copy-start.8 = (bf16[1,72,4096]{2,1,0:T(8,128)(2,1)S(1)}, bf16[1,72,4096]{2,1,0:T(8,128)(2,1)}, u32[]{:S(2)}) copy-start(bf16[1,72,4096]{2,1,0:T(8,128)(2,1)} %get-tuple-element.23) | copy-start | bytes 1769476
  27.7 34.6 %slice-start.4 = ((s8[4718592]{0:T(1024)(128)(4,1)}), s8[524288]{0:T(1024)(128)(4,1)S(1)}, s32[]{:S(2)}) async-start(s8[4718592]{0:T(1024)(128)(4,1)} %bitcast.140), calls=%async_computation.7 | async-start | bytes 1048576
  62.2 4.6 %collective-permute-start.3 = (bf16[4,72,4096]{2,1,0:T(8,128)(2,1)S(1)}, bf16[4,72,4096]{2,1,0:T(8,128)(2,1)S(1)}, u32[]{:S(2)}, u32[]{:S(2)}) collective-permute-start(bf16[4,72,4096]{2,1,0:T(8,128)(2,1)S(1)} %pad_maximum_fusion), channel_id=1, source_target_pairs={{0,1},{1,0},{2,3},{3,2},{4,5},{5,4},{6,7},{7,6},{8,9},{9,8},{10,11... | collective-permute-start | bytes 7077896 | tf_op jit(solution)/shard_map/ppermute | solution.py:33
  67.1 20.5 %copy-start.12 = (bf16[8,72,4096]{2,1,0:T(8,128)(2,1)}, bf16[8,72,4096]{2,1,0:T(8,128)(2,1)S(1)}, u32[]{:S(2)}) copy-start(bf16[8,72,4096]{2,1,0:T(8,128)(2,1)S(1)} %constant_dynamic-update-slice_fusion) | copy-start | bytes 14155780
  68.6 31.6 %collective-permute-start.4 = (bf16[72,4096]{1,0:T(8,128)(2,1)}, bf16[72,4096]{1,0:T(8,128)(2,1)}, u32[]{:S(2)}, u32[]{:S(2)}) collective-permute-start(bf16[72,4096]{1,0:T(8,128)(2,1)} %get-tuple-element.22), channel_id=1, source_target_pairs={{0,2},{2,4},{4,6},{6,0},{1,3},{3,5},{5,7},{7,1},{8,10},{10,12},{12... | collective-permute-start | bytes 1769480 | tf_op jit(solution)/shard_map/ppermute | solution.py:38
  81.7 40.4 %collective-permute-start.5 = (bf16[72,4096]{1,0:T(8,128)(2,1)}, bf16[72,4096]{1,0:T(8,128)(2,1)}, u32[]{:S(2)}, u32[]{:S(2)}) collective-permute-start(bf16[72,4096]{1,0:T(8,128)(2,1)} %get-tuple-element.21), channel_id=1, source_target_pairs={{0,4},{2,6},{4,0},{6,2},{1,5},{3,7},{5,1},{7,3},{8,12},{10,14},{12... | collective-permute-start | bytes 1769480 | tf_op jit(solution)/shard_map/ppermute | solution.py:38
  83.3 4.3 %copy-start.6 = (bf16[1,4096,384]{2,1,0:T(8,128)(2,1)S(1)}, bf16[1,4096,384]{2,1,0:T(8,128)(2,1)}, u32[]{:S(2)}) copy-start(bf16[1,4096,384]{2,1,0:T(8,128)(2,1)} %param.14) | copy-start | bytes 9437188
  83.3 38.8 %collective-permute-start.6 = (bf16[72,4096]{1,0:T(8,128)(2,1)}, bf16[72,4096]{1,0:T(8,128)(2,1)}, u32[]{:S(2)}, u32[]{:S(2)}) collective-permute-start(bf16[72,4096]{1,0:T(8,128)(2,1)} %get-tuple-element.20), channel_id=1, source_target_pairs={{0,6},{2,0},{4,2},{6,4},{1,7},{3,1},{5,3},{7,5},{8,14},{10,8},{12,... | collective-permute-start | bytes 1769480 | tf_op jit(solution)/shard_map/ppermute | solution.py:38
  99.3 24.6 %slice-start.1 = ((s8[4718592]{0:T(1024)(128)(4,1)}), s8[4194304]{0:T(1024)(128)(4,1)S(1)}, s32[]{:S(2)}) async-start(s8[4718592]{0:T(1024)(128)(4,1)} %bitcast.137), calls=%async_computation.4 | async-start | bytes 8388608
  99.6 22.5 %copy-start.9 = (bf16[1,72,4096]{2,1,0:T(8,128)(2,1)S(1)}, bf16[1,72,4096]{2,1,0:T(8,128)(2,1)}, u32[]{:S(2)}) copy-start(bf16[1,72,4096]{2,1,0:T(8,128)(2,1)} %get-tuple-element.19) | copy-start | bytes 1769476
  99.6 24.3 %slice-start.2 = ((s8[4718592]{0:T(1024)(128)(4,1)}), s8[524288]{0:T(1024)(128)(4,1)S(1)}, s32[]{:S(2)}) async-start(s8[4718592]{0:T(1024)(128)(4,1)} %bitcast.137), calls=%async_computation.5 | async-start | bytes 1048576
  100.2 27.1 %collective-permute-start.8 = (bf16[4,72,4096]{2,1,0:T(8,128)(2,1)S(1)}, bf16[4,72,4096]{2,1,0:T(8,128)(2,1)S(1)}, u32[]{:S(2)}, u32[]{:S(2)}) collective-permute-start(bf16[4,72,4096]{2,1,0:T(8,128)(2,1)S(1)} %bitcast.130), channel_id=1, source_target_pairs={{0,1},{1,0},{2,3},{3,2},{4,5},{5,4},{6,7},{7,6},{8,9},{9,8},{10,11... | collective-permute-start | bytes 7077896 | tf_op jit(solution)/shard_map/ppermute | solution.py:33
  123.8 5.6 %collective-permute-start.7 = (bf16[4,72,4096]{2,1,0:T(8,128)(2,1)S(1)}, bf16[4,72,4096]{2,1,0:T(8,128)(2,1)S(1)}, u32[]{:S(2)}, u32[]{:S(2)}) collective-permute-start(bf16[4,72,4096]{2,1,0:T(8,128)(2,1)S(1)} %pad_maximum_fusion.1), channel_id=1, source_target_pairs={{0,1},{1,0},{2,3},{3,2},{4,5},{5,4},{6,7},{7,6},{8,9},{9,8},{10,11... | collective-permute-start | bytes 7077896 | tf_op jit(solution)/shard_map/ppermute | solution.py:33
  127.3 2.5 copy-start.16
  129.4 1.3 copy-start.10
  129.4 1.5 copy-start.11
  137.4 2.7 copy-start.7
  142.8 3.7 %copy-start.1 = (f32[576,4096]{1,0:T(8,128)}, f32[576,4096]{1,0:T(8,128)S(1)}, u32[]{:S(2)}) copy-start(f32[576,4096]{1,0:T(8,128)S(1)} %convolution_add_fusion) | copy-start | bytes 28311556
  148.2 24.1 %collective-permute-start.13 = (bf16[4,72,4096]{2,1,0:T(8,128)(2,1)}, bf16[4,72,4096]{2,1,0:T(8,128)(2,1)}, u32[]{:S(2)}, u32[]{:S(2)}) collective-permute-start(bf16[4,72,4096]{2,1,0:T(8,128)(2,1)} %bitcast.35), channel_id=1, source_target_pairs={{0,1},{1,0},{2,3},{3,2},{4,5},{5,4},{6,7},{7,6},{8,9},{9,8},{10,11... | collective-permute-start | bytes 7077896 | tf_op jit(solution)/shard_map/ppermute | solution.py:33
  157.6 14.6 %slice-start = ((f32[576,4096]{1,0:T(8,128)}), f32[288,4096]{1,0:T(8,128)S(1)}, s32[]{:S(2)}) async-start(f32[576,4096]{1,0:T(8,128)} %copy-done.1), calls=%async_computation.3 | async-start | bytes 9437184 | tf_op jit(solution)/shard_map/slice | solution.py:52
  157.6 27.7 %collective-permute-start.9 = (bf16[72,4096]{1,0:T(8,128)(2,1)S(1)}, bf16[72,4096]{1,0:T(8,128)(2,1)S(1)}, u32[]{:S(2)}, u32[]{:S(2)}) collective-permute-start(bf16[72,4096]{1,0:T(8,128)(2,1)S(1)} %get-tuple-element.18), channel_id=1, source_target_pairs={{0,6},{2,0},{4,2},{6,4},{1,7},{3,1},{5,3},{7,5},{8,14},{10,8},{12,... | collective-permute-start | bytes 1769480 | tf_op jit(solution)/shard_map/ppermute | solution.py:38
  171.5 78.1 %collective-permute-start.10 = (bf16[72,4096]{1,0:T(8,128)(2,1)S(1)}, bf16[72,4096]{1,0:T(8,128)(2,1)S(1)}, u32[]{:S(2)}, u32[]{:S(2)}) collective-permute-start(bf16[72,4096]{1,0:T(8,128)(2,1)S(1)} %get-tuple-element.17), channel_id=1, source_target_pairs={{0,4},{2,6},{4,0},{6,2},{1,5},{3,7},{5,1},{7,3},{8,12},{10,14},{12... | collective-permute-start | bytes 1769480 | tf_op jit(solution)/shard_map/ppermute | solution.py:38
  172.2 77.4 %collective-permute-start.11 = (bf16[72,4096]{1,0:T(8,128)(2,1)S(1)}, bf16[72,4096]{1,0:T(8,128)(2,1)S(1)}, u32[]{:S(2)}, u32[]{:S(2)}) collective-permute-start(bf16[72,4096]{1,0:T(8,128)(2,1)S(1)} %get-tuple-element.16), channel_id=1, source_target_pairs={{0,2},{2,4},{4,6},{6,0},{1,3},{3,5},{5,7},{7,1},{8,10},{10,12},{12... | collective-permute-start | bytes 1769480 | tf_op jit(solution)/shard_map/ppermute | solution.py:38
  175.4 81.8 %collective-permute-start.14 = (bf16[72,4096]{1,0:T(8,128)(2,1)S(1)}, bf16[72,4096]{1,0:T(8,128)(2,1)S(1)}, u32[]{:S(2)}, u32[]{:S(2)}) collective-permute-start(bf16[72,4096]{1,0:T(8,128)(2,1)S(1)} %get-tuple-element.14), channel_id=1, source_target_pairs={{0,6},{2,0},{4,2},{6,4},{1,7},{3,1},{5,3},{7,5},{8,14},{10,8},{12,... | collective-permute-start | bytes 1769480 | tf_op jit(solution)/shard_map/ppermute | solution.py:38
  179.3 94.6 %collective-permute-start.15 = (bf16[72,4096]{1,0:T(8,128)(2,1)S(1)}, bf16[72,4096]{1,0:T(8,128)(2,1)S(1)}, u32[]{:S(2)}, u32[]{:S(2)}) collective-permute-start(bf16[72,4096]{1,0:T(8,128)(2,1)S(1)} %get-tuple-element.13), channel_id=1, source_target_pairs={{0,4},{2,6},{4,0},{6,2},{1,5},{3,7},{5,1},{7,3},{8,12},{10,14},{12... | collective-permute-start | bytes 1769480 | tf_op jit(solution)/shard_map/ppermute | solution.py:38
  185.3 88.7 %collective-permute-start.16 = (bf16[72,4096]{1,0:T(8,128)(2,1)S(1)}, bf16[72,4096]{1,0:T(8,128)(2,1)S(1)}, u32[]{:S(2)}, u32[]{:S(2)}) collective-permute-start(bf16[72,4096]{1,0:T(8,128)(2,1)S(1)} %get-tuple-element.12), channel_id=1, source_target_pairs={{0,2},{2,4},{4,6},{6,0},{1,3},{3,5},{5,7},{7,1},{8,10},{10,12},{12... | collective-permute-start | bytes 1769480 | tf_op jit(solution)/shard_map/ppermute | solution.py:38
  249.6 1.2 copy-start.2
  252.7 25.3 %collective-permute-start.12 = (bf16[1,128,4096]{2,1,0:T(8,128)(2,1)S(1)}, bf16[1,128,4096]{2,1,0:T(8,128)(2,1)}, u32[]{:S(2)}, u32[]{:S(2)}) collective-permute-start(bf16[1,128,4096]{2,1,0:T(8,128)(2,1)S(1)} %fusion.2), channel_id=1, source_target_pairs={{0,16},{1,17},{2,18},{3,19},{4,20},{5,21},{6,22},{7,23},{8,24},{9,... | collective-permute-start | bytes 3145736 | tf_op jit(solution)/shard_map/ppermute | solution.py:17
  274.0 0.7 copy-start.13
  274.7 1.2 copy-start.5
  276.8 26.3 %collective-permute-start.17 = (bf16[1,128,4096]{2,1,0:T(8,128)(2,1)S(1)}, bf16[1,128,4096]{2,1,0:T(8,128)(2,1)}, u32[]{:S(2)}, u32[]{:S(2)}) collective-permute-start(bf16[1,128,4096]{2,1,0:T(8,128)(2,1)S(1)} %fusion.27), channel_id=1, source_target_pairs={{16,0},{17,1},{18,2},{19,3},{20,4},{21,5},{22,6},{23,7},{24,8},{25... | collective-permute-start | bytes 3145736 | tf_op jit(solution)/shard_map/ppermute | solution.py:17
Sparse Core Ops, SparseCore 0:
  23.5 43.2 all-gather.2
  156.0 54.9 reduce-scatter.1

commit v4 on v2

--- a/solution.py
+++ b/solution.py
@@ -91,7 +91,11 @@
     down_full = lax.all_gather(down_weight[0], "dp", axis=1, tiled=True)
     gate_act = jnp.dot(arrived, gate_local, preferred_element_type=jnp.float32)
     up_act = jnp.dot(arrived, up_local, preferred_element_type=jnp.float32)
-    spike_rate = lif_rate(gate_act, up_act, leak_local).astype(jnp.bfloat16)
+    spike_exact, lif_pullback = jax.vjp(
+        lambda gate_in, up_in: lif_rate(gate_in, up_in, leak_local), gate_act, up_act
+    )
+    spike_rate = spike_exact.astype(jnp.bfloat16)
+    gate_slope, up_slope = lif_pullback(jnp.ones_like(spike_exact))
     out_part = jnp.dot(spike_rate, down_full, preferred_element_type=jnp.float32)
     expert_out = from_experts(out_part, experts, capacity)
     weights = route_gates[0]
@@ -117,12 +121,8 @@
     rate_grad = lax.dot_general(
         grad_rows, down_full, (((1,), (1,)), ((), ())), preferred_element_type=jnp.float32
     )
-    unused_rate, pullback = jax.vjp(
-        lambda gate_in, up_in: lif_rate(gate_in, up_in, leak_local), gate_act, up_act
-    )
-    gate_grad, up_act_grad = pullback(rate_grad)
-    gate_grad = gate_grad.astype(jnp.bfloat16)
-    up_act_grad = up_act_grad.astype(jnp.bfloat16)
+    gate_grad = (rate_grad * gate_slope).astype(jnp.bfloat16)
+    up_act_grad = (rate_grad * up_slope).astype(jnp.bfloat16)
     back_part = lax.dot_general(
         gate_grad, gate_local, (((1,), (1,)), ((), ())), preferred_element_type=jnp.float32
     )

time: 315 us -> 315 us (level)
  no operation moved by 1% of the time
where the time goes in v4:
time: 315 us; the launch traced here: 314 us
  waiting for transfers between devices  184 us (58%)
  matrix products  40.6 us (13%)
  starting transfers between devices  29.5 us (9%)
  local copies, waits for them, and re-layouts  28.7 us (9%)
  other arithmetic  17.2 us (5%)
  between operations  14.5 us (5%)
    ppermute x12, waiting for transfers between devices, shifted(): lax.ppermute(value, 'chip', [(source, (source + steps) % count) for sourc...  156 us
    ppermute x2, waiting for transfers between devices, passed_along(): lax.ppermute(value, axis, [(source, source + steps) for source in range(l...  25.4 us
    ppermute x12, starting transfers between devices, shifted(): lax.ppermute(value, 'chip', [(source, (source + steps) % count) for sourc...  23 us
    unnamed x53, local copies, waits for them, and re-layouts  15.8 us
    convert_element_type x2, other arithmetic, from_experts(): summed = (paired[0] + other.astype(jnp.float32)).astype(jnp.bfloat16)  9.35 us
    dot_general x1, matrix products, per_device(): jnp.dot(spike_rate, down_full, preferred_element_type=jnp.float32)  7.3 us
    dot_general x1, matrix products, per_device(): lax.dot_general(grad_rows, down_full, (((1,), (1,)), ((), ())), preferred...  6.32 us
  transfers between devices with their start and end apart: 20, of which 13 were waited for; matrix products, arithmetic and copies ran while one was open for 25% of the time, Pallas kernels for 0%

profile of v4, /device:TPU:8, one launch (start us, length us, event | category | flops | bytes accessed | tf_op | source)
XLA Modules:
  0.0 314.4 jit_solution(14193403305971080105)
XLA Ops:
  9.2 1.5 fusion.18
  10.8 1.2 reduce-window.6
  12.8 2.1 convolution_convert_fusion.1
  14.9 1.4 slice_bitcast_fusion.6
  16.4 3.0 collective-permute-start.1
  19.4 2.5 collective-permute-start
  22.8 2.2 fusion.26
  26.0 32.2 %collective-permute-done.2 = bf16[72,4096]{1,0:T(8,128)(2,1)} collective-permute-done((bf16[72,4096]{1,0:T(8,128)(2,1)}, bf16[72,4096]{1,0:T(8,128)(2,1)}, u32[]{:S(2)}, u32[]{:S(2)}) %collective-permute-start.2) | collective-permute-done | bytes 589856 | tf_op jit(solution)/shard_map/ppermute | solution.py:38
  58.2 11.8 %collective-permute-done = bf16[72,4096]{1,0:T(8,128)(2,1)} collective-permute-done((bf16[72,4096]{1,0:T(8,128)(2,1)}, bf16[72,4096]{1,0:T(8,128)(2,1)}, u32[]{:S(2)}, u32[]{:S(2)}) %collective-permute-start) | collective-permute-done | bytes 589856 | tf_op jit(solution)/shard_map/ppermute | solution.py:38
  70.0 1.7 pad_maximum_fusion
  75.1 1.2 collective-permute-done.3
  76.6 1.4 slice_bitcast_fusion.7
  78.0 1.1 collective-permute-start.11
  79.1 2.8 collective-permute-start.10
  81.9 3.5 %fusion.8 = f32[576,384]{1,0:T(8,128)} fusion(bf16[576,4096]{1,0:T(8,128)(2,1)S(1)} %bitcast.137, bf16[1,4096,384]{2,1,0:T(8,128)(2,1)S(1)} %copy-done.5), kind=kOutput, calls=%fused_computation.25 | convolution fusion | flops 1811939328 | bytes 8749056 | tf_op jit(solution)/shard_map/dot_general | solution.py:93
  85.5 3.5 %fusion.12 = f32[576,384]{1,0:T(8,128)} fusion(bf16[576,4096]{1,0:T(8,128)(2,1)S(1)} %bitcast.138, bf16[1,4096,384]{2,1,0:T(8,128)(2,1)S(1)} %copy-done), kind=kOutput, calls=%fused_computation.29 | convolution fusion | flops 1811939328 | bytes 8749056 | tf_op jit(solution)/shard_map/dot_general | solution.py:92
  89.8 7.3 %fusion.5 = f32[576,4096]{1,0:T(8,128)S(1)} fusion(bf16[1,384,4096]{2,1,0:T(8,128)(2,1)} %all-gather.3.cloned.1.call-done, f32[384]{0:T(512)S(1)} %reduce.2, f32[384]{0:T(512)S(1)} %broadcast_multiply_fusion, f32[576,384]{1,0:T(8,128)} %fusion.8, f32[576,384]{1,0:T(8,128)} %fusion.12), kind=kOutput, calls=%fused_computation.22 | convolution fusion | flops 1827643392 | bytes 14355456 | tf_op jit(solution)/shard_map/dot_general | solution.py:99
  97.1 1.8 slice.164
  99.5 18.0 %collective-permute-done.10 = bf16[72,4096]{1,0:T(8,128)(2,1)} collective-permute-done((bf16[72,4096]{1,0:T(8,128)(2,1)}, bf16[72,4096]{1,0:T(8,128)(2,1)}, u32[]{:S(2)}, u32[]{:S(2)}) %collective-permute-start.10) | collective-permute-done | bytes 589856 | tf_op jit(solution)/shard_map/ppermute | solution.py:38
  117.5 12.5 %collective-permute-done.9 = bf16[72,4096]{1,0:T(8,128)(2,1)} collective-permute-done((bf16[72,4096]{1,0:T(8,128)(2,1)}, bf16[72,4096]{1,0:T(8,128)(2,1)}, u32[]{:S(2)}, u32[]{:S(2)}) %collective-permute-start.9) | collective-permute-done | bytes 589856 | tf_op jit(solution)/shard_map/ppermute | solution.py:38
  130.0 1.7 pad_maximum_fusion.2
  134.0 1.3 constant_dynamic-update-slice_fusion.6
  136.9 6.3 %multiply_convert_fusion = (bf16[576,384]{1,0:T(8,128)(2,1)S(1)}, f32[576,384]{1,0:T(8,128)S(1)}, f32[576,384]{1,0:T(8,128)S(1)}) fusion(f32[576,384]{1,0:T(8,128)S(1)} %copy-done.9, f32[576,384]{1,0:T(8,128)S(1)} %copy-done.8, f32[384]{0:T(512)S(1)} %broadcast_multiply_fusion, f32[384]{0:T(512)S(1)} %reduce.2, bf16[576,4096]{1,0:T(8,128)(2,1)S(1)} %bitcast.134, ...), kind=kOutput, calls=%fused_computation.90 | convolution fusion | flops 1839808512 | bytes 11848704 | tf_op jit(solution)/shard_map/dot_general | solution.py:121
  143.3 2.8 fusion.10
  146.0 4.5 %convolution_add_fusion = f32[576,4096]{1,0:T(8,128)S(1)} fusion(f32[576,4096]{1,0:T(8,128)S(1)} %fusion.10, bf16[576,384]{1,0:T(8,128)(2,1)S(1)} %get-tuple-element.7, bf16[1,4096,384]{2,1,0:T(8,128)(2,1)} %param.14), kind=kOutput, calls=%fused_computation | convolution fusion | flops 1814298624 | bytes 22462464 | tf_op jit(solution)/shard_map/dot_general | solution.py:129
  150.6 1.8 slice.163
  152.9 6.9 %add_convert_fusion.1 = bf16[4,72,4096]{2,1,0:T(8,128)(2,1)} fusion(f32[4,72,4096]{2,1,0:T(8,128)S(1)} %bitcast.123, bf16[4,72,4096]{2,1,0:T(8,128)(2,1)} %collective-permute-done.4), kind=kLoop, calls=%fused_computation.11 | loop fusion | flops 3538944 | bytes 9437184 | tf_op jit(solution)/shard_map/convert_element_type | solution.py:52
  159.8 4.7 %convolution_convert_fusion = bf16[4096,384]{1,0:T(8,128)(2,1)} fusion(bf16[576,4096]{1,0:T(8,128)(2,1)S(1)} %bitcast.141, bf16[576,384]{1,0:T(8,128)(2,1)S(1)} %get-tuple-element.7), kind=kOutput, calls=%fused_computation.1 | convolution fusion | flops 1813512192 | bytes 8306688 | tf_op jit(solution)/shard_map/dot_general | solution.py:150
  164.5 1.8 fusion.105
  166.3 2.5 collective-permute-start.7
  168.8 3.7 %collective-permute-start.6 = (bf16[72,4096]{1,0:T(8,128)(2,1)S(1)}, bf16[72,4096]{1,0:T(8,128)(2,1)S(1)}, u32[]{:S(2)}, u32[]{:S(2)}) collective-permute-start(bf16[72,4096]{1,0:T(8,128)(2,1)S(1)} %get-tuple-element.19), channel_id=1, source_target_pairs={{0,4},{2,6},{4,0},{6,2},{1,5},{3,7},{5,1},{7,3},{8,12},{10,14},{12... | collective-permute-start | bytes 1769480 | tf_op jit(solution)/shard_map/ppermute | solution.py:38
  172.5 2.9 slice-done
  175.4 2.4 add_convert_fusion
  178.0 1.8 collective-permute-start.16
  179.8 1.5 collective-permute-start.15
  181.3 3.0 collective-permute-done.7
  184.3 4.0 %collective-permute-start.14 = (bf16[72,4096]{1,0:T(8,128)(2,1)S(1)}, bf16[72,4096]{1,0:T(8,128)(2,1)S(1)}, u32[]{:S(2)}, u32[]{:S(2)}) collective-permute-start(bf16[72,4096]{1,0:T(8,128)(2,1)S(1)} %get-tuple-element.12), channel_id=1, source_target_pairs={{0,6},{2,0},{4,2},{6,4},{1,7},{3,1},{5,3},{7,5},{8,14},{10,8},{12,... | collective-permute-start | bytes 1769480 | tf_op jit(solution)/shard_map/ppermute | solution.py:38
  188.3 32.2 %collective-permute-done.6 = bf16[72,4096]{1,0:T(8,128)(2,1)S(1)} collective-permute-done((bf16[72,4096]{1,0:T(8,128)(2,1)S(1)}, bf16[72,4096]{1,0:T(8,128)(2,1)S(1)}, u32[]{:S(2)}, u32[]{:S(2)}) %collective-permute-start.6) | collective-permute-done | bytes 589856 | tf_op jit(solution)/shard_map/ppermute | solution.py:38
  220.5 28.7 %collective-permute-done.5 = bf16[72,4096]{1,0:T(8,128)(2,1)S(1)} collective-permute-done((bf16[72,4096]{1,0:T(8,128)(2,1)S(1)}, bf16[72,4096]{1,0:T(8,128)(2,1)S(1)}, u32[]{:S(2)}, u32[]{:S(2)}) %collective-permute-start.5) | collective-permute-done | bytes 589856 | tf_op jit(solution)/shard_map/ppermute | solution.py:38
  250.4 1.9 fusion.2
  252.2 4.4 %collective-permute-start.8 = (bf16[1,128,4096]{2,1,0:T(8,128)(2,1)S(1)}, bf16[1,128,4096]{2,1,0:T(8,128)(2,1)}, u32[]{:S(2)}, u32[]{:S(2)}) collective-permute-start(bf16[1,128,4096]{2,1,0:T(8,128)(2,1)S(1)} %fusion.2), channel_id=1, source_target_pairs={{0,16},{1,17},{2,18},{3,19},{4,20},{5,21},{6,22},{7,23},{8,24},{9,... | collective-permute-start | bytes 3145736 | tf_op jit(solution)/shard_map/ppermute | solution.py:17
  256.7 1.7 collective-permute-done.16
  258.4 12.2 %collective-permute-done.15 = bf16[72,4096]{1,0:T(8,128)(2,1)S(1)} collective-permute-done((bf16[72,4096]{1,0:T(8,128)(2,1)S(1)}, bf16[72,4096]{1,0:T(8,128)(2,1)S(1)}, u32[]{:S(2)}, u32[]{:S(2)}) %collective-permute-start.15) | collective-permute-done | bytes 589856 | tf_op jit(solution)/shard_map/ppermute | solution.py:38
  270.5 3.4 %collective-permute-done.14 = bf16[72,4096]{1,0:T(8,128)(2,1)S(1)} collective-permute-done((bf16[72,4096]{1,0:T(8,128)(2,1)S(1)}, bf16[72,4096]{1,0:T(8,128)(2,1)S(1)}, u32[]{:S(2)}, u32[]{:S(2)}) %collective-permute-start.14) | collective-permute-done | bytes 589856 | tf_op jit(solution)/shard_map/ppermute | solution.py:38
  276.3 1.3 collective-permute-start.17
  277.6 25.4 %collective-permute-done.17 = bf16[1,128,4096]{2,1,0:T(8,128)(2,1)} collective-permute-done((bf16[1,128,4096]{2,1,0:T(8,128)(2,1)S(1)}, bf16[1,128,4096]{2,1,0:T(8,128)(2,1)}, u32[]{:S(2)}, u32[]{:S(2)}) %collective-permute-start.17) | collective-permute-done | bytes 1048608 | tf_op jit(solution)/shard_map/ppermute | solution.py:17
  302.9 2.3 copy.32
  305.2 2.3 copy.33
  (103 shorter events, 17.8 us)
Async XLA Ops:
  7.2 78.3 %copy-start = (bf16[1,4096,384]{2,1,0:T(8,128)(2,1)S(1)}, bf16[1,4096,384]{2,1,0:T(8,128)(2,1)}, u32[]{:S(2)}) copy-start(bf16[1,4096,384]{2,1,0:T(8,128)(2,1)} %param.13) | copy-start | bytes 9437188
  7.2 5.6 %copy-start.11 = (f32[1,4096]{1,0:T(1,128)S(1)}, f32[1,4096]{1,0:T(1,128)}, u32[]{:S(2)}) copy-start(f32[1,4096]{1,0:T(1,128)} %param.10) | copy-start | bytes 49156
  7.2 82.6 %all-gather.3.cloned.1.call-start = ((), (), s32[]{:S(2)}) async-start(), calls=%async_computation.2 | async-start | bytes 4718592 | tf_op jit(solution)/shard_map/all_gather | solution.py:91
  7.9 295.0 %reduce-scatter.2.cloned.1.call-start = ((), (), s32[]{:S(2)}) async-start(), calls=%async_computation.1 | async-start | bytes 4718592 | tf_op jit(solution)/shard_map/reduce_scatter | solution.py:154
  14.9 7.8 %copy-start.13 = (f32[1,128,2]{1,2,0:T(2,128)S(1)}, f32[1,128,2]{1,2,0:T(2,128)}, u32[]{:S(2)}) copy-start(f32[1,128,2]{1,2,0:T(2,128)} %param.12) | copy-start | bytes 3076
  14.9 7.8 %copy-start.12 = (f32[1,384]{1,0:T(1,128)S(1)}, f32[1,384]{1,0:T(1,128)}, u32[]{:S(2)}) copy-start(f32[1,384]{1,0:T(1,128)} %param.15) | copy-start | bytes 4612
  16.4 41.8 %collective-permute-start.2 = (bf16[72,4096]{1,0:T(8,128)(2,1)}, bf16[72,4096]{1,0:T(8,128)(2,1)}, u32[]{:S(2)}, u32[]{:S(2)}) collective-permute-start(bf16[72,4096]{1,0:T(8,128)(2,1)} %get-tuple-element.22), channel_id=1, source_target_pairs={{0,6},{2,0},{4,2},{6,4},{1,7},{3,1},{5,3},{7,5},{8,14},{10,8},{12,... | collective-permute-start | bytes 1769480 | tf_op jit(solution)/shard_map/ppermute | solution.py:38
  16.4 41.8 %collective-permute-start.1 = (bf16[72,4096]{1,0:T(8,128)(2,1)}, bf16[72,4096]{1,0:T(8,128)(2,1)}, u32[]{:S(2)}, u32[]{:S(2)}) collective-permute-start(bf16[72,4096]{1,0:T(8,128)(2,1)} %get-tuple-element.23), channel_id=1, source_target_pairs={{0,4},{2,6},{4,0},{6,2},{1,5},{3,7},{5,1},{7,3},{8,12},{10,14},{12... | collective-permute-start | bytes 1769480 | tf_op jit(solution)/shard_map/ppermute | solution.py:38
  19.4 50.6 %collective-permute-start = (bf16[72,4096]{1,0:T(8,128)(2,1)}, bf16[72,4096]{1,0:T(8,128)(2,1)}, u32[]{:S(2)}, u32[]{:S(2)}) collective-permute-start(bf16[72,4096]{1,0:T(8,128)(2,1)} %get-tuple-element.24), channel_id=1, source_target_pairs={{0,2},{2,4},{4,6},{6,0},{1,3},{3,5},{5,7},{7,1},{8,10},{10,12},{12... | collective-permute-start | bytes 1769480 | tf_op jit(solution)/shard_map/ppermute | solution.py:38
  22.8 2.3 copy-start.3
  22.8 49.0 %slice-start.3 = ((s8[4718592]{0:T(1024)(128)(4,1)}), s8[4194304]{0:T(1024)(128)(4,1)S(1)}, s32[]{:S(2)}) async-start(s8[4718592]{0:T(1024)(128)(4,1)} %bitcast.135), calls=%async_computation.6 | async-start | bytes 8388608
  25.0 45.0 %copy-start.7 = (bf16[1,72,4096]{2,1,0:T(8,128)(2,1)S(1)}, bf16[1,72,4096]{2,1,0:T(8,128)(2,1)}, u32[]{:S(2)}) copy-start(bf16[1,72,4096]{2,1,0:T(8,128)(2,1)} %get-tuple-element.21) | copy-start | bytes 1769476
  25.0 46.7 %slice-start.4 = ((s8[4718592]{0:T(1024)(128)(4,1)}), s8[524288]{0:T(1024)(128)(4,1)S(1)}, s32[]{:S(2)}) async-start(s8[4718592]{0:T(1024)(128)(4,1)} %bitcast.135), calls=%async_computation.7 | async-start | bytes 1048576
  71.7 4.6 %collective-permute-start.3 = (bf16[4,72,4096]{2,1,0:T(8,128)(2,1)S(1)}, bf16[4,72,4096]{2,1,0:T(8,128)(2,1)S(1)}, u32[]{:S(2)}, u32[]{:S(2)}) collective-permute-start(bf16[4,72,4096]{2,1,0:T(8,128)(2,1)S(1)} %pad_maximum_fusion), channel_id=1, source_target_pairs={{0,1},{1,0},{2,3},{3,2},{4,5},{5,4},{6,7},{7,6},{8,9},{9,8},{10,11... | collective-permute-start | bytes 7077896 | tf_op jit(solution)/shard_map/ppermute | solution.py:33
  76.6 8.9 %copy-start.10 = (bf16[8,72,4096]{2,1,0:T(8,128)(2,1)}, bf16[8,72,4096]{2,1,0:T(8,128)(2,1)S(1)}, u32[]{:S(2)}) copy-start(bf16[8,72,4096]{2,1,0:T(8,128)(2,1)S(1)} %constant_dynamic-update-slice_fusion) | copy-start | bytes 14155780
  76.6 5.4 %copy-start.5 = (bf16[1,4096,384]{2,1,0:T(8,128)(2,1)S(1)}, bf16[1,4096,384]{2,1,0:T(8,128)(2,1)}, u32[]{:S(2)}) copy-start(bf16[1,4096,384]{2,1,0:T(8,128)(2,1)} %param.14) | copy-start | bytes 9437188
  78.0 21.5 %collective-permute-start.11 = (bf16[72,4096]{1,0:T(8,128)(2,1)}, bf16[72,4096]{1,0:T(8,128)(2,1)}, u32[]{:S(2)}, u32[]{:S(2)}) collective-permute-start(bf16[72,4096]{1,0:T(8,128)(2,1)} %get-tuple-element.14), channel_id=1, source_target_pairs={{0,6},{2,0},{4,2},{6,4},{1,7},{3,1},{5,3},{7,5},{8,14},{10,8},{12,... | collective-permute-start | bytes 1769480 | tf_op jit(solution)/shard_map/ppermute | solution.py:38
  79.1 38.3 %collective-permute-start.10 = (bf16[72,4096]{1,0:T(8,128)(2,1)}, bf16[72,4096]{1,0:T(8,128)(2,1)}, u32[]{:S(2)}, u32[]{:S(2)}) collective-permute-start(bf16[72,4096]{1,0:T(8,128)(2,1)} %get-tuple-element.15), channel_id=1, source_target_pairs={{0,4},{2,6},{4,0},{6,2},{1,5},{3,7},{5,1},{7,3},{8,12},{10,14},{12... | collective-permute-start | bytes 1769480 | tf_op jit(solution)/shard_map/ppermute | solution.py:38
  81.9 48.1 %collective-permute-start.9 = (bf16[72,4096]{1,0:T(8,128)(2,1)}, bf16[72,4096]{1,0:T(8,128)(2,1)}, u32[]{:S(2)}, u32[]{:S(2)}) collective-permute-start(bf16[72,4096]{1,0:T(8,128)(2,1)} %get-tuple-element.16), channel_id=1, source_target_pairs={{0,2},{2,4},{4,6},{6,0},{1,3},{3,5},{5,7},{7,1},{8,10},{10,12},{12... | collective-permute-start | bytes 1769480 | tf_op jit(solution)/shard_map/ppermute | solution.py:38
  97.1 34.7 %slice-start.1 = ((s8[4718592]{0:T(1024)(128)(4,1)}), s8[4194304]{0:T(1024)(128)(4,1)S(1)}, s32[]{:S(2)}) async-start(s8[4718592]{0:T(1024)(128)(4,1)} %bitcast.132), calls=%async_computation.4 | async-start | bytes 8388608
  98.9 31.1 %copy-start.6 = (bf16[1,72,4096]{2,1,0:T(8,128)(2,1)S(1)}, bf16[1,72,4096]{2,1,0:T(8,128)(2,1)}, u32[]{:S(2)}) copy-start(bf16[1,72,4096]{2,1,0:T(8,128)(2,1)} %get-tuple-element.13) | copy-start | bytes 1769476
  98.9 32.9 %slice-start.2 = ((s8[4718592]{0:T(1024)(128)(4,1)}), s8[524288]{0:T(1024)(128)(4,1)S(1)}, s32[]{:S(2)}) async-start(s8[4718592]{0:T(1024)(128)(4,1)} %bitcast.132), calls=%async_computation.5 | async-start | bytes 1048576
  99.4 53.4 %collective-permute-start.4 = (bf16[4,72,4096]{2,1,0:T(8,128)(2,1)}, bf16[4,72,4096]{2,1,0:T(8,128)(2,1)}, u32[]{:S(2)}, u32[]{:S(2)}) collective-permute-start(bf16[4,72,4096]{2,1,0:T(8,128)(2,1)} %bitcast.18), channel_id=1, source_target_pairs={{0,1},{1,0},{2,3},{3,2},{4,5},{5,4},{6,7},{7,6},{8,9},{9,8},{10,11... | collective-permute-start | bytes 7077896 | tf_op jit(solution)/shard_map/ppermute | solution.py:33
  131.7 4.6 %collective-permute-start.12 = (bf16[4,72,4096]{2,1,0:T(8,128)(2,1)S(1)}, bf16[4,72,4096]{2,1,0:T(8,128)(2,1)S(1)}, u32[]{:S(2)}, u32[]{:S(2)}) collective-permute-start(bf16[4,72,4096]{2,1,0:T(8,128)(2,1)S(1)} %pad_maximum_fusion.2), channel_id=1, source_target_pairs={{0,1},{1,0},{2,3},{3,2},{4,5},{5,4},{6,7},{7,6},{8,9},{9,8},{10,11... | collective-permute-start | bytes 7077896 | tf_op jit(solution)/shard_map/ppermute | solution.py:33
  134.0 2.4 copy-start.14
  135.3 1.4 copy-start.8
  135.3 1.6 copy-start.9
  150.6 9.2 %copy-start.1 = (f32[576,4096]{1,0:T(8,128)}, f32[576,4096]{1,0:T(8,128)S(1)}, u32[]{:S(2)}) copy-start(f32[576,4096]{1,0:T(8,128)S(1)} %convolution_add_fusion) | copy-start | bytes 28311556
  150.6 9.2 %slice-start.5 = ((s8[4718592]{0:T(1024)(128)(4,1)}), s8[4194304]{0:T(1024)(128)(4,1)S(1)}, s32[]{:S(2)}) async-start(s8[4718592]{0:T(1024)(128)(4,1)} %bitcast.139), calls=%async_computation.8 | async-start | bytes 8388608
  152.4 20.1 %collective-permute-start.13 = (bf16[4,72,4096]{2,1,0:T(8,128)(2,1)}, bf16[4,72,4096]{2,1,0:T(8,128)(2,1)}, u32[]{:S(2)}, u32[]{:S(2)}) collective-permute-start(bf16[4,72,4096]{2,1,0:T(8,128)(2,1)} %bitcast.35), channel_id=1, source_target_pairs={{0,1},{1,0},{2,3},{3,2},{4,5},{5,4},{6,7},{7,6},{8,9},{9,8},{10,11... | collective-permute-start | bytes 7077896 | tf_op jit(solution)/shard_map/ppermute | solution.py:33
  152.9 6.9 %slice-start.6 = ((s8[4718592]{0:T(1024)(128)(4,1)}), s8[524288]{0:T(1024)(128)(4,1)S(1)}, s32[]{:S(2)}) async-start(s8[4718592]{0:T(1024)(128)(4,1)} %bitcast.139), calls=%async_computation.9 | async-start | bytes 1048576
  166.3 18.0 %collective-permute-start.7 = (bf16[72,4096]{1,0:T(8,128)(2,1)S(1)}, bf16[72,4096]{1,0:T(8,128)(2,1)S(1)}, u32[]{:S(2)}, u32[]{:S(2)}) collective-permute-start(bf16[72,4096]{1,0:T(8,128)(2,1)S(1)} %get-tuple-element.18), channel_id=1, source_target_pairs={{0,2},{2,4},{4,6},{6,0},{1,3},{3,5},{5,7},{7,1},{8,10},{10,12},{12... | collective-permute-start | bytes 1769480 | tf_op jit(solution)/shard_map/ppermute | solution.py:38
  168.8 51.6 %collective-permute-start.6 = (bf16[72,4096]{1,0:T(8,128)(2,1)S(1)}, bf16[72,4096]{1,0:T(8,128)(2,1)S(1)}, u32[]{:S(2)}, u32[]{:S(2)}) collective-permute-start(bf16[72,4096]{1,0:T(8,128)(2,1)S(1)} %get-tuple-element.19), channel_id=1, source_target_pairs={{0,4},{2,6},{4,0},{6,2},{1,5},{3,7},{5,1},{7,3},{8,12},{10,14},{12... | collective-permute-start | bytes 1769480 | tf_op jit(solution)/shard_map/ppermute | solution.py:38
  172.5 76.6 %collective-permute-start.5 = (bf16[72,4096]{1,0:T(8,128)(2,1)S(1)}, bf16[72,4096]{1,0:T(8,128)(2,1)S(1)}, u32[]{:S(2)}, u32[]{:S(2)}) collective-permute-start(bf16[72,4096]{1,0:T(8,128)(2,1)S(1)} %get-tuple-element.20), channel_id=1, source_target_pairs={{0,6},{2,0},{4,2},{6,4},{1,7},{3,1},{5,3},{7,5},{8,14},{10,8},{12,... | collective-permute-start | bytes 1769480 | tf_op jit(solution)/shard_map/ppermute | solution.py:38
  172.5 2.9 slice-start
  178.0 80.4 %collective-permute-start.16 = (bf16[72,4096]{1,0:T(8,128)(2,1)S(1)}, bf16[72,4096]{1,0:T(8,128)(2,1)S(1)}, u32[]{:S(2)}, u32[]{:S(2)}) collective-permute-start(bf16[72,4096]{1,0:T(8,128)(2,1)S(1)} %get-tuple-element.10), channel_id=1, source_target_pairs={{0,2},{2,4},{4,6},{6,0},{1,3},{3,5},{5,7},{7,1},{8,10},{10,12},{12... | collective-permute-start | bytes 1769480 | tf_op jit(solution)/shard_map/ppermute | solution.py:38
  179.8 90.8 %collective-permute-start.15 = (bf16[72,4096]{1,0:T(8,128)(2,1)S(1)}, bf16[72,4096]{1,0:T(8,128)(2,1)S(1)}, u32[]{:S(2)}, u32[]{:S(2)}) collective-permute-start(bf16[72,4096]{1,0:T(8,128)(2,1)S(1)} %get-tuple-element.11), channel_id=1, source_target_pairs={{0,4},{2,6},{4,0},{6,2},{1,5},{3,7},{5,1},{7,3},{8,12},{10,14},{12... | collective-permute-start | bytes 1769480 | tf_op jit(solution)/shard_map/ppermute | solution.py:38
  184.3 89.6 %collective-permute-start.14 = (bf16[72,4096]{1,0:T(8,128)(2,1)S(1)}, bf16[72,4096]{1,0:T(8,128)(2,1)S(1)}, u32[]{:S(2)}, u32[]{:S(2)}) collective-permute-start(bf16[72,4096]{1,0:T(8,128)(2,1)S(1)} %get-tuple-element.12), channel_id=1, source_target_pairs={{0,6},{2,0},{4,2},{6,4},{1,7},{3,1},{5,3},{7,5},{8,14},{10,8},{12,... | collective-permute-start | bytes 1769480 | tf_op jit(solution)/shard_map/ppermute | solution.py:38
  249.1 1.2 copy-start.2
  252.2 25.3 %collective-permute-start.8 = (bf16[1,128,4096]{2,1,0:T(8,128)(2,1)S(1)}, bf16[1,128,4096]{2,1,0:T(8,128)(2,1)}, u32[]{:S(2)}, u32[]{:S(2)}) collective-permute-start(bf16[1,128,4096]{2,1,0:T(8,128)(2,1)S(1)} %fusion.2), channel_id=1, source_target_pairs={{0,16},{1,17},{2,18},{3,19},{4,20},{5,21},{6,22},{7,23},{8,24},{9,... | collective-permute-start | bytes 3145736 | tf_op jit(solution)/shard_map/ppermute | solution.py:17
  274.2 1.2 copy-start.4
  276.3 26.7 %collective-permute-start.17 = (bf16[1,128,4096]{2,1,0:T(8,128)(2,1)S(1)}, bf16[1,128,4096]{2,1,0:T(8,128)(2,1)}, u32[]{:S(2)}, u32[]{:S(2)}) collective-permute-start(bf16[1,128,4096]{2,1,0:T(8,128)(2,1)S(1)} %fusion.24), channel_id=1, source_target_pairs={{16,0},{17,1},{18,2},{19,3},{20,4},{21,5},{22,6},{23,7},{24,8},{25... | collective-permute-start | bytes 3145736 | tf_op jit(solution)/shard_map/ppermute | solution.py:17
Sparse Core Ops, SparseCore 0:
  9.5 46.0 all-gather.2
  164.7 44.9 reduce-scatter.1

commit v5 on v2

--- a/solution.py
+++ b/solution.py
@@ -52,6 +52,33 @@
     summed = (paired[0] + other.astype(jnp.float32)).astype(jnp.bfloat16)
     returned = jnp.stack([summed[0]] + [shifted(summed[k], -k) for k in range(1, experts)])
     return returned.reshape(experts * capacity, model_width).astype(jnp.float32)
+
+
+def dp_shifted(value, steps):
+    count = lax.axis_size("dp")
+    return lax.ppermute(value, "dp", [(source, (source + steps) % count) for source in range(count)])
+
+
+def gather_replicas(piece):
+    count = lax.axis_size("dp")
+    here = lax.axis_index("dp")
+    width = piece.shape[1]
+    whole = jnp.zeros((piece.shape[0], width * count), piece.dtype)
+    for steps in range(count):
+        arrived = piece if steps == 0 else dp_shifted(piece, steps)
+        whole = lax.dynamic_update_slice_in_dim(whole, arrived, ((here - steps) % count) * width, 1)
+    return whole
+
+
+def sum_replicas(term):
+    count = lax.axis_size("dp")
+    here = lax.axis_index("dp")
+    rows = term.shape[0] // count
+    total = lax.dynamic_slice_in_dim(term, here * rows, rows, 0).astype(jnp.float32)
+    for steps in range(1, count):
+        chunk = lax.dynamic_slice_in_dim(term, ((here + steps) % count) * rows, rows, 0)
+        total = total + dp_shifted(chunk, steps).astype(jnp.float32)
+    return total.astype(jnp.bfloat16)
 
 
 def per_device(
@@ -88,7 +115,7 @@
     gate_local = gate_weight[0]
     up_local = up_weight[0]
     leak_local = leak_rates[0]
-    down_full = lax.all_gather(down_weight[0], "dp", axis=1, tiled=True)
+    down_full = gather_replicas(down_weight[0])
     gate_act = jnp.dot(arrived, gate_local, preferred_element_type=jnp.float32)
     up_act = jnp.dot(arrived, up_local, preferred_element_type=jnp.float32)
     spike_rate = lif_rate(gate_act, up_act, leak_local).astype(jnp.bfloat16)
@@ -151,9 +178,7 @@
         arrived, up_act_grad, (((0,), (0,)), ((), ())), preferred_element_type=jnp.float32
     )
     up_term = up_term.astype(jnp.bfloat16).astype(jnp.float32)
-    up_grad = lax.psum_scatter(up_term.astype(jnp.bfloat16), "dp", scatter_dimension=0, tiled=True)[
-        None
-    ]
+    up_grad = sum_replicas(up_term.astype(jnp.bfloat16))[None]
     return (passed_on, passed_back, up_grad)
 
 

time: 315 us -> 325 us (1.032)
  the two profiles are of different devices: /device:TPU:8 before, /device:TPU:0 now
where the time goes in v5:
time: 325 us; the launch traced here: 324 us
  waiting for transfers between devices  185 us (57%)
  starting transfers between devices  50.3 us (15%)
  matrix products  36.1 us (11%)
  local copies, waits for them, and re-layouts  32.3 us (10%)
  other arithmetic  19.5 us (6%)
    ppermute x12, waiting for transfers between devices, shifted(): lax.ppermute(value, 'chip', [(source, (source + steps) % count) for sourc...  160 us
    ppermute x12, starting transfers between devices, shifted(): lax.ppermute(value, 'chip', [(source, (source + steps) % count) for sourc...  41.3 us
    ppermute x2, waiting for transfers between devices, passed_along(): lax.ppermute(value, axis, [(source, source + steps) for source in range(l...  21 us
    unnamed x47, local copies, waits for them, and re-layouts  16.2 us
    convert_element_type x2, other arithmetic, from_experts(): summed = (paired[0] + other.astype(jnp.float32)).astype(jnp.bfloat16)  6.77 us
  transfers between devices with their start and end apart: 20, of which 10 were waited for; matrix products, arithmetic and copies ran while one was open for 17% of the time, Pallas kernels for 0%

profile of v5, /device:TPU:0, one launch (start us, length us, event | category | flops | bytes accessed | tf_op | source)
XLA Modules:
  0.0 324.3 jit_solution(13449736351998405272)
XLA Ops:
  3.9 1.5 fusion.14
  5.5 2.1 convolution_convert_fusion.1
  7.6 1.5 slice_bitcast_fusion.6
  9.0 3.1 collective-permute-start
  12.1 2.6 collective-permute-start.1
  16.0 1.5 collective-permute-start.4
  19.3 2.3 fusion
  22.1 1.7 constant_dynamic-update-slice_fusion.11
  23.8 5.0 %collective-permute-done = bf16[72,4096]{1,0:T(8,128)(2,1)} collective-permute-done((bf16[72,4096]{1,0:T(8,128)(2,1)}, bf16[72,4096]{1,0:T(8,128)(2,1)}, u32[]{:S(2)}, u32[]{:S(2)}) %collective-permute-start) | collective-permute-done | bytes 589856 | tf_op jit(solution)/shard_map/ppermute | solution.py:38
  28.8 24.4 %collective-permute-done.1 = bf16[72,4096]{1,0:T(8,128)(2,1)} collective-permute-done((bf16[72,4096]{1,0:T(8,128)(2,1)}, bf16[72,4096]{1,0:T(8,128)(2,1)}, u32[]{:S(2)}, u32[]{:S(2)}) %collective-permute-start.1) | collective-permute-done | bytes 589856 | tf_op jit(solution)/shard_map/ppermute | solution.py:38
  53.2 1.9 pad_maximum_fusion
  59.4 1.6 constant_dynamic-update-slice_fusion.10
  61.2 3.4 %copy-done.6 = bf16[1,4096,384]{2,1,0:T(8,128)(2,1)S(1)} copy-done((bf16[1,4096,384]{2,1,0:T(8,128)(2,1)S(1)}, bf16[1,4096,384]{2,1,0:T(8,128)(2,1)}, u32[]{:S(2)}) %copy-start.6) | copy-done | bytes 3145752
  64.6 2.6 fusion.4
  67.2 2.6 fusion.8
  69.8 4.9 %fusion.63 = f32[576,4096]{1,0:T(8,128)S(1)} fusion(bf16[384,4096]{1,0:T(8,128)(2,1)S(1)} %constant_dynamic-update-slice_fusion.10, f32[384]{0:T(512)S(1)} %reduce.2, f32[384]{0:T(512)S(1)} %broadcast_multiply_fusion, f32[576,384]{1,0:T(8,128)S(1)} %fusion.4, f32[576,384]{1,0:T(8,128)S(1)} %fusion.8), kind=kOutput, calls=%fused_computation.114 | convolution fusion | flops 1827643392 | bytes 14355456 | tf_op jit(solution)/shard_map/dot_general | solution.py:122
  74.7 1.7 slice.164
  78.3 13.2 %collective-permute-start.10 = (bf16[72,4096]{1,0:T(8,128)(2,1)S(1)}, bf16[72,4096]{1,0:T(8,128)(2,1)S(1)}, u32[]{:S(2)}, u32[]{:S(2)}) collective-permute-start(bf16[72,4096]{1,0:T(8,128)(2,1)S(1)} %get-tuple-element.14), channel_id=1, source_target_pairs={{0,2},{2,4},{4,6},{6,0},{1,3},{3,5},{5,7},{7,1},{8,10},{10,12},{12... | collective-permute-start | bytes 1769480 | tf_op jit(solution)/shard_map/ppermute | solution.py:38
  91.4 1.6 collective-permute-start.11
  93.9 12.9 %collective-permute-done.10 = bf16[72,4096]{1,0:T(8,128)(2,1)S(1)} collective-permute-done((bf16[72,4096]{1,0:T(8,128)(2,1)S(1)}, bf16[72,4096]{1,0:T(8,128)(2,1)S(1)}, u32[]{:S(2)}, u32[]{:S(2)}) %collective-permute-start.10) | collective-permute-done | bytes 589856 | tf_op jit(solution)/shard_map/ppermute | solution.py:38
  106.8 24.2 %collective-permute-done.11 = bf16[72,4096]{1,0:T(8,128)(2,1)S(1)} collective-permute-done((bf16[72,4096]{1,0:T(8,128)(2,1)S(1)}, bf16[72,4096]{1,0:T(8,128)(2,1)S(1)}, u32[]{:S(2)}, u32[]{:S(2)}) %collective-permute-start.11) | collective-permute-done | bytes 589856 | tf_op jit(solution)/shard_map/ppermute | solution.py:38
  131.5 4.4 %collective-permute-done.13 = bf16[4,72,4096]{2,1,0:T(8,128)(2,1)S(1)} collective-permute-done((bf16[4,72,4096]{2,1,0:T(8,128)(2,1)S(1)}, bf16[4,72,4096]{2,1,0:T(8,128)(2,1)S(1)}, u32[]{:S(2)}, u32[]{:S(2)}) %collective-permute-start.13) | collective-permute-done | bytes 2359328 | tf_op jit(solution)/shard_map/ppermute | solution.py:33
  136.0 6.3 %multiply_convert_fusion = (bf16[576,384]{1,0:T(8,128)(2,1)S(1)}, f32[576,384]{1,0:T(8,128)S(1)}) fusion(f32[576,384]{1,0:T(8,128)S(1)} %fusion.8, f32[576,384]{1,0:T(8,128)S(1)} %fusion.4, f32[384]{0:T(512)S(1)} %broadcast_multiply_fusion, f32[384]{0:T(512)S(1)} %reduce.2, bf16[576,4096]{1,0:T(8,128)(2,1)S(1)} %bitcast.135, ...), kind=kOutput, calls=%fused_computation.91 | convolution fusion | flops 1840693248 | bytes 10963968 | tf_op jit(solution)/shard_map/dot_general | solution.py:144
  142.3 2.7 fusion.6
  145.1 4.5 %convolution_add_fusion = f32[576,4096]{1,0:T(8,128)S(1)} fusion(f32[576,4096]{1,0:T(8,128)S(1)} %fusion.6, bf16[576,384]{1,0:T(8,128)(2,1)S(1)} %get-tuple-element.27, bf16[1,4096,384]{2,1,0:T(8,128)(2,1)} %param.14), kind=kOutput, calls=%fused_computation | convolution fusion | flops 1814298624 | bytes 22462464 | tf_op jit(solution)/shard_map/dot_general | solution.py:156
  149.6 2.0 slice.163
  151.8 4.1 %add_convert_fusion.1 = bf16[4,72,4096]{2,1,0:T(8,128)(2,1)S(1)} fusion(f32[4,72,4096]{2,1,0:T(8,128)S(1)} %bitcast.121, bf16[4,72,4096]{2,1,0:T(8,128)(2,1)} %collective-permute-done.5), kind=kLoop, calls=%fused_computation.11 | loop fusion | flops 3538944 | bytes 9437184 | tf_op jit(solution)/shard_map/convert_element_type | solution.py:52
  155.9 1.5 fusion.104
  157.3 14.3 %collective-permute-start.6 = (bf16[72,4096]{1,0:T(8,128)(2,1)}, bf16[72,4096]{1,0:T(8,128)(2,1)}, u32[]{:S(2)}, u32[]{:S(2)}) collective-permute-start(bf16[72,4096]{1,0:T(8,128)(2,1)} %get-tuple-element.18), channel_id=1, source_target_pairs={{0,6},{2,0},{4,2},{6,4},{1,7},{3,1},{5,3},{7,5},{8,14},{10,8},{12,... | collective-permute-start | bytes 1769480 | tf_op jit(solution)/shard_map/ppermute | solution.py:38
  172.2 13.6 %collective-permute-done.6 = bf16[72,4096]{1,0:T(8,128)(2,1)} collective-permute-done((bf16[72,4096]{1,0:T(8,128)(2,1)}, bf16[72,4096]{1,0:T(8,128)(2,1)}, u32[]{:S(2)}, u32[]{:S(2)}) %collective-permute-start.6) | collective-permute-done | bytes 589856 | tf_op jit(solution)/shard_map/ppermute | solution.py:38
  185.7 37.8 %collective-permute-done.7 = bf16[72,4096]{1,0:T(8,128)(2,1)} collective-permute-done((bf16[72,4096]{1,0:T(8,128)(2,1)}, bf16[72,4096]{1,0:T(8,128)(2,1)}, u32[]{:S(2)}, u32[]{:S(2)}) %collective-permute-start.7) | collective-permute-done | bytes 589856 | tf_op jit(solution)/shard_map/ppermute | solution.py:38
  223.5 2.0 pad_maximum_fusion.1
  225.5 2.8 fusion.2
  228.4 4.4 %collective-permute-start.9 = (bf16[1,128,4096]{2,1,0:T(8,128)(2,1)}, bf16[1,128,4096]{2,1,0:T(8,128)(2,1)}, u32[]{:S(2)}, u32[]{:S(2)}) collective-permute-start(bf16[1,128,4096]{2,1,0:T(8,128)(2,1)} %fusion.2), channel_id=1, source_target_pairs={{0,16},{1,17},{2,18},{3,19},{4,20},{5,21},{6,22},{7,23},{8,24},{9,... | collective-permute-start | bytes 3145736 | tf_op jit(solution)/shard_map/ppermute | solution.py:17
  232.8 2.3 slice-done
  235.1 2.7 add_convert_fusion
  238.1 1.8 collective-permute-start.16
  239.9 1.9 collective-permute-start.17
  241.9 3.5 %convolution_convert_fusion = bf16[4096,384]{1,0:T(8,128)(2,1)S(1)} fusion(bf16[576,4096]{1,0:T(8,128)(2,1)S(1)} %bitcast.134, bf16[576,384]{1,0:T(8,128)(2,1)S(1)} %copy-done.10), kind=kOutput, calls=%fused_computation.1 | convolution fusion | flops 1813512192 | bytes 8306688 | tf_op jit(solution)/shard_map/dot_general | solution.py:177
  245.4 1.4 constant_dynamic-slice_fusion
  246.8 1.5 collective-permute-start.19
  248.3 4.9 %collective-permute-done.15 = bf16[72,4096]{1,0:T(8,128)(2,1)S(1)} collective-permute-done((bf16[72,4096]{1,0:T(8,128)(2,1)S(1)}, bf16[72,4096]{1,0:T(8,128)(2,1)S(1)}, u32[]{:S(2)}, u32[]{:S(2)}) %collective-permute-start.15) | collective-permute-done | bytes 589856 | tf_op jit(solution)/shard_map/ppermute | solution.py:38
  253.2 37.1 %collective-permute-done.16 = bf16[72,4096]{1,0:T(8,128)(2,1)S(1)} collective-permute-done((bf16[72,4096]{1,0:T(8,128)(2,1)S(1)}, bf16[72,4096]{1,0:T(8,128)(2,1)S(1)}, u32[]{:S(2)}, u32[]{:S(2)}) %collective-permute-start.16) | collective-permute-done | bytes 589856 | tf_op jit(solution)/shard_map/ppermute | solution.py:38
  292.2 1.8 fusion.21
  295.4 3.4 %fusion.19 = bf16[1,2048,384]{2,1,0:T(8,128)(2,1)} fusion(bf16[2048,384]{1,0:T(8,128)(2,1)} %collective-permute-done.19, bf16[4096,384]{1,0:T(8,128)(2,1)} %copy-done.7, s32[]{:T(128)S(6)} %select_n.59), kind=kLoop, calls=%fused_computation.41 | loop fusion | flops 3145728 | bytes 4718596 | tf_op jit(solution)/shard_map/broadcast_in_dim | solution.py:181
  298.8 21.0 %collective-permute-done.18 = bf16[1,128,4096]{2,1,0:T(8,128)(2,1)} collective-permute-done((bf16[1,128,4096]{2,1,0:T(8,128)(2,1)}, bf16[1,128,4096]{2,1,0:T(8,128)(2,1)}, u32[]{:S(2)}, u32[]{:S(2)}) %collective-permute-start.18) | collective-permute-done | bytes 1048608 | tf_op jit(solution)/shard_map/ppermute | solution.py:17
  319.8 2.3 copy.34
  322.1 2.3 copy.35
  (98 shorter events, 18.8 us)
Async XLA Ops:
  0.6 66.6 %copy-start = (bf16[1,4096,384]{2,1,0:T(8,128)(2,1)S(1)}, bf16[1,4096,384]{2,1,0:T(8,128)(2,1)}, u32[]{:S(2)}) copy-start(bf16[1,4096,384]{2,1,0:T(8,128)(2,1)} %param.13) | copy-start | bytes 9437188
  7.6 10.9 %copy-start.15 = (f32[1,128,2]{1,2,0:T(2,128)S(1)}, f32[1,128,2]{1,2,0:T(2,128)}, u32[]{:S(2)}) copy-start(f32[1,128,2]{1,2,0:T(2,128)} %param.12) | copy-start | bytes 3076
  7.6 10.9 %copy-start.4 = (bf16[1,128,4096]{2,1,0:T(8,128)(2,1)S(1)}, bf16[1,128,4096]{2,1,0:T(8,128)(2,1)}, u32[]{:S(2)}) copy-start(bf16[1,128,4096]{2,1,0:T(8,128)(2,1)} %param.17) | copy-start | bytes 3145732
  9.0 19.7 %collective-permute-start = (bf16[72,4096]{1,0:T(8,128)(2,1)}, bf16[72,4096]{1,0:T(8,128)(2,1)}, u32[]{:S(2)}, u32[]{:S(2)}) collective-permute-start(bf16[72,4096]{1,0:T(8,128)(2,1)} %get-tuple-element.22), channel_id=1, source_target_pairs={{0,2},{2,4},{4,6},{6,0},{1,3},{3,5},{5,7},{7,1},{8,10},{10,12},{12... | collective-permute-start | bytes 1769480 | tf_op jit(solution)/shard_map/ppermute | solution.py:38
  12.1 41.1 %collective-permute-start.1 = (bf16[72,4096]{1,0:T(8,128)(2,1)}, bf16[72,4096]{1,0:T(8,128)(2,1)}, u32[]{:S(2)}, u32[]{:S(2)}) collective-permute-start(bf16[72,4096]{1,0:T(8,128)(2,1)} %get-tuple-element.21), channel_id=1, source_target_pairs={{0,4},{2,6},{4,0},{6,2},{1,5},{3,7},{5,1},{7,3},{8,12},{10,14},{12... | collective-permute-start | bytes 1769480 | tf_op jit(solution)/shard_map/ppermute | solution.py:38
  14.7 38.5 %collective-permute-start.2 = (bf16[72,4096]{1,0:T(8,128)(2,1)}, bf16[72,4096]{1,0:T(8,128)(2,1)}, u32[]{:S(2)}, u32[]{:S(2)}) collective-permute-start(bf16[72,4096]{1,0:T(8,128)(2,1)} %get-tuple-element.20), channel_id=1, source_target_pairs={{0,6},{2,0},{4,2},{6,4},{1,7},{3,1},{5,3},{7,5},{8,14},{10,8},{12,... | collective-permute-start | bytes 1769480 | tf_op jit(solution)/shard_map/ppermute | solution.py:38
  16.0 43.3 %collective-permute-start.4 = (bf16[384,2048]{1,0:T(8,128)(2,1)}, bf16[384,2048]{1,0:T(8,128)(2,1)}, u32[]{:S(2)}, u32[]{:S(2)}) collective-permute-start(bf16[384,2048]{1,0:T(8,128)(2,1)} %bitcast.16), channel_id=1, source_target_pairs={{0,8},{8,0},{1,9},{9,1},{2,10},{10,2},{3,11},{11,3},{4,12},{12,4},... | collective-permute-start | bytes 4718600 | tf_op jit(solution)/shard_map/ppermute | solution.py:59
  19.3 2.3 copy-start.14
  22.1 31.1 %copy-start.8 = (bf16[1,72,4096]{2,1,0:T(8,128)(2,1)S(1)}, bf16[1,72,4096]{2,1,0:T(8,128)(2,1)}, u32[]{:S(2)}) copy-start(bf16[1,72,4096]{2,1,0:T(8,128)(2,1)} %get-tuple-element.19) | copy-start | bytes 1769476
  53.2 2.9 copy-start.11
  55.1 6.0 %collective-permute-start.3 = (bf16[4,72,4096]{2,1,0:T(8,128)(2,1)S(1)}, bf16[4,72,4096]{2,1,0:T(8,128)(2,1)S(1)}, u32[]{:S(2)}, u32[]{:S(2)}) collective-permute-start(bf16[4,72,4096]{2,1,0:T(8,128)(2,1)S(1)} %pad_maximum_fusion), channel_id=1, source_target_pairs={{0,1},{1,0},{2,3},{3,2},{4,5},{5,4},{6,7},{7,6},{8,9},{9,8},{10,11... | collective-permute-start | bytes 7077896 | tf_op jit(solution)/shard_map/ppermute | solution.py:33
  61.0 3.6 %copy-start.6 = (bf16[1,4096,384]{2,1,0:T(8,128)(2,1)S(1)}, bf16[1,4096,384]{2,1,0:T(8,128)(2,1)}, u32[]{:S(2)}) copy-start(bf16[1,4096,384]{2,1,0:T(8,128)(2,1)} %param.14) | copy-start | bytes 9437188
  61.2 6.0 %copy-start.12 = (bf16[8,72,4096]{2,1,0:T(8,128)(2,1)}, bf16[8,72,4096]{2,1,0:T(8,128)(2,1)S(1)}, u32[]{:S(2)}) copy-start(bf16[8,72,4096]{2,1,0:T(8,128)(2,1)S(1)} %constant_dynamic-update-slice_fusion) | copy-start | bytes 14155780
  76.5 1.7 copy-start.3
  78.3 28.5 %collective-permute-start.10 = (bf16[72,4096]{1,0:T(8,128)(2,1)S(1)}, bf16[72,4096]{1,0:T(8,128)(2,1)S(1)}, u32[]{:S(2)}, u32[]{:S(2)}) collective-permute-start(bf16[72,4096]{1,0:T(8,128)(2,1)S(1)} %get-tuple-element.14), channel_id=1, source_target_pairs={{0,2},{2,4},{4,6},{6,0},{1,3},{3,5},{5,7},{7,1},{8,10},{10,12},{12... | collective-permute-start | bytes 1769480 | tf_op jit(solution)/shard_map/ppermute | solution.py:38
  91.4 39.5 %collective-permute-start.11 = (bf16[72,4096]{1,0:T(8,128)(2,1)S(1)}, bf16[72,4096]{1,0:T(8,128)(2,1)S(1)}, u32[]{:S(2)}, u32[]{:S(2)}) collective-permute-start(bf16[72,4096]{1,0:T(8,128)(2,1)S(1)} %get-tuple-element.13), channel_id=1, source_target_pairs={{0,4},{2,6},{4,0},{6,2},{1,5},{3,7},{5,1},{7,3},{8,12},{10,14},{12... | collective-permute-start | bytes 1769480 | tf_op jit(solution)/shard_map/ppermute | solution.py:38
  93.0 37.9 %collective-permute-start.12 = (bf16[72,4096]{1,0:T(8,128)(2,1)S(1)}, bf16[72,4096]{1,0:T(8,128)(2,1)S(1)}, u32[]{:S(2)}, u32[]{:S(2)}) collective-permute-start(bf16[72,4096]{1,0:T(8,128)(2,1)S(1)} %get-tuple-element.12), channel_id=1, source_target_pairs={{0,6},{2,0},{4,2},{6,4},{1,7},{3,1},{5,3},{7,5},{8,14},{10,8},{12,... | collective-permute-start | bytes 1769480 | tf_op jit(solution)/shard_map/ppermute | solution.py:38
  93.9 57.9 %collective-permute-start.5 = (bf16[4,72,4096]{2,1,0:T(8,128)(2,1)}, bf16[4,72,4096]{2,1,0:T(8,128)(2,1)}, u32[]{:S(2)}, u32[]{:S(2)}) collective-permute-start(bf16[4,72,4096]{2,1,0:T(8,128)(2,1)} %bitcast.18), channel_id=1, source_target_pairs={{0,1},{1,0},{2,3},{3,2},{4,5},{5,4},{6,7},{7,6},{8,9},{9,8},{10,11... | collective-permute-start | bytes 7077896 | tf_op jit(solution)/shard_map/ppermute | solution.py:33
  131.3 4.6 %collective-permute-start.13 = (bf16[4,72,4096]{2,1,0:T(8,128)(2,1)S(1)}, bf16[4,72,4096]{2,1,0:T(8,128)(2,1)S(1)}, u32[]{:S(2)}, u32[]{:S(2)}) collective-permute-start(bf16[4,72,4096]{2,1,0:T(8,128)(2,1)S(1)} %pad_maximum_fusion.2), channel_id=1, source_target_pairs={{0,1},{1,0},{2,3},{3,2},{4,5},{5,4},{6,7},{7,6},{8,9},{9,8},{10,11... | collective-permute-start | bytes 7077896 | tf_op jit(solution)/shard_map/ppermute | solution.py:33
  142.3 2.7 copy-start.9
  149.6 6.3 %copy-start.1 = (f32[576,4096]{1,0:T(8,128)}, f32[576,4096]{1,0:T(8,128)S(1)}, u32[]{:S(2)}) copy-start(f32[576,4096]{1,0:T(8,128)S(1)} %convolution_add_fusion) | copy-start | bytes 28311556
  151.6 81.2 %collective-permute-start.14 = (bf16[4,72,4096]{2,1,0:T(8,128)(2,1)}, bf16[4,72,4096]{2,1,0:T(8,128)(2,1)}, u32[]{:S(2)}, u32[]{:S(2)}) collective-permute-start(bf16[4,72,4096]{2,1,0:T(8,128)(2,1)} %bitcast.35), channel_id=1, source_target_pairs={{0,1},{1,0},{2,3},{3,2},{4,5},{5,4},{6,7},{7,6},{8,9},{9,8},{10,11... | collective-permute-start | bytes 7077896 | tf_op jit(solution)/shard_map/ppermute | solution.py:33
  157.3 28.4 %collective-permute-start.6 = (bf16[72,4096]{1,0:T(8,128)(2,1)}, bf16[72,4096]{1,0:T(8,128)(2,1)}, u32[]{:S(2)}, u32[]{:S(2)}) collective-permute-start(bf16[72,4096]{1,0:T(8,128)(2,1)} %get-tuple-element.18), channel_id=1, source_target_pairs={{0,6},{2,0},{4,2},{6,4},{1,7},{3,1},{5,3},{7,5},{8,14},{10,8},{12,... | collective-permute-start | bytes 1769480 | tf_op jit(solution)/shard_map/ppermute | solution.py:38
  171.6 51.9 %collective-permute-start.7 = (bf16[72,4096]{1,0:T(8,128)(2,1)}, bf16[72,4096]{1,0:T(8,128)(2,1)}, u32[]{:S(2)}, u32[]{:S(2)}) collective-permute-start(bf16[72,4096]{1,0:T(8,128)(2,1)} %get-tuple-element.17), channel_id=1, source_target_pairs={{0,4},{2,6},{4,0},{6,2},{1,5},{3,7},{5,1},{7,3},{8,12},{10,14},{12... | collective-permute-start | bytes 1769480 | tf_op jit(solution)/shard_map/ppermute | solution.py:38
  171.9 51.6 %collective-permute-start.8 = (bf16[72,4096]{1,0:T(8,128)(2,1)}, bf16[72,4096]{1,0:T(8,128)(2,1)}, u32[]{:S(2)}, u32[]{:S(2)}) collective-permute-start(bf16[72,4096]{1,0:T(8,128)(2,1)} %get-tuple-element.16), channel_id=1, source_target_pairs={{0,2},{2,4},{4,6},{6,0},{1,3},{3,5},{5,7},{7,1},{8,10},{10,12},{12... | collective-permute-start | bytes 1769480 | tf_op jit(solution)/shard_map/ppermute | solution.py:38
  223.5 2.0 copy-start.2
  228.4 67.0 %collective-permute-start.9 = (bf16[1,128,4096]{2,1,0:T(8,128)(2,1)}, bf16[1,128,4096]{2,1,0:T(8,128)(2,1)}, u32[]{:S(2)}, u32[]{:S(2)}) collective-permute-start(bf16[1,128,4096]{2,1,0:T(8,128)(2,1)} %fusion.2), channel_id=1, source_target_pairs={{0,16},{1,17},{2,18},{3,19},{4,20},{5,21},{6,22},{7,23},{8,24},{9,... | collective-permute-start | bytes 3145736 | tf_op jit(solution)/shard_map/ppermute | solution.py:17
  232.8 2.3 slice-start
  232.8 9.1 %slice-start.1 = ((s8[4718592]{0:T(1024)(128)(4,1)}), s8[4194304]{0:T(1024)(128)(4,1)S(1)}, s32[]{:S(2)}) async-start(s8[4718592]{0:T(1024)(128)(4,1)} %bitcast.132), calls=%async_computation.1 | async-start | bytes 8388608
  235.1 6.7 %slice-start.2 = ((s8[4718592]{0:T(1024)(128)(4,1)}), s8[524288]{0:T(1024)(128)(4,1)S(1)}, s32[]{:S(2)}) async-start(s8[4718592]{0:T(1024)(128)(4,1)} %bitcast.132), calls=%async_computation.2 | async-start | bytes 1048576
  237.8 4.0 %copy-start.10 = (bf16[576,384]{1,0:T(8,128)(2,1)S(1)}, bf16[576,384]{1,0:T(8,128)(2,1)}, u32[]{:S(2)}) copy-start(bf16[576,384]{1,0:T(8,128)(2,1)} %copy-done.9) | copy-start | bytes 1327108
  238.0 15.2 %collective-permute-start.15 = (bf16[72,4096]{1,0:T(8,128)(2,1)S(1)}, bf16[72,4096]{1,0:T(8,128)(2,1)S(1)}, u32[]{:S(2)}, u32[]{:S(2)}) collective-permute-start(bf16[72,4096]{1,0:T(8,128)(2,1)S(1)} %get-tuple-element.10), channel_id=1, source_target_pairs={{0,6},{2,0},{4,2},{6,4},{1,7},{3,1},{5,3},{7,5},{8,14},{10,8},{12,... | collective-permute-start | bytes 1769480 | tf_op jit(solution)/shard_map/ppermute | solution.py:38
  238.1 52.2 %collective-permute-start.16 = (bf16[72,4096]{1,0:T(8,128)(2,1)S(1)}, bf16[72,4096]{1,0:T(8,128)(2,1)S(1)}, u32[]{:S(2)}, u32[]{:S(2)}) collective-permute-start(bf16[72,4096]{1,0:T(8,128)(2,1)S(1)} %get-tuple-element.9), channel_id=1, source_target_pairs={{0,4},{2,6},{4,0},{6,2},{1,5},{3,7},{5,1},{7,3},{8,12},{10,14},{12... | collective-permute-start | bytes 1769480 | tf_op jit(solution)/shard_map/ppermute | solution.py:38
  239.9 50.4 %collective-permute-start.17 = (bf16[72,4096]{1,0:T(8,128)(2,1)S(1)}, bf16[72,4096]{1,0:T(8,128)(2,1)S(1)}, u32[]{:S(2)}, u32[]{:S(2)}) collective-permute-start(bf16[72,4096]{1,0:T(8,128)(2,1)S(1)} %get-tuple-element.8), channel_id=1, source_target_pairs={{0,2},{2,4},{4,6},{6,0},{1,3},{3,5},{5,7},{7,1},{8,10},{10,12},{12... | collective-permute-start | bytes 1769480 | tf_op jit(solution)/shard_map/ppermute | solution.py:38
  245.4 44.9 %copy-start.7 = (bf16[4096,384]{1,0:T(8,128)(2,1)}, bf16[4096,384]{1,0:T(8,128)(2,1)S(1)}, u32[]{:S(2)}) copy-start(bf16[4096,384]{1,0:T(8,128)(2,1)S(1)} %convolution_convert_fusion) | copy-start | bytes 9437188
  246.8 48.5 %collective-permute-start.19 = (bf16[2048,384]{1,0:T(8,128)(2,1)}, bf16[2048,384]{1,0:T(8,128)(2,1)}, u32[]{:S(2)}, u32[]{:S(2)}) collective-permute-start(bf16[2048,384]{1,0:T(8,128)(2,1)} %constant_dynamic-slice_fusion), channel_id=1, source_target_pairs={{0,8},{8,0},{1,9},{9,1},{2,10},{10,2},{3,11},{11,3},{4,12},{12,4},... | collective-permute-start | bytes 4718600 | tf_op jit(solution)/shard_map/ppermute | solution.py:59
  290.3 0.7 copy-start.13
  291.0 1.2 copy-start.5
  294.1 25.7 %collective-permute-start.18 = (bf16[1,128,4096]{2,1,0:T(8,128)(2,1)}, bf16[1,128,4096]{2,1,0:T(8,128)(2,1)}, u32[]{:S(2)}, u32[]{:S(2)}) collective-permute-start(bf16[1,128,4096]{2,1,0:T(8,128)(2,1)} %fusion.21), channel_id=1, source_target_pairs={{16,0},{17,1},{18,2},{19,3},{20,4},{21,5},{22,6},{23,7},{24,8},{25... | collective-permute-start | bytes 3145736 | tf_op jit(solution)/shard_map/ppermute | solution.py:17

commit v6 on v5

--- a/solution.py
+++ b/solution.py
@@ -45,11 +45,15 @@
     return both.reshape(-1, model_width)
 
 
-def from_experts(partials, experts, capacity):
+def combine_cores(partials, experts, capacity):
     model_width = partials.shape[1]
     paired = partials.reshape(2, experts, capacity, model_width)
     other = swap_cores(paired[1].astype(jnp.bfloat16))
-    summed = (paired[0] + other.astype(jnp.float32)).astype(jnp.bfloat16)
+    return (paired[0] + other.astype(jnp.float32)).astype(jnp.bfloat16)
+
+
+def from_experts(summed):
+    experts, capacity, model_width = summed.shape
     returned = jnp.stack([summed[0]] + [shifted(summed[k], -k) for k in range(1, experts)])
     return returned.reshape(experts * capacity, model_width).astype(jnp.float32)
 
@@ -120,16 +124,8 @@
     up_act = jnp.dot(arrived, up_local, preferred_element_type=jnp.float32)
     spike_rate = lif_rate(gate_act, up_act, leak_local).astype(jnp.bfloat16)
     out_part = jnp.dot(spike_rate, down_full, preferred_element_type=jnp.float32)
-    expert_out = from_experts(out_part, experts, capacity)
+    out_summed = combine_cores(out_part, experts, capacity)
     weights = route_gates[0]
-    mixing = jnp.where(pick_first.T, weights[:, 0:1], 0.0) + jnp.where(
-        pick_second.T, weights[:, 1:2], 0.0
-    )
-    moe_sum = jnp.dot(
-        mixing, expert_out, precision=lax.Precision.HIGHEST, preferred_element_type=jnp.float32
-    )
-    section_out = (tokens + moe_sum).astype(jnp.bfloat16)
-    passed_on = passed_along(section_out[None], "section", 1)
     upstream = cotangent[0].astype(jnp.float32)
     grad_first = (weights[:, 0:1] * upstream).astype(jnp.bfloat16)
     grad_second = (weights[:, 1:2] * upstream).astype(jnp.bfloat16)
@@ -156,7 +152,19 @@
     back_part = back_part + lax.dot_general(
         up_act_grad, up_local, (((1,), (1,)), ((), ())), preferred_element_type=jnp.float32
     )
-    route_back = from_experts(back_part, experts, capacity)
+    out_summed, back_summed = lax.optimization_barrier(
+        (out_summed, combine_cores(back_part, experts, capacity))
+    )
+    expert_out = from_experts(out_summed)
+    route_back = from_experts(back_summed)
+    mixing = jnp.where(pick_first.T, weights[:, 0:1], 0.0) + jnp.where(
+        pick_second.T, weights[:, 1:2], 0.0
+    )
+    moe_sum = jnp.dot(
+        mixing, expert_out, precision=lax.Precision.HIGHEST, preferred_element_type=jnp.float32
+    )
+    section_out = (tokens + moe_sum).astype(jnp.bfloat16)
+    passed_on = passed_along(section_out[None], "section", 1)
     norm_grad = (
         jnp.dot(
             pick_both.T.astype(jnp.float32),

time: 325 us -> 305 us (0.938)
  waiting for transfers between devices: 185 us -> 143 us
  starting transfers between devices: 50.3 us -> 75.2 us
  other arithmetic: 19.5 us -> 16 us
    ppermute x12, waiting for transfers between devices: 160 us -> 121 us  [shifted(): lax.ppermute(value, 'chip', [(source, (source + steps) % count) for sourc...]
    ppermute x12, starting transfers between devices: 41.3 us -> 66.3 us  [shifted(): lax.ppermute(value, 'chip', [(source, (source + steps) % count) for sourc...]
    unnamed x47 -> x49, local copies, waits for them, and re-layouts: 16.2 us -> 19.7 us
    ppermute x2, waiting for transfers between devices: 21 us -> 17.7 us  [passed_along(): lax.ppermute(value, axis, [(source, source + steps) for source in range(l...]
    slice x7 -> x8, local copies, waits for them, and re-layouts: 6.76 us -> 6.18 us  [the longest x2 3.66 us: combine_cores(): other = swap_cores(paired[1].astype(jnp.bfloat16))]
  transfers between devices with their start and end apart: 20 -> 20, of which waited for: 10 -> 9; matrix products, arithmetic and copies ran while one was open for 17% -> 19% of each run, Pallas kernels for 0% -> 0%
where the time goes in v6:
time: 305 us; the launch traced here: 304 us
  waiting for transfers between devices  143 us (47%)
  starting transfers between devices  75.2 us (25%)
  matrix products  34.4 us (11%)
  local copies, waits for them, and re-layouts  34 us (11%)
  other arithmetic  16 us (5%)
    ppermute x12, waiting for transfers between devices, shifted(): lax.ppermute(value, 'chip', [(source, (source + steps) % count) for sourc...  121 us
    ppermute x12, starting transfers between devices, shifted(): lax.ppermute(value, 'chip', [(source, (source + steps) % count) for sourc...  66.3 us
    unnamed x49, local copies, waits for them, and re-layouts  19.7 us
    ppermute x2, waiting for transfers between devices, passed_along(): lax.ppermute(value, axis, [(source, source + steps) for source in range(l...  17.7 us
    dot_general x1, matrix products, per_device(): lax.dot_general(grad_rows, down_full, (((1,), (1,)), ((), ())), preferred...  6.51 us
  transfers between devices with their start and end apart: 20, of which 9 were waited for; matrix products, arithmetic and copies ran while one was open for 19% of the time, Pallas kernels for 0%

profile of v6, /device:TPU:0, one launch (start us, length us, event | category | flops | bytes accessed | tf_op | source)
XLA Modules:
  0.0 304.3 jit_solution(9227499545343696817)
XLA Ops:
  1.9 1.2 reduce-window.6
  3.9 1.5 fusion.14
  5.5 2.1 convolution_convert_fusion.1
  7.6 1.5 slice_bitcast_fusion
  9.0 3.1 %collective-permute-start = (bf16[72,4096]{1,0:T(8,128)(2,1)}, bf16[72,4096]{1,0:T(8,128)(2,1)}, u32[]{:S(2)}, u32[]{:S(2)}) collective-permute-start(bf16[72,4096]{1,0:T(8,128)(2,1)} %get-tuple-element.26), channel_id=1, source_target_pairs={{0,2},{2,4},{4,6},{6,0},{1,3},{3,5},{5,7},{7,1},{8,10},{10,12},{12... | collective-permute-start | bytes 1769480 | tf_op jit(solution)/shard_map/ppermute | solution.py:38
  12.1 2.6 collective-permute-start.1
  14.7 1.3 collective-permute-start.2
  16.0 1.5 collective-permute-start.4
  19.3 2.4 fusion
  22.1 1.7 constant_dynamic-update-slice_fusion.11
  23.8 5.0 %collective-permute-done = bf16[72,4096]{1,0:T(8,128)(2,1)} collective-permute-done((bf16[72,4096]{1,0:T(8,128)(2,1)}, bf16[72,4096]{1,0:T(8,128)(2,1)}, u32[]{:S(2)}, u32[]{:S(2)}) %collective-permute-start) | collective-permute-done | bytes 589856 | tf_op jit(solution)/shard_map/ppermute | solution.py:38
  28.8 24.4 %collective-permute-done.1 = bf16[72,4096]{1,0:T(8,128)(2,1)} collective-permute-done((bf16[72,4096]{1,0:T(8,128)(2,1)}, bf16[72,4096]{1,0:T(8,128)(2,1)}, u32[]{:S(2)}, u32[]{:S(2)}) %collective-permute-start.1) | collective-permute-done | bytes 589856 | tf_op jit(solution)/shard_map/ppermute | solution.py:38
  53.2 1.9 pad_maximum_fusion
  59.4 1.6 constant_dynamic-update-slice_fusion.10
  61.2 2.8 copy-done.4
  64.2 13.2 %collective-permute-start.6 = (bf16[72,4096]{1,0:T(8,128)(2,1)S(1)}, bf16[72,4096]{1,0:T(8,128)(2,1)S(1)}, u32[]{:S(2)}, u32[]{:S(2)}) collective-permute-start(bf16[72,4096]{1,0:T(8,128)(2,1)S(1)} %get-tuple-element.22), channel_id=1, source_target_pairs={{0,2},{2,4},{4,6},{6,0},{1,3},{3,5},{5,7},{7,1},{8,10},{10,12},{12... | collective-permute-start | bytes 1769480 | tf_op jit(solution)/shard_map/ppermute | solution.py:38
  77.4 1.6 collective-permute-start.7
  79.8 2.6 fusion.4
  82.4 2.6 fusion.8
  85.0 4.9 %fusion.63 = f32[576,4096]{1,0:T(8,128)S(1)} fusion(bf16[384,4096]{1,0:T(8,128)(2,1)S(1)} %constant_dynamic-update-slice_fusion.10, f32[384]{0:T(512)S(1)} %reduce.2, f32[384]{0:T(512)S(1)} %broadcast_multiply_fusion, f32[576,384]{1,0:T(8,128)S(1)} %fusion.4, f32[576,384]{1,0:T(8,128)S(1)} %fusion.8), kind=kOutput, calls=%fused_computation.114 | convolution fusion | flops 1827643392 | bytes 14355456 | tf_op jit(solution)/shard_map/dot_general | solution.py:126
  89.9 1.9 slice.156
  92.7 24.2 %collective-permute-done.7 = bf16[72,4096]{1,0:T(8,128)(2,1)S(1)} collective-permute-done((bf16[72,4096]{1,0:T(8,128)(2,1)S(1)}, bf16[72,4096]{1,0:T(8,128)(2,1)S(1)}, u32[]{:S(2)}, u32[]{:S(2)}) %collective-permute-start.7) | collective-permute-done | bytes 589856 | tf_op jit(solution)/shard_map/ppermute | solution.py:38
  117.4 4.4 %collective-permute-done.9 = bf16[4,72,4096]{2,1,0:T(8,128)(2,1)S(1)} collective-permute-done((bf16[4,72,4096]{2,1,0:T(8,128)(2,1)S(1)}, bf16[4,72,4096]{2,1,0:T(8,128)(2,1)S(1)}, u32[]{:S(2)}, u32[]{:S(2)}) %collective-permute-start.9) | collective-permute-done | bytes 2359328 | tf_op jit(solution)/shard_map/ppermute | solution.py:33
  122.0 6.5 %multiply_convert_fusion = (bf16[576,384]{1,0:T(8,128)(2,1)S(1)}, f32[576,384]{1,0:T(8,128)S(1)}) fusion(f32[576,384]{1,0:T(8,128)S(1)} %fusion.8, f32[576,384]{1,0:T(8,128)S(1)} %fusion.4, f32[384]{0:T(512)S(1)} %broadcast_multiply_fusion, f32[384]{0:T(512)S(1)} %reduce.2, bf16[576,4096]{1,0:T(8,128)(2,1)S(1)} %bitcast.138, ...), kind=kOutput, calls=%fused_computation.91 | convolution fusion | flops 1840693248 | bytes 10963968 | tf_op jit(solution)/shard_map/dot_general | solution.py:140
  128.5 2.7 fusion.6
  131.2 2.6 convolution_add_fusion
  133.9 3.6 %copy-done.1 = f32[576,4096]{1,0:T(8,128)} copy-done((f32[576,4096]{1,0:T(8,128)}, f32[576,4096]{1,0:T(8,128)S(1)}, u32[]{:S(2)}) %copy-start.1) | copy-done | bytes 9437208
  137.5 1.7 slice.155
  139.4 2.3 slice-done.1
  141.7 2.6 add_convert_fusion.1
  145.6 3.5 %convolution_convert_fusion = bf16[4096,384]{1,0:T(8,128)(2,1)S(1)} fusion(bf16[576,4096]{1,0:T(8,128)(2,1)S(1)} %bitcast.137, bf16[576,384]{1,0:T(8,128)(2,1)S(1)} %copy-done.11), kind=kOutput, calls=%fused_computation.1 | convolution fusion | flops 1813512192 | bytes 8306688 | tf_op jit(solution)/shard_map/dot_general | solution.py:185
  149.1 1.4 constant_dynamic-slice_fusion
  150.5 1.5 collective-permute-start.19
  152.0 2.4 add_convert_fusion
  154.6 14.3 %collective-permute-start.15 = (bf16[72,4096]{1,0:T(8,128)(2,1)S(1)}, bf16[72,4096]{1,0:T(8,128)(2,1)S(1)}, u32[]{:S(2)}, u32[]{:S(2)}) collective-permute-start(bf16[72,4096]{1,0:T(8,128)(2,1)S(1)} %get-tuple-element.14), channel_id=1, source_target_pairs={{0,6},{2,0},{4,2},{6,4},{1,7},{3,1},{5,3},{7,5},{8,14},{10,8},{12,... | collective-permute-start | bytes 1769480 | tf_op jit(solution)/shard_map/ppermute | solution.py:38
  169.7 3.5 %collective-permute-start.11 = (bf16[72,4096]{1,0:T(8,128)(2,1)S(1)}, bf16[72,4096]{1,0:T(8,128)(2,1)S(1)}, u32[]{:S(2)}, u32[]{:S(2)}) collective-permute-start(bf16[72,4096]{1,0:T(8,128)(2,1)S(1)} %get-tuple-element.18), channel_id=1, source_target_pairs={{0,6},{2,0},{4,2},{6,4},{1,7},{3,1},{5,3},{7,5},{8,14},{10,8},{12,... | collective-permute-start | bytes 1769480 | tf_op jit(solution)/shard_map/ppermute | solution.py:38
  173.3 9.5 %collective-permute-done.15 = bf16[72,4096]{1,0:T(8,128)(2,1)S(1)} collective-permute-done((bf16[72,4096]{1,0:T(8,128)(2,1)S(1)}, bf16[72,4096]{1,0:T(8,128)(2,1)S(1)}, u32[]{:S(2)}, u32[]{:S(2)}) %collective-permute-start.15) | collective-permute-done | bytes 589856 | tf_op jit(solution)/shard_map/ppermute | solution.py:38
  182.7 25.2 %collective-permute-start.12 = (bf16[72,4096]{1,0:T(8,128)(2,1)S(1)}, bf16[72,4096]{1,0:T(8,128)(2,1)S(1)}, u32[]{:S(2)}, u32[]{:S(2)}) collective-permute-start(bf16[72,4096]{1,0:T(8,128)(2,1)S(1)} %get-tuple-element.17), channel_id=1, source_target_pairs={{0,4},{2,6},{4,0},{6,2},{1,5},{3,7},{5,1},{7,3},{8,12},{10,14},{12... | collective-permute-start | bytes 1769480 | tf_op jit(solution)/shard_map/ppermute | solution.py:38
  208.0 32.3 %collective-permute-done.16 = bf16[72,4096]{1,0:T(8,128)(2,1)S(1)} collective-permute-done((bf16[72,4096]{1,0:T(8,128)(2,1)S(1)}, bf16[72,4096]{1,0:T(8,128)(2,1)S(1)}, u32[]{:S(2)}, u32[]{:S(2)}) %collective-permute-start.16) | collective-permute-done | bytes 589856 | tf_op jit(solution)/shard_map/ppermute | solution.py:38
  242.7 1.8 fusion.21
  244.6 1.3 collective-permute-start.18
  245.9 25.1 %collective-permute-done.12 = bf16[72,4096]{1,0:T(8,128)(2,1)S(1)} collective-permute-done((bf16[72,4096]{1,0:T(8,128)(2,1)S(1)}, bf16[72,4096]{1,0:T(8,128)(2,1)S(1)}, u32[]{:S(2)}, u32[]{:S(2)}) %collective-permute-start.12) | collective-permute-done | bytes 589856 | tf_op jit(solution)/shard_map/ppermute | solution.py:38
  271.3 2.9 fusion.2
  274.2 4.4 %collective-permute-start.14 = (bf16[1,128,4096]{2,1,0:T(8,128)(2,1)}, bf16[1,128,4096]{2,1,0:T(8,128)(2,1)}, u32[]{:S(2)}, u32[]{:S(2)}) collective-permute-start(bf16[1,128,4096]{2,1,0:T(8,128)(2,1)} %fusion.2), channel_id=1, source_target_pairs={{0,16},{1,17},{2,18},{3,19},{4,20},{5,21},{6,22},{7,23},{8,24},{9,... | collective-permute-start | bytes 3145736 | tf_op jit(solution)/shard_map/ppermute | solution.py:17
  278.5 3.4 %fusion.19 = bf16[1,2048,384]{2,1,0:T(8,128)(2,1)} fusion(bf16[2048,384]{1,0:T(8,128)(2,1)} %collective-permute-done.19, bf16[4096,384]{1,0:T(8,128)(2,1)} %copy-done.8, s32[]{:T(128)S(6)} %select_n.59), kind=kLoop, calls=%fused_computation.41 | loop fusion | flops 3145728 | bytes 4718596 | tf_op jit(solution)/shard_map/broadcast_in_dim | solution.py:189
  282.0 17.7 %collective-permute-done.14 = bf16[1,128,4096]{2,1,0:T(8,128)(2,1)} collective-permute-done((bf16[1,128,4096]{2,1,0:T(8,128)(2,1)}, bf16[1,128,4096]{2,1,0:T(8,128)(2,1)}, u32[]{:S(2)}, u32[]{:S(2)}) %collective-permute-start.14) | collective-permute-done | bytes 1048608 | tf_op jit(solution)/shard_map/ppermute | solution.py:17
  299.7 2.3 copy.34
  302.0 2.3 copy.35
  (101 shorter events, 16.3 us)
Async XLA Ops:
  0.6 81.8 %copy-start = (bf16[1,4096,384]{2,1,0:T(8,128)(2,1)S(1)}, bf16[1,4096,384]{2,1,0:T(8,128)(2,1)}, u32[]{:S(2)}) copy-start(bf16[1,4096,384]{2,1,0:T(8,128)(2,1)} %param.13) | copy-start | bytes 9437188
  7.6 10.8 %copy-start.16 = (f32[1,128,2]{1,2,0:T(2,128)S(1)}, f32[1,128,2]{1,2,0:T(2,128)}, u32[]{:S(2)}) copy-start(f32[1,128,2]{1,2,0:T(2,128)} %param.12) | copy-start | bytes 3076
  7.6 10.8 %copy-start.5 = (bf16[1,128,4096]{2,1,0:T(8,128)(2,1)S(1)}, bf16[1,128,4096]{2,1,0:T(8,128)(2,1)}, u32[]{:S(2)}) copy-start(bf16[1,128,4096]{2,1,0:T(8,128)(2,1)} %param.17) | copy-start | bytes 3145732
  9.0 19.7 %collective-permute-start = (bf16[72,4096]{1,0:T(8,128)(2,1)}, bf16[72,4096]{1,0:T(8,128)(2,1)}, u32[]{:S(2)}, u32[]{:S(2)}) collective-permute-start(bf16[72,4096]{1,0:T(8,128)(2,1)} %get-tuple-element.26), channel_id=1, source_target_pairs={{0,2},{2,4},{4,6},{6,0},{1,3},{3,5},{5,7},{7,1},{8,10},{10,12},{12... | collective-permute-start | bytes 1769480 | tf_op jit(solution)/shard_map/ppermute | solution.py:38
  12.1 41.1 %collective-permute-start.1 = (bf16[72,4096]{1,0:T(8,128)(2,1)}, bf16[72,4096]{1,0:T(8,128)(2,1)}, u32[]{:S(2)}, u32[]{:S(2)}) collective-permute-start(bf16[72,4096]{1,0:T(8,128)(2,1)} %get-tuple-element.25), channel_id=1, source_target_pairs={{0,4},{2,6},{4,0},{6,2},{1,5},{3,7},{5,1},{7,3},{8,12},{10,14},{12... | collective-permute-start | bytes 1769480 | tf_op jit(solution)/shard_map/ppermute | solution.py:38
  14.7 38.5 %collective-permute-start.2 = (bf16[72,4096]{1,0:T(8,128)(2,1)}, bf16[72,4096]{1,0:T(8,128)(2,1)}, u32[]{:S(2)}, u32[]{:S(2)}) collective-permute-start(bf16[72,4096]{1,0:T(8,128)(2,1)} %get-tuple-element.24), channel_id=1, source_target_pairs={{0,6},{2,0},{4,2},{6,4},{1,7},{3,1},{5,3},{7,5},{8,14},{10,8},{12,... | collective-permute-start | bytes 1769480 | tf_op jit(solution)/shard_map/ppermute | solution.py:38
  16.0 43.3 %collective-permute-start.4 = (bf16[384,2048]{1,0:T(8,128)(2,1)}, bf16[384,2048]{1,0:T(8,128)(2,1)}, u32[]{:S(2)}, u32[]{:S(2)}) collective-permute-start(bf16[384,2048]{1,0:T(8,128)(2,1)} %bitcast.16), channel_id=1, source_target_pairs={{0,8},{8,0},{1,9},{9,1},{2,10},{10,2},{3,11},{11,3},{4,12},{12,4},... | collective-permute-start | bytes 4718600 | tf_op jit(solution)/shard_map/ppermute | solution.py:63
  19.3 2.4 copy-start.15
  22.1 31.1 %copy-start.9 = (bf16[1,72,4096]{2,1,0:T(8,128)(2,1)S(1)}, bf16[1,72,4096]{2,1,0:T(8,128)(2,1)}, u32[]{:S(2)}) copy-start(bf16[1,72,4096]{2,1,0:T(8,128)(2,1)} %get-tuple-element.23) | copy-start | bytes 1769476
  53.2 2.9 copy-start.12
  55.1 6.0 %collective-permute-start.3 = (bf16[4,72,4096]{2,1,0:T(8,128)(2,1)S(1)}, bf16[4,72,4096]{2,1,0:T(8,128)(2,1)S(1)}, u32[]{:S(2)}, u32[]{:S(2)}) collective-permute-start(bf16[4,72,4096]{2,1,0:T(8,128)(2,1)S(1)} %pad_maximum_fusion), channel_id=1, source_target_pairs={{0,1},{1,0},{2,3},{3,2},{4,5},{5,4},{6,7},{7,6},{8,9},{9,8},{10,11... | collective-permute-start | bytes 7077896 | tf_op jit(solution)/shard_map/ppermute | solution.py:33
  61.0 3.0 copy-start.4
  61.2 21.2 %copy-start.13 = (bf16[8,72,4096]{2,1,0:T(8,128)(2,1)}, bf16[8,72,4096]{2,1,0:T(8,128)(2,1)S(1)}, u32[]{:S(2)}) copy-start(bf16[8,72,4096]{2,1,0:T(8,128)(2,1)S(1)} %constant_dynamic-update-slice_fusion) | copy-start | bytes 14155780
  64.0 15.9 %copy-start.7 = (bf16[1,4096,384]{2,1,0:T(8,128)(2,1)S(1)}, bf16[1,4096,384]{2,1,0:T(8,128)(2,1)}, u32[]{:S(2)}) copy-start(bf16[1,4096,384]{2,1,0:T(8,128)(2,1)} %param.14) | copy-start | bytes 9437188
  64.2 28.5 %collective-permute-start.6 = (bf16[72,4096]{1,0:T(8,128)(2,1)S(1)}, bf16[72,4096]{1,0:T(8,128)(2,1)S(1)}, u32[]{:S(2)}, u32[]{:S(2)}) collective-permute-start(bf16[72,4096]{1,0:T(8,128)(2,1)S(1)} %get-tuple-element.22), channel_id=1, source_target_pairs={{0,2},{2,4},{4,6},{6,0},{1,3},{3,5},{5,7},{7,1},{8,10},{10,12},{12... | collective-permute-start | bytes 1769480 | tf_op jit(solution)/shard_map/ppermute | solution.py:38
  77.4 39.5 %collective-permute-start.7 = (bf16[72,4096]{1,0:T(8,128)(2,1)S(1)}, bf16[72,4096]{1,0:T(8,128)(2,1)S(1)}, u32[]{:S(2)}, u32[]{:S(2)}) collective-permute-start(bf16[72,4096]{1,0:T(8,128)(2,1)S(1)} %get-tuple-element.21), channel_id=1, source_target_pairs={{0,4},{2,6},{4,0},{6,2},{1,5},{3,7},{5,1},{7,3},{8,12},{10,14},{12... | collective-permute-start | bytes 1769480 | tf_op jit(solution)/shard_map/ppermute | solution.py:38
  79.0 37.9 %collective-permute-start.8 = (bf16[72,4096]{1,0:T(8,128)(2,1)S(1)}, bf16[72,4096]{1,0:T(8,128)(2,1)S(1)}, u32[]{:S(2)}, u32[]{:S(2)}) collective-permute-start(bf16[72,4096]{1,0:T(8,128)(2,1)S(1)} %get-tuple-element.20), channel_id=1, source_target_pairs={{0,6},{2,0},{4,2},{6,4},{1,7},{3,1},{5,3},{7,5},{8,14},{10,8},{12,... | collective-permute-start | bytes 1769480 | tf_op jit(solution)/shard_map/ppermute | solution.py:38
  89.9 27.5 %copy-start.3 = (f32[576,4096]{1,0:T(8,128)}, f32[576,4096]{1,0:T(8,128)S(1)}, u32[]{:S(2)}) copy-start(f32[576,4096]{1,0:T(8,128)S(1)} %fusion.63) | copy-start | bytes 28311556
  91.9 47.5 %collective-permute-start.5 = (bf16[4,72,4096]{2,1,0:T(8,128)(2,1)}, bf16[4,72,4096]{2,1,0:T(8,128)(2,1)}, u32[]{:S(2)}, u32[]{:S(2)}) collective-permute-start(bf16[4,72,4096]{2,1,0:T(8,128)(2,1)} %bitcast.18), channel_id=1, source_target_pairs={{0,1},{1,0},{2,3},{3,2},{4,5},{5,4},{6,7},{7,6},{8,9},{9,8},{10,11... | collective-permute-start | bytes 7077896 | tf_op jit(solution)/shard_map/ppermute | solution.py:33
  117.2 4.6 %collective-permute-start.9 = (bf16[4,72,4096]{2,1,0:T(8,128)(2,1)S(1)}, bf16[4,72,4096]{2,1,0:T(8,128)(2,1)S(1)}, u32[]{:S(2)}, u32[]{:S(2)}) collective-permute-start(bf16[4,72,4096]{2,1,0:T(8,128)(2,1)S(1)} %pad_maximum_fusion.1), channel_id=1, source_target_pairs={{0,1},{1,0},{2,3},{3,2},{4,5},{5,4},{6,7},{7,6},{8,9},{9,8},{10,11... | collective-permute-start | bytes 7077896 | tf_op jit(solution)/shard_map/ppermute | solution.py:33
  128.5 2.7 copy-start.10
  133.9 3.7 %copy-start.1 = (f32[576,4096]{1,0:T(8,128)}, f32[576,4096]{1,0:T(8,128)S(1)}, u32[]{:S(2)}) copy-start(f32[576,4096]{1,0:T(8,128)S(1)} %convolution_add_fusion) | copy-start | bytes 28311556
  139.3 12.7 %collective-permute-start.10 = (bf16[4,72,4096]{2,1,0:T(8,128)(2,1)}, bf16[4,72,4096]{2,1,0:T(8,128)(2,1)}, u32[]{:S(2)}, u32[]{:S(2)}) collective-permute-start(bf16[4,72,4096]{2,1,0:T(8,128)(2,1)} %bitcast.27), channel_id=1, source_target_pairs={{0,1},{1,0},{2,3},{3,2},{4,5},{5,4},{6,7},{7,6},{8,9},{9,8},{10,11... | collective-permute-start | bytes 7077896 | tf_op jit(solution)/shard_map/ppermute | solution.py:33
  139.4 2.3 slice-start.1
  141.7 2.9 slice-start.2
  144.3 1.1 copy-start.11
  144.3 1.2 slice-start.3
  145.6 6.4 %slice-start = ((f32[576,4096]{1,0:T(8,128)}), f32[288,4096]{1,0:T(8,128)S(1)}, s32[]{:S(2)}) async-start(f32[576,4096]{1,0:T(8,128)} %copy-done.1), calls=%async_computation | async-start | bytes 9437184 | tf_op jit(solution)/shard_map/slice | solution.py:52
  149.1 2.9 copy-start.8
  150.5 128.0 %collective-permute-start.19 = (bf16[2048,384]{1,0:T(8,128)(2,1)}, bf16[2048,384]{1,0:T(8,128)(2,1)}, u32[]{:S(2)}, u32[]{:S(2)}) collective-permute-start(bf16[2048,384]{1,0:T(8,128)(2,1)} %constant_dynamic-slice_fusion), channel_id=1, source_target_pairs={{0,8},{8,0},{1,9},{9,1},{2,10},{10,2},{3,11},{11,3},{4,12},{12,4},... | collective-permute-start | bytes 4718600 | tf_op jit(solution)/shard_map/ppermute | solution.py:63
  154.6 28.1 %collective-permute-start.15 = (bf16[72,4096]{1,0:T(8,128)(2,1)S(1)}, bf16[72,4096]{1,0:T(8,128)(2,1)S(1)}, u32[]{:S(2)}, u32[]{:S(2)}) collective-permute-start(bf16[72,4096]{1,0:T(8,128)(2,1)S(1)} %get-tuple-element.14), channel_id=1, source_target_pairs={{0,6},{2,0},{4,2},{6,4},{1,7},{3,1},{5,3},{7,5},{8,14},{10,8},{12,... | collective-permute-start | bytes 1769480 | tf_op jit(solution)/shard_map/ppermute | solution.py:38
  168.9 71.3 %collective-permute-start.16 = (bf16[72,4096]{1,0:T(8,128)(2,1)S(1)}, bf16[72,4096]{1,0:T(8,128)(2,1)S(1)}, u32[]{:S(2)}, u32[]{:S(2)}) collective-permute-start(bf16[72,4096]{1,0:T(8,128)(2,1)S(1)} %get-tuple-element.13), channel_id=1, source_target_pairs={{0,4},{2,6},{4,0},{6,2},{1,5},{3,7},{5,1},{7,3},{8,12},{10,14},{12... | collective-permute-start | bytes 1769480 | tf_op jit(solution)/shard_map/ppermute | solution.py:38
  169.2 71.1 %collective-permute-start.17 = (bf16[72,4096]{1,0:T(8,128)(2,1)S(1)}, bf16[72,4096]{1,0:T(8,128)(2,1)S(1)}, u32[]{:S(2)}, u32[]{:S(2)}) collective-permute-start(bf16[72,4096]{1,0:T(8,128)(2,1)S(1)} %get-tuple-element.12), channel_id=1, source_target_pairs={{0,2},{2,4},{4,6},{6,0},{1,3},{3,5},{5,7},{7,1},{8,10},{10,12},{12... | collective-permute-start | bytes 1769480 | tf_op jit(solution)/shard_map/ppermute | solution.py:38
  169.7 76.1 %collective-permute-start.11 = (bf16[72,4096]{1,0:T(8,128)(2,1)S(1)}, bf16[72,4096]{1,0:T(8,128)(2,1)S(1)}, u32[]{:S(2)}, u32[]{:S(2)}) collective-permute-start(bf16[72,4096]{1,0:T(8,128)(2,1)S(1)} %get-tuple-element.18), channel_id=1, source_target_pairs={{0,6},{2,0},{4,2},{6,4},{1,7},{3,1},{5,3},{7,5},{8,14},{10,8},{12,... | collective-permute-start | bytes 1769480 | tf_op jit(solution)/shard_map/ppermute | solution.py:38
  182.7 88.3 %collective-permute-start.12 = (bf16[72,4096]{1,0:T(8,128)(2,1)S(1)}, bf16[72,4096]{1,0:T(8,128)(2,1)S(1)}, u32[]{:S(2)}, u32[]{:S(2)}) collective-permute-start(bf16[72,4096]{1,0:T(8,128)(2,1)S(1)} %get-tuple-element.17), channel_id=1, source_target_pairs={{0,4},{2,6},{4,0},{6,2},{1,5},{3,7},{5,1},{7,3},{8,12},{10,14},{12... | collective-permute-start | bytes 1769480 | tf_op jit(solution)/shard_map/ppermute | solution.py:38
  240.3 30.7 %collective-permute-start.13 = (bf16[72,4096]{1,0:T(8,128)(2,1)S(1)}, bf16[72,4096]{1,0:T(8,128)(2,1)S(1)}, u32[]{:S(2)}, u32[]{:S(2)}) collective-permute-start(bf16[72,4096]{1,0:T(8,128)(2,1)S(1)} %get-tuple-element.16), channel_id=1, source_target_pairs={{0,2},{2,4},{4,6},{6,0},{1,3},{3,5},{5,7},{7,1},{8,10},{10,12},{12... | collective-permute-start | bytes 1769480 | tf_op jit(solution)/shard_map/ppermute | solution.py:38
  240.3 1.2 copy-start.2
  240.3 1.2 copy-start.14
  241.5 1.2 copy-start.6
  244.6 37.4 %collective-permute-start.18 = (bf16[1,128,4096]{2,1,0:T(8,128)(2,1)}, bf16[1,128,4096]{2,1,0:T(8,128)(2,1)}, u32[]{:S(2)}, u32[]{:S(2)}) collective-permute-start(bf16[1,128,4096]{2,1,0:T(8,128)(2,1)} %fusion.21), channel_id=1, source_target_pairs={{16,0},{17,1},{18,2},{19,3},{20,4},{21,5},{22,6},{23,7},{24,8},{25... | collective-permute-start | bytes 3145736 | tf_op jit(solution)/shard_map/ppermute | solution.py:17
  274.2 25.5 %collective-permute-start.14 = (bf16[1,128,4096]{2,1,0:T(8,128)(2,1)}, bf16[1,128,4096]{2,1,0:T(8,128)(2,1)}, u32[]{:S(2)}, u32[]{:S(2)}) collective-permute-start(bf16[1,128,4096]{2,1,0:T(8,128)(2,1)} %fusion.2), channel_id=1, source_target_pairs={{0,16},{1,17},{2,18},{3,19},{4,20},{5,21},{6,22},{7,23},{8,24},{9,... | collective-permute-start | bytes 3145736 | tf_op jit(solution)/shard_map/ppermute | solution.py:17

commit v7 on v6

--- a/solution.py
+++ b/solution.py
@@ -156,6 +156,7 @@
         (out_summed, combine_cores(back_part, experts, capacity))
     )
     expert_out = from_experts(out_summed)
+    back_summed, expert_out = lax.optimization_barrier((back_summed, expert_out))
     route_back = from_experts(back_summed)
     mixing = jnp.where(pick_first.T, weights[:, 0:1], 0.0) + jnp.where(
         pick_second.T, weights[:, 1:2], 0.0

time: 305 us -> 304 us (level); the launches traced: 304 us -> 299 us
  starting transfers between devices: 75.2 us -> 50 us
  waiting for transfers between devices: 143 us -> 162 us
  local copies, waits for them, and re-layouts: 34 us -> 28.9 us
  matrix products: 34.4 us -> 38.7 us
    ppermute x12, starting transfers between devices: 66.3 us -> 40.8 us  [shifted(): lax.ppermute(value, 'chip', [(source, (source + steps) % count) for sourc...]
    ppermute x12, waiting for transfers between devices: 121 us -> 137 us  [shifted(): lax.ppermute(value, 'chip', [(source, (source + steps) % count) for sourc...]
    unnamed x49 -> x53, local copies, waits for them, and re-layouts: 19.7 us -> 14.7 us
    ppermute x2, waiting for transfers between devices: 17.7 us -> 21.1 us  [passed_along(): lax.ppermute(value, axis, [(source, source + steps) for source in range(l...]
  transfers between devices with their start and end apart: 20 -> 20, of which waited for: 9 -> 9; matrix products, arithmetic and copies ran while one was open for 19% -> 20% of each run, Pallas kernels for 0% -> 0%
where the time goes in v7:
time: 304 us; the launch traced here: 299 us
  waiting for transfers between devices  162 us (53%)
  starting transfers between devices  50 us (16%)
  matrix products  38.7 us (13%)
  local copies, waits for them, and re-layouts  28.9 us (10%)
  other arithmetic  17.7 us (6%)
    ppermute x12, waiting for transfers between devices, shifted(): lax.ppermute(value, 'chip', [(source, (source + steps) % count) for sourc...  137 us
    ppermute x12, starting transfers between devices, shifted(): lax.ppermute(value, 'chip', [(source, (source + steps) % count) for sourc...  40.8 us
    ppermute x2, waiting for transfers between devices, passed_along(): lax.ppermute(value, axis, [(source, source + steps) for source in range(l...  21.1 us
    unnamed x53, local copies, waits for them, and re-layouts  14.7 us
    dot_general x1, matrix products, per_device(): lax.dot_general(grad_rows, down_full, (((1,), (1,)), ((), ())), preferred...  6.5 us
  transfers between devices with their start and end apart: 20, of which 9 were waited for; matrix products, arithmetic and copies ran while one was open for 20% of the time, Pallas kernels for 0%

profile of v7, /device:TPU:0, one launch (start us, length us, event | category | flops | bytes accessed | tf_op | source)
XLA Modules:
  0.0 299.2 jit_solution(16334237865628679184)
XLA Ops:
  1.9 1.2 reduce-window.6
  3.9 1.5 fusion.14
  5.5 2.1 convolution_convert_fusion.1
  7.6 1.5 slice_bitcast_fusion
  9.0 3.1 %collective-permute-start = (bf16[72,4096]{1,0:T(8,128)(2,1)}, bf16[72,4096]{1,0:T(8,128)(2,1)}, u32[]{:S(2)}, u32[]{:S(2)}) collective-permute-start(bf16[72,4096]{1,0:T(8,128)(2,1)} %get-tuple-element.30), channel_id=1, source_target_pairs={{0,2},{2,4},{4,6},{6,0},{1,3},{3,5},{5,7},{7,1},{8,10},{10,12},{12... | collective-permute-start | bytes 1769480 | tf_op jit(solution)/shard_map/ppermute | solution.py:38
  12.1 2.6 collective-permute-start.1
  14.7 1.3 collective-permute-start.2
  16.0 1.5 collective-permute-start.4
  19.3 2.4 fusion
  22.1 1.8 constant_dynamic-update-slice_fusion.11
  23.9 4.8 %collective-permute-done = bf16[72,4096]{1,0:T(8,128)(2,1)} collective-permute-done((bf16[72,4096]{1,0:T(8,128)(2,1)}, bf16[72,4096]{1,0:T(8,128)(2,1)}, u32[]{:S(2)}, u32[]{:S(2)}) %collective-permute-start) | collective-permute-done | bytes 589856 | tf_op jit(solution)/shard_map/ppermute | solution.py:38
  28.8 24.4 %collective-permute-done.1 = bf16[72,4096]{1,0:T(8,128)(2,1)} collective-permute-done((bf16[72,4096]{1,0:T(8,128)(2,1)}, bf16[72,4096]{1,0:T(8,128)(2,1)}, u32[]{:S(2)}, u32[]{:S(2)}) %collective-permute-start.1) | collective-permute-done | bytes 589856 | tf_op jit(solution)/shard_map/ppermute | solution.py:38
  53.2 1.7 pad_maximum_fusion
  58.3 1.6 constant_dynamic-update-slice_fusion.10
  60.3 2.4 copy-done.4
  63.0 13.2 %collective-permute-start.6 = (bf16[72,4096]{1,0:T(8,128)(2,1)S(1)}, bf16[72,4096]{1,0:T(8,128)(2,1)S(1)}, u32[]{:S(2)}, u32[]{:S(2)}) collective-permute-start(bf16[72,4096]{1,0:T(8,128)(2,1)S(1)} %get-tuple-element.26), channel_id=1, source_target_pairs={{0,2},{2,4},{4,6},{6,0},{1,3},{3,5},{5,7},{7,1},{8,10},{10,12},{12... | collective-permute-start | bytes 1769480 | tf_op jit(solution)/shard_map/ppermute | solution.py:38
  76.1 1.6 collective-permute-start.7
  78.7 2.6 fusion.4
  81.3 2.6 fusion.8
  84.0 4.9 %fusion.63 = f32[576,4096]{1,0:T(8,128)S(1)} fusion(bf16[384,4096]{1,0:T(8,128)(2,1)S(1)} %constant_dynamic-update-slice_fusion.10, f32[384]{0:T(512)S(1)} %reduce.2, f32[384]{0:T(512)S(1)} %broadcast_multiply_fusion, f32[576,384]{1,0:T(8,128)S(1)} %fusion.4, f32[576,384]{1,0:T(8,128)S(1)} %fusion.8), kind=kOutput, calls=%fused_computation.115 | convolution fusion | flops 1827643392 | bytes 14355456 | tf_op jit(solution)/shard_map/dot_general | solution.py:126
  88.8 2.0 slice.156
  91.5 25.0 %collective-permute-done.7 = bf16[72,4096]{1,0:T(8,128)(2,1)S(1)} collective-permute-done((bf16[72,4096]{1,0:T(8,128)(2,1)S(1)}, bf16[72,4096]{1,0:T(8,128)(2,1)S(1)}, u32[]{:S(2)}, u32[]{:S(2)}) %collective-permute-start.7) | collective-permute-done | bytes 589856 | tf_op jit(solution)/shard_map/ppermute | solution.py:38
  117.0 4.4 %collective-permute-done.9 = bf16[4,72,4096]{2,1,0:T(8,128)(2,1)S(1)} collective-permute-done((bf16[4,72,4096]{2,1,0:T(8,128)(2,1)S(1)}, bf16[4,72,4096]{2,1,0:T(8,128)(2,1)S(1)}, u32[]{:S(2)}, u32[]{:S(2)}) %collective-permute-start.9) | collective-permute-done | bytes 2359328 | tf_op jit(solution)/shard_map/ppermute | solution.py:33
  121.6 6.5 %multiply_convert_fusion = (bf16[576,384]{1,0:T(8,128)(2,1)S(1)}, f32[576,384]{1,0:T(8,128)S(1)}) fusion(f32[576,384]{1,0:T(8,128)S(1)} %fusion.8, f32[576,384]{1,0:T(8,128)S(1)} %fusion.4, f32[384]{0:T(512)S(1)} %broadcast_multiply_fusion, f32[384]{0:T(512)S(1)} %reduce.2, bf16[576,4096]{1,0:T(8,128)(2,1)S(1)} %bitcast.140, ...), kind=kOutput, calls=%fused_computation.92 | convolution fusion | flops 1840693248 | bytes 10963968 | tf_op jit(solution)/shard_map/dot_general | solution.py:140
  128.1 2.7 fusion.6
  130.8 2.6 convolution_add_fusion
  134.0 2.1 slice-done
  136.2 2.4 add_convert_fusion.1
  138.9 2.2 add_convert_fusion
  141.1 1.2 fusion.104
  142.3 13.9 %collective-permute-start.11 = (bf16[72,4096]{1,0:T(8,128)(2,1)}, bf16[72,4096]{1,0:T(8,128)(2,1)S(1)}, u32[]{:S(2)}, u32[]{:S(2)}) collective-permute-start(bf16[72,4096]{1,0:T(8,128)(2,1)} %get-tuple-element.22), channel_id=1, source_target_pairs={{0,6},{2,0},{4,2},{6,4},{1,7},{3,1},{5,3},{7,5},{8,14},{10,8},{12,... | collective-permute-start | bytes 1769480 | tf_op jit(solution)/shard_map/ppermute | solution.py:38
  157.2 5.7 %convolution_convert_fusion = bf16[4096,384]{1,0:T(8,128)(2,1)S(1)} fusion(bf16[576,4096]{1,0:T(8,128)(2,1)} %bitcast.139, bf16[576,384]{1,0:T(8,128)(2,1)} %copy-done.11), kind=kOutput, calls=%fused_computation.1 | convolution fusion | flops 1813512192 | bytes 8306688 | tf_op jit(solution)/shard_map/dot_general | solution.py:186
  162.9 7.5 %collective-permute-done.11 = bf16[72,4096]{1,0:T(8,128)(2,1)S(1)} collective-permute-done((bf16[72,4096]{1,0:T(8,128)(2,1)}, bf16[72,4096]{1,0:T(8,128)(2,1)S(1)}, u32[]{:S(2)}, u32[]{:S(2)}) %collective-permute-start.11) | collective-permute-done | bytes 589856 | tf_op jit(solution)/shard_map/ppermute | solution.py:38
  170.3 38.1 %collective-permute-done.12 = bf16[72,4096]{1,0:T(8,128)(2,1)S(1)} collective-permute-done((bf16[72,4096]{1,0:T(8,128)(2,1)}, bf16[72,4096]{1,0:T(8,128)(2,1)S(1)}, u32[]{:S(2)}, u32[]{:S(2)}) %collective-permute-start.12) | collective-permute-done | bytes 589856 | tf_op jit(solution)/shard_map/ppermute | solution.py:38
  209.4 1.7 pad_maximum_fusion.2
  213.1 1.2 collective-permute-start.16
  214.3 1.9 collective-permute-start.17
  216.2 1.3 constant_dynamic-slice_fusion
  217.5 1.5 collective-permute-start.19
  219.0 4.9 %fusion.2 = bf16[1,128,4096]{2,1,0:T(8,128)(2,1)} fusion(f32[288,4096]{1,0:T(8,128)S(1)} %bitcast_convert_fusion, bf16[1,128,4096]{2,1,0:T(8,128)(2,1)S(1)} %copy-done.2, f32[128]{0:T(128)S(1)} %get-tuple-element.31, s32[128]{0:T(128)S(1)} %get-tuple-element.14, f32[128]{0:T(128)S(1)} %get-tuple-element.32, s32[128]{0:T(128)S(1)} %get-tuple-element.13), kind=kOutput, calls=%fused_computation.12 | convolution fusion | flops 1813696512 | bytes 6817792 | tf_op jit(solution)/shard_map/dot_general | solution.py:164
  224.0 4.5 %collective-permute-start.14 = (bf16[1,128,4096]{2,1,0:T(8,128)(2,1)}, bf16[1,128,4096]{2,1,0:T(8,128)(2,1)}, u32[]{:S(2)}, u32[]{:S(2)}) collective-permute-start(bf16[1,128,4096]{2,1,0:T(8,128)(2,1)} %fusion.2), channel_id=1, source_target_pairs={{0,16},{1,17},{2,18},{3,19},{4,20},{5,21},{6,22},{7,23},{8,24},{9,... | collective-permute-start | bytes 3145736 | tf_op jit(solution)/shard_map/ppermute | solution.py:17
  228.5 36.4 %collective-permute-done.16 = bf16[72,4096]{1,0:T(8,128)(2,1)S(1)} collective-permute-done((bf16[72,4096]{1,0:T(8,128)(2,1)S(1)}, bf16[72,4096]{1,0:T(8,128)(2,1)S(1)}, u32[]{:S(2)}, u32[]{:S(2)}) %collective-permute-start.16) | collective-permute-done | bytes 589856 | tf_op jit(solution)/shard_map/ppermute | solution.py:38
  266.4 1.8 fusion.21
  268.3 1.3 collective-permute-start.18
  269.6 3.6 %fusion.19 = bf16[1,2048,384]{2,1,0:T(8,128)(2,1)} fusion(bf16[2048,384]{1,0:T(8,128)(2,1)} %collective-permute-done.19, bf16[4096,384]{1,0:T(8,128)(2,1)} %copy-done.9, s32[]{:T(128)S(6)} %select_n.59), kind=kLoop, calls=%fused_computation.42 | loop fusion | flops 3145728 | bytes 4718596 | tf_op jit(solution)/shard_map/broadcast_in_dim | solution.py:190
  273.2 21.1 %collective-permute-done.18 = bf16[1,128,4096]{2,1,0:T(8,128)(2,1)} collective-permute-done((bf16[1,128,4096]{2,1,0:T(8,128)(2,1)}, bf16[1,128,4096]{2,1,0:T(8,128)(2,1)}, u32[]{:S(2)}, u32[]{:S(2)}) %collective-permute-start.18) | collective-permute-done | bytes 1048608 | tf_op jit(solution)/shard_map/ppermute | solution.py:17
  294.2 2.3 copy.34
  296.5 2.3 copy.35
  (105 shorter events, 16.6 us)
Async XLA Ops:
  0.6 80.7 %copy-start = (bf16[1,4096,384]{2,1,0:T(8,128)(2,1)S(1)}, bf16[1,4096,384]{2,1,0:T(8,128)(2,1)}, u32[]{:S(2)}) copy-start(bf16[1,4096,384]{2,1,0:T(8,128)(2,1)} %param.13) | copy-start | bytes 9437188
  7.6 10.8 %copy-start.18 = (f32[1,128,2]{1,2,0:T(2,128)S(1)}, f32[1,128,2]{1,2,0:T(2,128)}, u32[]{:S(2)}) copy-start(f32[1,128,2]{1,2,0:T(2,128)} %param.12) | copy-start | bytes 3076
  7.6 10.8 %copy-start.5 = (bf16[1,128,4096]{2,1,0:T(8,128)(2,1)S(1)}, bf16[1,128,4096]{2,1,0:T(8,128)(2,1)}, u32[]{:S(2)}) copy-start(bf16[1,128,4096]{2,1,0:T(8,128)(2,1)} %param.17) | copy-start | bytes 3145732
  9.0 19.7 %collective-permute-start = (bf16[72,4096]{1,0:T(8,128)(2,1)}, bf16[72,4096]{1,0:T(8,128)(2,1)}, u32[]{:S(2)}, u32[]{:S(2)}) collective-permute-start(bf16[72,4096]{1,0:T(8,128)(2,1)} %get-tuple-element.30), channel_id=1, source_target_pairs={{0,2},{2,4},{4,6},{6,0},{1,3},{3,5},{5,7},{7,1},{8,10},{10,12},{12... | collective-permute-start | bytes 1769480 | tf_op jit(solution)/shard_map/ppermute | solution.py:38
  12.1 41.1 %collective-permute-start.1 = (bf16[72,4096]{1,0:T(8,128)(2,1)}, bf16[72,4096]{1,0:T(8,128)(2,1)}, u32[]{:S(2)}, u32[]{:S(2)}) collective-permute-start(bf16[72,4096]{1,0:T(8,128)(2,1)} %get-tuple-element.29), channel_id=1, source_target_pairs={{0,4},{2,6},{4,0},{6,2},{1,5},{3,7},{5,1},{7,3},{8,12},{10,14},{12... | collective-permute-start | bytes 1769480 | tf_op jit(solution)/shard_map/ppermute | solution.py:38
  14.7 38.5 %collective-permute-start.2 = (bf16[72,4096]{1,0:T(8,128)(2,1)}, bf16[72,4096]{1,0:T(8,128)(2,1)}, u32[]{:S(2)}, u32[]{:S(2)}) collective-permute-start(bf16[72,4096]{1,0:T(8,128)(2,1)} %get-tuple-element.28), channel_id=1, source_target_pairs={{0,6},{2,0},{4,2},{6,4},{1,7},{3,1},{5,3},{7,5},{8,14},{10,8},{12,... | collective-permute-start | bytes 1769480 | tf_op jit(solution)/shard_map/ppermute | solution.py:38
  16.0 42.3 %collective-permute-start.4 = (bf16[384,2048]{1,0:T(8,128)(2,1)}, bf16[384,2048]{1,0:T(8,128)(2,1)}, u32[]{:S(2)}, u32[]{:S(2)}) collective-permute-start(bf16[384,2048]{1,0:T(8,128)(2,1)} %bitcast.16), channel_id=1, source_target_pairs={{0,8},{8,0},{1,9},{9,1},{2,10},{10,2},{3,11},{11,3},{4,12},{12,4},... | collective-permute-start | bytes 4718600 | tf_op jit(solution)/shard_map/ppermute | solution.py:63
  19.3 2.4 copy-start.17
  21.7 31.5 %copy-start.10 = (bf16[1,72,4096]{2,1,0:T(8,128)(2,1)S(1)}, bf16[1,72,4096]{2,1,0:T(8,128)(2,1)}, u32[]{:S(2)}) copy-start(bf16[1,72,4096]{2,1,0:T(8,128)(2,1)} %get-tuple-element.27) | copy-start | bytes 1769476
  21.7 33.3 %slice-start.1 = ((s8[4718592]{0:T(1024)(128)(4,1)}), s8[4194304]{0:T(1024)(128)(4,1)S(1)}, s32[]{:S(2)}) async-start(s8[4718592]{0:T(1024)(128)(4,1)} %bitcast.135), calls=%async_computation.1 | async-start | bytes 8388608
  22.1 32.9 %slice-start.2 = ((s8[4718592]{0:T(1024)(128)(4,1)}), s8[524288]{0:T(1024)(128)(4,1)S(1)}, s32[]{:S(2)}) async-start(s8[4718592]{0:T(1024)(128)(4,1)} %bitcast.135), calls=%async_computation.2 | async-start | bytes 1048576
  54.9 5.1 %collective-permute-start.3 = (bf16[4,72,4096]{2,1,0:T(8,128)(2,1)S(1)}, bf16[4,72,4096]{2,1,0:T(8,128)(2,1)S(1)}, u32[]{:S(2)}, u32[]{:S(2)}) collective-permute-start(bf16[4,72,4096]{2,1,0:T(8,128)(2,1)S(1)} %pad_maximum_fusion), channel_id=1, source_target_pairs={{0,1},{1,0},{2,3},{3,2},{4,5},{5,4},{6,7},{7,6},{8,9},{9,8},{10,11... | collective-permute-start | bytes 7077896 | tf_op jit(solution)/shard_map/ppermute | solution.py:33
  60.0 2.7 copy-start.4
  60.2 21.1 %copy-start.15 = (bf16[8,72,4096]{2,1,0:T(8,128)(2,1)}, bf16[8,72,4096]{2,1,0:T(8,128)(2,1)S(1)}, u32[]{:S(2)}) copy-start(bf16[8,72,4096]{2,1,0:T(8,128)(2,1)S(1)} %constant_dynamic-update-slice_fusion) | copy-start | bytes 14155780
  60.3 18.5 %copy-start.8 = (bf16[1,4096,384]{2,1,0:T(8,128)(2,1)S(1)}, bf16[1,4096,384]{2,1,0:T(8,128)(2,1)}, u32[]{:S(2)}) copy-start(bf16[1,4096,384]{2,1,0:T(8,128)(2,1)} %param.14) | copy-start | bytes 9437188
  63.0 28.5 %collective-permute-start.6 = (bf16[72,4096]{1,0:T(8,128)(2,1)S(1)}, bf16[72,4096]{1,0:T(8,128)(2,1)S(1)}, u32[]{:S(2)}, u32[]{:S(2)}) collective-permute-start(bf16[72,4096]{1,0:T(8,128)(2,1)S(1)} %get-tuple-element.26), channel_id=1, source_target_pairs={{0,2},{2,4},{4,6},{6,0},{1,3},{3,5},{5,7},{7,1},{8,10},{10,12},{12... | collective-permute-start | bytes 1769480 | tf_op jit(solution)/shard_map/ppermute | solution.py:38
  76.1 40.4 %collective-permute-start.7 = (bf16[72,4096]{1,0:T(8,128)(2,1)S(1)}, bf16[72,4096]{1,0:T(8,128)(2,1)S(1)}, u32[]{:S(2)}, u32[]{:S(2)}) collective-permute-start(bf16[72,4096]{1,0:T(8,128)(2,1)S(1)} %get-tuple-element.25), channel_id=1, source_target_pairs={{0,4},{2,6},{4,0},{6,2},{1,5},{3,7},{5,1},{7,3},{8,12},{10,14},{12... | collective-permute-start | bytes 1769480 | tf_op jit(solution)/shard_map/ppermute | solution.py:38
  77.7 38.8 %collective-permute-start.8 = (bf16[72,4096]{1,0:T(8,128)(2,1)S(1)}, bf16[72,4096]{1,0:T(8,128)(2,1)S(1)}, u32[]{:S(2)}, u32[]{:S(2)}) collective-permute-start(bf16[72,4096]{1,0:T(8,128)(2,1)S(1)} %get-tuple-element.24), channel_id=1, source_target_pairs={{0,6},{2,0},{4,2},{6,4},{1,7},{3,1},{5,3},{7,5},{8,14},{10,8},{12,... | collective-permute-start | bytes 1769480 | tf_op jit(solution)/shard_map/ppermute | solution.py:38
  88.8 28.0 %copy-start.3 = (f32[576,4096]{1,0:T(8,128)}, f32[576,4096]{1,0:T(8,128)S(1)}, u32[]{:S(2)}) copy-start(f32[576,4096]{1,0:T(8,128)S(1)} %fusion.63) | copy-start | bytes 28311556
  90.8 43.2 %collective-permute-start.5 = (bf16[4,72,4096]{2,1,0:T(8,128)(2,1)}, bf16[4,72,4096]{2,1,0:T(8,128)(2,1)}, u32[]{:S(2)}, u32[]{:S(2)}) collective-permute-start(bf16[4,72,4096]{2,1,0:T(8,128)(2,1)} %bitcast.18), channel_id=1, source_target_pairs={{0,1},{1,0},{2,3},{3,2},{4,5},{5,4},{6,7},{7,6},{8,9},{9,8},{10,11... | collective-permute-start | bytes 7077896 | tf_op jit(solution)/shard_map/ppermute | solution.py:33
  116.8 4.6 %collective-permute-start.9 = (bf16[4,72,4096]{2,1,0:T(8,128)(2,1)S(1)}, bf16[4,72,4096]{2,1,0:T(8,128)(2,1)S(1)}, u32[]{:S(2)}, u32[]{:S(2)}) collective-permute-start(bf16[4,72,4096]{2,1,0:T(8,128)(2,1)S(1)} %pad_maximum_fusion.1), channel_id=1, source_target_pairs={{0,1},{1,0},{2,3},{3,2},{4,5},{5,4},{6,7},{7,6},{8,9},{9,8},{10,11... | collective-permute-start | bytes 7077896 | tf_op jit(solution)/shard_map/ppermute | solution.py:33
  128.1 2.7 copy-start.11
  133.8 2.3 slice-start
  133.8 5.1 %collective-permute-start.10 = (bf16[4,72,4096]{2,1,0:T(8,128)(2,1)S(1)}, bf16[4,72,4096]{2,1,0:T(8,128)(2,1)S(1)}, u32[]{:S(2)}, u32[]{:S(2)}) collective-permute-start(bf16[4,72,4096]{2,1,0:T(8,128)(2,1)S(1)} %bitcast.128), channel_id=1, source_target_pairs={{0,1},{1,0},{2,3},{3,2},{4,5},{5,4},{6,7},{7,6},{8,9},{9,8},{10,11... | collective-permute-start | bytes 7077896 | tf_op jit(solution)/shard_map/ppermute | solution.py:33
  142.3 28.0 %collective-permute-start.11 = (bf16[72,4096]{1,0:T(8,128)(2,1)}, bf16[72,4096]{1,0:T(8,128)(2,1)S(1)}, u32[]{:S(2)}, u32[]{:S(2)}) collective-permute-start(bf16[72,4096]{1,0:T(8,128)(2,1)} %get-tuple-element.22), channel_id=1, source_target_pairs={{0,6},{2,0},{4,2},{6,4},{1,7},{3,1},{5,3},{7,5},{8,14},{10,8},{12,... | collective-permute-start | bytes 1769480 | tf_op jit(solution)/shard_map/ppermute | solution.py:38
  156.2 52.2 %collective-permute-start.12 = (bf16[72,4096]{1,0:T(8,128)(2,1)}, bf16[72,4096]{1,0:T(8,128)(2,1)S(1)}, u32[]{:S(2)}, u32[]{:S(2)}) collective-permute-start(bf16[72,4096]{1,0:T(8,128)(2,1)} %get-tuple-element.21), channel_id=1, source_target_pairs={{0,4},{2,6},{4,0},{6,2},{1,5},{3,7},{5,1},{7,3},{8,12},{10,14},{12... | collective-permute-start | bytes 1769480 | tf_op jit(solution)/shard_map/ppermute | solution.py:38
  156.9 51.5 %collective-permute-start.13 = (bf16[72,4096]{1,0:T(8,128)(2,1)}, bf16[72,4096]{1,0:T(8,128)(2,1)S(1)}, u32[]{:S(2)}, u32[]{:S(2)}) collective-permute-start(bf16[72,4096]{1,0:T(8,128)(2,1)} %get-tuple-element.20), channel_id=1, source_target_pairs={{0,2},{2,4},{4,6},{6,0},{1,3},{3,5},{5,7},{7,1},{8,10},{10,12},{12... | collective-permute-start | bytes 1769480 | tf_op jit(solution)/shard_map/ppermute | solution.py:38
  162.9 53.4 %copy-start.9 = (bf16[4096,384]{1,0:T(8,128)(2,1)}, bf16[4096,384]{1,0:T(8,128)(2,1)S(1)}, u32[]{:S(2)}) copy-start(bf16[4096,384]{1,0:T(8,128)(2,1)S(1)} %convolution_convert_fusion) | copy-start | bytes 9437188
  170.3 38.1 %copy-start.12 = (bf16[72,4096]{1,0:T(8,128)(2,1)}, bf16[72,4096]{1,0:T(8,128)(2,1)S(1)}, u32[]{:S(2)}) copy-start(bf16[72,4096]{1,0:T(8,128)(2,1)S(1)} %collective-permute-done.11) | copy-start | bytes 1769476
  208.4 0.8 copy-start.13
  208.4 1.0 copy-start.14
  211.1 1.7 copy-start.7
  212.8 6.2 %copy-start.2 = (bf16[1,128,4096]{2,1,0:T(8,128)(2,1)S(1)}, bf16[1,128,4096]{2,1,0:T(8,128)(2,1)}, u32[]{:S(2)}) copy-start(bf16[1,128,4096]{2,1,0:T(8,128)(2,1)} %param.9) | copy-start | bytes 3145732
  213.0 15.5 %collective-permute-start.15 = (bf16[72,4096]{1,0:T(8,128)(2,1)S(1)}, bf16[72,4096]{1,0:T(8,128)(2,1)S(1)}, u32[]{:S(2)}, u32[]{:S(2)}) collective-permute-start(bf16[72,4096]{1,0:T(8,128)(2,1)S(1)} %get-tuple-element.18), channel_id=1, source_target_pairs={{0,6},{2,0},{4,2},{6,4},{1,7},{3,1},{5,3},{7,5},{8,14},{10,8},{12,... | collective-permute-start | bytes 1769480 | tf_op jit(solution)/shard_map/ppermute | solution.py:38
  213.1 51.8 %collective-permute-start.16 = (bf16[72,4096]{1,0:T(8,128)(2,1)S(1)}, bf16[72,4096]{1,0:T(8,128)(2,1)S(1)}, u32[]{:S(2)}, u32[]{:S(2)}) collective-permute-start(bf16[72,4096]{1,0:T(8,128)(2,1)S(1)} %get-tuple-element.17), channel_id=1, source_target_pairs={{0,4},{2,6},{4,0},{6,2},{1,5},{3,7},{5,1},{7,3},{8,12},{10,14},{12... | collective-permute-start | bytes 1769480 | tf_op jit(solution)/shard_map/ppermute | solution.py:38
  214.3 50.6 %collective-permute-start.17 = (bf16[72,4096]{1,0:T(8,128)(2,1)S(1)}, bf16[72,4096]{1,0:T(8,128)(2,1)S(1)}, u32[]{:S(2)}, u32[]{:S(2)}) collective-permute-start(bf16[72,4096]{1,0:T(8,128)(2,1)S(1)} %get-tuple-element.16), channel_id=1, source_target_pairs={{0,2},{2,4},{4,6},{6,0},{1,3},{3,5},{5,7},{7,1},{8,10},{10,12},{12... | collective-permute-start | bytes 1769480 | tf_op jit(solution)/shard_map/ppermute | solution.py:38
  217.5 52.0 %collective-permute-start.19 = (bf16[2048,384]{1,0:T(8,128)(2,1)}, bf16[2048,384]{1,0:T(8,128)(2,1)}, u32[]{:S(2)}, u32[]{:S(2)}) collective-permute-start(bf16[2048,384]{1,0:T(8,128)(2,1)} %constant_dynamic-slice_fusion), channel_id=1, source_target_pairs={{0,8},{8,0},{1,9},{9,1},{2,10},{10,2},{3,11},{11,3},{4,12},{12,4},... | collective-permute-start | bytes 4718600 | tf_op jit(solution)/shard_map/ppermute | solution.py:63
  224.0 41.3 %copy-start.16 = (f32[1,4096]{1,0:T(1,128)S(1)}, f32[1,4096]{1,0:T(1,128)}, u32[]{:S(2)}) copy-start(f32[1,4096]{1,0:T(1,128)} %param.10) | copy-start | bytes 49156
  224.0 49.2 %collective-permute-start.14 = (bf16[1,128,4096]{2,1,0:T(8,128)(2,1)}, bf16[1,128,4096]{2,1,0:T(8,128)(2,1)}, u32[]{:S(2)}, u32[]{:S(2)}) collective-permute-start(bf16[1,128,4096]{2,1,0:T(8,128)(2,1)} %fusion.2), channel_id=1, source_target_pairs={{0,16},{1,17},{2,18},{3,19},{4,20},{5,21},{6,22},{7,23},{8,24},{9,... | collective-permute-start | bytes 3145736 | tf_op jit(solution)/shard_map/ppermute | solution.py:17
  265.2 1.2 copy-start.6
  268.3 26.0 %collective-permute-start.18 = (bf16[1,128,4096]{2,1,0:T(8,128)(2,1)}, bf16[1,128,4096]{2,1,0:T(8,128)(2,1)}, u32[]{:S(2)}, u32[]{:S(2)}) collective-permute-start(bf16[1,128,4096]{2,1,0:T(8,128)(2,1)} %fusion.21), channel_id=1, source_target_pairs={{16,0},{17,1},{18,2},{19,3},{20,4},{21,5},{22,6},{23,7},{24,8},{25... | collective-permute-start | bytes 3145736 | tf_op jit(solution)/shard_map/ppermute | solution.py:17
  269.6 29.2 %copy-start.1 = (bf16[1,4096,384]{2,1,0:T(8,128)(2,1)S(1)}, bf16[1,4096,384]{2,1,0:T(8,128)(2,1)}, u32[]{:S(2)}) copy-start(bf16[1,4096,384]{2,1,0:T(8,128)(2,1)} %param.13) | copy-start | bytes 9437188

commit v8 on v7

--- a/solution.py
+++ b/solution.py
@@ -158,23 +158,14 @@
     expert_out = from_experts(out_summed)
     back_summed, expert_out = lax.optimization_barrier((back_summed, expert_out))
     route_back = from_experts(back_summed)
-    mixing = jnp.where(pick_first.T, weights[:, 0:1], 0.0) + jnp.where(
-        pick_second.T, weights[:, 1:2], 0.0
-    )
-    moe_sum = jnp.dot(
-        mixing, expert_out, precision=lax.Precision.HIGHEST, preferred_element_type=jnp.float32
-    )
+    moe_sum = weights[:, 0:1] * jnp.take(expert_out, places[:, 0], axis=0) + weights[
+        :, 1:2
+    ] * jnp.take(expert_out, places[:, 1], axis=0)
     section_out = (tokens + moe_sum).astype(jnp.bfloat16)
     passed_on = passed_along(section_out[None], "section", 1)
     norm_grad = (
-        jnp.dot(
-            pick_both.T.astype(jnp.float32),
-            route_back,
-            precision=lax.Precision.HIGHEST,
-            preferred_element_type=jnp.float32,
-        )
-        * gain_row
-    )
+        jnp.take(route_back, places[:, 0], axis=0) + jnp.take(route_back, places[:, 1], axis=0)
+    ) * gain_row
     section_back = (
         upstream
         + inv_rms * norm_grad

time: 304 us -> 338 us (1.11)
  local copies, waits for them, and re-layouts: 28.9 us -> 58 us
  other arithmetic: 17.7 us -> 28.7 us
  matrix products: 38.7 us -> 31 us
  starting transfers between devices: 50 us -> 56.4 us
  waiting for transfers between devices: 162 us -> 157 us
    gather x0 -> x4, local copies, waits for them, and re-layouts: none -> 22 us  [the longest x1 5.86 us: per_device(): jnp.take(route_back, places[:, 1], axis=0)]
    ppermute x12, starting transfers between devices: 40.8 us -> 47.4 us  [shifted(): lax.ppermute(value, 'chip', [(source, (source + steps) % count) for sourc...]
    dot_general x2 -> x0, matrix products: 5.78 us -> none  [the longest x1 4.92 us: per_device(): jnp.dot(mixing, expert_out, precision=lax.Precision.HIGHEST, preferred_el...]
    convert_element_type x1 -> x2, other arithmetic: 0.7 us -> 5.7 us  [from_experts(): return returned.reshape(experts * capacity, model_width).astype(jnp.float32)]
    ppermute x12, waiting for transfers between devices: 137 us -> 132 us  [shifted(): lax.ppermute(value, 'chip', [(source, (source + steps) % count) for sourc...]
    unnamed x53 -> x55, local copies, waits for them, and re-layouts: 14.7 us -> 18 us
  transfers between devices with their start and end apart: 20 -> 20, of which waited for: 9 -> 10; matrix products, arithmetic and copies ran while one was open for 20% -> 25% of each run, Pallas kernels for 0% -> 0%
where the time goes in v8:
time: 338 us; the launch traced here: 333 us
  waiting for transfers between devices  157 us (46%)
  local copies, waits for them, and re-layouts  58 us (17%)
  starting transfers between devices  56.4 us (17%)
  matrix products  31 us (9%)
  other arithmetic  28.7 us (8%)
    ppermute x12, waiting for transfers between devices, shifted(): lax.ppermute(value, 'chip', [(source, (source + steps) % count) for sourc...  132 us
    ppermute x12, starting transfers between devices, shifted(): lax.ppermute(value, 'chip', [(source, (source + steps) % count) for sourc...  47.4 us
    ppermute x2, waiting for transfers between devices, passed_along(): lax.ppermute(value, axis, [(source, source + steps) for source in range(l...  21 us
    unnamed x55, local copies, waits for them, and re-layouts  18 us
  transfers between devices with their start and end apart: 20, of which 10 were waited for; matrix products, arithmetic and copies ran while one was open for 25% of the time, Pallas kernels for 0%

profile of v8, /device:TPU:0, one launch (start us, length us, event | category | flops | bytes accessed | tf_op | source)
XLA Modules:
  0.0 333.0 jit_solution(15563506219390081678)
XLA Ops:
  5.5 2.1 convolution_convert_fusion.1
  9.1 4.1 %collective-permute-start.1 = (bf16[72,4096]{1,0:T(8,128)(2,1)}, bf16[72,4096]{1,0:T(8,128)(2,1)}, u32[]{:S(2)}, u32[]{:S(2)}) collective-permute-start(bf16[72,4096]{1,0:T(8,128)(2,1)} %get-tuple-element.30), channel_id=1, source_target_pairs={{0,4},{2,6},{4,0},{6,2},{1,5},{3,7},{5,1},{7,3},{8,12},{10,14},{12... | collective-permute-start | bytes 1769480 | tf_op jit(solution)/shard_map/ppermute | solution.py:38
  18.4 2.3 fusion
  22.9 18.3 %collective-permute-done.1 = bf16[72,4096]{1,0:T(8,128)(2,1)} collective-permute-done((bf16[72,4096]{1,0:T(8,128)(2,1)}, bf16[72,4096]{1,0:T(8,128)(2,1)}, u32[]{:S(2)}, u32[]{:S(2)}) %collective-permute-start.1) | collective-permute-done | bytes 589856 | tf_op jit(solution)/shard_map/ppermute | solution.py:38
  41.2 12.1 %collective-permute-done = bf16[72,4096]{1,0:T(8,128)(2,1)} collective-permute-done((bf16[72,4096]{1,0:T(8,128)(2,1)}, bf16[72,4096]{1,0:T(8,128)(2,1)}, u32[]{:S(2)}, u32[]{:S(2)}) %collective-permute-start) | collective-permute-done | bytes 589856 | tf_op jit(solution)/shard_map/ppermute | solution.py:38
  53.3 1.9 pad_maximum_fusion
  61.3 2.8 copy-done.6
  64.3 12.2 %collective-permute-start.6 = (bf16[72,4096]{1,0:T(8,128)(2,1)S(1)}, bf16[72,4096]{1,0:T(8,128)(2,1)S(1)}, u32[]{:S(2)}, u32[]{:S(2)}) collective-permute-start(bf16[72,4096]{1,0:T(8,128)(2,1)S(1)} %get-tuple-element.27), channel_id=1, source_target_pairs={{0,2},{2,4},{4,6},{6,0},{1,3},{3,5},{5,7},{7,1},{8,10},{10,12},{12... | collective-permute-start | bytes 1769480 | tf_op jit(solution)/shard_map/ppermute | solution.py:38
  76.5 2.0 collective-permute-start.7
  78.5 3.0 collective-permute-start.8
  81.5 2.6 fusion.2
  84.2 2.6 fusion.6
  86.8 4.9 %fusion.65 = f32[576,4096]{1,0:T(8,128)S(1)} fusion(bf16[384,4096]{1,0:T(8,128)(2,1)S(1)} %constant_dynamic-update-slice_fusion.10, f32[384]{0:T(512)S(1)} %reduce.1, f32[384]{0:T(512)S(1)} %broadcast_multiply_fusion, f32[576,384]{1,0:T(8,128)S(1)} %fusion.2, f32[576,384]{1,0:T(8,128)S(1)} %fusion.6), kind=kOutput, calls=%fused_computation.124 | convolution fusion | flops 1827643392 | bytes 14355456 | tf_op jit(solution)/shard_map/dot_general | solution.py:126
  91.6 1.9 slice.168
  93.6 12.7 %collective-permute-done.7 = bf16[72,4096]{1,0:T(8,128)(2,1)S(1)} collective-permute-done((bf16[72,4096]{1,0:T(8,128)(2,1)S(1)}, bf16[72,4096]{1,0:T(8,128)(2,1)S(1)}, u32[]{:S(2)}, u32[]{:S(2)}) %collective-permute-start.7) | collective-permute-done | bytes 589856 | tf_op jit(solution)/shard_map/ppermute | solution.py:38
  106.3 8.3 %collective-permute-done.8 = bf16[72,4096]{1,0:T(8,128)(2,1)S(1)} collective-permute-done((bf16[72,4096]{1,0:T(8,128)(2,1)S(1)}, bf16[72,4096]{1,0:T(8,128)(2,1)S(1)}, u32[]{:S(2)}, u32[]{:S(2)}) %collective-permute-start.8) | collective-permute-done | bytes 589856 | tf_op jit(solution)/shard_map/ppermute | solution.py:38
  115.2 4.4 %collective-permute-done.9 = bf16[4,72,4096]{2,1,0:T(8,128)(2,1)S(1)} collective-permute-done((bf16[4,72,4096]{2,1,0:T(8,128)(2,1)S(1)}, bf16[4,72,4096]{2,1,0:T(8,128)(2,1)S(1)}, u32[]{:S(2)}, u32[]{:S(2)}) %collective-permute-start.9) | collective-permute-done | bytes 2359328 | tf_op jit(solution)/shard_map/ppermute | solution.py:33
  119.7 6.5 %multiply_convert_fusion = (bf16[576,384]{1,0:T(8,128)(2,1)S(1)}, f32[576,384]{1,0:T(8,128)S(1)}) fusion(f32[576,384]{1,0:T(8,128)S(1)} %fusion.6, f32[576,384]{1,0:T(8,128)S(1)} %fusion.2, f32[384]{0:T(512)S(1)} %broadcast_multiply_fusion, f32[384]{0:T(512)S(1)} %reduce.1, bf16[576,4096]{1,0:T(8,128)(2,1)S(1)} %bitcast.138, ...), kind=kOutput, calls=%fused_computation.101 | convolution fusion | flops 1840693248 | bytes 10963968 | tf_op jit(solution)/shard_map/dot_general | solution.py:140
  126.2 2.7 fusion.4
  129.0 2.6 convolution_add_fusion
  131.6 3.7 %copy-done.2 = f32[576,4096]{1,0:T(8,128)} copy-done((f32[576,4096]{1,0:T(8,128)}, f32[576,4096]{1,0:T(8,128)S(1)}, u32[]{:S(2)}) %copy-start.2) | copy-done | bytes 9437208
  135.3 1.8 slice.167
  137.2 2.3 slice-done.1
  139.6 2.4 add_convert_fusion.1
  142.0 2.3 slice-done
  144.3 2.4 add_convert_fusion
  146.9 17.9 %collective-permute-start.11 = (bf16[72,4096]{1,0:T(8,128)(2,1)S(1)}, bf16[72,4096]{1,0:T(8,128)(2,1)S(1)}, u32[]{:S(2)}, u32[]{:S(2)}) collective-permute-start(bf16[72,4096]{1,0:T(8,128)(2,1)S(1)} %get-tuple-element.23), channel_id=1, source_target_pairs={{0,6},{2,0},{4,2},{6,4},{1,7},{3,1},{5,3},{7,5},{8,14},{10,8},{12,... | collective-permute-start | bytes 1769480 | tf_op jit(solution)/shard_map/ppermute | solution.py:38
  165.5 13.1 %collective-permute-done.11 = bf16[72,4096]{1,0:T(8,128)(2,1)S(1)} collective-permute-done((bf16[72,4096]{1,0:T(8,128)(2,1)S(1)}, bf16[72,4096]{1,0:T(8,128)(2,1)S(1)}, u32[]{:S(2)}, u32[]{:S(2)}) %collective-permute-start.11) | collective-permute-done | bytes 589856 | tf_op jit(solution)/shard_map/ppermute | solution.py:38
  178.7 36.3 %collective-permute-done.12 = bf16[72,4096]{1,0:T(8,128)(2,1)S(1)} collective-permute-done((bf16[72,4096]{1,0:T(8,128)(2,1)S(1)}, bf16[72,4096]{1,0:T(8,128)(2,1)S(1)}, u32[]{:S(2)}, u32[]{:S(2)}) %collective-permute-start.12) | collective-permute-done | bytes 589856 | tf_op jit(solution)/shard_map/ppermute | solution.py:38
  215.3 2.9 bitcast_convert_fusion
  219.7 3.5 %collective-permute-start.16 = (bf16[72,4096]{1,0:T(8,128)(2,1)}, bf16[72,4096]{1,0:T(8,128)(2,1)}, u32[]{:S(2)}, u32[]{:S(2)}) collective-permute-start(bf16[72,4096]{1,0:T(8,128)(2,1)} %get-tuple-element.18), channel_id=1, source_target_pairs={{0,4},{2,6},{4,0},{6,2},{1,5},{3,7},{5,1},{7,3},{8,12},{10,14},{12... | collective-permute-start | bytes 1769480 | tf_op jit(solution)/shard_map/ppermute | solution.py:38
  223.2 2.0 collective-permute-start.17
  225.2 3.7 %convolution_convert_fusion = bf16[4096,384]{1,0:T(8,128)(2,1)S(1)} fusion(bf16[576,4096]{1,0:T(8,128)(2,1)S(1)} %bitcast.137, bf16[576,384]{1,0:T(8,128)(2,1)S(1)} %copy-done.14), kind=kOutput, calls=%fused_computation.5 | convolution fusion | flops 1813512192 | bytes 8306688 | tf_op jit(solution)/shard_map/dot_general | solution.py:177
  231.9 5.8 %gather_fusion = f32[128,4096]{1,0:T(8,128)} fusion(f32[288,4096]{1,0:T(8,128)} %bitcast_convert_fusion, s32[1024]{0:T(1024)S(1)} %pad_clamp_fusion.1), kind=kCustom, calls=%fused_computation.clone | custom fusion | bytes 4194816 | tf_op jit(solution)/shard_map/jit(_take)/gather | solution.py:161
  237.6 5.8 %gather_fusion.1 = f32[128,4096]{1,0:T(8,128)} fusion(f32[288,4096]{1,0:T(8,128)} %bitcast_convert_fusion, s32[1024]{0:T(1024)S(1)} %pad_clamp_fusion), kind=kCustom, calls=%fused_computation.1.clone | custom fusion | bytes 4194816 | tf_op jit(solution)/shard_map/jit(_take)/gather | solution.py:163
  243.4 31.0 %collective-permute-done.16 = bf16[72,4096]{1,0:T(8,128)(2,1)} collective-permute-done((bf16[72,4096]{1,0:T(8,128)(2,1)}, bf16[72,4096]{1,0:T(8,128)(2,1)}, u32[]{:S(2)}, u32[]{:S(2)}) %collective-permute-start.16) | collective-permute-done | bytes 589856 | tf_op jit(solution)/shard_map/ppermute | solution.py:38
  274.4 1.9 pad_maximum_fusion.3
  276.3 2.9 bitcast_convert_fusion.1
  279.2 4.6 %gather_fusion.2 = f32[128,4096]{1,0:T(8,128)S(1)} fusion(f32[288,4096]{1,0:T(8,128)} %bitcast_convert_fusion.1, s32[1024]{0:T(1024)S(1)} %pad_clamp_fusion.1), kind=kCustom, calls=%fused_computation.2.clone | custom fusion | bytes 4194816 | tf_op jit(solution)/shard_map/jit(_take)/gather | solution.py:167
  283.8 5.9 %gather_fusion.3 = f32[128,4096]{1,0:T(8,128)} fusion(f32[288,4096]{1,0:T(8,128)} %bitcast_convert_fusion.1, s32[1024]{0:T(1024)S(1)} %pad_clamp_fusion), kind=kCustom, calls=%fused_computation.3.clone | custom fusion | bytes 4194816 | tf_op jit(solution)/shard_map/jit(_take)/gather | solution.py:167
  289.6 2.4 fusion.17
  292.8 4.9 %fusion.23 = (bf16[1,128,4096]{2,1,0:T(8,128)(2,1)}, bf16[1,128,4096]{2,1,0:T(8,128)(2,1)}) fusion(bf16[1,128,4096]{2,1,0:T(8,128)(2,1)S(1)} %copy-done.8, bf16[1,128,4096]{2,1,0:T(8,128)(2,1)S(1)} %copy-done.5, f32[128]{0:T(128)S(1)} %broadcast_multiply_fusion.1, f32[128]{0:T(128)S(1)} %get-tuple-element.36, f32[128]{0:T(128)S(1)} %get-tuple-element.37, ...), kind=kLoop, calls=%fused_computation.62 | loop fusion | flops 9961472 | bytes 12602112 | tf_op jit(solution)/shard_map/broadcast_in_dim | solution.py:176
  297.7 4.4 %collective-permute-start.14 = (bf16[1,128,4096]{2,1,0:T(8,128)(2,1)}, bf16[1,128,4096]{2,1,0:T(8,128)(2,1)}, u32[]{:S(2)}, u32[]{:S(2)}) collective-permute-start(bf16[1,128,4096]{2,1,0:T(8,128)(2,1)} %get-tuple-element.33), channel_id=1, source_target_pairs={{0,16},{1,17},{2,18},{3,19},{4,20},{5,21},{6,22},{7,23},{8,24},{9,... | collective-permute-start | bytes 3145736 | tf_op jit(solution)/shard_map/ppermute | solution.py:17
  303.4 3.6 %fusion.20 = bf16[1,2048,384]{2,1,0:T(8,128)(2,1)} fusion(bf16[2048,384]{1,0:T(8,128)(2,1)} %collective-permute-done.19, bf16[4096,384]{1,0:T(8,128)(2,1)} %copy-done.11, s32[]{:T(128)S(6)} %select_n.57), kind=kLoop, calls=%fused_computation.50 | loop fusion | flops 3145728 | bytes 4718596 | tf_op jit(solution)/shard_map/broadcast_in_dim | solution.py:181
  307.0 15.9 %collective-permute-done.14 = bf16[1,128,4096]{2,1,0:T(8,128)(2,1)} collective-permute-done((bf16[1,128,4096]{2,1,0:T(8,128)(2,1)}, bf16[1,128,4096]{2,1,0:T(8,128)(2,1)}, u32[]{:S(2)}, u32[]{:S(2)}) %collective-permute-start.14) | collective-permute-done | bytes 1048608 | tf_op jit(solution)/shard_map/ppermute | solution.py:17
  322.9 5.1 %collective-permute-done.18 = bf16[1,128,4096]{2,1,0:T(8,128)(2,1)} collective-permute-done((bf16[1,128,4096]{2,1,0:T(8,128)(2,1)}, bf16[1,128,4096]{2,1,0:T(8,128)(2,1)}, u32[]{:S(2)}, u32[]{:S(2)}) %collective-permute-start.18) | collective-permute-done | bytes 1048608 | tf_op jit(solution)/shard_map/ppermute | solution.py:17
  328.0 2.3 copy.34
  330.3 2.3 copy.35
  (116 shorter events, 28.4 us)
Async XLA Ops:
  0.6 83.5 %copy-start = (bf16[1,4096,384]{2,1,0:T(8,128)(2,1)S(1)}, bf16[1,4096,384]{2,1,0:T(8,128)(2,1)}, u32[]{:S(2)}) copy-start(bf16[1,4096,384]{2,1,0:T(8,128)(2,1)} %param.15) | copy-start | bytes 9437188
  7.6 9.9 %copy-start.19 = (f32[1,128,2]{1,2,0:T(2,128)S(1)}, f32[1,128,2]{1,2,0:T(2,128)}, u32[]{:S(2)}) copy-start(f32[1,128,2]{1,2,0:T(2,128)} %param.14) | copy-start | bytes 3076
  7.6 9.9 %copy-start.7 = (bf16[1,128,4096]{2,1,0:T(8,128)(2,1)S(1)}, bf16[1,128,4096]{2,1,0:T(8,128)(2,1)}, u32[]{:S(2)}) copy-start(bf16[1,128,4096]{2,1,0:T(8,128)(2,1)} %param.19) | copy-start | bytes 3145732
  9.1 32.1 %collective-permute-start.1 = (bf16[72,4096]{1,0:T(8,128)(2,1)}, bf16[72,4096]{1,0:T(8,128)(2,1)}, u32[]{:S(2)}, u32[]{:S(2)}) collective-permute-start(bf16[72,4096]{1,0:T(8,128)(2,1)} %get-tuple-element.30), channel_id=1, source_target_pairs={{0,4},{2,6},{4,0},{6,2},{1,5},{3,7},{5,1},{7,3},{8,12},{10,14},{12... | collective-permute-start | bytes 1769480 | tf_op jit(solution)/shard_map/ppermute | solution.py:38
  13.1 28.0 %collective-permute-start.2 = (bf16[72,4096]{1,0:T(8,128)(2,1)}, bf16[72,4096]{1,0:T(8,128)(2,1)}, u32[]{:S(2)}, u32[]{:S(2)}) collective-permute-start(bf16[72,4096]{1,0:T(8,128)(2,1)} %get-tuple-element.29), channel_id=1, source_target_pairs={{0,6},{2,0},{4,2},{6,4},{1,7},{3,1},{5,3},{7,5},{8,14},{10,8},{12,... | collective-permute-start | bytes 1769480 | tf_op jit(solution)/shard_map/ppermute | solution.py:38
  14.5 38.8 %collective-permute-start = (bf16[72,4096]{1,0:T(8,128)(2,1)}, bf16[72,4096]{1,0:T(8,128)(2,1)}, u32[]{:S(2)}, u32[]{:S(2)}) collective-permute-start(bf16[72,4096]{1,0:T(8,128)(2,1)} %get-tuple-element.31), channel_id=1, source_target_pairs={{0,2},{2,4},{4,6},{6,0},{1,3},{3,5},{5,7},{7,1},{8,10},{10,12},{12... | collective-permute-start | bytes 1769480 | tf_op jit(solution)/shard_map/ppermute | solution.py:38
  15.2 44.3 %collective-permute-start.4 = (bf16[384,2048]{1,0:T(8,128)(2,1)}, bf16[384,2048]{1,0:T(8,128)(2,1)}, u32[]{:S(2)}, u32[]{:S(2)}) collective-permute-start(bf16[384,2048]{1,0:T(8,128)(2,1)} %bitcast.15), channel_id=1, source_target_pairs={{0,8},{8,0},{1,9},{9,1},{2,10},{10,2},{3,11},{11,3},{4,12},{12,4},... | collective-permute-start | bytes 4718600 | tf_op jit(solution)/shard_map/ppermute | solution.py:63
  18.4 2.4 copy-start.18
  21.2 32.1 %copy-start.12 = (bf16[1,72,4096]{2,1,0:T(8,128)(2,1)S(1)}, bf16[1,72,4096]{2,1,0:T(8,128)(2,1)}, u32[]{:S(2)}) copy-start(bf16[1,72,4096]{2,1,0:T(8,128)(2,1)} %get-tuple-element.28) | copy-start | bytes 1769476
  53.3 2.9 copy-start.16
  55.1 6.0 %collective-permute-start.3 = (bf16[4,72,4096]{2,1,0:T(8,128)(2,1)S(1)}, bf16[4,72,4096]{2,1,0:T(8,128)(2,1)S(1)}, u32[]{:S(2)}, u32[]{:S(2)}) collective-permute-start(bf16[4,72,4096]{2,1,0:T(8,128)(2,1)S(1)} %pad_maximum_fusion), channel_id=1, source_target_pairs={{0,1},{1,0},{2,3},{3,2},{4,5},{5,4},{6,7},{7,6},{8,9},{9,8},{10,11... | collective-permute-start | bytes 7077896 | tf_op jit(solution)/shard_map/ppermute | solution.py:33
  61.1 3.0 copy-start.6
  61.3 22.9 %copy-start.17 = (bf16[8,72,4096]{2,1,0:T(8,128)(2,1)}, bf16[8,72,4096]{2,1,0:T(8,128)(2,1)S(1)}, u32[]{:S(2)}) copy-start(bf16[8,72,4096]{2,1,0:T(8,128)(2,1)S(1)} %constant_dynamic-update-slice_fusion) | copy-start | bytes 14155780
  64.0 17.5 %copy-start.10 = (bf16[1,4096,384]{2,1,0:T(8,128)(2,1)S(1)}, bf16[1,4096,384]{2,1,0:T(8,128)(2,1)}, u32[]{:S(2)}) copy-start(bf16[1,4096,384]{2,1,0:T(8,128)(2,1)} %param.16) | copy-start | bytes 9437188
  64.3 29.3 %collective-permute-start.6 = (bf16[72,4096]{1,0:T(8,128)(2,1)S(1)}, bf16[72,4096]{1,0:T(8,128)(2,1)S(1)}, u32[]{:S(2)}, u32[]{:S(2)}) collective-permute-start(bf16[72,4096]{1,0:T(8,128)(2,1)S(1)} %get-tuple-element.27), channel_id=1, source_target_pairs={{0,2},{2,4},{4,6},{6,0},{1,3},{3,5},{5,7},{7,1},{8,10},{10,12},{12... | collective-permute-start | bytes 1769480 | tf_op jit(solution)/shard_map/ppermute | solution.py:38
  76.5 29.8 %collective-permute-start.7 = (bf16[72,4096]{1,0:T(8,128)(2,1)S(1)}, bf16[72,4096]{1,0:T(8,128)(2,1)S(1)}, u32[]{:S(2)}, u32[]{:S(2)}) collective-permute-start(bf16[72,4096]{1,0:T(8,128)(2,1)S(1)} %get-tuple-element.26), channel_id=1, source_target_pairs={{0,4},{2,6},{4,0},{6,2},{1,5},{3,7},{5,1},{7,3},{8,12},{10,14},{12... | collective-permute-start | bytes 1769480 | tf_op jit(solution)/shard_map/ppermute | solution.py:38
  78.5 36.1 %collective-permute-start.8 = (bf16[72,4096]{1,0:T(8,128)(2,1)S(1)}, bf16[72,4096]{1,0:T(8,128)(2,1)S(1)}, u32[]{:S(2)}, u32[]{:S(2)}) collective-permute-start(bf16[72,4096]{1,0:T(8,128)(2,1)S(1)} %get-tuple-element.25), channel_id=1, source_target_pairs={{0,6},{2,0},{4,2},{6,4},{1,7},{3,1},{5,3},{7,5},{8,14},{10,8},{12,... | collective-permute-start | bytes 1769480 | tf_op jit(solution)/shard_map/ppermute | solution.py:38
  91.6 23.5 %copy-start.3 = (f32[576,4096]{1,0:T(8,128)}, f32[576,4096]{1,0:T(8,128)S(1)}, u32[]{:S(2)}) copy-start(f32[576,4096]{1,0:T(8,128)S(1)} %fusion.65) | copy-start | bytes 28311556
  93.6 43.7 %collective-permute-start.5 = (bf16[4,72,4096]{2,1,0:T(8,128)(2,1)}, bf16[4,72,4096]{2,1,0:T(8,128)(2,1)}, u32[]{:S(2)}, u32[]{:S(2)}) collective-permute-start(bf16[4,72,4096]{2,1,0:T(8,128)(2,1)} %bitcast.17), channel_id=1, source_target_pairs={{0,1},{1,0},{2,3},{3,2},{4,5},{5,4},{6,7},{7,6},{8,9},{9,8},{10,11... | collective-permute-start | bytes 7077896 | tf_op jit(solution)/shard_map/ppermute | solution.py:33
  114.9 4.6 %collective-permute-start.9 = (bf16[4,72,4096]{2,1,0:T(8,128)(2,1)S(1)}, bf16[4,72,4096]{2,1,0:T(8,128)(2,1)S(1)}, u32[]{:S(2)}, u32[]{:S(2)}) collective-permute-start(bf16[4,72,4096]{2,1,0:T(8,128)(2,1)S(1)} %pad_maximum_fusion.1), channel_id=1, source_target_pairs={{0,1},{1,0},{2,3},{3,2},{4,5},{5,4},{6,7},{7,6},{8,9},{9,8},{10,11... | collective-permute-start | bytes 7077896 | tf_op jit(solution)/shard_map/ppermute | solution.py:33
  126.2 2.7 copy-start.13
  131.6 3.7 %copy-start.2 = (f32[576,4096]{1,0:T(8,128)}, f32[576,4096]{1,0:T(8,128)S(1)}, u32[]{:S(2)}) copy-start(f32[576,4096]{1,0:T(8,128)S(1)} %convolution_add_fusion) | copy-start | bytes 28311556
  137.1 4.9 %collective-permute-start.10 = (bf16[4,72,4096]{2,1,0:T(8,128)(2,1)}, bf16[4,72,4096]{2,1,0:T(8,128)(2,1)}, u32[]{:S(2)}, u32[]{:S(2)}) collective-permute-start(bf16[4,72,4096]{2,1,0:T(8,128)(2,1)} %bitcast.27), channel_id=1, source_target_pairs={{0,1},{1,0},{2,3},{3,2},{4,5},{5,4},{6,7},{7,6},{8,9},{9,8},{10,11... | collective-permute-start | bytes 7077896 | tf_op jit(solution)/shard_map/ppermute | solution.py:33
  137.2 2.3 slice-start.1
  142.0 2.3 slice-start
  146.9 31.8 %collective-permute-start.11 = (bf16[72,4096]{1,0:T(8,128)(2,1)S(1)}, bf16[72,4096]{1,0:T(8,128)(2,1)S(1)}, u32[]{:S(2)}, u32[]{:S(2)}) collective-permute-start(bf16[72,4096]{1,0:T(8,128)(2,1)S(1)} %get-tuple-element.23), channel_id=1, source_target_pairs={{0,6},{2,0},{4,2},{6,4},{1,7},{3,1},{5,3},{7,5},{8,14},{10,8},{12,... | collective-permute-start | bytes 1769480 | tf_op jit(solution)/shard_map/ppermute | solution.py:38
  164.9 50.2 %collective-permute-start.12 = (bf16[72,4096]{1,0:T(8,128)(2,1)S(1)}, bf16[72,4096]{1,0:T(8,128)(2,1)S(1)}, u32[]{:S(2)}, u32[]{:S(2)}) collective-permute-start(bf16[72,4096]{1,0:T(8,128)(2,1)S(1)} %get-tuple-element.22), channel_id=1, source_target_pairs={{0,4},{2,6},{4,0},{6,2},{1,5},{3,7},{5,1},{7,3},{8,12},{10,14},{12... | collective-permute-start | bytes 1769480 | tf_op jit(solution)/shard_map/ppermute | solution.py:38
  164.9 50.2 %collective-permute-start.13 = (bf16[72,4096]{1,0:T(8,128)(2,1)S(1)}, bf16[72,4096]{1,0:T(8,128)(2,1)S(1)}, u32[]{:S(2)}, u32[]{:S(2)}) collective-permute-start(bf16[72,4096]{1,0:T(8,128)(2,1)S(1)} %get-tuple-element.21), channel_id=1, source_target_pairs={{0,2},{2,4},{4,6},{6,0},{1,3},{3,5},{5,7},{7,1},{8,10},{10,12},{12... | collective-permute-start | bytes 1769480 | tf_op jit(solution)/shard_map/ppermute | solution.py:38
  215.0 10.2 %slice-start.2 = ((s8[4718592]{0:T(1024)(128)(4,1)}), s8[4194304]{0:T(1024)(128)(4,1)S(1)}, s32[]{:S(2)}) async-start(s8[4718592]{0:T(1024)(128)(4,1)} %bitcast.135), calls=%async_computation.2 | async-start | bytes 8388608
  215.3 9.9 %slice-start.3 = ((s8[4718592]{0:T(1024)(128)(4,1)}), s8[524288]{0:T(1024)(128)(4,1)S(1)}, s32[]{:S(2)}) async-start(s8[4718592]{0:T(1024)(128)(4,1)} %bitcast.135), calls=%async_computation.3 | async-start | bytes 1048576
  218.2 7.0 %copy-start.14 = (bf16[576,384]{1,0:T(8,128)(2,1)S(1)}, bf16[576,384]{1,0:T(8,128)(2,1)}, u32[]{:S(2)}) copy-start(bf16[576,384]{1,0:T(8,128)(2,1)} %copy-done.13) | copy-start | bytes 1327108
  219.7 23.8 %collective-permute-start.15 = (bf16[72,4096]{1,0:T(8,128)(2,1)}, bf16[72,4096]{1,0:T(8,128)(2,1)}, u32[]{:S(2)}, u32[]{:S(2)}) collective-permute-start(bf16[72,4096]{1,0:T(8,128)(2,1)} %get-tuple-element.19), channel_id=1, source_target_pairs={{0,6},{2,0},{4,2},{6,4},{1,7},{3,1},{5,3},{7,5},{8,14},{10,8},{12,... | collective-permute-start | bytes 1769480 | tf_op jit(solution)/shard_map/ppermute | solution.py:38
  219.7 54.7 %collective-permute-start.16 = (bf16[72,4096]{1,0:T(8,128)(2,1)}, bf16[72,4096]{1,0:T(8,128)(2,1)}, u32[]{:S(2)}, u32[]{:S(2)}) collective-permute-start(bf16[72,4096]{1,0:T(8,128)(2,1)} %get-tuple-element.18), channel_id=1, source_target_pairs={{0,4},{2,6},{4,0},{6,2},{1,5},{3,7},{5,1},{7,3},{8,12},{10,14},{12... | collective-permute-start | bytes 1769480 | tf_op jit(solution)/shard_map/ppermute | solution.py:38
  223.2 51.2 %collective-permute-start.17 = (bf16[72,4096]{1,0:T(8,128)(2,1)}, bf16[72,4096]{1,0:T(8,128)(2,1)}, u32[]{:S(2)}, u32[]{:S(2)}) collective-permute-start(bf16[72,4096]{1,0:T(8,128)(2,1)} %get-tuple-element.17), channel_id=1, source_target_pairs={{0,2},{2,4},{4,6},{6,0},{1,3},{3,5},{5,7},{7,1},{8,10},{10,12},{12... | collective-permute-start | bytes 1769480 | tf_op jit(solution)/shard_map/ppermute | solution.py:38
  228.9 8.7 %copy-start.11 = (bf16[4096,384]{1,0:T(8,128)(2,1)}, bf16[4096,384]{1,0:T(8,128)(2,1)S(1)}, u32[]{:S(2)}) copy-start(bf16[4096,384]{1,0:T(8,128)(2,1)S(1)} %convolution_convert_fusion) | copy-start | bytes 9437188
  230.4 73.0 %collective-permute-start.19 = (bf16[2048,384]{1,0:T(8,128)(2,1)}, bf16[2048,384]{1,0:T(8,128)(2,1)}, u32[]{:S(2)}, u32[]{:S(2)}) collective-permute-start(bf16[2048,384]{1,0:T(8,128)(2,1)} %constant_dynamic-slice_fusion), channel_id=1, source_target_pairs={{0,8},{8,0},{1,9},{9,1},{2,10},{10,2},{3,11},{11,3},{4,12},{12,4},... | collective-permute-start | bytes 4718600 | tf_op jit(solution)/shard_map/ppermute | solution.py:63
  283.7 5.9 %copy-start.5 = (bf16[1,128,4096]{2,1,0:T(8,128)(2,1)S(1)}, bf16[1,128,4096]{2,1,0:T(8,128)(2,1)}, u32[]{:S(2)}) copy-start(bf16[1,128,4096]{2,1,0:T(8,128)(2,1)} %param.11) | copy-start | bytes 3145732
  283.7 5.9 %copy-start.15 = (f32[1,4096]{1,0:T(1,128)S(1)}, f32[1,4096]{1,0:T(1,128)}, u32[]{:S(2)}) copy-start(f32[1,4096]{1,0:T(1,128)} %param.12) | copy-start | bytes 49156
  289.6 2.4 copy-start.4
  289.6 2.5 copy-start.8
  289.6 3.2 copy-start.9
  297.7 25.2 %collective-permute-start.14 = (bf16[1,128,4096]{2,1,0:T(8,128)(2,1)}, bf16[1,128,4096]{2,1,0:T(8,128)(2,1)}, u32[]{:S(2)}, u32[]{:S(2)}) collective-permute-start(bf16[1,128,4096]{2,1,0:T(8,128)(2,1)} %get-tuple-element.33), channel_id=1, source_target_pairs={{0,16},{1,17},{2,18},{3,19},{4,20},{5,21},{6,22},{7,23},{8,24},{9,... | collective-permute-start | bytes 3145736 | tf_op jit(solution)/shard_map/ppermute | solution.py:17
  302.1 25.9 %collective-permute-start.18 = (bf16[1,128,4096]{2,1,0:T(8,128)(2,1)}, bf16[1,128,4096]{2,1,0:T(8,128)(2,1)}, u32[]{:S(2)}, u32[]{:S(2)}) collective-permute-start(bf16[1,128,4096]{2,1,0:T(8,128)(2,1)} %get-tuple-element.32), channel_id=1, source_target_pairs={{16,0},{17,1},{18,2},{19,3},{20,4},{21,5},{22,6},{23,7},{24,8},{25... | collective-permute-start | bytes 3145736 | tf_op jit(solution)/shard_map/ppermute | solution.py:17
  303.4 29.2 %copy-start.1 = (bf16[1,4096,384]{2,1,0:T(8,128)(2,1)S(1)}, bf16[1,4096,384]{2,1,0:T(8,128)(2,1)}, u32[]{:S(2)}) copy-start(bf16[1,4096,384]{2,1,0:T(8,128)(2,1)} %param.15) | copy-start | bytes 9437188

commit v9 on v7

--- a/solution.py
+++ b/solution.py
@@ -14,7 +14,10 @@
 def passed_along(value, axis, steps):
     count = lax.axis_size(axis)
     leading, last = (max(0, -steps), min(count, count - steps))
-    return lax.ppermute(value, axis, [(source, source + steps) for source in range(leading, last)])
+    moved = lax.ppermute(value, axis, [(source, source + steps) for source in range(leading, last)])
+    receiver = lax.axis_index(axis)
+    has_source = jnp.logical_and(receiver - steps >= 0, receiver - steps < count)
+    return jnp.where(has_source, moved, jnp.zeros_like(moved))
 
 
 def lif_rate(gate_act, up_act, leak_rate):

time: 304 us -> 299 us (0.984)
  local copies, waits for them, and re-layouts: 28.9 us -> 23.2 us
  waiting for transfers between devices: 162 us -> 166 us
    unnamed x53 -> x49, local copies, waits for them, and re-layouts: 14.7 us -> 10.1 us
    ppermute x12, waiting for transfers between devices: 137 us -> 140 us  [shifted(): lax.ppermute(value, 'chip', [(source, (source + steps) % count) for sourc...]
  transfers between devices with their start and end apart: 20 -> 20, of which waited for: 9 -> 10; matrix products, arithmetic and copies ran while one was open for 20% -> 19% of each run, Pallas kernels for 0% -> 0%
where the time goes in v9:
time: 299 us; the launch traced here: 294 us
  waiting for transfers between devices  166 us (56%)
  starting transfers between devices  48.9 us (16%)
  matrix products  37.7 us (13%)
  local copies, waits for them, and re-layouts  23.2 us (8%)
  other arithmetic  16.9 us (6%)
    ppermute x12, waiting for transfers between devices, shifted(): lax.ppermute(value, 'chip', [(source, (source + steps) % count) for sourc...  140 us
    ppermute x12, starting transfers between devices, shifted(): lax.ppermute(value, 'chip', [(source, (source + steps) % count) for sourc...  40.8 us
    ppermute x2, waiting for transfers between devices, passed_along(): lax.ppermute(value, axis, [(source, source + steps) for source in range(l...  21.7 us
    unnamed x49, local copies, waits for them, and re-layouts  10.1 us
    dot_general x1, matrix products, per_device(): lax.dot_general(grad_rows, down_full, (((1,), (1,)), ((), ())), preferred...  6.51 us
  transfers between devices with their start and end apart: 20, of which 10 were waited for; matrix products, arithmetic and copies ran while one was open for 19% of the time, Pallas kernels for 0%

profile of v9, /device:TPU:0, one launch (start us, length us, event | category | flops | bytes accessed | tf_op | source)
XLA Modules:
  0.0 294.4 jit_solution(17807512844046278863)
XLA Ops:
  1.9 1.2 reduce-window.6
  3.9 1.5 fusion.14
  5.5 2.1 convolution_convert_fusion.1
  7.6 1.5 slice_bitcast_fusion
  9.0 3.1 %collective-permute-start = (bf16[72,4096]{1,0:T(8,128)(2,1)}, bf16[72,4096]{1,0:T(8,128)(2,1)}, u32[]{:S(2)}, u32[]{:S(2)}) collective-permute-start(bf16[72,4096]{1,0:T(8,128)(2,1)} %get-tuple-element.30), channel_id=1, source_target_pairs={{0,2},{2,4},{4,6},{6,0},{1,3},{3,5},{5,7},{7,1},{8,10},{10,12},{12... | collective-permute-start | bytes 1769480 | tf_op jit(solution)/shard_map/ppermute | solution.py:41
  12.1 2.6 collective-permute-start.1
  14.7 1.3 collective-permute-start.2
  16.0 1.5 collective-permute-start.4
  19.3 2.3 fusion
  22.1 1.8 constant_dynamic-update-slice_fusion.11
  23.9 4.8 %collective-permute-done = bf16[72,4096]{1,0:T(8,128)(2,1)} collective-permute-done((bf16[72,4096]{1,0:T(8,128)(2,1)}, bf16[72,4096]{1,0:T(8,128)(2,1)}, u32[]{:S(2)}, u32[]{:S(2)}) %collective-permute-start) | collective-permute-done | bytes 589856 | tf_op jit(solution)/shard_map/ppermute | solution.py:41
  28.8 24.4 %collective-permute-done.1 = bf16[72,4096]{1,0:T(8,128)(2,1)} collective-permute-done((bf16[72,4096]{1,0:T(8,128)(2,1)}, bf16[72,4096]{1,0:T(8,128)(2,1)}, u32[]{:S(2)}, u32[]{:S(2)}) %collective-permute-start.1) | collective-permute-done | bytes 589856 | tf_op jit(solution)/shard_map/ppermute | solution.py:41
  53.2 1.7 pad_maximum_fusion
  55.0 1.1 constant_dynamic-update-slice_fusion.3
  56.1 1.1 constant_dynamic-update-slice_fusion.2
  57.2 1.1 constant_dynamic-update-slice_fusion.1
  58.3 1.6 constant_dynamic-update-slice_fusion.10
  60.3 2.4 copy-done.4
  63.0 13.2 %collective-permute-start.6 = (bf16[72,4096]{1,0:T(8,128)(2,1)S(1)}, bf16[72,4096]{1,0:T(8,128)(2,1)S(1)}, u32[]{:S(2)}, u32[]{:S(2)}) collective-permute-start(bf16[72,4096]{1,0:T(8,128)(2,1)S(1)} %get-tuple-element.26), channel_id=1, source_target_pairs={{0,2},{2,4},{4,6},{6,0},{1,3},{3,5},{5,7},{7,1},{8,10},{10,12},{12... | collective-permute-start | bytes 1769480 | tf_op jit(solution)/shard_map/ppermute | solution.py:41
  76.1 1.6 collective-permute-start.7
  78.7 2.6 fusion.4
  81.3 2.6 fusion.8
  84.0 4.9 %fusion.63 = f32[576,4096]{1,0:T(8,128)S(1)} fusion(bf16[384,4096]{1,0:T(8,128)(2,1)S(1)} %constant_dynamic-update-slice_fusion.10, f32[384]{0:T(512)S(1)} %reduce.2, f32[384]{0:T(512)S(1)} %broadcast_multiply_fusion, f32[576,384]{1,0:T(8,128)S(1)} %fusion.4, f32[576,384]{1,0:T(8,128)S(1)} %fusion.8), kind=kOutput, calls=%fused_computation.117 | convolution fusion | flops 1827643392 | bytes 14355456 | tf_op jit(solution)/shard_map/dot_general | solution.py:129
  88.8 2.0 slice.156
  91.5 25.0 %collective-permute-done.7 = bf16[72,4096]{1,0:T(8,128)(2,1)S(1)} collective-permute-done((bf16[72,4096]{1,0:T(8,128)(2,1)S(1)}, bf16[72,4096]{1,0:T(8,128)(2,1)S(1)}, u32[]{:S(2)}, u32[]{:S(2)}) %collective-permute-start.7) | collective-permute-done | bytes 589856 | tf_op jit(solution)/shard_map/ppermute | solution.py:41
  117.0 4.4 %collective-permute-done.9 = bf16[4,72,4096]{2,1,0:T(8,128)(2,1)S(1)} collective-permute-done((bf16[4,72,4096]{2,1,0:T(8,128)(2,1)S(1)}, bf16[4,72,4096]{2,1,0:T(8,128)(2,1)S(1)}, u32[]{:S(2)}, u32[]{:S(2)}) %collective-permute-start.9) | collective-permute-done | bytes 2359328 | tf_op jit(solution)/shard_map/ppermute | solution.py:36
  121.6 6.5 %multiply_convert_fusion = (bf16[576,384]{1,0:T(8,128)(2,1)S(1)}, f32[576,384]{1,0:T(8,128)S(1)}) fusion(f32[576,384]{1,0:T(8,128)S(1)} %fusion.8, f32[576,384]{1,0:T(8,128)S(1)} %fusion.4, f32[384]{0:T(512)S(1)} %broadcast_multiply_fusion, f32[384]{0:T(512)S(1)} %reduce.2, bf16[576,4096]{1,0:T(8,128)(2,1)S(1)} %bitcast.140, ...), kind=kOutput, calls=%fused_computation.94 | convolution fusion | flops 1840693248 | bytes 10963968 | tf_op jit(solution)/shard_map/dot_general | solution.py:143
  128.1 2.7 fusion.6
  130.8 2.6 convolution_add_fusion
  134.0 2.1 slice-done
  136.2 2.4 add_convert_fusion.1
  138.9 2.2 add_convert_fusion
  141.1 1.2 fusion.104
  142.4 13.8 %collective-permute-start.11 = (bf16[72,4096]{1,0:T(8,128)(2,1)}, bf16[72,4096]{1,0:T(8,128)(2,1)S(1)}, u32[]{:S(2)}, u32[]{:S(2)}) collective-permute-start(bf16[72,4096]{1,0:T(8,128)(2,1)} %get-tuple-element.22), channel_id=1, source_target_pairs={{0,6},{2,0},{4,2},{6,4},{1,7},{3,1},{5,3},{7,5},{8,14},{10,8},{12,... | collective-permute-start | bytes 1769480 | tf_op jit(solution)/shard_map/ppermute | solution.py:41
  157.2 5.7 %convolution_convert_fusion = bf16[4096,384]{1,0:T(8,128)(2,1)S(1)} fusion(bf16[576,4096]{1,0:T(8,128)(2,1)} %bitcast.139, bf16[576,384]{1,0:T(8,128)(2,1)} %copy-done.10), kind=kOutput, calls=%fused_computation.1 | convolution fusion | flops 1813512192 | bytes 8306688 | tf_op jit(solution)/shard_map/dot_general | solution.py:189
  162.9 7.5 %collective-permute-done.11 = bf16[72,4096]{1,0:T(8,128)(2,1)S(1)} collective-permute-done((bf16[72,4096]{1,0:T(8,128)(2,1)}, bf16[72,4096]{1,0:T(8,128)(2,1)S(1)}, u32[]{:S(2)}, u32[]{:S(2)}) %collective-permute-start.11) | collective-permute-done | bytes 589856 | tf_op jit(solution)/shard_map/ppermute | solution.py:41
  170.3 38.1 %collective-permute-done.12 = bf16[72,4096]{1,0:T(8,128)(2,1)S(1)} collective-permute-done((bf16[72,4096]{1,0:T(8,128)(2,1)}, bf16[72,4096]{1,0:T(8,128)(2,1)S(1)}, u32[]{:S(2)}, u32[]{:S(2)}) %collective-permute-start.12) | collective-permute-done | bytes 589856 | tf_op jit(solution)/shard_map/ppermute | solution.py:41
  209.4 1.7 pad_maximum_fusion.2
  213.1 1.2 collective-permute-start.16
  214.3 1.9 collective-permute-start.17
  216.4 1.5 collective-permute-start.19
  217.9 3.9 %fusion.2 = bf16[1,128,4096]{2,1,0:T(8,128)(2,1)S(1)} fusion(f32[288,4096]{1,0:T(8,128)S(1)} %bitcast_convert_fusion, bf16[1,128,4096]{2,1,0:T(8,128)(2,1)S(1)} %copy-done.2, f32[128]{0:T(128)S(1)} %get-tuple-element.31, s32[128]{0:T(128)S(1)} %get-tuple-element.14, f32[128]{0:T(128)S(1)} %get-tuple-element.32, s32[128]{0:T(128)S(1)} %get-tuple-element.13), kind=kOutput, calls=%fused_computation.12 | convolution fusion | flops 1813696512 | bytes 6817792 | tf_op jit(solution)/shard_map/dot_general | solution.py:167
  221.9 3.5 %collective-permute-start.14 = (bf16[1,128,4096]{2,1,0:T(8,128)(2,1)S(1)}, bf16[1,128,4096]{2,1,0:T(8,128)(2,1)S(1)}, u32[]{:S(2)}, u32[]{:S(2)}) collective-permute-start(bf16[1,128,4096]{2,1,0:T(8,128)(2,1)S(1)} %fusion.2), channel_id=1, source_target_pairs={{0,16},{1,17},{2,18},{3,19},{4,20},{5,21},{6,22},{7,23},{8,24},{9,... | collective-permute-start | bytes 3145736 | tf_op jit(solution)/shard_map/ppermute | solution.py:17
  225.4 3.1 %collective-permute-done.15 = bf16[72,4096]{1,0:T(8,128)(2,1)S(1)} collective-permute-done((bf16[72,4096]{1,0:T(8,128)(2,1)S(1)}, bf16[72,4096]{1,0:T(8,128)(2,1)S(1)}, u32[]{:S(2)}, u32[]{:S(2)}) %collective-permute-start.15) | collective-permute-done | bytes 589856 | tf_op jit(solution)/shard_map/ppermute | solution.py:41
  228.5 36.4 %collective-permute-done.16 = bf16[72,4096]{1,0:T(8,128)(2,1)S(1)} collective-permute-done((bf16[72,4096]{1,0:T(8,128)(2,1)S(1)}, bf16[72,4096]{1,0:T(8,128)(2,1)S(1)}, u32[]{:S(2)}, u32[]{:S(2)}) %collective-permute-start.16) | collective-permute-done | bytes 589856 | tf_op jit(solution)/shard_map/ppermute | solution.py:41
  267.3 1.3 collective-permute-start.18
  268.6 1.6 fusion.19
  271.3 21.7 %collective-permute-done.18 = bf16[1,128,4096]{2,1,0:T(8,128)(2,1)S(1)} collective-permute-done((bf16[1,128,4096]{2,1,0:T(8,128)(2,1)S(1)}, bf16[1,128,4096]{2,1,0:T(8,128)(2,1)S(1)}, u32[]{:S(2)}, u32[]{:S(2)}) %collective-permute-start.18) | collective-permute-done | bytes 1048608 | tf_op jit(solution)/shard_map/ppermute | solution.py:17
  (103 shorter events, 16.3 us)
Async XLA Ops:
  0.6 80.7 %copy-start = (bf16[1,4096,384]{2,1,0:T(8,128)(2,1)S(1)}, bf16[1,4096,384]{2,1,0:T(8,128)(2,1)}, u32[]{:S(2)}) copy-start(bf16[1,4096,384]{2,1,0:T(8,128)(2,1)} %param.13) | copy-start | bytes 9437188
  7.6 10.8 %copy-start.17 = (f32[1,128,2]{1,2,0:T(2,128)S(1)}, f32[1,128,2]{1,2,0:T(2,128)}, u32[]{:S(2)}) copy-start(f32[1,128,2]{1,2,0:T(2,128)} %param.12) | copy-start | bytes 3076
  7.6 10.8 %copy-start.5 = (bf16[1,128,4096]{2,1,0:T(8,128)(2,1)S(1)}, bf16[1,128,4096]{2,1,0:T(8,128)(2,1)}, u32[]{:S(2)}) copy-start(bf16[1,128,4096]{2,1,0:T(8,128)(2,1)} %param.17) | copy-start | bytes 3145732
  9.0 19.7 %collective-permute-start = (bf16[72,4096]{1,0:T(8,128)(2,1)}, bf16[72,4096]{1,0:T(8,128)(2,1)}, u32[]{:S(2)}, u32[]{:S(2)}) collective-permute-start(bf16[72,4096]{1,0:T(8,128)(2,1)} %get-tuple-element.30), channel_id=1, source_target_pairs={{0,2},{2,4},{4,6},{6,0},{1,3},{3,5},{5,7},{7,1},{8,10},{10,12},{12... | collective-permute-start | bytes 1769480 | tf_op jit(solution)/shard_map/ppermute | solution.py:41
  12.1 41.1 %collective-permute-start.1 = (bf16[72,4096]{1,0:T(8,128)(2,1)}, bf16[72,4096]{1,0:T(8,128)(2,1)}, u32[]{:S(2)}, u32[]{:S(2)}) collective-permute-start(bf16[72,4096]{1,0:T(8,128)(2,1)} %get-tuple-element.29), channel_id=1, source_target_pairs={{0,4},{2,6},{4,0},{6,2},{1,5},{3,7},{5,1},{7,3},{8,12},{10,14},{12... | collective-permute-start | bytes 1769480 | tf_op jit(solution)/shard_map/ppermute | solution.py:41
  14.7 38.5 %collective-permute-start.2 = (bf16[72,4096]{1,0:T(8,128)(2,1)}, bf16[72,4096]{1,0:T(8,128)(2,1)}, u32[]{:S(2)}, u32[]{:S(2)}) collective-permute-start(bf16[72,4096]{1,0:T(8,128)(2,1)} %get-tuple-element.28), channel_id=1, source_target_pairs={{0,6},{2,0},{4,2},{6,4},{1,7},{3,1},{5,3},{7,5},{8,14},{10,8},{12,... | collective-permute-start | bytes 1769480 | tf_op jit(solution)/shard_map/ppermute | solution.py:41
  16.0 42.3 %collective-permute-start.4 = (bf16[384,2048]{1,0:T(8,128)(2,1)}, bf16[384,2048]{1,0:T(8,128)(2,1)}, u32[]{:S(2)}, u32[]{:S(2)}) collective-permute-start(bf16[384,2048]{1,0:T(8,128)(2,1)} %bitcast.16), channel_id=1, source_target_pairs={{0,8},{8,0},{1,9},{9,1},{2,10},{10,2},{3,11},{11,3},{4,12},{12,4},... | collective-permute-start | bytes 4718600 | tf_op jit(solution)/shard_map/ppermute | solution.py:66
  19.3 2.4 copy-start.16
  21.7 31.5 %copy-start.9 = (bf16[1,72,4096]{2,1,0:T(8,128)(2,1)S(1)}, bf16[1,72,4096]{2,1,0:T(8,128)(2,1)}, u32[]{:S(2)}) copy-start(bf16[1,72,4096]{2,1,0:T(8,128)(2,1)} %get-tuple-element.27) | copy-start | bytes 1769476
  21.7 33.3 %slice-start.1 = ((s8[4718592]{0:T(1024)(128)(4,1)}), s8[4194304]{0:T(1024)(128)(4,1)S(1)}, s32[]{:S(2)}) async-start(s8[4718592]{0:T(1024)(128)(4,1)} %bitcast.135), calls=%async_computation.1 | async-start | bytes 8388608
  22.1 32.9 %slice-start.2 = ((s8[4718592]{0:T(1024)(128)(4,1)}), s8[524288]{0:T(1024)(128)(4,1)S(1)}, s32[]{:S(2)}) async-start(s8[4718592]{0:T(1024)(128)(4,1)} %bitcast.135), calls=%async_computation.2 | async-start | bytes 1048576
  54.9 5.1 %collective-permute-start.3 = (bf16[4,72,4096]{2,1,0:T(8,128)(2,1)S(1)}, bf16[4,72,4096]{2,1,0:T(8,128)(2,1)S(1)}, u32[]{:S(2)}, u32[]{:S(2)}) collective-permute-start(bf16[4,72,4096]{2,1,0:T(8,128)(2,1)S(1)} %pad_maximum_fusion), channel_id=1, source_target_pairs={{0,1},{1,0},{2,3},{3,2},{4,5},{5,4},{6,7},{7,6},{8,9},{9,8},{10,11... | collective-permute-start | bytes 7077896 | tf_op jit(solution)/shard_map/ppermute | solution.py:36
  60.0 2.7 copy-start.4
  60.2 21.1 %copy-start.14 = (bf16[8,72,4096]{2,1,0:T(8,128)(2,1)}, bf16[8,72,4096]{2,1,0:T(8,128)(2,1)S(1)}, u32[]{:S(2)}) copy-start(bf16[8,72,4096]{2,1,0:T(8,128)(2,1)S(1)} %constant_dynamic-update-slice_fusion) | copy-start | bytes 14155780
  60.3 18.5 %copy-start.8 = (bf16[1,4096,384]{2,1,0:T(8,128)(2,1)S(1)}, bf16[1,4096,384]{2,1,0:T(8,128)(2,1)}, u32[]{:S(2)}) copy-start(bf16[1,4096,384]{2,1,0:T(8,128)(2,1)} %param.14) | copy-start | bytes 9437188
  63.0 28.5 %collective-permute-start.6 = (bf16[72,4096]{1,0:T(8,128)(2,1)S(1)}, bf16[72,4096]{1,0:T(8,128)(2,1)S(1)}, u32[]{:S(2)}, u32[]{:S(2)}) collective-permute-start(bf16[72,4096]{1,0:T(8,128)(2,1)S(1)} %get-tuple-element.26), channel_id=1, source_target_pairs={{0,2},{2,4},{4,6},{6,0},{1,3},{3,5},{5,7},{7,1},{8,10},{10,12},{12... | collective-permute-start | bytes 1769480 | tf_op jit(solution)/shard_map/ppermute | solution.py:41
  76.1 40.4 %collective-permute-start.7 = (bf16[72,4096]{1,0:T(8,128)(2,1)S(1)}, bf16[72,4096]{1,0:T(8,128)(2,1)S(1)}, u32[]{:S(2)}, u32[]{:S(2)}) collective-permute-start(bf16[72,4096]{1,0:T(8,128)(2,1)S(1)} %get-tuple-element.25), channel_id=1, source_target_pairs={{0,4},{2,6},{4,0},{6,2},{1,5},{3,7},{5,1},{7,3},{8,12},{10,14},{12... | collective-permute-start | bytes 1769480 | tf_op jit(solution)/shard_map/ppermute | solution.py:41
  77.7 38.8 %collective-permute-start.8 = (bf16[72,4096]{1,0:T(8,128)(2,1)S(1)}, bf16[72,4096]{1,0:T(8,128)(2,1)S(1)}, u32[]{:S(2)}, u32[]{:S(2)}) collective-permute-start(bf16[72,4096]{1,0:T(8,128)(2,1)S(1)} %get-tuple-element.24), channel_id=1, source_target_pairs={{0,6},{2,0},{4,2},{6,4},{1,7},{3,1},{5,3},{7,5},{8,14},{10,8},{12,... | collective-permute-start | bytes 1769480 | tf_op jit(solution)/shard_map/ppermute | solution.py:41
  88.8 28.0 %copy-start.3 = (f32[576,4096]{1,0:T(8,128)}, f32[576,4096]{1,0:T(8,128)S(1)}, u32[]{:S(2)}) copy-start(f32[576,4096]{1,0:T(8,128)S(1)} %fusion.63) | copy-start | bytes 28311556
  90.8 43.2 %collective-permute-start.5 = (bf16[4,72,4096]{2,1,0:T(8,128)(2,1)}, bf16[4,72,4096]{2,1,0:T(8,128)(2,1)}, u32[]{:S(2)}, u32[]{:S(2)}) collective-permute-start(bf16[4,72,4096]{2,1,0:T(8,128)(2,1)} %bitcast.18), channel_id=1, source_target_pairs={{0,1},{1,0},{2,3},{3,2},{4,5},{5,4},{6,7},{7,6},{8,9},{9,8},{10,11... | collective-permute-start | bytes 7077896 | tf_op jit(solution)/shard_map/ppermute | solution.py:36
  116.8 4.6 %collective-permute-start.9 = (bf16[4,72,4096]{2,1,0:T(8,128)(2,1)S(1)}, bf16[4,72,4096]{2,1,0:T(8,128)(2,1)S(1)}, u32[]{:S(2)}, u32[]{:S(2)}) collective-permute-start(bf16[4,72,4096]{2,1,0:T(8,128)(2,1)S(1)} %pad_maximum_fusion.1), channel_id=1, source_target_pairs={{0,1},{1,0},{2,3},{3,2},{4,5},{5,4},{6,7},{7,6},{8,9},{9,8},{10,11... | collective-permute-start | bytes 7077896 | tf_op jit(solution)/shard_map/ppermute | solution.py:36
  128.1 2.7 copy-start.10
  133.8 2.3 slice-start
  133.8 5.1 %collective-permute-start.10 = (bf16[4,72,4096]{2,1,0:T(8,128)(2,1)S(1)}, bf16[4,72,4096]{2,1,0:T(8,128)(2,1)S(1)}, u32[]{:S(2)}, u32[]{:S(2)}) collective-permute-start(bf16[4,72,4096]{2,1,0:T(8,128)(2,1)S(1)} %bitcast.128), channel_id=1, source_target_pairs={{0,1},{1,0},{2,3},{3,2},{4,5},{5,4},{6,7},{7,6},{8,9},{9,8},{10,11... | collective-permute-start | bytes 7077896 | tf_op jit(solution)/shard_map/ppermute | solution.py:36
  142.4 28.0 %collective-permute-start.11 = (bf16[72,4096]{1,0:T(8,128)(2,1)}, bf16[72,4096]{1,0:T(8,128)(2,1)S(1)}, u32[]{:S(2)}, u32[]{:S(2)}) collective-permute-start(bf16[72,4096]{1,0:T(8,128)(2,1)} %get-tuple-element.22), channel_id=1, source_target_pairs={{0,6},{2,0},{4,2},{6,4},{1,7},{3,1},{5,3},{7,5},{8,14},{10,8},{12,... | collective-permute-start | bytes 1769480 | tf_op jit(solution)/shard_map/ppermute | solution.py:41
  156.2 52.2 %collective-permute-start.12 = (bf16[72,4096]{1,0:T(8,128)(2,1)}, bf16[72,4096]{1,0:T(8,128)(2,1)S(1)}, u32[]{:S(2)}, u32[]{:S(2)}) collective-permute-start(bf16[72,4096]{1,0:T(8,128)(2,1)} %get-tuple-element.21), channel_id=1, source_target_pairs={{0,4},{2,6},{4,0},{6,2},{1,5},{3,7},{5,1},{7,3},{8,12},{10,14},{12... | collective-permute-start | bytes 1769480 | tf_op jit(solution)/shard_map/ppermute | solution.py:41
  156.9 51.5 %collective-permute-start.13 = (bf16[72,4096]{1,0:T(8,128)(2,1)}, bf16[72,4096]{1,0:T(8,128)(2,1)S(1)}, u32[]{:S(2)}, u32[]{:S(2)}) collective-permute-start(bf16[72,4096]{1,0:T(8,128)(2,1)} %get-tuple-element.20), channel_id=1, source_target_pairs={{0,2},{2,4},{4,6},{6,0},{1,3},{3,5},{5,7},{7,1},{8,10},{10,12},{12... | collective-permute-start | bytes 1769480 | tf_op jit(solution)/shard_map/ppermute | solution.py:41
  170.3 38.1 %copy-start.11 = (bf16[72,4096]{1,0:T(8,128)(2,1)}, bf16[72,4096]{1,0:T(8,128)(2,1)S(1)}, u32[]{:S(2)}) copy-start(bf16[72,4096]{1,0:T(8,128)(2,1)S(1)} %collective-permute-done.11) | copy-start | bytes 1769476
  208.4 0.8 copy-start.12
  208.4 1.0 copy-start.13
  211.1 1.7 copy-start.7
  212.8 5.1 %copy-start.2 = (bf16[1,128,4096]{2,1,0:T(8,128)(2,1)S(1)}, bf16[1,128,4096]{2,1,0:T(8,128)(2,1)}, u32[]{:S(2)}) copy-start(bf16[1,128,4096]{2,1,0:T(8,128)(2,1)} %param.9) | copy-start | bytes 3145732
  213.0 15.5 %collective-permute-start.15 = (bf16[72,4096]{1,0:T(8,128)(2,1)S(1)}, bf16[72,4096]{1,0:T(8,128)(2,1)S(1)}, u32[]{:S(2)}, u32[]{:S(2)}) collective-permute-start(bf16[72,4096]{1,0:T(8,128)(2,1)S(1)} %get-tuple-element.18), channel_id=1, source_target_pairs={{0,6},{2,0},{4,2},{6,4},{1,7},{3,1},{5,3},{7,5},{8,14},{10,8},{12,... | collective-permute-start | bytes 1769480 | tf_op jit(solution)/shard_map/ppermute | solution.py:41
  213.1 51.8 %collective-permute-start.16 = (bf16[72,4096]{1,0:T(8,128)(2,1)S(1)}, bf16[72,4096]{1,0:T(8,128)(2,1)S(1)}, u32[]{:S(2)}, u32[]{:S(2)}) collective-permute-start(bf16[72,4096]{1,0:T(8,128)(2,1)S(1)} %get-tuple-element.17), channel_id=1, source_target_pairs={{0,4},{2,6},{4,0},{6,2},{1,5},{3,7},{5,1},{7,3},{8,12},{10,14},{12... | collective-permute-start | bytes 1769480 | tf_op jit(solution)/shard_map/ppermute | solution.py:41
  214.3 50.6 %collective-permute-start.17 = (bf16[72,4096]{1,0:T(8,128)(2,1)S(1)}, bf16[72,4096]{1,0:T(8,128)(2,1)S(1)}, u32[]{:S(2)}, u32[]{:S(2)}) collective-permute-start(bf16[72,4096]{1,0:T(8,128)(2,1)S(1)} %get-tuple-element.16), channel_id=1, source_target_pairs={{0,2},{2,4},{4,6},{6,0},{1,3},{3,5},{5,7},{7,1},{8,10},{10,12},{12... | collective-permute-start | bytes 1769480 | tf_op jit(solution)/shard_map/ppermute | solution.py:41
  216.4 52.2 %collective-permute-start.19 = (bf16[2048,384]{1,0:T(8,128)(2,1)S(1)}, bf16[2048,384]{1,0:T(8,128)(2,1)S(1)}, u32[]{:S(2)}, u32[]{:S(2)}) collective-permute-start(bf16[2048,384]{1,0:T(8,128)(2,1)S(1)} %constant_dynamic-slice_fusion), channel_id=1, source_target_pairs={{0,8},{8,0},{1,9},{9,1},{2,10},{10,2},{3,11},{11,3},{4,12},{12,4},... | collective-permute-start | bytes 4718600 | tf_op jit(solution)/shard_map/ppermute | solution.py:66
  221.9 43.3 %copy-start.15 = (f32[1,4096]{1,0:T(1,128)S(1)}, f32[1,4096]{1,0:T(1,128)}, u32[]{:S(2)}) copy-start(f32[1,4096]{1,0:T(1,128)} %param.10) | copy-start | bytes 49156
  221.9 48.3 %collective-permute-start.14 = (bf16[1,128,4096]{2,1,0:T(8,128)(2,1)S(1)}, bf16[1,128,4096]{2,1,0:T(8,128)(2,1)S(1)}, u32[]{:S(2)}, u32[]{:S(2)}) collective-permute-start(bf16[1,128,4096]{2,1,0:T(8,128)(2,1)S(1)} %fusion.2), channel_id=1, source_target_pairs={{0,16},{1,17},{2,18},{3,19},{4,20},{5,21},{6,22},{7,23},{8,24},{9,... | collective-permute-start | bytes 3145736 | tf_op jit(solution)/shard_map/ppermute | solution.py:17
  265.2 1.2 copy-start.6
  267.3 25.7 %collective-permute-start.18 = (bf16[1,128,4096]{2,1,0:T(8,128)(2,1)S(1)}, bf16[1,128,4096]{2,1,0:T(8,128)(2,1)S(1)}, u32[]{:S(2)}, u32[]{:S(2)}) collective-permute-start(bf16[1,128,4096]{2,1,0:T(8,128)(2,1)S(1)} %fusion.21), channel_id=1, source_target_pairs={{16,0},{17,1},{18,2},{19,3},{20,4},{21,5},{22,6},{23,7},{24,8},{25... | collective-permute-start | bytes 3145736 | tf_op jit(solution)/shard_map/ppermute | solution.py:17
  268.6 25.4 %copy-start.1 = (bf16[1,4096,384]{2,1,0:T(8,128)(2,1)S(1)}, bf16[1,4096,384]{2,1,0:T(8,128)(2,1)}, u32[]{:S(2)}) copy-start(bf16[1,4096,384]{2,1,0:T(8,128)(2,1)} %param.13) | copy-start | bytes 9437188

commit v10 on v9

--- a/solution.py
+++ b/solution.py
@@ -43,8 +43,8 @@
 
 def to_experts(blocks):
     model_width = blocks.shape[2]
-    mine = jnp.stack([blocks[0]] + [shifted(blocks[k], k) for k in range(1, blocks.shape[0])])
-    both = jnp.concatenate([mine, swap_cores(mine)], axis=0)
+    received = [blocks[0]] + [shifted(blocks[k], k) for k in range(1, blocks.shape[0])]
+    both = jnp.stack(received + [swap_cores(block) for block in received])
     return both.reshape(-1, model_width)
 
 

time: 299 us -> 292 us (0.977)
  waiting for transfers between devices: 166 us -> 161 us
  other arithmetic: 16.9 us -> 13.6 us
    unnamed x49 -> x45, local copies, waits for them, and re-layouts: 10.1 us -> 10.2 us
  transfers between devices with their start and end apart: 20 -> 26, of which waited for: 10 -> 10; matrix products, arithmetic and copies ran while one was open for 19% -> 19% of each run, Pallas kernels for 0% -> 0%
where the time goes in v10:
time: 292 us; the launch traced here: 287 us
  waiting for transfers between devices  161 us (55%)
  starting transfers between devices  48.6 us (17%)
  matrix products  39.4 us (13%)
  local copies, waits for them, and re-layouts  23.3 us (8%)
  other arithmetic  13.6 us (5%)
    ppermute x12, waiting for transfers between devices, shifted(): lax.ppermute(value, 'chip', [(source, (source + steps) % count) for sourc...  137 us
    ppermute x12, starting transfers between devices, shifted(): lax.ppermute(value, 'chip', [(source, (source + steps) % count) for sourc...  38.8 us
    ppermute x2, waiting for transfers between devices, passed_along(): lax.ppermute(value, axis, [(source, source + steps) for source in range(l...  21.5 us
    unnamed x45, local copies, waits for them, and re-layouts  10.2 us
    dot_general x1, matrix products, per_device(): lax.dot_general(grad_rows, down_full, (((1,), (1,)), ((), ())), preferred...  7.26 us
  transfers between devices with their start and end apart: 26, of which 10 were waited for; matrix products, arithmetic and copies ran while one was open for 19% of the time, Pallas kernels for 0%

profile of v10, /device:TPU:0, one launch (start us, length us, event | category | flops | bytes accessed | tf_op | source)
XLA Modules:
  0.0 287.1 jit_solution(17343411354661304585)
XLA Ops:
  1.9 1.2 reduce-window.6
  3.9 1.5 fusion.14
  5.5 2.1 convolution_convert_fusion.1
  7.6 1.5 fusion.106
  9.0 3.1 %collective-permute-start = (bf16[72,4096]{1,0:T(8,128)(2,1)}, bf16[72,4096]{1,0:T(8,128)(2,1)}, u32[]{:S(2)}, u32[]{:S(2)}) collective-permute-start(bf16[72,4096]{1,0:T(8,128)(2,1)} %get-tuple-element.30), channel_id=1, source_target_pairs={{0,2},{2,4},{4,6},{6,0},{1,3},{3,5},{5,7},{7,1},{8,10},{10,12},{12... | collective-permute-start | bytes 1769480 | tf_op jit(solution)/shard_map/ppermute | solution.py:41
  12.1 2.6 collective-permute-start.1
  14.7 1.3 collective-permute-start.2
  16.0 1.5 collective-permute-start.7
  19.3 2.4 fusion
  22.1 1.8 constant_dynamic-update-slice_fusion.1
  23.9 4.9 %collective-permute-done = bf16[72,4096]{1,0:T(8,128)(2,1)} collective-permute-done((bf16[72,4096]{1,0:T(8,128)(2,1)}, bf16[72,4096]{1,0:T(8,128)(2,1)}, u32[]{:S(2)}, u32[]{:S(2)}) %collective-permute-start) | collective-permute-done | bytes 589856 | tf_op jit(solution)/shard_map/ppermute | solution.py:41
  28.8 1.1 bitcast_dynamic-update-slice_fusion.14
  29.9 23.3 %collective-permute-done.1 = bf16[72,4096]{1,0:T(8,128)(2,1)} collective-permute-done((bf16[72,4096]{1,0:T(8,128)(2,1)}, bf16[72,4096]{1,0:T(8,128)(2,1)}, u32[]{:S(2)}, u32[]{:S(2)}) %collective-permute-start.1) | collective-permute-done | bytes 589856 | tf_op jit(solution)/shard_map/ppermute | solution.py:41
  53.2 1.1 bitcast_dynamic-update-slice_fusion.13
  54.9 1.2 bitcast_dynamic-update-slice_fusion.12
  56.1 1.1 bitcast_dynamic-update-slice_fusion.11
  57.6 11.4 %collective-permute-start.9 = (bf16[72,4096]{1,0:T(8,128)(2,1)S(1)}, bf16[72,4096]{1,0:T(8,128)(2,1)S(1)}, u32[]{:S(2)}, u32[]{:S(2)}) collective-permute-start(bf16[72,4096]{1,0:T(8,128)(2,1)S(1)} %get-tuple-element.26), channel_id=1, source_target_pairs={{0,2},{2,4},{4,6},{6,0},{1,3},{3,5},{5,7},{7,1},{8,10},{10,12},{12... | collective-permute-start | bytes 1769480 | tf_op jit(solution)/shard_map/ppermute | solution.py:41
  69.0 3.4 %collective-permute-start.10 = (bf16[72,4096]{1,0:T(8,128)(2,1)S(1)}, bf16[72,4096]{1,0:T(8,128)(2,1)S(1)}, u32[]{:S(2)}, u32[]{:S(2)}) collective-permute-start(bf16[72,4096]{1,0:T(8,128)(2,1)S(1)} %get-tuple-element.25), channel_id=1, source_target_pairs={{0,4},{2,6},{4,0},{6,2},{1,5},{3,7},{5,1},{7,3},{8,12},{10,14},{12... | collective-permute-start | bytes 1769480 | tf_op jit(solution)/shard_map/ppermute | solution.py:41
  72.6 2.6 fusion.4
  75.2 2.6 fusion.8
  77.9 1.6 constant_dynamic-update-slice_fusion
  79.5 4.9 %fusion.63 = f32[576,4096]{1,0:T(8,128)S(1)} fusion(bf16[384,4096]{1,0:T(8,128)(2,1)S(1)} %constant_dynamic-update-slice_fusion, f32[384]{0:T(512)S(1)} %reduce.2, f32[384]{0:T(512)S(1)} %broadcast_multiply_fusion, f32[576,384]{1,0:T(8,128)S(1)} %fusion.4, f32[576,384]{1,0:T(8,128)S(1)} %fusion.8), kind=kOutput, calls=%fused_computation.129 | convolution fusion | flops 1827643392 | bytes 14355456 | tf_op jit(solution)/shard_map/dot_general | solution.py:129
  84.4 1.9 slice.152
  86.9 23.8 %collective-permute-done.10 = bf16[72,4096]{1,0:T(8,128)(2,1)S(1)} collective-permute-done((bf16[72,4096]{1,0:T(8,128)(2,1)S(1)}, bf16[72,4096]{1,0:T(8,128)(2,1)S(1)}, u32[]{:S(2)}, u32[]{:S(2)}) %collective-permute-start.10) | collective-permute-done | bytes 589856 | tf_op jit(solution)/shard_map/ppermute | solution.py:41
  111.5 1.2 collective-permute-done.14
  113.6 7.3 %multiply_convert_fusion = (bf16[576,384]{1,0:T(8,128)(2,1)}, f32[576,384]{1,0:T(8,128)S(1)}) fusion(f32[576,384]{1,0:T(8,128)S(1)} %fusion.8, f32[576,384]{1,0:T(8,128)S(1)} %fusion.4, f32[384]{0:T(512)S(1)} %broadcast_multiply_fusion, f32[384]{0:T(512)S(1)} %reduce.2, bf16[576,4096]{1,0:T(8,128)(2,1)S(1)} %bitcast.144, ...), kind=kOutput, calls=%fused_computation.92 | convolution fusion | flops 1840693248 | bytes 10963968 | tf_op jit(solution)/shard_map/dot_general | solution.py:143
  120.9 2.7 fusion.6
  123.6 3.7 %convolution_add_fusion = f32[576,4096]{1,0:T(8,128)S(1)} fusion(f32[576,4096]{1,0:T(8,128)S(1)} %fusion.6, bf16[576,384]{1,0:T(8,128)(2,1)} %get-tuple-element.35, bf16[1,4096,384]{2,1,0:T(8,128)(2,1)S(1)} %copy-done.8), kind=kOutput, calls=%fused_computation | convolution fusion | flops 1814298624 | bytes 22462464 | tf_op jit(solution)/shard_map/dot_general | solution.py:155
  127.8 3.1 %copy-done.2 = f32[576,4096]{1,0:T(8,128)} copy-done((f32[576,4096]{1,0:T(8,128)}, f32[576,4096]{1,0:T(8,128)S(1)}, u32[]{:S(2)}) %copy-start.2) | copy-done | bytes 9437208
  130.9 2.3 slice-done.1
  133.2 2.6 add_convert_fusion.1
  137.0 1.2 fusion.104
  138.3 12.5 %collective-permute-start.17 = (bf16[72,4096]{1,0:T(8,128)(2,1)}, bf16[72,4096]{1,0:T(8,128)(2,1)}, u32[]{:S(2)}, u32[]{:S(2)}) collective-permute-start(bf16[72,4096]{1,0:T(8,128)(2,1)} %get-tuple-element.22), channel_id=1, source_target_pairs={{0,6},{2,0},{4,2},{6,4},{1,7},{3,1},{5,3},{7,5},{8,14},{10,8},{12,... | collective-permute-start | bytes 1769480 | tf_op jit(solution)/shard_map/ppermute | solution.py:41
  150.8 1.2 collective-permute-start.18
  152.3 5.6 %convolution_convert_fusion = bf16[4096,384]{1,0:T(8,128)(2,1)S(1)} fusion(bf16[576,4096]{1,0:T(8,128)(2,1)} %bitcast.143, bf16[576,384]{1,0:T(8,128)(2,1)S(1)} %copy-done.9), kind=kOutput, calls=%fused_computation.1 | convolution fusion | flops 1813512192 | bytes 8306688 | tf_op jit(solution)/shard_map/dot_general | solution.py:189
  157.9 7.1 %collective-permute-done.17 = bf16[72,4096]{1,0:T(8,128)(2,1)} collective-permute-done((bf16[72,4096]{1,0:T(8,128)(2,1)}, bf16[72,4096]{1,0:T(8,128)(2,1)}, u32[]{:S(2)}, u32[]{:S(2)}) %collective-permute-start.17) | collective-permute-done | bytes 589856 | tf_op jit(solution)/shard_map/ppermute | solution.py:41
  165.0 38.7 %collective-permute-done.18 = bf16[72,4096]{1,0:T(8,128)(2,1)} collective-permute-done((bf16[72,4096]{1,0:T(8,128)(2,1)}, bf16[72,4096]{1,0:T(8,128)(2,1)}, u32[]{:S(2)}, u32[]{:S(2)}) %collective-permute-start.18) | collective-permute-done | bytes 589856 | tf_op jit(solution)/shard_map/ppermute | solution.py:41
  203.6 1.7 pad_maximum_fusion
  207.3 1.9 collective-permute-start.23
  209.4 1.6 collective-permute-start.25
  211.0 4.0 %fusion.2 = bf16[1,128,4096]{2,1,0:T(8,128)(2,1)S(1)} fusion(f32[288,4096]{1,0:T(8,128)S(1)} %bitcast_convert_fusion, bf16[1,128,4096]{2,1,0:T(8,128)(2,1)S(1)} %copy-done.3, f32[128]{0:T(128)S(1)} %get-tuple-element.31, s32[128]{0:T(128)S(1)} %get-tuple-element.14, f32[128]{0:T(128)S(1)} %get-tuple-element.32, s32[128]{0:T(128)S(1)} %get-tuple-element.13), kind=kOutput, calls=%fused_computation.12 | convolution fusion | flops 1813696512 | bytes 6817792 | tf_op jit(solution)/shard_map/dot_general | solution.py:167
  215.0 3.5 %collective-permute-start.20 = (bf16[1,128,4096]{2,1,0:T(8,128)(2,1)S(1)}, bf16[1,128,4096]{2,1,0:T(8,128)(2,1)S(1)}, u32[]{:S(2)}, u32[]{:S(2)}) collective-permute-start(bf16[1,128,4096]{2,1,0:T(8,128)(2,1)S(1)} %fusion.2), channel_id=1, source_target_pairs={{0,16},{1,17},{2,18},{3,19},{4,20},{5,21},{6,22},{7,23},{8,24},{9,... | collective-permute-start | bytes 3145736 | tf_op jit(solution)/shard_map/ppermute | solution.py:17
  218.5 3.6 %collective-permute-done.21 = bf16[72,4096]{1,0:T(8,128)(2,1)S(1)} collective-permute-done((bf16[72,4096]{1,0:T(8,128)(2,1)S(1)}, bf16[72,4096]{1,0:T(8,128)(2,1)S(1)}, u32[]{:S(2)}, u32[]{:S(2)}) %collective-permute-start.21) | collective-permute-done | bytes 589856 | tf_op jit(solution)/shard_map/ppermute | solution.py:41
  222.0 35.7 %collective-permute-done.22 = bf16[72,4096]{1,0:T(8,128)(2,1)S(1)} collective-permute-done((bf16[72,4096]{1,0:T(8,128)(2,1)S(1)}, bf16[72,4096]{1,0:T(8,128)(2,1)S(1)}, u32[]{:S(2)}, u32[]{:S(2)}) %collective-permute-start.22) | collective-permute-done | bytes 589856 | tf_op jit(solution)/shard_map/ppermute | solution.py:41
  260.1 1.3 collective-permute-start.24
  261.4 1.6 fusion.19
  263.1 1.0 broadcast_select_fusion.1
  264.1 21.5 %collective-permute-done.24 = bf16[1,128,4096]{2,1,0:T(8,128)(2,1)S(1)} collective-permute-done((bf16[1,128,4096]{2,1,0:T(8,128)(2,1)S(1)}, bf16[1,128,4096]{2,1,0:T(8,128)(2,1)S(1)}, u32[]{:S(2)}, u32[]{:S(2)}) %collective-permute-start.24) | collective-permute-done | bytes 1048608 | tf_op jit(solution)/shard_map/ppermute | solution.py:17
  (109 shorter events, 14.9 us)
Async XLA Ops:
  0.6 74.6 %copy-start = (bf16[1,4096,384]{2,1,0:T(8,128)(2,1)S(1)}, bf16[1,4096,384]{2,1,0:T(8,128)(2,1)}, u32[]{:S(2)}) copy-start(bf16[1,4096,384]{2,1,0:T(8,128)(2,1)} %param.13) | copy-start | bytes 9437188
  7.6 10.8 %copy-start.14 = (f32[1,128,2]{1,2,0:T(2,128)S(1)}, f32[1,128,2]{1,2,0:T(2,128)}, u32[]{:S(2)}) copy-start(f32[1,128,2]{1,2,0:T(2,128)} %param.12) | copy-start | bytes 3076
  7.6 10.8 %copy-start.6 = (bf16[1,128,4096]{2,1,0:T(8,128)(2,1)S(1)}, bf16[1,128,4096]{2,1,0:T(8,128)(2,1)}, u32[]{:S(2)}) copy-start(bf16[1,128,4096]{2,1,0:T(8,128)(2,1)} %param.17) | copy-start | bytes 3145732
  9.0 19.7 %collective-permute-start = (bf16[72,4096]{1,0:T(8,128)(2,1)}, bf16[72,4096]{1,0:T(8,128)(2,1)}, u32[]{:S(2)}, u32[]{:S(2)}) collective-permute-start(bf16[72,4096]{1,0:T(8,128)(2,1)} %get-tuple-element.30), channel_id=1, source_target_pairs={{0,2},{2,4},{4,6},{6,0},{1,3},{3,5},{5,7},{7,1},{8,10},{10,12},{12... | collective-permute-start | bytes 1769480 | tf_op jit(solution)/shard_map/ppermute | solution.py:41
  12.1 41.1 %collective-permute-start.1 = (bf16[72,4096]{1,0:T(8,128)(2,1)}, bf16[72,4096]{1,0:T(8,128)(2,1)}, u32[]{:S(2)}, u32[]{:S(2)}) collective-permute-start(bf16[72,4096]{1,0:T(8,128)(2,1)} %get-tuple-element.29), channel_id=1, source_target_pairs={{0,4},{2,6},{4,0},{6,2},{1,5},{3,7},{5,1},{7,3},{8,12},{10,14},{12... | collective-permute-start | bytes 1769480 | tf_op jit(solution)/shard_map/ppermute | solution.py:41
  14.7 39.6 %collective-permute-start.2 = (bf16[72,4096]{1,0:T(8,128)(2,1)}, bf16[72,4096]{1,0:T(8,128)(2,1)}, u32[]{:S(2)}, u32[]{:S(2)}) collective-permute-start(bf16[72,4096]{1,0:T(8,128)(2,1)} %get-tuple-element.28), channel_id=1, source_target_pairs={{0,6},{2,0},{4,2},{6,4},{1,7},{3,1},{5,3},{7,5},{8,14},{10,8},{12,... | collective-permute-start | bytes 1769480 | tf_op jit(solution)/shard_map/ppermute | solution.py:41
  16.0 40.1 %collective-permute-start.3 = (bf16[72,4096]{1,0:T(8,128)(2,1)}, bf16[72,4096]{1,0:T(8,128)(2,1)}, u32[]{:S(2)}, u32[]{:S(2)}) collective-permute-start(bf16[72,4096]{1,0:T(8,128)(2,1)} %get-tuple-element.27), channel_id=1, source_target_pairs={{0,1},{1,0},{2,3},{3,2},{4,5},{5,4},{6,7},{7,6},{8,9},{9,8},{10,11... | collective-permute-start | bytes 1769480 | tf_op jit(solution)/shard_map/ppermute | solution.py:36
  16.0 61.8 %collective-permute-start.7 = (bf16[384,2048]{1,0:T(8,128)(2,1)}, bf16[384,2048]{1,0:T(8,128)(2,1)}, u32[]{:S(2)}, u32[]{:S(2)}) collective-permute-start(bf16[384,2048]{1,0:T(8,128)(2,1)} %bitcast.20), channel_id=1, source_target_pairs={{0,8},{8,0},{1,9},{9,1},{2,10},{10,2},{3,11},{11,3},{4,12},{12,4},... | collective-permute-start | bytes 4718600 | tf_op jit(solution)/shard_map/ppermute | solution.py:66
  19.3 2.4 copy-start.13
  21.7 7.1 %copy-start.10 = (bf16[8,72,4096]{2,1,0:T(8,128)(2,1)S(1)}, bf16[8,72,4096]{2,1,0:T(8,128)(2,1)}, u32[]{:S(2)}) copy-start(bf16[8,72,4096]{2,1,0:T(8,128)(2,1)} %bitcast_dynamic-update-slice_fusion.15) | copy-start | bytes 14155780
  28.8 28.5 %collective-permute-start.4 = (bf16[72,4096]{1,0:T(8,128)(2,1)}, bf16[72,4096]{1,0:T(8,128)(2,1)S(1)}, u32[]{:S(2)}, u32[]{:S(2)}) collective-permute-start(bf16[72,4096]{1,0:T(8,128)(2,1)} %collective-permute-done), channel_id=1, source_target_pairs={{0,1},{1,0},{2,3},{3,2},{4,5},{5,4},{6,7},{7,6},{8,9},{9,8},{10,11... | collective-permute-start | bytes 1769480 | tf_op jit(solution)/shard_map/ppermute | solution.py:36
  53.2 4.1 %collective-permute-start.5 = (bf16[72,4096]{1,0:T(8,128)(2,1)}, bf16[72,4096]{1,0:T(8,128)(2,1)S(1)}, u32[]{:S(2)}, u32[]{:S(2)}) collective-permute-start(bf16[72,4096]{1,0:T(8,128)(2,1)} %collective-permute-done.1), channel_id=1, source_target_pairs={{0,1},{1,0},{2,3},{3,2},{4,5},{5,4},{6,7},{7,6},{8,9},{9,8},{10,11... | collective-permute-start | bytes 1769480 | tf_op jit(solution)/shard_map/ppermute | solution.py:36
  54.3 3.1 %copy-start.5 = (bf16[288,4096]{1,0:T(8,128)(2,1)S(1)}, bf16[288,4096]{1,0:T(8,128)(2,1)}, u32[]{:S(2)}) copy-start(bf16[288,4096]{1,0:T(8,128)(2,1)} %fusion) | copy-start | bytes 7077892
  54.3 3.0 %collective-permute-start.6 = (bf16[72,4096]{1,0:T(8,128)(2,1)}, bf16[72,4096]{1,0:T(8,128)(2,1)S(1)}, u32[]{:S(2)}, u32[]{:S(2)}) collective-permute-start(bf16[72,4096]{1,0:T(8,128)(2,1)} %collective-permute-done.2), channel_id=1, source_target_pairs={{0,1},{1,0},{2,3},{3,2},{4,5},{5,4},{6,7},{7,6},{8,9},{9,8},{10,11... | collective-permute-start | bytes 1769480 | tf_op jit(solution)/shard_map/ppermute | solution.py:36
  57.3 15.2 %copy-start.8 = (bf16[1,4096,384]{2,1,0:T(8,128)(2,1)S(1)}, bf16[1,4096,384]{2,1,0:T(8,128)(2,1)}, u32[]{:S(2)}) copy-start(bf16[1,4096,384]{2,1,0:T(8,128)(2,1)} %param.14) | copy-start | bytes 9437188
  57.4 17.8 %copy-start.11 = (bf16[8,72,4096]{2,1,0:T(8,128)(2,1)}, bf16[8,72,4096]{2,1,0:T(8,128)(2,1)S(1)}, u32[]{:S(2)}) copy-start(bf16[8,72,4096]{2,1,0:T(8,128)(2,1)S(1)} %bitcast_dynamic-update-slice_fusion.8) | copy-start | bytes 14155780
  57.6 29.2 %collective-permute-start.9 = (bf16[72,4096]{1,0:T(8,128)(2,1)S(1)}, bf16[72,4096]{1,0:T(8,128)(2,1)S(1)}, u32[]{:S(2)}, u32[]{:S(2)}) collective-permute-start(bf16[72,4096]{1,0:T(8,128)(2,1)S(1)} %get-tuple-element.26), channel_id=1, source_target_pairs={{0,2},{2,4},{4,6},{6,0},{1,3},{3,5},{5,7},{7,1},{8,10},{10,12},{12... | collective-permute-start | bytes 1769480 | tf_op jit(solution)/shard_map/ppermute | solution.py:41
  69.0 41.7 %collective-permute-start.10 = (bf16[72,4096]{1,0:T(8,128)(2,1)S(1)}, bf16[72,4096]{1,0:T(8,128)(2,1)S(1)}, u32[]{:S(2)}, u32[]{:S(2)}) collective-permute-start(bf16[72,4096]{1,0:T(8,128)(2,1)S(1)} %get-tuple-element.25), channel_id=1, source_target_pairs={{0,4},{2,6},{4,0},{6,2},{1,5},{3,7},{5,1},{7,3},{8,12},{10,14},{12... | collective-permute-start | bytes 1769480 | tf_op jit(solution)/shard_map/ppermute | solution.py:41
  72.3 38.4 %collective-permute-start.11 = (bf16[72,4096]{1,0:T(8,128)(2,1)S(1)}, bf16[72,4096]{1,0:T(8,128)(2,1)S(1)}, u32[]{:S(2)}, u32[]{:S(2)}) collective-permute-start(bf16[72,4096]{1,0:T(8,128)(2,1)S(1)} %get-tuple-element.24), channel_id=1, source_target_pairs={{0,6},{2,0},{4,2},{6,4},{1,7},{3,1},{5,3},{7,5},{8,14},{10,8},{12,... | collective-permute-start | bytes 1769480 | tf_op jit(solution)/shard_map/ppermute | solution.py:41
  72.5 38.9 %collective-permute-start.12 = (bf16[72,4096]{1,0:T(8,128)(2,1)S(1)}, bf16[72,4096]{1,0:T(8,128)(2,1)S(1)}, u32[]{:S(2)}, u32[]{:S(2)}) collective-permute-start(bf16[72,4096]{1,0:T(8,128)(2,1)S(1)} %get-tuple-element.23), channel_id=1, source_target_pairs={{0,1},{1,0},{2,3},{3,2},{4,5},{5,4},{6,7},{7,6},{8,9},{9,8},{10,11... | collective-permute-start | bytes 1769480 | tf_op jit(solution)/shard_map/ppermute | solution.py:36
  84.4 36.5 %copy-start.4 = (f32[576,4096]{1,0:T(8,128)}, f32[576,4096]{1,0:T(8,128)S(1)}, u32[]{:S(2)}) copy-start(f32[576,4096]{1,0:T(8,128)S(1)} %fusion.63) | copy-start | bytes 28311556
  86.3 44.6 %collective-permute-start.8 = (bf16[4,72,4096]{2,1,0:T(8,128)(2,1)}, bf16[4,72,4096]{2,1,0:T(8,128)(2,1)}, u32[]{:S(2)}, u32[]{:S(2)}) collective-permute-start(bf16[4,72,4096]{2,1,0:T(8,128)(2,1)} %bitcast.22), channel_id=1, source_target_pairs={{0,1},{1,0},{2,3},{3,2},{4,5},{5,4},{6,7},{7,6},{8,9},{9,8},{10,11... | collective-permute-start | bytes 7077896 | tf_op jit(solution)/shard_map/ppermute | solution.py:36
  86.8 24.6 %collective-permute-start.13 = (bf16[72,4096]{1,0:T(8,128)(2,1)S(1)}, bf16[72,4096]{1,0:T(8,128)(2,1)S(1)}, u32[]{:S(2)}, u32[]{:S(2)}) collective-permute-start(bf16[72,4096]{1,0:T(8,128)(2,1)S(1)} %collective-permute-done.9), channel_id=1, source_target_pairs={{0,1},{1,0},{2,3},{3,2},{4,5},{5,4},{6,7},{7,6},{8,9},{9,8},{10,11... | collective-permute-start | bytes 1769480 | tf_op jit(solution)/shard_map/ppermute | solution.py:36
  110.7 2.0 collective-permute-start.14
  110.8 2.8 collective-permute-start.15
  127.3 3.6 %copy-start.2 = (f32[576,4096]{1,0:T(8,128)}, f32[576,4096]{1,0:T(8,128)S(1)}, u32[]{:S(2)}) copy-start(f32[576,4096]{1,0:T(8,128)S(1)} %convolution_add_fusion) | copy-start | bytes 28311556
  127.6 8.2 %collective-permute-start.16 = (bf16[4,72,4096]{2,1,0:T(8,128)(2,1)S(1)}, bf16[4,72,4096]{2,1,0:T(8,128)(2,1)S(1)}, u32[]{:S(2)}, u32[]{:S(2)}) collective-permute-start(bf16[4,72,4096]{2,1,0:T(8,128)(2,1)S(1)} %bitcast.137), channel_id=1, source_target_pairs={{0,1},{1,0},{2,3},{3,2},{4,5},{5,4},{6,7},{7,6},{8,9},{9,8},{10,11... | collective-permute-start | bytes 7077896 | tf_op jit(solution)/shard_map/ppermute | solution.py:36
  130.9 2.3 slice-start.1
  133.2 3.0 %slice-start = ((f32[576,4096]{1,0:T(8,128)}), f32[288,4096]{1,0:T(8,128)S(1)}, s32[]{:S(2)}) async-start(f32[576,4096]{1,0:T(8,128)} %copy-done.2), calls=%async_computation | async-start | bytes 9437184 | tf_op jit(solution)/shard_map/slice | solution.py:55
  137.0 15.3 %copy-start.9 = (bf16[576,384]{1,0:T(8,128)(2,1)S(1)}, bf16[576,384]{1,0:T(8,128)(2,1)}, u32[]{:S(2)}) copy-start(bf16[576,384]{1,0:T(8,128)(2,1)} %get-tuple-element.35) | copy-start | bytes 1327108
  138.3 26.7 %collective-permute-start.17 = (bf16[72,4096]{1,0:T(8,128)(2,1)}, bf16[72,4096]{1,0:T(8,128)(2,1)}, u32[]{:S(2)}, u32[]{:S(2)}) collective-permute-start(bf16[72,4096]{1,0:T(8,128)(2,1)} %get-tuple-element.22), channel_id=1, source_target_pairs={{0,6},{2,0},{4,2},{6,4},{1,7},{3,1},{5,3},{7,5},{8,14},{10,8},{12,... | collective-permute-start | bytes 1769480 | tf_op jit(solution)/shard_map/ppermute | solution.py:41
  150.8 52.8 %collective-permute-start.18 = (bf16[72,4096]{1,0:T(8,128)(2,1)}, bf16[72,4096]{1,0:T(8,128)(2,1)}, u32[]{:S(2)}, u32[]{:S(2)}) collective-permute-start(bf16[72,4096]{1,0:T(8,128)(2,1)} %get-tuple-element.21), channel_id=1, source_target_pairs={{0,4},{2,6},{4,0},{6,2},{1,5},{3,7},{5,1},{7,3},{8,12},{10,14},{12... | collective-permute-start | bytes 1769480 | tf_op jit(solution)/shard_map/ppermute | solution.py:41
  152.0 51.6 %collective-permute-start.19 = (bf16[72,4096]{1,0:T(8,128)(2,1)}, bf16[72,4096]{1,0:T(8,128)(2,1)}, u32[]{:S(2)}, u32[]{:S(2)}) collective-permute-start(bf16[72,4096]{1,0:T(8,128)(2,1)} %get-tuple-element.20), channel_id=1, source_target_pairs={{0,2},{2,4},{4,6},{6,0},{1,3},{3,5},{5,7},{7,1},{8,10},{10,12},{12... | collective-permute-start | bytes 1769480 | tf_op jit(solution)/shard_map/ppermute | solution.py:41
  206.0 4.9 %copy-start.3 = (bf16[1,128,4096]{2,1,0:T(8,128)(2,1)S(1)}, bf16[1,128,4096]{2,1,0:T(8,128)(2,1)}, u32[]{:S(2)}) copy-start(bf16[1,128,4096]{2,1,0:T(8,128)(2,1)} %param.9) | copy-start | bytes 3145732
  206.3 15.7 %collective-permute-start.21 = (bf16[72,4096]{1,0:T(8,128)(2,1)S(1)}, bf16[72,4096]{1,0:T(8,128)(2,1)S(1)}, u32[]{:S(2)}, u32[]{:S(2)}) collective-permute-start(bf16[72,4096]{1,0:T(8,128)(2,1)S(1)} %get-tuple-element.18), channel_id=1, source_target_pairs={{0,6},{2,0},{4,2},{6,4},{1,7},{3,1},{5,3},{7,5},{8,14},{10,8},{12,... | collective-permute-start | bytes 1769480 | tf_op jit(solution)/shard_map/ppermute | solution.py:41
  206.4 51.4 %collective-permute-start.22 = (bf16[72,4096]{1,0:T(8,128)(2,1)S(1)}, bf16[72,4096]{1,0:T(8,128)(2,1)S(1)}, u32[]{:S(2)}, u32[]{:S(2)}) collective-permute-start(bf16[72,4096]{1,0:T(8,128)(2,1)S(1)} %get-tuple-element.17), channel_id=1, source_target_pairs={{0,4},{2,6},{4,0},{6,2},{1,5},{3,7},{5,1},{7,3},{8,12},{10,14},{12... | collective-permute-start | bytes 1769480 | tf_op jit(solution)/shard_map/ppermute | solution.py:41
  207.3 50.5 %collective-permute-start.23 = (bf16[72,4096]{1,0:T(8,128)(2,1)S(1)}, bf16[72,4096]{1,0:T(8,128)(2,1)S(1)}, u32[]{:S(2)}, u32[]{:S(2)}) collective-permute-start(bf16[72,4096]{1,0:T(8,128)(2,1)S(1)} %get-tuple-element.16), channel_id=1, source_target_pairs={{0,2},{2,4},{4,6},{6,0},{1,3},{3,5},{5,7},{7,1},{8,10},{10,12},{12... | collective-permute-start | bytes 1769480 | tf_op jit(solution)/shard_map/ppermute | solution.py:41
  209.4 52.0 %collective-permute-start.25 = (bf16[2048,384]{1,0:T(8,128)(2,1)S(1)}, bf16[2048,384]{1,0:T(8,128)(2,1)S(1)}, u32[]{:S(2)}, u32[]{:S(2)}) collective-permute-start(bf16[2048,384]{1,0:T(8,128)(2,1)S(1)} %constant_dynamic-slice_fusion), channel_id=1, source_target_pairs={{0,8},{8,0},{1,9},{9,1},{2,10},{10,2},{3,11},{11,3},{4,12},{12,4},... | collective-permute-start | bytes 4718600 | tf_op jit(solution)/shard_map/ppermute | solution.py:66
  214.9 43.1 %copy-start.12 = (f32[1,4096]{1,0:T(1,128)S(1)}, f32[1,4096]{1,0:T(1,128)}, u32[]{:S(2)}) copy-start(f32[1,4096]{1,0:T(1,128)} %param.10) | copy-start | bytes 49156
  215.0 48.1 %collective-permute-start.20 = (bf16[1,128,4096]{2,1,0:T(8,128)(2,1)S(1)}, bf16[1,128,4096]{2,1,0:T(8,128)(2,1)S(1)}, u32[]{:S(2)}, u32[]{:S(2)}) collective-permute-start(bf16[1,128,4096]{2,1,0:T(8,128)(2,1)S(1)} %fusion.2), channel_id=1, source_target_pairs={{0,16},{1,17},{2,18},{3,19},{4,20},{5,21},{6,22},{7,23},{8,24},{9,... | collective-permute-start | bytes 3145736 | tf_op jit(solution)/shard_map/ppermute | solution.py:17
  258.0 1.2 copy-start.7
  260.1 25.5 %collective-permute-start.24 = (bf16[1,128,4096]{2,1,0:T(8,128)(2,1)S(1)}, bf16[1,128,4096]{2,1,0:T(8,128)(2,1)S(1)}, u32[]{:S(2)}, u32[]{:S(2)}) collective-permute-start(bf16[1,128,4096]{2,1,0:T(8,128)(2,1)S(1)} %fusion.21), channel_id=1, source_target_pairs={{16,0},{17,1},{18,2},{19,3},{20,4},{21,5},{22,6},{23,7},{24,8},{25... | collective-permute-start | bytes 3145736 | tf_op jit(solution)/shard_map/ppermute | solution.py:17
  261.4 25.2 %copy-start.1 = (bf16[1,4096,384]{2,1,0:T(8,128)(2,1)S(1)}, bf16[1,4096,384]{2,1,0:T(8,128)(2,1)}, u32[]{:S(2)}) copy-start(bf16[1,4096,384]{2,1,0:T(8,128)(2,1)} %param.13) | copy-start | bytes 9437188

commit v11 on v10

--- a/solution.py
+++ b/solution.py
@@ -51,12 +51,15 @@
 def combine_cores(partials, experts, capacity):
     model_width = partials.shape[1]
     paired = partials.reshape(2, experts, capacity, model_width)
-    other = swap_cores(paired[1].astype(jnp.bfloat16))
-    return (paired[0] + other.astype(jnp.float32)).astype(jnp.bfloat16)
+    return [
+        (paired[0, k] + swap_cores(paired[1, k].astype(jnp.bfloat16)).astype(jnp.float32)).astype(jnp.bfloat16)
+        for k in range(experts)
+    ]
 
 
 def from_experts(summed):
-    experts, capacity, model_width = summed.shape
+    experts = len(summed)
+    capacity, model_width = summed[0].shape
     returned = jnp.stack([summed[0]] + [shifted(summed[k], -k) for k in range(1, experts)])
     return returned.reshape(experts * capacity, model_width).astype(jnp.float32)
 

time: 292 us -> 301 us (1.031)
  other arithmetic: 13.6 us -> 17.7 us
  matrix products: 39.4 us -> 42.9 us
  local copies, waits for them, and re-layouts: 23.3 us -> 26.6 us
    unnamed x45 -> x59, local copies, waits for them, and re-layouts: 10.2 us -> 17.1 us
    slice x10 -> x2, local copies, waits for them, and re-layouts: 6.71 us -> 0.18 us  [the longest x4 2.8 us: combine_cores(): return (paired[0] + other.astype(jnp.float32)).astype(jnp.bfloat16)]
    ppermute x12, waiting for transfers between devices: 137 us -> 131 us  [shifted(): lax.ppermute(value, 'chip', [(source, (source + steps) % count) for sourc...]
    ppermute x10 -> x16, waiting for transfers between devices: 2.03 us -> 5.19 us  [swap_cores(): return lax.ppermute(value, 'core', [(0, 1), (1, 0)])]
  transfers between devices with their start and end apart: 26 -> 32, of which waited for: 10 -> 11; matrix products, arithmetic and copies ran while one was open for 19% -> 23% of each run, Pallas kernels for 0% -> 0%
where the time goes in v11:
time: 301 us; the launch traced here: 296 us
  waiting for transfers between devices  158 us (52%)
  starting transfers between devices  49.7 us (17%)
  matrix products  42.9 us (14%)
  local copies, waits for them, and re-layouts  26.6 us (9%)
  other arithmetic  17.7 us (6%)
    ppermute x12, waiting for transfers between devices, shifted(): lax.ppermute(value, 'chip', [(source, (source + steps) % count) for sourc...  131 us
    ppermute x12, starting transfers between devices, shifted(): lax.ppermute(value, 'chip', [(source, (source + steps) % count) for sourc...  38.7 us
    ppermute x2, waiting for transfers between devices, passed_along(): lax.ppermute(value, axis, [(source, source + steps) for source in range(l...  21.7 us
    unnamed x59, local copies, waits for them, and re-layouts  17.1 us
    dot_general x1, matrix products, per_device(): lax.dot_general(grad_rows, down_full, (((1,), (1,)), ((), ())), preferred...  6.51 us
    convert_element_type x2, other arithmetic, combine_cores(): (paired[0, k] + swap_cores(paired[1, k].astype(jnp.bfloat16)).astype(jnp....  6.1 us
  transfers between devices with their start and end apart: 32, of which 11 were waited for; matrix products, arithmetic and copies ran while one was open for 23% of the time, Pallas kernels for 0%

profile of v11, /device:TPU:0, one launch (start us, length us, event | category | flops | bytes accessed | tf_op | source)
XLA Modules:
  0.0 296.5 jit_solution(10538230144194181051)
XLA Ops:
  1.9 1.2 reduce-window.6
  3.9 1.5 fusion.14
  5.5 2.1 convolution_convert_fusion.1
  7.6 1.4 fusion.120
  9.0 3.1 %collective-permute-start = (bf16[72,4096]{1,0:T(8,128)(2,1)}, bf16[72,4096]{1,0:T(8,128)(2,1)}, u32[]{:S(2)}, u32[]{:S(2)}) collective-permute-start(bf16[72,4096]{1,0:T(8,128)(2,1)} %get-tuple-element.56), channel_id=1, source_target_pairs={{0,2},{2,4},{4,6},{6,0},{1,3},{3,5},{5,7},{7,1},{8,10},{10,12},{12... | collective-permute-start | bytes 1769480 | tf_op jit(solution)/shard_map/ppermute | solution.py:41
  12.1 2.6 collective-permute-start.1
  14.7 1.3 collective-permute-start.2
  16.0 1.5 collective-permute-start.7
  19.2 2.4 fusion
  22.0 1.8 constant_dynamic-update-slice_fusion.1
  23.9 4.9 %collective-permute-done = bf16[72,4096]{1,0:T(8,128)(2,1)} collective-permute-done((bf16[72,4096]{1,0:T(8,128)(2,1)}, bf16[72,4096]{1,0:T(8,128)(2,1)}, u32[]{:S(2)}, u32[]{:S(2)}) %collective-permute-start) | collective-permute-done | bytes 589856 | tf_op jit(solution)/shard_map/ppermute | solution.py:41
  29.8 23.3 %collective-permute-done.1 = bf16[72,4096]{1,0:T(8,128)(2,1)} collective-permute-done((bf16[72,4096]{1,0:T(8,128)(2,1)}, bf16[72,4096]{1,0:T(8,128)(2,1)}, u32[]{:S(2)}, u32[]{:S(2)}) %collective-permute-start.1) | collective-permute-done | bytes 589856 | tf_op jit(solution)/shard_map/ppermute | solution.py:41
  54.9 1.2 bitcast_dynamic-update-slice_fusion.12
  56.1 1.1 bitcast_dynamic-update-slice_fusion.11
  57.4 1.4 fusion.119
  58.8 11.3 %collective-permute-start.12 = (bf16[72,4096]{1,0:T(8,128)(2,1)}, bf16[72,4096]{1,0:T(8,128)(2,1)}, u32[]{:S(2)}, u32[]{:S(2)}) collective-permute-start(bf16[72,4096]{1,0:T(8,128)(2,1)} %get-tuple-element.52), channel_id=1, source_target_pairs={{0,2},{2,4},{4,6},{6,0},{1,3},{3,5},{5,7},{7,1},{8,10},{10,12},{12... | collective-permute-start | bytes 1769480 | tf_op jit(solution)/shard_map/ppermute | solution.py:41
  70.2 3.4 %collective-permute-start.13 = (bf16[72,4096]{1,0:T(8,128)(2,1)}, bf16[72,4096]{1,0:T(8,128)(2,1)}, u32[]{:S(2)}, u32[]{:S(2)}) collective-permute-start(bf16[72,4096]{1,0:T(8,128)(2,1)} %get-tuple-element.51), channel_id=1, source_target_pairs={{0,4},{2,6},{4,0},{6,2},{1,5},{3,7},{5,1},{7,3},{8,12},{10,14},{12... | collective-permute-start | bytes 1769480 | tf_op jit(solution)/shard_map/ppermute | solution.py:41
  73.8 2.6 fusion.4
  76.4 2.6 fusion.8
  79.9 1.6 constant_dynamic-update-slice_fusion
  81.5 4.9 %fusion.79 = f32[576,4096]{1,0:T(8,128)S(1)} fusion(bf16[384,4096]{1,0:T(8,128)(2,1)S(1)} %constant_dynamic-update-slice_fusion, f32[384]{0:T(512)S(1)} %reduce.2, f32[384]{0:T(512)S(1)} %broadcast_multiply_fusion, f32[576,384]{1,0:T(8,128)S(1)} %fusion.4, f32[576,384]{1,0:T(8,128)S(1)} %fusion.8), kind=kOutput, calls=%fused_computation.151 | convolution fusion | flops 1827643392 | bytes 14355456 | tf_op jit(solution)/shard_map/dot_general | solution.py:132
  87.2 2.9 copy-done.2
  90.1 1.4 slice_bitcast_fusion.12
  92.0 1.2 copy-done.18
  94.3 17.9 %collective-permute-done.13 = bf16[72,4096]{1,0:T(8,128)(2,1)} collective-permute-done((bf16[72,4096]{1,0:T(8,128)(2,1)}, bf16[72,4096]{1,0:T(8,128)(2,1)}, u32[]{:S(2)}, u32[]{:S(2)}) %collective-permute-start.13) | collective-permute-done | bytes 589856 | tf_op jit(solution)/shard_map/ppermute | solution.py:41
  113.9 1.4 bitcast_dynamic-update-slice_fusion.4
  117.8 2.0 collective-permute-done.17
  120.0 2.0 collective-permute-done.18
  122.1 6.5 %multiply_convert_fusion = (bf16[576,384]{1,0:T(8,128)(2,1)S(1)}, f32[576,384]{1,0:T(8,128)S(1)}) fusion(f32[576,384]{1,0:T(8,128)S(1)} %fusion.8, f32[576,384]{1,0:T(8,128)S(1)} %fusion.4, f32[384]{0:T(512)S(1)} %broadcast_multiply_fusion, f32[384]{0:T(512)S(1)} %reduce.2, bf16[576,4096]{1,0:T(8,128)(2,1)S(1)} %bitcast.199, ...), kind=kOutput, calls=%fused_computation.112 | convolution fusion | flops 1840693248 | bytes 10963968 | tf_op jit(solution)/shard_map/dot_general | solution.py:146
  128.6 5.3 %fusion.6 = f32[576,4096]{1,0:T(8,128)} fusion(bf16[1,4096,384]{2,1,0:T(8,128)(2,1)S(1)} %copy-done, f32[576,384]{1,0:T(8,128)S(1)} %fusion.8, f32[576,384]{1,0:T(8,128)S(1)} %get-tuple-element.62, f32[576,384]{1,0:T(8,128)S(1)} %fusion.4), kind=kOutput, calls=%fused_computation.19 | convolution fusion | flops 1814372352 | bytes 15237120 | tf_op jit(solution)/shard_map/dot_general | solution.py:155
  133.9 5.2 %convolution_add_fusion = f32[576,4096]{1,0:T(8,128)S(1)} fusion(f32[576,4096]{1,0:T(8,128)} %fusion.6, bf16[576,384]{1,0:T(8,128)(2,1)S(1)} %get-tuple-element.61, bf16[1,4096,384]{2,1,0:T(8,128)(2,1)S(1)} %copy-done.7), kind=kOutput, calls=%fused_computation | convolution fusion | flops 1814298624 | bytes 22462464 | tf_op jit(solution)/shard_map/dot_general | solution.py:158
  141.2 4.3 %fusion.29 = (bf16[72,4096]{1,0:T(8,128)(2,1)}, bf16[72,4096]{1,0:T(8,128)(2,1)}, bf16[72,4096]{1,0:T(8,128)(2,1)}, bf16[72,4096]{1,0:T(8,128)(2,1)}) fusion(f32[2,4,72,4096]{3,2,1,0:T(8,128)} %bitcast.189, bf16[72,4096]{1,0:T(8,128)(2,1)S(1)} %collective-permute-done.11, bf16[72,4096]{1,0:T(8,128)(2,1)S(1)} %collective-permute-done.10, ...), kind=kLoop, calls=%fused_computation.61 | loop fusion | flops 3538944 | bytes 9437184 | tf_op jit(solution)/shard_map/convert_element_type | solution.py:55
  145.5 1.8 fusion.21
  147.3 12.5 %collective-permute-start.23 = (bf16[72,4096]{1,0:T(8,128)(2,1)}, bf16[72,4096]{1,0:T(8,128)(2,1)}, u32[]{:S(2)}, u32[]{:S(2)}) collective-permute-start(bf16[72,4096]{1,0:T(8,128)(2,1)} %get-tuple-element.23), channel_id=1, source_target_pairs={{0,6},{2,0},{4,2},{6,4},{1,7},{3,1},{5,3},{7,5},{8,14},{10,8},{12,... | collective-permute-start | bytes 1769480 | tf_op jit(solution)/shard_map/ppermute | solution.py:41
  160.7 5.7 %convolution_convert_fusion = bf16[4096,384]{1,0:T(8,128)(2,1)S(1)} fusion(bf16[576,4096]{1,0:T(8,128)(2,1)} %bitcast.198, bf16[576,384]{1,0:T(8,128)(2,1)} %copy-done.12), kind=kOutput, calls=%fused_computation.1 | convolution fusion | flops 1813512192 | bytes 8306688 | tf_op jit(solution)/shard_map/dot_general | solution.py:192
  166.4 7.6 %collective-permute-done.23 = bf16[72,4096]{1,0:T(8,128)(2,1)} collective-permute-done((bf16[72,4096]{1,0:T(8,128)(2,1)}, bf16[72,4096]{1,0:T(8,128)(2,1)}, u32[]{:S(2)}, u32[]{:S(2)}) %collective-permute-start.23) | collective-permute-done | bytes 589856 | tf_op jit(solution)/shard_map/ppermute | solution.py:41
  174.0 37.9 %collective-permute-done.24 = bf16[72,4096]{1,0:T(8,128)(2,1)} collective-permute-done((bf16[72,4096]{1,0:T(8,128)(2,1)}, bf16[72,4096]{1,0:T(8,128)(2,1)}, u32[]{:S(2)}, u32[]{:S(2)}) %collective-permute-start.24) | collective-permute-done | bytes 589856 | tf_op jit(solution)/shard_map/ppermute | solution.py:41
  211.9 1.7 pad_maximum_fusion
  214.8 1.6 collective-permute-start.28
  216.5 1.9 collective-permute-start.29
  218.5 1.6 collective-permute-start.31
  220.1 3.9 %fusion.2 = bf16[1,128,4096]{2,1,0:T(8,128)(2,1)S(1)} fusion(f32[288,4096]{1,0:T(8,128)S(1)} %bitcast_convert_fusion, bf16[1,128,4096]{2,1,0:T(8,128)(2,1)S(1)} %copy-done.1, f32[128]{0:T(128)S(1)} %get-tuple-element.57, s32[128]{0:T(128)S(1)} %get-tuple-element.32, f32[128]{0:T(128)S(1)} %get-tuple-element.58, s32[128]{0:T(128)S(1)} %get-tuple-element.31), kind=kOutput, calls=%fused_computation.8 | convolution fusion | flops 1813696512 | bytes 6817792 | tf_op jit(solution)/shard_map/dot_general | solution.py:170
  224.0 3.5 %collective-permute-start.26 = (bf16[1,128,4096]{2,1,0:T(8,128)(2,1)S(1)}, bf16[1,128,4096]{2,1,0:T(8,128)(2,1)S(1)}, u32[]{:S(2)}, u32[]{:S(2)}) collective-permute-start(bf16[1,128,4096]{2,1,0:T(8,128)(2,1)S(1)} %fusion.2), channel_id=1, source_target_pairs={{0,16},{1,17},{2,18},{3,19},{4,20},{5,21},{6,22},{7,23},{8,24},{9,... | collective-permute-start | bytes 3145736 | tf_op jit(solution)/shard_map/ppermute | solution.py:17
  227.5 2.8 collective-permute-done.27
  230.3 36.7 %collective-permute-done.28 = bf16[72,4096]{1,0:T(8,128)(2,1)S(1)} collective-permute-done((bf16[72,4096]{1,0:T(8,128)(2,1)S(1)}, bf16[72,4096]{1,0:T(8,128)(2,1)S(1)}, u32[]{:S(2)}, u32[]{:S(2)}) %collective-permute-start.28) | collective-permute-done | bytes 589856 | tf_op jit(solution)/shard_map/ppermute | solution.py:41
  269.3 1.3 collective-permute-start.30
  270.6 1.6 fusion.19
  273.3 21.7 %collective-permute-done.30 = bf16[1,128,4096]{2,1,0:T(8,128)(2,1)S(1)} collective-permute-done((bf16[1,128,4096]{2,1,0:T(8,128)(2,1)S(1)}, bf16[1,128,4096]{2,1,0:T(8,128)(2,1)S(1)}, u32[]{:S(2)}, u32[]{:S(2)}) %collective-permute-start.30) | collective-permute-done | bytes 1048608 | tf_op jit(solution)/shard_map/ppermute | solution.py:17
  (131 shorter events, 23.5 us)
Async XLA Ops:
  0.6 75.8 %copy-start = (bf16[1,4096,384]{2,1,0:T(8,128)(2,1)S(1)}, bf16[1,4096,384]{2,1,0:T(8,128)(2,1)}, u32[]{:S(2)}) copy-start(bf16[1,4096,384]{2,1,0:T(8,128)(2,1)} %param.13) | copy-start | bytes 9437188
  7.6 10.8 %copy-start.21 = (f32[1,128,2]{1,2,0:T(2,128)S(1)}, f32[1,128,2]{1,2,0:T(2,128)}, u32[]{:S(2)}) copy-start(f32[1,128,2]{1,2,0:T(2,128)} %param.12) | copy-start | bytes 3076
  7.6 10.8 %copy-start.4 = (bf16[1,128,4096]{2,1,0:T(8,128)(2,1)S(1)}, bf16[1,128,4096]{2,1,0:T(8,128)(2,1)}, u32[]{:S(2)}) copy-start(bf16[1,128,4096]{2,1,0:T(8,128)(2,1)} %param.17) | copy-start | bytes 3145732
  9.0 19.7 %collective-permute-start = (bf16[72,4096]{1,0:T(8,128)(2,1)}, bf16[72,4096]{1,0:T(8,128)(2,1)}, u32[]{:S(2)}, u32[]{:S(2)}) collective-permute-start(bf16[72,4096]{1,0:T(8,128)(2,1)} %get-tuple-element.56), channel_id=1, source_target_pairs={{0,2},{2,4},{4,6},{6,0},{1,3},{3,5},{5,7},{7,1},{8,10},{10,12},{12... | collective-permute-start | bytes 1769480 | tf_op jit(solution)/shard_map/ppermute | solution.py:41
  12.1 41.1 %collective-permute-start.1 = (bf16[72,4096]{1,0:T(8,128)(2,1)}, bf16[72,4096]{1,0:T(8,128)(2,1)}, u32[]{:S(2)}, u32[]{:S(2)}) collective-permute-start(bf16[72,4096]{1,0:T(8,128)(2,1)} %get-tuple-element.55), channel_id=1, source_target_pairs={{0,4},{2,6},{4,0},{6,2},{1,5},{3,7},{5,1},{7,3},{8,12},{10,14},{12... | collective-permute-start | bytes 1769480 | tf_op jit(solution)/shard_map/ppermute | solution.py:41
  14.7 39.6 %collective-permute-start.2 = (bf16[72,4096]{1,0:T(8,128)(2,1)}, bf16[72,4096]{1,0:T(8,128)(2,1)}, u32[]{:S(2)}, u32[]{:S(2)}) collective-permute-start(bf16[72,4096]{1,0:T(8,128)(2,1)} %get-tuple-element.54), channel_id=1, source_target_pairs={{0,6},{2,0},{4,2},{6,4},{1,7},{3,1},{5,3},{7,5},{8,14},{10,8},{12,... | collective-permute-start | bytes 1769480 | tf_op jit(solution)/shard_map/ppermute | solution.py:41
  16.0 40.1 %collective-permute-start.3 = (bf16[72,4096]{1,0:T(8,128)(2,1)}, bf16[72,4096]{1,0:T(8,128)(2,1)}, u32[]{:S(2)}, u32[]{:S(2)}) collective-permute-start(bf16[72,4096]{1,0:T(8,128)(2,1)} %get-tuple-element.53), channel_id=1, source_target_pairs={{0,1},{1,0},{2,3},{3,2},{4,5},{5,4},{6,7},{7,6},{8,9},{9,8},{10,11... | collective-permute-start | bytes 1769480 | tf_op jit(solution)/shard_map/ppermute | solution.py:36
  16.0 63.9 %collective-permute-start.7 = (bf16[384,2048]{1,0:T(8,128)(2,1)}, bf16[384,2048]{1,0:T(8,128)(2,1)}, u32[]{:S(2)}, u32[]{:S(2)}) collective-permute-start(bf16[384,2048]{1,0:T(8,128)(2,1)} %bitcast.20), channel_id=1, source_target_pairs={{0,8},{8,0},{1,9},{9,1},{2,10},{10,2},{3,11},{11,3},{4,12},{12,4},... | collective-permute-start | bytes 4718600 | tf_op jit(solution)/shard_map/ppermute | solution.py:69
  21.7 7.1 %copy-start.16 = (bf16[8,72,4096]{2,1,0:T(8,128)(2,1)S(1)}, bf16[8,72,4096]{2,1,0:T(8,128)(2,1)}, u32[]{:S(2)}) copy-start(bf16[8,72,4096]{2,1,0:T(8,128)(2,1)} %bitcast_dynamic-update-slice_fusion.15) | copy-start | bytes 14155780
  28.7 28.5 %collective-permute-start.4 = (bf16[72,4096]{1,0:T(8,128)(2,1)}, bf16[72,4096]{1,0:T(8,128)(2,1)S(1)}, u32[]{:S(2)}, u32[]{:S(2)}) collective-permute-start(bf16[72,4096]{1,0:T(8,128)(2,1)} %collective-permute-done), channel_id=1, source_target_pairs={{0,1},{1,0},{2,3},{3,2},{4,5},{5,4},{6,7},{7,6},{8,9},{9,8},{10,11... | collective-permute-start | bytes 1769480 | tf_op jit(solution)/shard_map/ppermute | solution.py:36
  53.2 4.1 %collective-permute-start.5 = (bf16[72,4096]{1,0:T(8,128)(2,1)}, bf16[72,4096]{1,0:T(8,128)(2,1)S(1)}, u32[]{:S(2)}, u32[]{:S(2)}) collective-permute-start(bf16[72,4096]{1,0:T(8,128)(2,1)} %collective-permute-done.1), channel_id=1, source_target_pairs={{0,1},{1,0},{2,3},{3,2},{4,5},{5,4},{6,7},{7,6},{8,9},{9,8},{10,11... | collective-permute-start | bytes 1769480 | tf_op jit(solution)/shard_map/ppermute | solution.py:36
  54.3 3.0 %collective-permute-start.6 = (bf16[72,4096]{1,0:T(8,128)(2,1)}, bf16[72,4096]{1,0:T(8,128)(2,1)S(1)}, u32[]{:S(2)}, u32[]{:S(2)}) collective-permute-start(bf16[72,4096]{1,0:T(8,128)(2,1)} %collective-permute-done.2), channel_id=1, source_target_pairs={{0,1},{1,0},{2,3},{3,2},{4,5},{5,4},{6,7},{7,6},{8,9},{9,8},{10,11... | collective-permute-start | bytes 1769480 | tf_op jit(solution)/shard_map/ppermute | solution.py:36
  57.3 16.4 %copy-start.6 = (bf16[1,4096,384]{2,1,0:T(8,128)(2,1)S(1)}, bf16[1,4096,384]{2,1,0:T(8,128)(2,1)}, u32[]{:S(2)}) copy-start(bf16[1,4096,384]{2,1,0:T(8,128)(2,1)} %param.14) | copy-start | bytes 9437188
  57.4 19.0 %copy-start.17 = (bf16[8,72,4096]{2,1,0:T(8,128)(2,1)}, bf16[8,72,4096]{2,1,0:T(8,128)(2,1)S(1)}, u32[]{:S(2)}) copy-start(bf16[8,72,4096]{2,1,0:T(8,128)(2,1)S(1)} %bitcast_dynamic-update-slice_fusion.8) | copy-start | bytes 14155780
  58.8 33.2 %collective-permute-start.12 = (bf16[72,4096]{1,0:T(8,128)(2,1)}, bf16[72,4096]{1,0:T(8,128)(2,1)}, u32[]{:S(2)}, u32[]{:S(2)}) collective-permute-start(bf16[72,4096]{1,0:T(8,128)(2,1)} %get-tuple-element.52), channel_id=1, source_target_pairs={{0,2},{2,4},{4,6},{6,0},{1,3},{3,5},{5,7},{7,1},{8,10},{10,12},{12... | collective-permute-start | bytes 1769480 | tf_op jit(solution)/shard_map/ppermute | solution.py:41
  70.2 42.0 %collective-permute-start.13 = (bf16[72,4096]{1,0:T(8,128)(2,1)}, bf16[72,4096]{1,0:T(8,128)(2,1)}, u32[]{:S(2)}, u32[]{:S(2)}) collective-permute-start(bf16[72,4096]{1,0:T(8,128)(2,1)} %get-tuple-element.51), channel_id=1, source_target_pairs={{0,4},{2,6},{4,0},{6,2},{1,5},{3,7},{5,1},{7,3},{8,12},{10,14},{12... | collective-permute-start | bytes 1769480 | tf_op jit(solution)/shard_map/ppermute | solution.py:41
  73.5 39.8 %collective-permute-start.14 = (bf16[72,4096]{1,0:T(8,128)(2,1)}, bf16[72,4096]{1,0:T(8,128)(2,1)}, u32[]{:S(2)}, u32[]{:S(2)}) collective-permute-start(bf16[72,4096]{1,0:T(8,128)(2,1)} %get-tuple-element.50), channel_id=1, source_target_pairs={{0,6},{2,0},{4,2},{6,4},{1,7},{3,1},{5,3},{7,5},{8,14},{10,8},{12,... | collective-permute-start | bytes 1769480 | tf_op jit(solution)/shard_map/ppermute | solution.py:41
  73.7 41.6 %collective-permute-start.15 = (bf16[72,4096]{1,0:T(8,128)(2,1)}, bf16[72,4096]{1,0:T(8,128)(2,1)}, u32[]{:S(2)}, u32[]{:S(2)}) collective-permute-start(bf16[72,4096]{1,0:T(8,128)(2,1)} %get-tuple-element.49), channel_id=1, source_target_pairs={{0,1},{1,0},{2,3},{3,2},{4,5},{5,4},{6,7},{7,6},{8,9},{9,8},{10,11... | collective-permute-start | bytes 1769480 | tf_op jit(solution)/shard_map/ppermute | solution.py:36
  81.5 4.9 %copy-start.8 = (bf16[384,4096]{1,0:T(8,128)(2,1)}, bf16[384,4096]{1,0:T(8,128)(2,1)S(1)}, u32[]{:S(2)}) copy-start(bf16[384,4096]{1,0:T(8,128)(2,1)S(1)} %constant_dynamic-update-slice_fusion) | copy-start | bytes 9437188
  86.4 3.6 %copy-start.2 = (f32[576,4096]{1,0:T(8,128)}, f32[576,4096]{1,0:T(8,128)S(1)}, u32[]{:S(2)}) copy-start(f32[576,4096]{1,0:T(8,128)S(1)} %fusion.79) | copy-start | bytes 28311556
  90.0 3.2 %copy-start.18 = (bf16[8,72,4096]{2,1,0:T(8,128)(2,1)S(1)}, bf16[8,72,4096]{2,1,0:T(8,128)(2,1)}, u32[]{:S(2)}) copy-start(bf16[8,72,4096]{2,1,0:T(8,128)(2,1)} %bitcast_dynamic-update-slice_fusion.7) | copy-start | bytes 14155780
  91.5 48.8 %collective-permute-start.10 = (bf16[72,4096]{1,0:T(8,128)(2,1)}, bf16[72,4096]{1,0:T(8,128)(2,1)S(1)}, u32[]{:S(2)}, u32[]{:S(2)}) collective-permute-start(bf16[72,4096]{1,0:T(8,128)(2,1)} %get-tuple-element.46), channel_id=1, source_target_pairs={{0,1},{1,0},{2,3},{3,2},{4,5},{5,4},{6,7},{7,6},{8,9},{9,8},{10,11... | collective-permute-start | bytes 1769480 | tf_op jit(solution)/shard_map/ppermute | solution.py:36
  92.0 48.7 %collective-permute-start.11 = (bf16[72,4096]{1,0:T(8,128)(2,1)}, bf16[72,4096]{1,0:T(8,128)(2,1)S(1)}, u32[]{:S(2)}, u32[]{:S(2)}) collective-permute-start(bf16[72,4096]{1,0:T(8,128)(2,1)} %get-tuple-element.45), channel_id=1, source_target_pairs={{0,1},{1,0},{2,3},{3,2},{4,5},{5,4},{6,7},{7,6},{8,9},{9,8},{10,11... | collective-permute-start | bytes 1769480 | tf_op jit(solution)/shard_map/ppermute | solution.py:36
  112.2 28.6 %collective-permute-start.8 = (bf16[72,4096]{1,0:T(8,128)(2,1)}, bf16[72,4096]{1,0:T(8,128)(2,1)S(1)}, u32[]{:S(2)}, u32[]{:S(2)}) collective-permute-start(bf16[72,4096]{1,0:T(8,128)(2,1)} %get-tuple-element.48), channel_id=1, source_target_pairs={{0,1},{1,0},{2,3},{3,2},{4,5},{5,4},{6,7},{7,6},{8,9},{9,8},{10,11... | collective-permute-start | bytes 1769480 | tf_op jit(solution)/shard_map/ppermute | solution.py:36
  113.3 8.8 %copy-start.9 = (bf16[384,4096]{1,0:T(8,128)(2,1)S(1)}, bf16[384,4096]{1,0:T(8,128)(2,1)}, u32[]{:S(2)}) copy-start(bf16[384,4096]{1,0:T(8,128)(2,1)} %copy-done.8) | copy-start | bytes 9437188
  113.3 27.9 %collective-permute-start.9 = (bf16[72,4096]{1,0:T(8,128)(2,1)}, bf16[72,4096]{1,0:T(8,128)(2,1)}, u32[]{:S(2)}, u32[]{:S(2)}) collective-permute-start(bf16[72,4096]{1,0:T(8,128)(2,1)} %get-tuple-element.47), channel_id=1, source_target_pairs={{0,1},{1,0},{2,3},{3,2},{4,5},{5,4},{6,7},{7,6},{8,9},{9,8},{10,11... | collective-permute-start | bytes 1769480 | tf_op jit(solution)/shard_map/ppermute | solution.py:36
  115.3 2.3 collective-permute-start.16
  117.6 2.2 collective-permute-start.17
  119.8 2.2 collective-permute-start.18
  128.6 5.3 %copy-start.12 = (bf16[576,384]{1,0:T(8,128)(2,1)}, bf16[576,384]{1,0:T(8,128)(2,1)S(1)}, u32[]{:S(2)}) copy-start(bf16[576,384]{1,0:T(8,128)(2,1)S(1)} %get-tuple-element.61) | copy-start | bytes 1327108
  128.6 5.3 %copy-start.7 = (bf16[1,4096,384]{2,1,0:T(8,128)(2,1)S(1)}, bf16[1,4096,384]{2,1,0:T(8,128)(2,1)}, u32[]{:S(2)}) copy-start(bf16[1,4096,384]{2,1,0:T(8,128)(2,1)} %param.14) | copy-start | bytes 9437188
  140.1 5.4 %collective-permute-start.19 = (bf16[72,4096]{1,0:T(8,128)(2,1)S(1)}, bf16[72,4096]{1,0:T(8,128)(2,1)S(1)}, u32[]{:S(2)}, u32[]{:S(2)}) collective-permute-start(bf16[72,4096]{1,0:T(8,128)(2,1)S(1)} %get-tuple-element.44), channel_id=1, source_target_pairs={{0,1},{1,0},{2,3},{3,2},{4,5},{5,4},{6,7},{7,6},{8,9},{9,8},{10,11... | collective-permute-start | bytes 1769480 | tf_op jit(solution)/shard_map/ppermute | solution.py:36
  140.3 5.2 %collective-permute-start.20 = (bf16[72,4096]{1,0:T(8,128)(2,1)S(1)}, bf16[72,4096]{1,0:T(8,128)(2,1)S(1)}, u32[]{:S(2)}, u32[]{:S(2)}) collective-permute-start(bf16[72,4096]{1,0:T(8,128)(2,1)S(1)} %get-tuple-element.43), channel_id=1, source_target_pairs={{0,1},{1,0},{2,3},{3,2},{4,5},{5,4},{6,7},{7,6},{8,9},{9,8},{10,11... | collective-permute-start | bytes 1769480 | tf_op jit(solution)/shard_map/ppermute | solution.py:36
  140.7 4.9 %collective-permute-start.21 = (bf16[72,4096]{1,0:T(8,128)(2,1)S(1)}, bf16[72,4096]{1,0:T(8,128)(2,1)S(1)}, u32[]{:S(2)}, u32[]{:S(2)}) collective-permute-start(bf16[72,4096]{1,0:T(8,128)(2,1)S(1)} %get-tuple-element.42), channel_id=1, source_target_pairs={{0,1},{1,0},{2,3},{3,2},{4,5},{5,4},{6,7},{7,6},{8,9},{9,8},{10,11... | collective-permute-start | bytes 1769480 | tf_op jit(solution)/shard_map/ppermute | solution.py:36
  140.8 4.7 %collective-permute-start.22 = (bf16[72,4096]{1,0:T(8,128)(2,1)S(1)}, bf16[72,4096]{1,0:T(8,128)(2,1)S(1)}, u32[]{:S(2)}, u32[]{:S(2)}) collective-permute-start(bf16[72,4096]{1,0:T(8,128)(2,1)S(1)} %get-tuple-element.41), channel_id=1, source_target_pairs={{0,1},{1,0},{2,3},{3,2},{4,5},{5,4},{6,7},{7,6},{8,9},{9,8},{10,11... | collective-permute-start | bytes 1769480 | tf_op jit(solution)/shard_map/ppermute | solution.py:36
  147.3 26.7 %collective-permute-start.23 = (bf16[72,4096]{1,0:T(8,128)(2,1)}, bf16[72,4096]{1,0:T(8,128)(2,1)}, u32[]{:S(2)}, u32[]{:S(2)}) collective-permute-start(bf16[72,4096]{1,0:T(8,128)(2,1)} %get-tuple-element.23), channel_id=1, source_target_pairs={{0,6},{2,0},{4,2},{6,4},{1,7},{3,1},{5,3},{7,5},{8,14},{10,8},{12,... | collective-permute-start | bytes 1769480 | tf_op jit(solution)/shard_map/ppermute | solution.py:41
  159.9 52.0 %collective-permute-start.24 = (bf16[72,4096]{1,0:T(8,128)(2,1)}, bf16[72,4096]{1,0:T(8,128)(2,1)}, u32[]{:S(2)}, u32[]{:S(2)}) collective-permute-start(bf16[72,4096]{1,0:T(8,128)(2,1)} %get-tuple-element.24), channel_id=1, source_target_pairs={{0,4},{2,6},{4,0},{6,2},{1,5},{3,7},{5,1},{7,3},{8,12},{10,14},{12... | collective-permute-start | bytes 1769480 | tf_op jit(solution)/shard_map/ppermute | solution.py:41
  160.0 51.8 %collective-permute-start.25 = (bf16[72,4096]{1,0:T(8,128)(2,1)}, bf16[72,4096]{1,0:T(8,128)(2,1)}, u32[]{:S(2)}, u32[]{:S(2)}) collective-permute-start(bf16[72,4096]{1,0:T(8,128)(2,1)} %get-tuple-element.25), channel_id=1, source_target_pairs={{0,2},{2,4},{4,6},{6,0},{1,3},{3,5},{5,7},{7,1},{8,10},{10,12},{12... | collective-permute-start | bytes 1769480 | tf_op jit(solution)/shard_map/ppermute | solution.py:41
  160.6 51.2 %copy-start.11 = (bf16[72,4096]{1,0:T(8,128)(2,1)S(1)}, bf16[72,4096]{1,0:T(8,128)(2,1)}, u32[]{:S(2)}) copy-start(bf16[72,4096]{1,0:T(8,128)(2,1)} %get-tuple-element.22) | copy-start | bytes 1769476
  214.7 5.4 %copy-start.1 = (bf16[1,128,4096]{2,1,0:T(8,128)(2,1)S(1)}, bf16[1,128,4096]{2,1,0:T(8,128)(2,1)}, u32[]{:S(2)}) copy-start(bf16[1,128,4096]{2,1,0:T(8,128)(2,1)} %param.9) | copy-start | bytes 3145732
  214.7 15.6 %collective-permute-start.27 = (bf16[72,4096]{1,0:T(8,128)(2,1)S(1)}, bf16[72,4096]{1,0:T(8,128)(2,1)S(1)}, u32[]{:S(2)}, u32[]{:S(2)}) collective-permute-start(bf16[72,4096]{1,0:T(8,128)(2,1)S(1)} %copy-done.15), channel_id=1, source_target_pairs={{0,6},{2,0},{4,2},{6,4},{1,7},{3,1},{5,3},{7,5},{8,14},{10,8},{12,... | collective-permute-start | bytes 1769480 | tf_op jit(solution)/shard_map/ppermute | solution.py:41
  214.8 52.2 %collective-permute-start.28 = (bf16[72,4096]{1,0:T(8,128)(2,1)S(1)}, bf16[72,4096]{1,0:T(8,128)(2,1)S(1)}, u32[]{:S(2)}, u32[]{:S(2)}) collective-permute-start(bf16[72,4096]{1,0:T(8,128)(2,1)S(1)} %copy-done.14), channel_id=1, source_target_pairs={{0,4},{2,6},{4,0},{6,2},{1,5},{3,7},{5,1},{7,3},{8,12},{10,14},{12... | collective-permute-start | bytes 1769480 | tf_op jit(solution)/shard_map/ppermute | solution.py:41
  216.5 50.5 %collective-permute-start.29 = (bf16[72,4096]{1,0:T(8,128)(2,1)S(1)}, bf16[72,4096]{1,0:T(8,128)(2,1)S(1)}, u32[]{:S(2)}, u32[]{:S(2)}) collective-permute-start(bf16[72,4096]{1,0:T(8,128)(2,1)S(1)} %copy-done.13), channel_id=1, source_target_pairs={{0,2},{2,4},{4,6},{6,0},{1,3},{3,5},{5,7},{7,1},{8,10},{10,12},{12... | collective-permute-start | bytes 1769480 | tf_op jit(solution)/shard_map/ppermute | solution.py:41
  218.5 48.5 %copy-start.10 = (bf16[72,4096]{1,0:T(8,128)(2,1)S(1)}, bf16[72,4096]{1,0:T(8,128)(2,1)}, u32[]{:S(2)}) copy-start(bf16[72,4096]{1,0:T(8,128)(2,1)} %get-tuple-element.27) | copy-start | bytes 1769476
  218.5 52.1 %collective-permute-start.31 = (bf16[2048,384]{1,0:T(8,128)(2,1)S(1)}, bf16[2048,384]{1,0:T(8,128)(2,1)S(1)}, u32[]{:S(2)}, u32[]{:S(2)}) collective-permute-start(bf16[2048,384]{1,0:T(8,128)(2,1)S(1)} %constant_dynamic-slice_fusion), channel_id=1, source_target_pairs={{0,8},{8,0},{1,9},{9,1},{2,10},{10,2},{3,11},{11,3},{4,12},{12,4},... | collective-permute-start | bytes 4718600 | tf_op jit(solution)/shard_map/ppermute | solution.py:69
  224.0 43.3 %copy-start.19 = (f32[1,4096]{1,0:T(1,128)S(1)}, f32[1,4096]{1,0:T(1,128)}, u32[]{:S(2)}) copy-start(f32[1,4096]{1,0:T(1,128)} %param.10) | copy-start | bytes 49156
  224.0 48.2 %collective-permute-start.26 = (bf16[1,128,4096]{2,1,0:T(8,128)(2,1)S(1)}, bf16[1,128,4096]{2,1,0:T(8,128)(2,1)S(1)}, u32[]{:S(2)}, u32[]{:S(2)}) collective-permute-start(bf16[1,128,4096]{2,1,0:T(8,128)(2,1)S(1)} %fusion.2), channel_id=1, source_target_pairs={{0,16},{1,17},{2,18},{3,19},{4,20},{5,21},{6,22},{7,23},{8,24},{9,... | collective-permute-start | bytes 3145736 | tf_op jit(solution)/shard_map/ppermute | solution.py:17
  269.3 25.7 %collective-permute-start.30 = (bf16[1,128,4096]{2,1,0:T(8,128)(2,1)S(1)}, bf16[1,128,4096]{2,1,0:T(8,128)(2,1)S(1)}, u32[]{:S(2)}, u32[]{:S(2)}) collective-permute-start(bf16[1,128,4096]{2,1,0:T(8,128)(2,1)S(1)} %fusion.37), channel_id=1, source_target_pairs={{16,0},{17,1},{18,2},{19,3},{20,4},{21,5},{22,6},{23,7},{24,8},{25... | collective-permute-start | bytes 3145736 | tf_op jit(solution)/shard_map/ppermute | solution.py:17
  (6 other events, 11.9 us)

commit v12 on v10

--- a/solution.py
+++ b/solution.py
@@ -125,7 +125,11 @@
     down_full = gather_replicas(down_weight[0])
     gate_act = jnp.dot(arrived, gate_local, preferred_element_type=jnp.float32)
     up_act = jnp.dot(arrived, up_local, preferred_element_type=jnp.float32)
-    spike_rate = lif_rate(gate_act, up_act, leak_local).astype(jnp.bfloat16)
+    spike_exact, lif_pullback = jax.vjp(
+        lambda gate_in, up_in: lif_rate(gate_in, up_in, leak_local), gate_act, up_act
+    )
+    spike_rate = spike_exact.astype(jnp.bfloat16)
+    gate_slope, up_slope = lif_pullback(jnp.ones_like(spike_exact))
     out_part = jnp.dot(spike_rate, down_full, preferred_element_type=jnp.float32)
     out_summed = combine_cores(out_part, experts, capacity)
     weights = route_gates[0]
@@ -143,12 +147,8 @@
     rate_grad = lax.dot_general(
         grad_rows, down_full, (((1,), (1,)), ((), ())), preferred_element_type=jnp.float32
     )
-    unused_rate, pullback = jax.vjp(
-        lambda gate_in, up_in: lif_rate(gate_in, up_in, leak_local), gate_act, up_act
-    )
-    gate_grad, up_act_grad = pullback(rate_grad)
-    gate_grad = gate_grad.astype(jnp.bfloat16)
-    up_act_grad = up_act_grad.astype(jnp.bfloat16)
+    gate_grad = (rate_grad * gate_slope).astype(jnp.bfloat16)
+    up_act_grad = (rate_grad * up_slope).astype(jnp.bfloat16)
     back_part = lax.dot_general(
         gate_grad, gate_local, (((1,), (1,)), ((), ())), preferred_element_type=jnp.float32
     )

time: 292 us -> 292 us (level)
  waiting for transfers between devices: 161 us -> 157 us
  local copies, waits for them, and re-layouts: 23.3 us -> 26.7 us
    unnamed x45, local copies, waits for them, and re-layouts: 10.2 us -> 13.8 us
    ppermute x12, waiting for transfers between devices: 137 us -> 134 us  [shifted(): lax.ppermute(value, 'chip', [(source, (source + steps) % count) for sourc...]
where the time goes in v12:
time: 292 us; the launch traced here: 287 us
  waiting for transfers between devices  157 us (54%)
  starting transfers between devices  48.6 us (17%)
  matrix products  39.2 us (13%)
  local copies, waits for them, and re-layouts  26.7 us (9%)
  other arithmetic  13.6 us (5%)
    ppermute x12, waiting for transfers between devices, shifted(): lax.ppermute(value, 'chip', [(source, (source + steps) % count) for sourc...  134 us
    ppermute x12, starting transfers between devices, shifted(): lax.ppermute(value, 'chip', [(source, (source + steps) % count) for sourc...  38.8 us
    ppermute x2, waiting for transfers between devices, passed_along(): lax.ppermute(value, axis, [(source, source + steps) for source in range(l...  21.5 us
    unnamed x45, local copies, waits for them, and re-layouts  13.8 us
    dot_general x1, matrix products, per_device(): lax.dot_general(grad_rows, down_full, (((1,), (1,)), ((), ())), preferred...  7.02 us
  transfers between devices with their start and end apart: 26, of which 10 were waited for; matrix products, arithmetic and copies ran while one was open for 19% of the time, Pallas kernels for 0%

profile of v12, /device:TPU:0, one launch (start us, length us, event | category | flops | bytes accessed | tf_op | source)
XLA Modules:
  0.0 286.9 jit_solution(2348481816653347242)
XLA Ops:
  1.9 1.2 reduce-window.6
  3.9 1.5 fusion.14
  5.5 2.1 convolution_convert_fusion.1
  7.6 1.5 fusion.105
  9.0 3.1 %collective-permute-start = (bf16[72,4096]{1,0:T(8,128)(2,1)}, bf16[72,4096]{1,0:T(8,128)(2,1)}, u32[]{:S(2)}, u32[]{:S(2)}) collective-permute-start(bf16[72,4096]{1,0:T(8,128)(2,1)} %get-tuple-element.32), channel_id=1, source_target_pairs={{0,2},{2,4},{4,6},{6,0},{1,3},{3,5},{5,7},{7,1},{8,10},{10,12},{12... | collective-permute-start | bytes 1769480 | tf_op jit(solution)/shard_map/ppermute | solution.py:41
  12.1 2.6 collective-permute-start.1
  14.7 1.3 collective-permute-start.2
  16.0 1.5 collective-permute-start.7
  19.3 2.4 fusion
  22.1 1.8 constant_dynamic-update-slice_fusion.1
  23.9 4.9 %collective-permute-done = bf16[72,4096]{1,0:T(8,128)(2,1)} collective-permute-done((bf16[72,4096]{1,0:T(8,128)(2,1)}, bf16[72,4096]{1,0:T(8,128)(2,1)}, u32[]{:S(2)}, u32[]{:S(2)}) %collective-permute-start) | collective-permute-done | bytes 589856 | tf_op jit(solution)/shard_map/ppermute | solution.py:41
  28.8 1.1 bitcast_dynamic-update-slice_fusion.14
  29.9 23.3 %collective-permute-done.1 = bf16[72,4096]{1,0:T(8,128)(2,1)} collective-permute-done((bf16[72,4096]{1,0:T(8,128)(2,1)}, bf16[72,4096]{1,0:T(8,128)(2,1)}, u32[]{:S(2)}, u32[]{:S(2)}) %collective-permute-start.1) | collective-permute-done | bytes 589856 | tf_op jit(solution)/shard_map/ppermute | solution.py:41
  53.2 1.1 bitcast_dynamic-update-slice_fusion.13
  54.9 1.2 bitcast_dynamic-update-slice_fusion.12
  56.1 1.1 bitcast_dynamic-update-slice_fusion.11
  57.6 11.4 %collective-permute-start.9 = (bf16[72,4096]{1,0:T(8,128)(2,1)S(1)}, bf16[72,4096]{1,0:T(8,128)(2,1)S(1)}, u32[]{:S(2)}, u32[]{:S(2)}) collective-permute-start(bf16[72,4096]{1,0:T(8,128)(2,1)S(1)} %get-tuple-element.28), channel_id=1, source_target_pairs={{0,2},{2,4},{4,6},{6,0},{1,3},{3,5},{5,7},{7,1},{8,10},{10,12},{12... | collective-permute-start | bytes 1769480 | tf_op jit(solution)/shard_map/ppermute | solution.py:41
  69.0 3.4 %collective-permute-start.10 = (bf16[72,4096]{1,0:T(8,128)(2,1)S(1)}, bf16[72,4096]{1,0:T(8,128)(2,1)S(1)}, u32[]{:S(2)}, u32[]{:S(2)}) collective-permute-start(bf16[72,4096]{1,0:T(8,128)(2,1)S(1)} %get-tuple-element.27), channel_id=1, source_target_pairs={{0,4},{2,6},{4,0},{6,2},{1,5},{3,7},{5,1},{7,3},{8,12},{10,14},{12... | collective-permute-start | bytes 1769480 | tf_op jit(solution)/shard_map/ppermute | solution.py:41
  72.6 2.6 fusion.4
  75.2 2.6 fusion.8
  77.9 1.6 constant_dynamic-update-slice_fusion
  79.5 4.9 %fusion.61 = f32[576,4096]{1,0:T(8,128)S(1)} fusion(bf16[384,4096]{1,0:T(8,128)(2,1)S(1)} %constant_dynamic-update-slice_fusion, f32[384]{0:T(512)S(1)} %reduce.2, f32[384]{0:T(512)S(1)} %broadcast_multiply_fusion, f32[576,384]{1,0:T(8,128)S(1)} %fusion.4, f32[576,384]{1,0:T(8,128)S(1)} %fusion.8), kind=kOutput, calls=%fused_computation.126 | convolution fusion | flops 1827643392 | bytes 14355456 | tf_op jit(solution)/shard_map/dot_general | solution.py:133
  84.4 3.6 %copy-done.4 = f32[576,4096]{1,0:T(8,128)} copy-done((f32[576,4096]{1,0:T(8,128)}, f32[576,4096]{1,0:T(8,128)S(1)}, u32[]{:S(2)}) %copy-start.4) | copy-done | bytes 9437208
  88.0 1.7 slice.152
  90.3 20.4 %collective-permute-done.10 = bf16[72,4096]{1,0:T(8,128)(2,1)S(1)} collective-permute-done((bf16[72,4096]{1,0:T(8,128)(2,1)S(1)}, bf16[72,4096]{1,0:T(8,128)(2,1)S(1)}, u32[]{:S(2)}, u32[]{:S(2)}) %collective-permute-start.10) | collective-permute-done | bytes 589856 | tf_op jit(solution)/shard_map/ppermute | solution.py:41
  111.5 1.2 collective-permute-done.14
  113.6 7.0 %multiply_convert_fusion = (bf16[576,384]{1,0:T(8,128)(2,1)}, f32[576,384]{1,0:T(8,128)S(1)}, f32[576,384]{1,0:T(8,128)S(1)}) fusion(f32[576,384]{1,0:T(8,128)S(1)} %fusion.8, f32[576,384]{1,0:T(8,128)S(1)} %fusion.4, f32[384]{0:T(512)S(1)} %broadcast_multiply_fusion, f32[384]{0:T(512)S(1)} %reduce.2, bf16[576,4096]{1,0:T(8,128)(2,1)S(1)} %bitcast.144, ...), kind=kOutput, calls=%fused_computation.89 | convolution fusion | flops 1839808512 | bytes 11848704 | tf_op jit(solution)/shard_map/dot_general | solution.py:147
  120.6 2.8 fusion.6
  123.4 3.7 %convolution_add_fusion = f32[576,4096]{1,0:T(8,128)S(1)} fusion(f32[576,4096]{1,0:T(8,128)S(1)} %fusion.6, bf16[576,384]{1,0:T(8,128)(2,1)} %get-tuple-element.15, bf16[1,4096,384]{2,1,0:T(8,128)(2,1)S(1)} %copy-done.8), kind=kOutput, calls=%fused_computation | convolution fusion | flops 1814298624 | bytes 22462464 | tf_op jit(solution)/shard_map/dot_general | solution.py:155
  127.6 3.1 %copy-done.2 = f32[576,4096]{1,0:T(8,128)} copy-done((f32[576,4096]{1,0:T(8,128)}, f32[576,4096]{1,0:T(8,128)S(1)}, u32[]{:S(2)}) %copy-start.2) | copy-done | bytes 9437208
  130.7 2.3 slice-done.1
  133.0 2.6 add_convert_fusion.1
  136.9 1.2 fusion.103
  138.1 12.5 %collective-permute-start.17 = (bf16[72,4096]{1,0:T(8,128)(2,1)}, bf16[72,4096]{1,0:T(8,128)(2,1)}, u32[]{:S(2)}, u32[]{:S(2)}) collective-permute-start(bf16[72,4096]{1,0:T(8,128)(2,1)} %get-tuple-element.24), channel_id=1, source_target_pairs={{0,6},{2,0},{4,2},{6,4},{1,7},{3,1},{5,3},{7,5},{8,14},{10,8},{12,... | collective-permute-start | bytes 1769480 | tf_op jit(solution)/shard_map/ppermute | solution.py:41
  150.6 1.2 collective-permute-start.18
  152.1 5.6 %convolution_convert_fusion = bf16[4096,384]{1,0:T(8,128)(2,1)S(1)} fusion(bf16[576,4096]{1,0:T(8,128)(2,1)} %bitcast.143, bf16[576,384]{1,0:T(8,128)(2,1)S(1)} %copy-done.9), kind=kOutput, calls=%fused_computation.1 | convolution fusion | flops 1813512192 | bytes 8306688 | tf_op jit(solution)/shard_map/dot_general | solution.py:189
  157.7 7.1 %collective-permute-done.17 = bf16[72,4096]{1,0:T(8,128)(2,1)} collective-permute-done((bf16[72,4096]{1,0:T(8,128)(2,1)}, bf16[72,4096]{1,0:T(8,128)(2,1)}, u32[]{:S(2)}, u32[]{:S(2)}) %collective-permute-start.17) | collective-permute-done | bytes 589856 | tf_op jit(solution)/shard_map/ppermute | solution.py:41
  164.8 38.7 %collective-permute-done.18 = bf16[72,4096]{1,0:T(8,128)(2,1)} collective-permute-done((bf16[72,4096]{1,0:T(8,128)(2,1)}, bf16[72,4096]{1,0:T(8,128)(2,1)}, u32[]{:S(2)}, u32[]{:S(2)}) %collective-permute-start.18) | collective-permute-done | bytes 589856 | tf_op jit(solution)/shard_map/ppermute | solution.py:41
  203.4 1.7 pad_maximum_fusion
  207.1 1.9 collective-permute-start.23
  209.2 1.6 collective-permute-start.25
  210.8 4.0 %fusion.2 = bf16[1,128,4096]{2,1,0:T(8,128)(2,1)S(1)} fusion(f32[288,4096]{1,0:T(8,128)S(1)} %bitcast_convert_fusion, bf16[1,128,4096]{2,1,0:T(8,128)(2,1)S(1)} %copy-done.3, f32[128]{0:T(128)S(1)} %get-tuple-element.33, s32[128]{0:T(128)S(1)} %get-tuple-element.14, f32[128]{0:T(128)S(1)} %get-tuple-element.34, s32[128]{0:T(128)S(1)} %get-tuple-element.13), kind=kOutput, calls=%fused_computation.12 | convolution fusion | flops 1813696512 | bytes 6817792 | tf_op jit(solution)/shard_map/dot_general | solution.py:167
  214.8 3.5 %collective-permute-start.20 = (bf16[1,128,4096]{2,1,0:T(8,128)(2,1)S(1)}, bf16[1,128,4096]{2,1,0:T(8,128)(2,1)S(1)}, u32[]{:S(2)}, u32[]{:S(2)}) collective-permute-start(bf16[1,128,4096]{2,1,0:T(8,128)(2,1)S(1)} %fusion.2), channel_id=1, source_target_pairs={{0,16},{1,17},{2,18},{3,19},{4,20},{5,21},{6,22},{7,23},{8,24},{9,... | collective-permute-start | bytes 3145736 | tf_op jit(solution)/shard_map/ppermute | solution.py:17
  218.3 3.6 %collective-permute-done.21 = bf16[72,4096]{1,0:T(8,128)(2,1)S(1)} collective-permute-done((bf16[72,4096]{1,0:T(8,128)(2,1)S(1)}, bf16[72,4096]{1,0:T(8,128)(2,1)S(1)}, u32[]{:S(2)}, u32[]{:S(2)}) %collective-permute-start.21) | collective-permute-done | bytes 589856 | tf_op jit(solution)/shard_map/ppermute | solution.py:41
  221.8 35.7 %collective-permute-done.22 = bf16[72,4096]{1,0:T(8,128)(2,1)S(1)} collective-permute-done((bf16[72,4096]{1,0:T(8,128)(2,1)S(1)}, bf16[72,4096]{1,0:T(8,128)(2,1)S(1)}, u32[]{:S(2)}, u32[]{:S(2)}) %collective-permute-start.22) | collective-permute-done | bytes 589856 | tf_op jit(solution)/shard_map/ppermute | solution.py:41
  259.9 1.3 collective-permute-start.24
  261.2 1.6 fusion.19
  263.9 21.5 %collective-permute-done.24 = bf16[1,128,4096]{2,1,0:T(8,128)(2,1)S(1)} collective-permute-done((bf16[1,128,4096]{2,1,0:T(8,128)(2,1)S(1)}, bf16[1,128,4096]{2,1,0:T(8,128)(2,1)S(1)}, u32[]{:S(2)}, u32[]{:S(2)}) %collective-permute-start.24) | collective-permute-done | bytes 1048608 | tf_op jit(solution)/shard_map/ppermute | solution.py:17
  (109 shorter events, 16.0 us)
Async XLA Ops:
  0.6 74.6 %copy-start = (bf16[1,4096,384]{2,1,0:T(8,128)(2,1)S(1)}, bf16[1,4096,384]{2,1,0:T(8,128)(2,1)}, u32[]{:S(2)}) copy-start(bf16[1,4096,384]{2,1,0:T(8,128)(2,1)} %param.13) | copy-start | bytes 9437188
  7.6 10.8 %copy-start.14 = (f32[1,128,2]{1,2,0:T(2,128)S(1)}, f32[1,128,2]{1,2,0:T(2,128)}, u32[]{:S(2)}) copy-start(f32[1,128,2]{1,2,0:T(2,128)} %param.12) | copy-start | bytes 3076
  7.6 10.8 %copy-start.6 = (bf16[1,128,4096]{2,1,0:T(8,128)(2,1)S(1)}, bf16[1,128,4096]{2,1,0:T(8,128)(2,1)}, u32[]{:S(2)}) copy-start(bf16[1,128,4096]{2,1,0:T(8,128)(2,1)} %param.17) | copy-start | bytes 3145732
  9.0 19.7 %collective-permute-start = (bf16[72,4096]{1,0:T(8,128)(2,1)}, bf16[72,4096]{1,0:T(8,128)(2,1)}, u32[]{:S(2)}, u32[]{:S(2)}) collective-permute-start(bf16[72,4096]{1,0:T(8,128)(2,1)} %get-tuple-element.32), channel_id=1, source_target_pairs={{0,2},{2,4},{4,6},{6,0},{1,3},{3,5},{5,7},{7,1},{8,10},{10,12},{12... | collective-permute-start | bytes 1769480 | tf_op jit(solution)/shard_map/ppermute | solution.py:41
  12.1 41.1 %collective-permute-start.1 = (bf16[72,4096]{1,0:T(8,128)(2,1)}, bf16[72,4096]{1,0:T(8,128)(2,1)}, u32[]{:S(2)}, u32[]{:S(2)}) collective-permute-start(bf16[72,4096]{1,0:T(8,128)(2,1)} %get-tuple-element.31), channel_id=1, source_target_pairs={{0,4},{2,6},{4,0},{6,2},{1,5},{3,7},{5,1},{7,3},{8,12},{10,14},{12... | collective-permute-start | bytes 1769480 | tf_op jit(solution)/shard_map/ppermute | solution.py:41
  14.7 39.6 %collective-permute-start.2 = (bf16[72,4096]{1,0:T(8,128)(2,1)}, bf16[72,4096]{1,0:T(8,128)(2,1)}, u32[]{:S(2)}, u32[]{:S(2)}) collective-permute-start(bf16[72,4096]{1,0:T(8,128)(2,1)} %get-tuple-element.30), channel_id=1, source_target_pairs={{0,6},{2,0},{4,2},{6,4},{1,7},{3,1},{5,3},{7,5},{8,14},{10,8},{12,... | collective-permute-start | bytes 1769480 | tf_op jit(solution)/shard_map/ppermute | solution.py:41
  16.0 40.1 %collective-permute-start.3 = (bf16[72,4096]{1,0:T(8,128)(2,1)}, bf16[72,4096]{1,0:T(8,128)(2,1)}, u32[]{:S(2)}, u32[]{:S(2)}) collective-permute-start(bf16[72,4096]{1,0:T(8,128)(2,1)} %get-tuple-element.29), channel_id=1, source_target_pairs={{0,1},{1,0},{2,3},{3,2},{4,5},{5,4},{6,7},{7,6},{8,9},{9,8},{10,11... | collective-permute-start | bytes 1769480 | tf_op jit(solution)/shard_map/ppermute | solution.py:36
  16.0 61.8 %collective-permute-start.7 = (bf16[384,2048]{1,0:T(8,128)(2,1)}, bf16[384,2048]{1,0:T(8,128)(2,1)}, u32[]{:S(2)}, u32[]{:S(2)}) collective-permute-start(bf16[384,2048]{1,0:T(8,128)(2,1)} %bitcast.20), channel_id=1, source_target_pairs={{0,8},{8,0},{1,9},{9,1},{2,10},{10,2},{3,11},{11,3},{4,12},{12,4},... | collective-permute-start | bytes 4718600 | tf_op jit(solution)/shard_map/ppermute | solution.py:66
  19.3 2.4 copy-start.13
  21.7 7.1 %copy-start.10 = (bf16[8,72,4096]{2,1,0:T(8,128)(2,1)S(1)}, bf16[8,72,4096]{2,1,0:T(8,128)(2,1)}, u32[]{:S(2)}) copy-start(bf16[8,72,4096]{2,1,0:T(8,128)(2,1)} %bitcast_dynamic-update-slice_fusion.15) | copy-start | bytes 14155780
  28.8 28.5 %collective-permute-start.4 = (bf16[72,4096]{1,0:T(8,128)(2,1)}, bf16[72,4096]{1,0:T(8,128)(2,1)S(1)}, u32[]{:S(2)}, u32[]{:S(2)}) collective-permute-start(bf16[72,4096]{1,0:T(8,128)(2,1)} %collective-permute-done), channel_id=1, source_target_pairs={{0,1},{1,0},{2,3},{3,2},{4,5},{5,4},{6,7},{7,6},{8,9},{9,8},{10,11... | collective-permute-start | bytes 1769480 | tf_op jit(solution)/shard_map/ppermute | solution.py:36
  53.2 4.1 %collective-permute-start.5 = (bf16[72,4096]{1,0:T(8,128)(2,1)}, bf16[72,4096]{1,0:T(8,128)(2,1)S(1)}, u32[]{:S(2)}, u32[]{:S(2)}) collective-permute-start(bf16[72,4096]{1,0:T(8,128)(2,1)} %collective-permute-done.1), channel_id=1, source_target_pairs={{0,1},{1,0},{2,3},{3,2},{4,5},{5,4},{6,7},{7,6},{8,9},{9,8},{10,11... | collective-permute-start | bytes 1769480 | tf_op jit(solution)/shard_map/ppermute | solution.py:36
  54.3 3.1 %copy-start.5 = (bf16[288,4096]{1,0:T(8,128)(2,1)S(1)}, bf16[288,4096]{1,0:T(8,128)(2,1)}, u32[]{:S(2)}) copy-start(bf16[288,4096]{1,0:T(8,128)(2,1)} %fusion) | copy-start | bytes 7077892
  54.3 3.0 %collective-permute-start.6 = (bf16[72,4096]{1,0:T(8,128)(2,1)}, bf16[72,4096]{1,0:T(8,128)(2,1)S(1)}, u32[]{:S(2)}, u32[]{:S(2)}) collective-permute-start(bf16[72,4096]{1,0:T(8,128)(2,1)} %collective-permute-done.2), channel_id=1, source_target_pairs={{0,1},{1,0},{2,3},{3,2},{4,5},{5,4},{6,7},{7,6},{8,9},{9,8},{10,11... | collective-permute-start | bytes 1769480 | tf_op jit(solution)/shard_map/ppermute | solution.py:36
  57.3 15.2 %copy-start.8 = (bf16[1,4096,384]{2,1,0:T(8,128)(2,1)S(1)}, bf16[1,4096,384]{2,1,0:T(8,128)(2,1)}, u32[]{:S(2)}) copy-start(bf16[1,4096,384]{2,1,0:T(8,128)(2,1)} %param.14) | copy-start | bytes 9437188
  57.4 17.8 %copy-start.11 = (bf16[8,72,4096]{2,1,0:T(8,128)(2,1)}, bf16[8,72,4096]{2,1,0:T(8,128)(2,1)S(1)}, u32[]{:S(2)}) copy-start(bf16[8,72,4096]{2,1,0:T(8,128)(2,1)S(1)} %bitcast_dynamic-update-slice_fusion.8) | copy-start | bytes 14155780
  57.6 32.7 %collective-permute-start.9 = (bf16[72,4096]{1,0:T(8,128)(2,1)S(1)}, bf16[72,4096]{1,0:T(8,128)(2,1)S(1)}, u32[]{:S(2)}, u32[]{:S(2)}) collective-permute-start(bf16[72,4096]{1,0:T(8,128)(2,1)S(1)} %get-tuple-element.28), channel_id=1, source_target_pairs={{0,2},{2,4},{4,6},{6,0},{1,3},{3,5},{5,7},{7,1},{8,10},{10,12},{12... | collective-permute-start | bytes 1769480 | tf_op jit(solution)/shard_map/ppermute | solution.py:41
  69.0 41.7 %collective-permute-start.10 = (bf16[72,4096]{1,0:T(8,128)(2,1)S(1)}, bf16[72,4096]{1,0:T(8,128)(2,1)S(1)}, u32[]{:S(2)}, u32[]{:S(2)}) collective-permute-start(bf16[72,4096]{1,0:T(8,128)(2,1)S(1)} %get-tuple-element.27), channel_id=1, source_target_pairs={{0,4},{2,6},{4,0},{6,2},{1,5},{3,7},{5,1},{7,3},{8,12},{10,14},{12... | collective-permute-start | bytes 1769480 | tf_op jit(solution)/shard_map/ppermute | solution.py:41
  72.3 38.4 %collective-permute-start.11 = (bf16[72,4096]{1,0:T(8,128)(2,1)S(1)}, bf16[72,4096]{1,0:T(8,128)(2,1)S(1)}, u32[]{:S(2)}, u32[]{:S(2)}) collective-permute-start(bf16[72,4096]{1,0:T(8,128)(2,1)S(1)} %get-tuple-element.26), channel_id=1, source_target_pairs={{0,6},{2,0},{4,2},{6,4},{1,7},{3,1},{5,3},{7,5},{8,14},{10,8},{12,... | collective-permute-start | bytes 1769480 | tf_op jit(solution)/shard_map/ppermute | solution.py:41
  72.5 38.9 %collective-permute-start.12 = (bf16[72,4096]{1,0:T(8,128)(2,1)S(1)}, bf16[72,4096]{1,0:T(8,128)(2,1)S(1)}, u32[]{:S(2)}, u32[]{:S(2)}) collective-permute-start(bf16[72,4096]{1,0:T(8,128)(2,1)S(1)} %get-tuple-element.25), channel_id=1, source_target_pairs={{0,1},{1,0},{2,3},{3,2},{4,5},{5,4},{6,7},{7,6},{8,9},{9,8},{10,11... | collective-permute-start | bytes 1769480 | tf_op jit(solution)/shard_map/ppermute | solution.py:36
  84.4 3.7 %copy-start.4 = (f32[576,4096]{1,0:T(8,128)}, f32[576,4096]{1,0:T(8,128)S(1)}, u32[]{:S(2)}) copy-start(f32[576,4096]{1,0:T(8,128)S(1)} %fusion.61) | copy-start | bytes 28311556
  89.8 40.9 %collective-permute-start.8 = (bf16[4,72,4096]{2,1,0:T(8,128)(2,1)}, bf16[4,72,4096]{2,1,0:T(8,128)(2,1)}, u32[]{:S(2)}, u32[]{:S(2)}) collective-permute-start(bf16[4,72,4096]{2,1,0:T(8,128)(2,1)} %bitcast.22), channel_id=1, source_target_pairs={{0,1},{1,0},{2,3},{3,2},{4,5},{5,4},{6,7},{7,6},{8,9},{9,8},{10,11... | collective-permute-start | bytes 7077896 | tf_op jit(solution)/shard_map/ppermute | solution.py:36
  90.3 21.2 %collective-permute-start.13 = (bf16[72,4096]{1,0:T(8,128)(2,1)S(1)}, bf16[72,4096]{1,0:T(8,128)(2,1)S(1)}, u32[]{:S(2)}, u32[]{:S(2)}) collective-permute-start(bf16[72,4096]{1,0:T(8,128)(2,1)S(1)} %collective-permute-done.9), channel_id=1, source_target_pairs={{0,1},{1,0},{2,3},{3,2},{4,5},{5,4},{6,7},{7,6},{8,9},{9,8},{10,11... | collective-permute-start | bytes 1769480 | tf_op jit(solution)/shard_map/ppermute | solution.py:36
  110.7 2.0 collective-permute-start.14
  110.8 2.8 collective-permute-start.15
  127.1 3.6 %copy-start.2 = (f32[576,4096]{1,0:T(8,128)}, f32[576,4096]{1,0:T(8,128)S(1)}, u32[]{:S(2)}) copy-start(f32[576,4096]{1,0:T(8,128)S(1)} %convolution_add_fusion) | copy-start | bytes 28311556
  127.4 8.2 %collective-permute-start.16 = (bf16[4,72,4096]{2,1,0:T(8,128)(2,1)S(1)}, bf16[4,72,4096]{2,1,0:T(8,128)(2,1)S(1)}, u32[]{:S(2)}, u32[]{:S(2)}) collective-permute-start(bf16[4,72,4096]{2,1,0:T(8,128)(2,1)S(1)} %bitcast.137), channel_id=1, source_target_pairs={{0,1},{1,0},{2,3},{3,2},{4,5},{5,4},{6,7},{7,6},{8,9},{9,8},{10,11... | collective-permute-start | bytes 7077896 | tf_op jit(solution)/shard_map/ppermute | solution.py:36
  130.7 2.3 slice-start.1
  133.0 3.0 %slice-start = ((f32[576,4096]{1,0:T(8,128)}), f32[288,4096]{1,0:T(8,128)S(1)}, s32[]{:S(2)}) async-start(f32[576,4096]{1,0:T(8,128)} %copy-done.2), calls=%async_computation | async-start | bytes 9437184 | tf_op jit(solution)/shard_map/slice | solution.py:55
  136.9 15.3 %copy-start.9 = (bf16[576,384]{1,0:T(8,128)(2,1)S(1)}, bf16[576,384]{1,0:T(8,128)(2,1)}, u32[]{:S(2)}) copy-start(bf16[576,384]{1,0:T(8,128)(2,1)} %get-tuple-element.15) | copy-start | bytes 1327108
  138.1 26.7 %collective-permute-start.17 = (bf16[72,4096]{1,0:T(8,128)(2,1)}, bf16[72,4096]{1,0:T(8,128)(2,1)}, u32[]{:S(2)}, u32[]{:S(2)}) collective-permute-start(bf16[72,4096]{1,0:T(8,128)(2,1)} %get-tuple-element.24), channel_id=1, source_target_pairs={{0,6},{2,0},{4,2},{6,4},{1,7},{3,1},{5,3},{7,5},{8,14},{10,8},{12,... | collective-permute-start | bytes 1769480 | tf_op jit(solution)/shard_map/ppermute | solution.py:41
  150.6 52.8 %collective-permute-start.18 = (bf16[72,4096]{1,0:T(8,128)(2,1)}, bf16[72,4096]{1,0:T(8,128)(2,1)}, u32[]{:S(2)}, u32[]{:S(2)}) collective-permute-start(bf16[72,4096]{1,0:T(8,128)(2,1)} %get-tuple-element.23), channel_id=1, source_target_pairs={{0,4},{2,6},{4,0},{6,2},{1,5},{3,7},{5,1},{7,3},{8,12},{10,14},{12... | collective-permute-start | bytes 1769480 | tf_op jit(solution)/shard_map/ppermute | solution.py:41
  151.9 51.6 %collective-permute-start.19 = (bf16[72,4096]{1,0:T(8,128)(2,1)}, bf16[72,4096]{1,0:T(8,128)(2,1)}, u32[]{:S(2)}, u32[]{:S(2)}) collective-permute-start(bf16[72,4096]{1,0:T(8,128)(2,1)} %get-tuple-element.22), channel_id=1, source_target_pairs={{0,2},{2,4},{4,6},{6,0},{1,3},{3,5},{5,7},{7,1},{8,10},{10,12},{12... | collective-permute-start | bytes 1769480 | tf_op jit(solution)/shard_map/ppermute | solution.py:41
  205.9 4.9 %copy-start.3 = (bf16[1,128,4096]{2,1,0:T(8,128)(2,1)S(1)}, bf16[1,128,4096]{2,1,0:T(8,128)(2,1)}, u32[]{:S(2)}) copy-start(bf16[1,128,4096]{2,1,0:T(8,128)(2,1)} %param.9) | copy-start | bytes 3145732
  206.1 15.7 %collective-permute-start.21 = (bf16[72,4096]{1,0:T(8,128)(2,1)S(1)}, bf16[72,4096]{1,0:T(8,128)(2,1)S(1)}, u32[]{:S(2)}, u32[]{:S(2)}) collective-permute-start(bf16[72,4096]{1,0:T(8,128)(2,1)S(1)} %get-tuple-element.20), channel_id=1, source_target_pairs={{0,6},{2,0},{4,2},{6,4},{1,7},{3,1},{5,3},{7,5},{8,14},{10,8},{12,... | collective-permute-start | bytes 1769480 | tf_op jit(solution)/shard_map/ppermute | solution.py:41
  206.2 51.4 %collective-permute-start.22 = (bf16[72,4096]{1,0:T(8,128)(2,1)S(1)}, bf16[72,4096]{1,0:T(8,128)(2,1)S(1)}, u32[]{:S(2)}, u32[]{:S(2)}) collective-permute-start(bf16[72,4096]{1,0:T(8,128)(2,1)S(1)} %get-tuple-element.19), channel_id=1, source_target_pairs={{0,4},{2,6},{4,0},{6,2},{1,5},{3,7},{5,1},{7,3},{8,12},{10,14},{12... | collective-permute-start | bytes 1769480 | tf_op jit(solution)/shard_map/ppermute | solution.py:41
  207.1 50.5 %collective-permute-start.23 = (bf16[72,4096]{1,0:T(8,128)(2,1)S(1)}, bf16[72,4096]{1,0:T(8,128)(2,1)S(1)}, u32[]{:S(2)}, u32[]{:S(2)}) collective-permute-start(bf16[72,4096]{1,0:T(8,128)(2,1)S(1)} %get-tuple-element.18), channel_id=1, source_target_pairs={{0,2},{2,4},{4,6},{6,0},{1,3},{3,5},{5,7},{7,1},{8,10},{10,12},{12... | collective-permute-start | bytes 1769480 | tf_op jit(solution)/shard_map/ppermute | solution.py:41
  209.2 52.0 %collective-permute-start.25 = (bf16[2048,384]{1,0:T(8,128)(2,1)S(1)}, bf16[2048,384]{1,0:T(8,128)(2,1)S(1)}, u32[]{:S(2)}, u32[]{:S(2)}) collective-permute-start(bf16[2048,384]{1,0:T(8,128)(2,1)S(1)} %constant_dynamic-slice_fusion), channel_id=1, source_target_pairs={{0,8},{8,0},{1,9},{9,1},{2,10},{10,2},{3,11},{11,3},{4,12},{12,4},... | collective-permute-start | bytes 4718600 | tf_op jit(solution)/shard_map/ppermute | solution.py:66
  214.8 43.1 %copy-start.12 = (f32[1,4096]{1,0:T(1,128)S(1)}, f32[1,4096]{1,0:T(1,128)}, u32[]{:S(2)}) copy-start(f32[1,4096]{1,0:T(1,128)} %param.10) | copy-start | bytes 49156
  214.8 48.1 %collective-permute-start.20 = (bf16[1,128,4096]{2,1,0:T(8,128)(2,1)S(1)}, bf16[1,128,4096]{2,1,0:T(8,128)(2,1)S(1)}, u32[]{:S(2)}, u32[]{:S(2)}) collective-permute-start(bf16[1,128,4096]{2,1,0:T(8,128)(2,1)S(1)} %fusion.2), channel_id=1, source_target_pairs={{0,16},{1,17},{2,18},{3,19},{4,20},{5,21},{6,22},{7,23},{8,24},{9,... | collective-permute-start | bytes 3145736 | tf_op jit(solution)/shard_map/ppermute | solution.py:17
  257.9 1.2 copy-start.7
  259.9 25.5 %collective-permute-start.24 = (bf16[1,128,4096]{2,1,0:T(8,128)(2,1)S(1)}, bf16[1,128,4096]{2,1,0:T(8,128)(2,1)S(1)}, u32[]{:S(2)}, u32[]{:S(2)}) collective-permute-start(bf16[1,128,4096]{2,1,0:T(8,128)(2,1)S(1)} %fusion.21), channel_id=1, source_target_pairs={{16,0},{17,1},{18,2},{19,3},{20,4},{21,5},{22,6},{23,7},{24,8},{25... | collective-permute-start | bytes 3145736 | tf_op jit(solution)/shard_map/ppermute | solution.py:17
  261.2 25.2 %copy-start.1 = (bf16[1,4096,384]{2,1,0:T(8,128)(2,1)S(1)}, bf16[1,4096,384]{2,1,0:T(8,128)(2,1)}, u32[]{:S(2)}) copy-start(bf16[1,4096,384]{2,1,0:T(8,128)(2,1)} %param.13) | copy-start | bytes 9437188
